TPU v7x, 32 devices: a whole 2x2x4 slice. The times are simulated.
32 devices in a mesh: ctx: 16 (over z, x, core), fsdp: 2 (over y).
Axes of the slice: x: 2, y: 2, z: 4, core: 2. Of those that a mesh axis runs over, the one named last changes fastest.
Arguments:
- activations: bfloat16 [4096, 8192], P('ctx', 'fsdp'), may hold values from -8.5 to 8.5
- w_query: bfloat16 [8192, 8192], P('ctx', 'fsdp'), may hold values from -0.044194174 to 0.044194174
- w_key: bfloat16 [8192, 1024], P('ctx', 'fsdp'), may hold values from -0.044194174 to 0.044194174
- w_value: bfloat16 [8192, 1024], P('ctx', 'fsdp'), may hold values from -0.0625 to 0.0625
- seed_words: int32 [1], replicated, may hold values from 0 to 1073741823
- stream_offset: int32 [1], replicated, may hold values from 0 to 1048575
- layer_index: int32 [1], replicated, may hold values from 0 to 79
Outputs:
- attention: bfloat16 [4096, 8192], P('ctx', 'fsdp')
All inputs are finite; a program needn't handle non-finite values.
Results may differ from a plain program's by a relative error of at most 0.007.
Values may be sent and summed in bfloat16 or wider, within the bound.
No kernel may reach another device: no remote copies, remote signals or barrier semaphores. Data moves between devices by JAX's collectives and lax.ppermute only.
A program may use at most 320 MiB of HBM per device.

v0:
```python
import math

import jax
import jax.numpy as jnp
from jax import lax
from jax.sharding import PartitionSpec as P

HQ = 64
KV = 8
HD = 128


golden = -1640531535
drop_rate = 0.1
drop_level = 1677722
rope_theta = 500000.0
masked_score = -1e30


def shift_down(values, amount):
    return lax.shift_right_logical(values, jnp.full(values.shape, amount, jnp.int32))


def scramble(values):
    values = jnp.bitwise_xor(values, shift_down(values, 16))
    values = values * jnp.int32(-2048144789)
    values = jnp.bitwise_xor(values, shift_down(values, 13))
    values = values * jnp.int32(-1028477387)
    return jnp.bitwise_xor(values, shift_down(values, 16))


def head_word(seed_words, stream_offset, layer_index, head_ids):
    inner = scramble(head_ids + stream_offset[0])
    middle = scramble(layer_index[0] * jnp.int32(golden) + inner)
    return scramble(seed_words[0] + middle)


def keep_factor(row_words, key_positions):
    mixed_bits = scramble(row_words[:, None] + key_positions[None, :] * jnp.int32(golden))
    return shift_down(mixed_bits, 8) >= drop_level


def rotate(values, positions):
    half_width = values.shape[-1] // 2
    exponent = jnp.arange(half_width, dtype=jnp.float32) * 2.0 / values.shape[-1]
    frequency = rope_theta ** (-exponent)
    angles = positions.astype(jnp.float32)[:, None] * frequency[None, :]
    cosine = jnp.cos(angles)
    sine_part = jnp.sin(angles)
    first_half = values[..., :half_width]
    second_half = values[..., half_width:]
    return jnp.concatenate(
        [
            first_half * cosine - second_half * sine_part,
            second_half * cosine + first_half * sine_part,
        ],
        axis=-1,
    )


def shards(activations, w_query, w_key, w_value, seed_words, stream_offset, layer_index):
    ctx_count = lax.axis_size("ctx")
    ctx_place = lax.axis_index("ctx")
    fsdp_place = lax.axis_index("fsdp")
    tok_rows = activations.shape[0]
    local_heads = w_query.shape[1] // HD
    local_groups = w_key.shape[1] // HD
    splits = max(1, ctx_count // local_heads)
    owned_heads = max(1, local_heads // ctx_count)
    piece_rows = tok_rows // splits
    query_count = ctx_count * piece_rows
    full_rows = lax.all_gather(activations, "fsdp", axis=1, tiled=True)
    positions = ctx_place * tok_rows + jnp.arange(tok_rows, dtype=jnp.int32)

    def add_rows(running, weight):
        row_count = weight.shape[0]
        shaped = weight.reshape(row_count, running.shape[0], HD)
        return jnp.einsum("tn,nhe->hte", full_rows, shaped, preferred_element_type=jnp.float32)

    zero_query = jnp.zeros((local_heads, tok_rows, HD), jnp.float32)
    zero_group = jnp.zeros((local_groups, tok_rows, HD), jnp.float32)
    query_sum = add_rows(zero_query, lax.all_gather(w_query, "ctx", axis=0, tiled=True))
    key_sum = add_rows(zero_group, lax.all_gather(w_key, "ctx", axis=0, tiled=True))
    value_sum = add_rows(zero_group, lax.all_gather(w_value, "ctx", axis=0, tiled=True))
    keys = rotate(key_sum, positions).astype(jnp.bfloat16)
    values = value_sum.astype(jnp.bfloat16)
    queries = (
        rotate(query_sum, positions)
        .astype(jnp.bfloat16)
        .reshape(local_heads * splits, piece_rows, HD)
    )
    received = lax.all_to_all(queries, "ctx", split_axis=0, concat_axis=1, tiled=True)
    slots = ctx_place * owned_heads + jnp.arange(owned_heads, dtype=jnp.int32)
    head_local = slots // splits
    part_index = slots % splits
    head_global = fsdp_place * local_heads + head_local
    group_local = head_local // (HQ // KV)
    source_rows = jnp.arange(ctx_count, dtype=jnp.int32)[None, :, None] * tok_rows
    inner_rows = (
        part_index[:, None, None] * piece_rows
        + jnp.arange(piece_rows, dtype=jnp.int32)[None, None, :]
    )
    query_pos = (source_rows + inner_rows).reshape(owned_heads, query_count)
    words = head_word(seed_words, stream_offset, layer_index, head_global)
    row_words = scramble(jnp.bitwise_xor(words[:, None], query_pos))
    query_block = math.gcd(query_count, 512)
    score_scale = HD ** (-0.5)
    start_state = (
        jnp.full((owned_heads, query_count), masked_score, jnp.float32),
        jnp.zeros((owned_heads, query_count), jnp.float32),
        jnp.zeros((owned_heads, query_count, HD), jnp.float32),
    )
    key_piece = lax.all_gather(keys, "ctx", axis=1, tiled=True)
    value_piece = lax.all_gather(values, "ctx", axis=1, tiled=True)
    key_count = key_piece.shape[1]
    key_block = math.gcd(key_count, 512)
    key_steps = key_count // key_block
    block_total = query_count // query_block * key_steps
    outcomes = []
    for head_slot in range(owned_heads):
        head_keys = lax.dynamic_index_in_dim(key_piece, group_local[head_slot], 0, keepdims=False)
        head_values = lax.dynamic_index_in_dim(
            value_piece, group_local[head_slot], 0, keepdims=False
        )
        head_queries = received[head_slot]
        head_pos = query_pos[head_slot]
        head_words = row_words[head_slot]

        def advance(flat_index, state):
            query_start = flat_index // key_steps * query_block
            key_start = flat_index % key_steps * key_block
            block_pos = lax.dynamic_slice_in_dim(head_pos, query_start, query_block)
            key_pos = key_start + jnp.arange(key_block, dtype=jnp.int32)
            top_all, sum_all, accum_all = state
            block_queries = lax.dynamic_slice_in_dim(head_queries, query_start, query_block, 0)
            block_words = lax.dynamic_slice_in_dim(head_words, query_start, query_block)
            block_keys = lax.dynamic_slice_in_dim(head_keys, key_start, key_block, 0)
            block_values = lax.dynamic_slice_in_dim(head_values, key_start, key_block, 0)
            scores = (
                jnp.einsum(
                    "qe,ke->qk", block_queries, block_keys, preferred_element_type=jnp.float32
                )
                * score_scale
            )
            visible = key_pos[None, :] <= block_pos[:, None]
            old_top = lax.dynamic_slice_in_dim(top_all, query_start, query_block)
            new_top = jnp.maximum(
                old_top, jnp.max(jnp.where(visible, scores, masked_score), axis=1)
            )
            weights = jnp.where(visible, jnp.exp(scores - new_top[:, None]), 0.0)
            factor = jnp.exp(old_top - new_top)
            dropped = jnp.where(keep_factor(block_words, key_pos), weights, 0.0).astype(
                jnp.bfloat16
            )
            old_sum = lax.dynamic_slice_in_dim(sum_all, query_start, query_block)
            old_accum = lax.dynamic_slice_in_dim(accum_all, query_start, query_block, 0)
            new_sum = old_sum * factor + jnp.sum(weights, axis=1)
            new_accum = old_accum * factor[:, None] + jnp.einsum(
                "qk,ke->qe", dropped, block_values, preferred_element_type=jnp.float32
            )
            return (
                lax.dynamic_update_slice_in_dim(top_all, new_top, query_start, 0),
                lax.dynamic_update_slice_in_dim(sum_all, new_sum, query_start, 0),
                lax.dynamic_update_slice_in_dim(accum_all, new_accum, query_start, 0),
            )

        outcome = lax.fori_loop(
            0,
            block_total,
            advance,
            (start_state[0][head_slot], start_state[1][head_slot], start_state[2][head_slot]),
        )
        outcomes.append(outcome)
    top_all = jnp.stack([outcome[0] for outcome in outcomes])
    sum_all = jnp.stack([outcome[1] for outcome in outcomes])
    accum_all = jnp.stack([outcome[2] for outcome in outcomes])
    attended = (accum_all / (sum_all * (1.0 - drop_rate))[..., None]).astype(jnp.bfloat16)
    returned = lax.all_to_all(attended, "ctx", split_axis=1, concat_axis=0, tiled=True)
    return (
        returned.reshape(local_heads, tok_rows, HD)
        .transpose(1, 0, 2)
        .reshape(tok_rows, local_heads * HD)
    )


def solution(mesh):
    placed = (P("ctx", "fsdp"), P("ctx", "fsdp"), P("ctx", "fsdp"), P("ctx", "fsdp"), P(), P(), P())
    return jax.shard_map(
        shards, mesh=mesh, in_specs=placed, out_specs=P("ctx", "fsdp"), check_vma=False
    )
```

profile of v0, /device:TPU:0, one launch (start us, length us, event | category | flops | bytes accessed | tf_op | source)
XLA Modules:
  0.0 1313.0 jit_solution(4340345081472851318)
XLA Ops:
  9.7 77.4 %all-gather.11.cloned.1.call-done = bf16[8192,512]{1,0:T(8,128)(2,1)} async-done(((bf16[512,512]{1,0:T(8,128)(2,1)}), bf16[8192,512]{1,0:T(8,128)(2,1)}) %all-gather.11.cloned.1.call-update) | async-done | bytes 8388624 | tf_op jit(solution)/shard_map/all_gather | solution.py:83
  87.1 11.6 copy.45
  98.8 44.9 %all-gather.9.cloned.1.call-done = bf16[256,8192]{1,0:T(8,128)(2,1)} async-done(((bf16[256,4096]{1,0:T(8,128)(2,1)}), bf16[256,8192]{1,0:T(8,128)(2,1)}) %all-gather.9.cloned.1.call-update) | async-done | bytes 4194320 | tf_op jit(solution)/shard_map/all_gather | solution.py:72
  143.7 6.9 fusion.72
  151.5 69.3 %all-gather.15.cloned.1.call-done = bf16[8192,512]{1,0:T(8,128)(2,1)} async-done(((bf16[512,512]{1,0:T(8,128)(2,1)}), bf16[8192,512]{1,0:T(8,128)(2,1)}) %all-gather.15.cloned.1.call-update) | async-done | bytes 8388624 | tf_op jit(solution)/shard_map/all_gather | solution.py:84
  220.8 12.1 copy.47
  232.9 7.7 fusion.78
  240.6 306.1 %all-gather.7.cloned.1.call-done = bf16[8192,4096]{1,0:T(8,128)(2,1)} async-done(((bf16[512,4096]{1,0:T(8,128)(2,1)}), bf16[8192,4096]{1,0:T(8,128)(2,1)}) %all-gather.7.cloned.1.call-update) | async-done | bytes 67108880 | tf_op jit(solution)/shard_map/all_gather | solution.py:82
  546.7 82.8 %copy.43 = bf16[8192,4096]{0,1:T(8,128)(2,1)} copy(bf16[8192,4096]{1,0:T(8,128)(2,1)} %all-gather.7.cloned.1.call-done) | data formatting | bytes 134217728 | tf_op jit(solution)/shard_map/all_gather | solution.py:82
  629.4 29.4 %fusion.69 = f32[32,256,128]{1,2,0:T(8,128)} fusion(bf16[8192,32,128]{0,2,1:T(8,128)(2,1)} %bitcast, bf16[256,8192]{1,0:T(8,128)(2,1)} %all-gather.9.cloned.1.call-done), kind=kOutput, calls=%fused_computation.96 | convolution fusion | flops 17179869184 | bytes 75497472 | tf_op jit(solution)/shard_map/tn,nhe->hte/dot_general | solution.py:78
  658.8 2.9 subtract_convert_fusion
  663.2 9.5 all-to-all-start
  679.2 2.8 constant_dynamic-slice_fusion.3
  682.0 2.3 copy.50
  684.3 3.2 constant_dynamic-slice_fusion.2
  687.4 2.3 copy.51
  691.0 2.3 copy.48
  693.2 20.6 %all-to-all-done = bf16[32,256,128]{1,2,0:T(8,128)(2,1)S(1)} async-done(((bf16[32,256,128]{1,2,0:T(8,128)(2,1)}), bf16[32,256,128]{1,2,0:T(8,128)(2,1)S(1)}, u32[]{:S(2)}, u32[]{:S(2)}) %all-to-all-start) | async-done | bytes 2097184 | tf_op jit(solution)/shard_map/all_to_all | solution.py:92
  715.0 2.3 copy.49
  717.4 255.0 %while.39 = (s32[]{:T(128)}, f32[4096]{0:T(1024)S(1)}, f32[4096]{0:T(1024)S(1)}, f32[4096,128]{1,0:T(8,128)S(1)}, s32[4096]{0:T(1024)S(1)}, /*index=5*/bf16[4096...) while((s32[]{:T(128)}, f32[4096]{0:T(1024)S(1)}, ...), condition=%wide.region_7.8_spmd, body=%wide.region_4.7_spmd.sunk | while | flops 140642336 | bytes 4188568 | solution.py:167
  731.5 1.9 fusion.118
  739.4 1.9 fusion.118
  743.4 1.9 fusion.118
  747.4 1.9 fusion.118
  751.4 1.9 fusion.118
  779.3 1.9 fusion.118
  787.3 1.9 fusion.118
  791.3 1.9 fusion.118
  795.3 1.9 fusion.118
  799.2 1.9 fusion.118
  807.2 1.9 fusion.118
  835.1 1.9 fusion.118
  839.1 1.9 fusion.118
  843.1 1.9 fusion.118
  847.1 1.9 fusion.118
  855.1 1.9 fusion.118
  883.0 1.9 fusion.118
  891.0 1.9 fusion.118
  894.9 1.9 fusion.118
  898.9 1.9 fusion.118
  910.9 1.9 fusion.118
  914.9 1.9 fusion.118
  974.2 254.9 %while.38 = (s32[]{:T(128)}, f32[4096]{0:T(1024)S(1)}, f32[4096]{0:T(1024)S(1)}, f32[4096,128]{1,0:T(8,128)S(1)}, s32[4096]{0:T(1024)S(1)}, /*index=5*/bf16[4096...) while((s32[]{:T(128)}, f32[4096]{0:T(1024)S(1)}, ...), condition=%wide.region_3.4_spmd, body=%wide.region_0.3_spmd.sunk | while | flops 140642336 | bytes 4188568 | solution.py:167
  1167.6 1.9 fusion.113
  1171.6 1.9 fusion.113
  1175.6 1.9 fusion.113
  1179.5 1.9 fusion.113
  1183.5 1.9 fusion.113
  1187.5 1.9 fusion.113
  1191.5 1.9 fusion.113
  1195.4 1.9 fusion.113
  1199.4 1.9 fusion.113
  1203.4 1.9 fusion.113
  1207.4 1.9 fusion.113
  1211.3 1.9 fusion.113
  1215.3 1.9 fusion.113
  1219.3 1.9 fusion.113
  1223.3 1.9 fusion.113
  1227.2 1.9 fusion.113
  1229.2 2.0 copy.52
  1231.2 9.3 fusion.68
  1240.5 58.3 %all_to_all.33 = bf16[2,4096,128]{2,0,1:T(2,128)(2,1)S(1)} all-to-all(bf16[2,4096,128]{2,0,1:T(2,128)(2,1)S(1)} %fusion.68), channel_id=1, replica_groups=mesh['ctx'=16,'fsdp'=2] {'ctx'}, dimensions={1} | all-to-all | bytes 4194304 | tf_op jit(solution)/shard_map/all_to_all | solution.py:178
  1299.2 2.9 copy.55
  1302.1 4.1 copy.56
  (1289 shorter events, 443.7 us)
Async XLA Ops:
  6.5 80.6 %all-gather.11.cloned.1.call-start = ((), (), s32[]{:S(2)}) async-start(), calls=%async_computation.4 | async-start | bytes 8912896 | tf_op jit(solution)/shard_map/all_gather | solution.py:83
  7.3 136.5 %all-gather.9.cloned.1.call-start = ((), (), s32[]{:S(2)}) async-start(), calls=%async_computation.3 | async-start | bytes 6291456 | tf_op jit(solution)/shard_map/all_gather | solution.py:72
  8.0 212.8 %all-gather.15.cloned.1.call-start = ((), (), s32[]{:S(2)}) async-start(), calls=%async_computation.6 | async-start | bytes 8912896 | tf_op jit(solution)/shard_map/all_gather | solution.py:84
  8.7 537.9 %all-gather.7.cloned.1.call-start = ((), (), s32[]{:S(2)}) async-start(), calls=%async_computation.2 | async-start | bytes 71303168 | tf_op jit(solution)/shard_map/all_gather | solution.py:82
  9.3 669.9 %all-gather.13.cloned.1.call-start = ((), (), s32[]{:S(2)}) async-start(), calls=%async_computation.5 | async-start | bytes 4456448 | tf_op jit(solution)/shard_map/all_gather | solution.py:113
  151.5 532.8 %all-gather.17.cloned.1.call-start = ((), (), s32[]{:S(2)}) async-start(), calls=%async_computation.7 | async-start | bytes 4456448 | tf_op jit(solution)/shard_map/all_gather | solution.py:114
  663.2 50.6 %all-to-all-start = ((bf16[32,256,128]{1,2,0:T(8,128)(2,1)}), bf16[32,256,128]{1,2,0:T(8,128)(2,1)S(1)}, u32[]{:S(2)}, u32[]{:S(2)}) async-start(bf16[32,256,128]{1,2,0:T(8,128)(2,1)} %pad_maximum_fusion), calls=%async_computation | async-start | bytes 4194304 | tf_op jit(solution)/shard_map/all_to_all | solution.py:92
  972.4 1.7 copy-start
Sparse Core Ops, SparseCore 0:
  9.5 77.5 all-gather.10
  88.7 54.9 all-gather.8
  145.9 74.8 all-gather.14
  222.3 324.3 all-gather.6
  548.7 53.1 all-gather.12
  603.9 51.3 all-gather.16
where the time goes:
time: 1320 us; the launch traced here: 1310 us
  waiting for transfers between devices  521 us (39%)
  matrix products  446 us (34%)
  local copies, waits for them, and re-layouts  156 us (12%)
  other arithmetic  95.8 us (7%)
  blocking collectives  58.3 us (4%)
  between operations  19.1 us (1%)
    all_gather x1, waiting for transfers between devices, shards(): lax.all_gather(w_query, 'ctx', axis=0, tiled=True)  306 us
    dot_general x128, matrix products, advance(): jnp.einsum('qk,ke->qe', dropped, block_values, preferred_element_type=jnp...  238 us
    dot_general x128, matrix products, advance(): jnp.einsum('qe,ke->qk', block_queries, block_keys, preferred_element_type...  164 us
    all_gather x1, local copies, waits for them, and re-layouts, shards(): lax.all_gather(w_query, 'ctx', axis=0, tiled=True)  82.8 us
    all_gather x1, waiting for transfers between devices, shards(): lax.all_gather(w_key, 'ctx', axis=0, tiled=True)  77.4 us
    all_gather x1, waiting for transfers between devices, shards(): lax.all_gather(w_value, 'ctx', axis=0, tiled=True)  69.3 us
    all_to_all x1, blocking collectives, shards(): lax.all_to_all(attended, 'ctx', split_axis=1, concat_axis=0, tiled=True)  58.3 us
    all_gather x1, waiting for transfers between devices, shards(): full_rows = lax.all_gather(activations, 'fsdp', axis=1, tiled=True)  44.9 us
  transfers between devices with their start and end apart: 7, of which 5 were waited for; matrix products, arithmetic and copies ran while one was open for 13% of the time, Pallas kernels for 0%

commit v1 on v0

v1 whole, which is shorter than its diff:
```python
import jax
import jax.numpy as jnp
import numpy as np
from jax import lax
from jax.sharding import Mesh
from jax.sharding import PartitionSpec as P

HQ = 64
KV = 8
HD = 128


golden = -1640531535
drop_rate = 0.1
drop_level = 1677722
rope_theta = 500000.0
masked_score = -1e30


def shift_down(values, amount):
    return lax.shift_right_logical(values, jnp.full(values.shape, amount, jnp.int32))


def scramble(values):
    values = jnp.bitwise_xor(values, shift_down(values, 16))
    values = values * jnp.int32(-2048144789)
    values = jnp.bitwise_xor(values, shift_down(values, 13))
    values = values * jnp.int32(-1028477387)
    return jnp.bitwise_xor(values, shift_down(values, 16))


def head_word(seed_words, stream_offset, layer_index, head_ids):
    inner = scramble(head_ids + stream_offset[0])
    middle = scramble(layer_index[0] * jnp.int32(golden) + inner)
    return scramble(seed_words[0] + middle)


def rotation(positions):
    half_width = HD // 2
    exponent = jnp.arange(half_width, dtype=jnp.float32) * 2.0 / HD
    frequency = rope_theta ** (-exponent)
    angles = positions.astype(jnp.float32)[:, None] * frequency[None, :]
    return jnp.cos(angles), jnp.sin(angles)


def rotate(values, cosine, sine_part):
    half_width = HD // 2
    first_half = values[..., :half_width]
    second_half = values[..., half_width:]
    return jnp.concatenate(
        [
            first_half * cosine - second_half * sine_part,
            second_half * cosine + first_half * sine_part,
        ],
        axis=-1,
    )


def shards(activations, w_query, w_key, w_value, seed_words, stream_offset, layer_index):
    n_g = lax.axis_size("cg")
    n_t = lax.axis_size("ct")
    g = lax.axis_index("cg")
    t = lax.axis_index("ct")
    f = lax.axis_index("fsdp")
    tok = activations.shape[0]
    d_rows = w_query.shape[0]
    group_heads = HQ // KV
    local_heads = w_query.shape[1] // HD
    qcols = group_heads * HD
    rows = n_g * tok

    full_rows = lax.all_gather(activations, "fsdp", axis=1, tiled=True)
    grp_rows = lax.all_gather(full_rows, "cg", axis=0, tiled=True)

    local_w = jnp.concatenate(
        [
            w_query.reshape(d_rows, n_g, qcols),
            w_key.reshape(d_rows, n_g, HD),
            w_value.reshape(d_rows, n_g, HD),
        ],
        axis=2,
    )
    mine = lax.all_to_all(local_w, "cg", split_axis=1, concat_axis=0, tiled=True)
    mine = mine.reshape(n_g, d_rows, qcols + 2 * HD)
    every = lax.all_gather(mine, "ct", axis=0, tiled=False)
    every = every.transpose(1, 0, 2, 3).reshape(n_g * n_t * d_rows, qcols + 2 * HD)

    mixed = jnp.dot(grp_rows, every, preferred_element_type=jnp.float32)
    chunk_of_row = n_t * (jnp.arange(rows, dtype=jnp.int32) // tok) + t
    positions = chunk_of_row * tok + jnp.arange(rows, dtype=jnp.int32) % tok
    cosine, sine_part = rotation(positions)
    queries = rotate(
        mixed[:, :qcols].reshape(rows, group_heads, HD), cosine[:, None, :], sine_part[:, None, :]
    ).astype(jnp.bfloat16)
    keys = rotate(mixed[:, qcols : qcols + HD], cosine, sine_part).astype(jnp.bfloat16)
    values = mixed[:, qcols + HD :].astype(jnp.bfloat16)

    pair = jnp.stack([keys, values], axis=1)
    pair = lax.all_gather(pair, "ct", axis=0, tiled=False)
    pair = pair.reshape(n_t, n_g, tok, 2, HD).transpose(1, 0, 2, 3, 4)
    pair = pair.reshape(n_g * n_t * tok, 2, HD)
    all_keys = pair[:, 0]
    all_values = pair[:, 1]

    head_global = f * local_heads + g * group_heads + jnp.arange(group_heads, dtype=jnp.int32)
    words = head_word(seed_words, stream_offset, layer_index, head_global)
    score_scale = HD ** (-0.5)
    pieces = []
    for chunk in range(n_g):
        span = n_t * (chunk + 1) * tok
        query_pos = (n_t * chunk + t) * tok + jnp.arange(tok, dtype=jnp.int32)
        key_pos = jnp.arange(span, dtype=jnp.int32)
        chunk_queries = queries[chunk * tok : (chunk + 1) * tok]
        scores = (
            jnp.einsum(
                "qhe,ke->hqk",
                chunk_queries,
                all_keys[:span],
                preferred_element_type=jnp.float32,
            )
            * score_scale
        )
        visible = key_pos[None, None, :] <= query_pos[None, :, None]
        highest = jnp.max(jnp.where(visible, scores, masked_score), axis=2, keepdims=True)
        weights = jnp.where(visible, jnp.exp(scores - highest), 0.0)
        summed = jnp.sum(weights, axis=2)
        row_words = scramble(jnp.bitwise_xor(words[:, None], query_pos[None, :]))
        mixed_bits = scramble(row_words[:, :, None] + (key_pos * jnp.int32(golden))[None, None, :])
        keep = shift_down(mixed_bits, 8) >= drop_level
        dropped = jnp.where(keep, weights, 0.0).astype(jnp.bfloat16)
        attended = jnp.einsum(
            "hqk,ke->hqe", dropped, all_values[:span], preferred_element_type=jnp.float32
        )
        result = (attended / (summed * (1.0 - drop_rate))[:, :, None]).astype(jnp.bfloat16)
        pieces.append(result.transpose(1, 0, 2).reshape(tok, qcols))
    out_rows = jnp.stack(pieces, axis=0)
    returned = lax.all_to_all(out_rows, "cg", split_axis=0, concat_axis=2, tiled=True)
    return returned.reshape(tok, n_g * qcols)


def solution(mesh):
    ctx = mesh.shape["ctx"]
    fsdp = mesh.shape["fsdp"]
    n_g = KV // fsdp
    n_t = ctx // n_g
    order = [mesh.axis_names.index("ctx"), mesh.axis_names.index("fsdp")]
    devices = np.transpose(mesh.devices, order).reshape(n_g, n_t, fsdp)
    grid = Mesh(devices, ("cg", "ct", "fsdp"))
    spec = P(("cg", "ct"), "fsdp")
    placed = (spec, spec, spec, spec, P(), P(), P())
    return jax.shard_map(shards, mesh=grid, in_specs=placed, out_specs=spec, check_vma=False)
```

time: 1320 us -> 807 us (0.61)
  matrix products: 446 us -> 117 us
  local copies, waits for them, and re-layouts: 156 us -> 58 us
  other arithmetic: 95.8 us -> 39.6 us
    dot_general x259 -> x6, matrix products: 446 us -> 76.8 us  [the longest x4 40.3 us: shards(): jnp.einsum('hqk,ke->hqe', dropped, all_values[:span], preferred_element_t...]
    all_gather x3 -> x0, local copies, waits for them, and re-layouts: 106 us -> none  [the longest x1 82.8 us: shards(): lax.all_gather(w_query, 'ctx', axis=0, tiled=True)]
    all_to_all x1, waiting for transfers between devices: 20.6 us -> 115 us  [shards(): lax.all_to_all(local_w, 'cg', split_axis=1, concat_axis=0, tiled=True)]
    all_gather x5 -> x3, waiting for transfers between devices: 453 us -> 397 us  [the longest x1 271 us: shards(): grp_rows = lax.all_gather(full_rows, 'cg', axis=0, tiled=True)]
    dynamic_update_slice x256 -> x0, other arithmetic: 49.7 us -> none  [the longest x128 24.9 us: advance(): lax.dynamic_update_slice_in_dim(sum_all, new_sum, query_start, 0)]
    all_gather x1, waiting for transfers between devices: 44.9 us -> 0.02 us  [shards(): full_rows = lax.all_gather(activations, 'fsdp', axis=1, tiled=True)]
    sub x0 -> x3, matrix products: none -> 40.1 us  [shards(): weights = jnp.where(visible, jnp.exp(scores - highest), 0.0)]
    dynamic_slice x262 -> x0, local copies, waits for them, and re-layouts: 33.7 us -> none  [the longest x128 9.97 us: advance(): block_pos = lax.dynamic_slice_in_dim(head_pos, query_start, query_block)]
  transfers between devices with their start and end apart: 7 -> 5, of which waited for: 5 -> 4; matrix products, arithmetic and copies ran while one was open for 13% -> 6% of each run, Pallas kernels for 0% -> 0%
where the time goes in v1:
time: 807 us; the launch traced here: 804 us
  waiting for transfers between devices  514 us (64%)
  matrix products  117 us (14%)
  local copies, waits for them, and re-layouts  58 us (7%)
  blocking collectives  53 us (7%)
  other arithmetic  39.6 us (5%)
  between operations  15.6 us (2%)
    all_gather x1, waiting for transfers between devices, shards(): grp_rows = lax.all_gather(full_rows, 'cg', axis=0, tiled=True)  271 us
    all_gather x1, waiting for transfers between devices, shards(): every = lax.all_gather(mine, 'ct', axis=0, tiled=False)  125 us
    all_to_all x1, waiting for transfers between devices, shards(): lax.all_to_all(local_w, 'cg', split_axis=1, concat_axis=0, tiled=True)  115 us
    all_to_all x1, blocking collectives, shards(): lax.all_to_all(out_rows, 'cg', split_axis=0, concat_axis=2, tiled=True)  53 us
    dot_general x4, matrix products, shards(): jnp.einsum('hqk,ke->hqe', dropped, all_values[:span], preferred_element_t...  40.3 us
    sub x3, matrix products, shards(): weights = jnp.where(visible, jnp.exp(scores - highest), 0.0)  40.1 us
    dot_general x1, matrix products, shards(): mixed = jnp.dot(grp_rows, every, preferred_element_type=jnp.float32)  27.1 us
    transpose x1, local copies, waits for them, and re-layouts, shards(): every.transpose(1, 0, 2, 3).reshape(n_g * n_t * d_rows, qcols + 2 * HD)  17.9 us
  transfers between devices with their start and end apart: 5, of which 4 were waited for; matrix products, arithmetic and copies ran while one was open for 6% of the time, Pallas kernels for 0%

profile of v1, /device:TPU:0, one launch (start us, length us, event | category | flops | bytes accessed | tf_op | source)
XLA Modules:
  0.0 803.6 jit_solution(11053821689720977109)
XLA Ops:
  6.5 1.3 copy.72
  7.8 1.3 copy.71
  9.0 6.5 copy.70
  15.5 6.8 pad_maximum_fusion
  22.3 6.3 all-to-all-start
  28.6 0.0 all-gather.7.cloned.1.call-start
  28.6 0.7 all-gather.7.cloned.1.call-update
  29.3 0.0 all-gather.11.cloned.1.call-start
  29.4 115.3 %all-to-all-done = bf16[512,4,1280]{0,2,1:T(8,128)(2,1)} async-done(((bf16[512,4,1280]{0,2,1:T(8,128)(2,1)}), bf16[512,4,1280]{0,2,1:T(8,128)(2,1)}, u32[]{:S(2)}, u32[]{:S(2)}) %all-to-all-start) | async-done | bytes 5242912 | tf_op jit(solution)/shard_map/all_to_all | solution.py:83
  144.7 7.9 copy.73
  152.6 0.0 all-gather.11.cloned.1.call-update
  152.6 0.0 all-gather.9.cloned.1.call-start
  152.7 0.0 all-gather.7.cloned.1.call-done
  152.7 0.7 all-gather.9.cloned.1.call-update
  153.4 0.2 all-gather.13.cloned.1.call-start
  155.6 0.6 iota_multiply_fusion.2
  156.2 0.6 iota_multiply_fusion.1
  156.8 0.7 shift-right-logical_xor_fusion.21
  157.5 0.9 iota_compare_fusion.3
  158.4 125.2 %all-gather.11.cloned.1.call-done = bf16[16,512,1,1280]{3,1,2,0:T(8,128)(2,1)} async-done(((bf16[4,512,1,1280]{3,1,2,0:T(8,128)(2,1)}), bf16[16,512,1,1280]{3,1,2,0:T(8,128)(2,1)}) %all-gather.11.cloned.1.call-update) | async-done | bytes 20971536 | tf_op jit(solution)/shard_map/all_gather | solution.py:85
  283.5 17.9 %copy.74 = bf16[4,4,512,1280]{3,2,1,0:T(8,128)(2,1)} copy(bf16[4,4,512,1280]{3,2,0,1:T(8,128)(2,1)} %bitcast.184) | data formatting | bytes 41943040 | tf_op jit(solution)/shard_map/transpose | solution.py:86
  301.5 270.5 %all-gather.9.cloned.1.call-done = bf16[1024,8192]{1,0:T(8,128)(2,1)} async-done(((bf16[256,8192]{1,0:T(8,128)(2,1)}), bf16[1024,8192]{1,0:T(8,128)(2,1)}) %all-gather.9.cloned.1.call-update) | async-done | bytes 16777232 | tf_op jit(solution)/shard_map/all_gather | solution.py:73
  572.0 27.1 %convolution_bitcast_fusion = f32[1024,1280]{0,1:T(8,128)S(1)} fusion(bf16[8192,1280]{1,0:T(8,128)(2,1)} %bitcast.185, bf16[1024,8192]{1,0:T(8,128)(2,1)} %all-gather.9.cloned.1.call-done), kind=kOutput, calls=%fused_computation.73 | convolution fusion | flops 21474836480 | bytes 42991616 | tf_op jit(solution)/shard_map/dot_general | solution.py:88
  599.1 0.0 copy-start
  599.1 2.3 copy-done
  601.4 1.1 multiply_cosine_fusion
  602.5 0.8 pad_maximum_fusion.3
  603.4 0.0 all-gather.13.cloned.1.call-update
  603.4 0.0 slice-start
  603.4 0.6 iota_multiply_fusion.3
  604.0 1.2 iota_compare_fusion.2
  605.2 1.4 iota_compare_fusion.1
  606.6 1.7 iota_compare_fusion
  608.2 1.8 fusion.146
  610.0 3.8 copy.103
  613.8 2.7 copy.102
  616.6 0.2 copy.79
  616.8 0.2 copy.77
  617.0 6.0 subtract_convert_fusion
  622.9 1.4 all-gather.13.cloned.1.call-done
  624.3 4.5 reshape.476
  628.8 4.8 copy.75
  633.6 9.5 %fusion.67 = f32[2048,256,8]{1,0,2:T(8,128)} fusion(bf16[1024,8,64]{2,0,1:T(8,128)(2,1)S(1)} %get-tuple-element.5, bf16[1024,8,64]{2,0,1:T(8,128)(2,1)} %get-tuple-element.6, bf16[4096,2,128]{2,0,1:T(8,128)(2,1)} %bitcast.190), kind=kOutput, calls=%fused_computation.111 | convolution fusion | flops 1074790400 | bytes 20447232 | tf_op jit(solution)/shard_map/qhe,ke->hqk/dot_general | solution.py:115
  643.1 0.0 copy-done.2
  643.1 18.1 %fusion.147 = (f32[8,256]{1,0:T(8,128)S(1)}, bf16[8,256,4096]{1,2,0:T(8,128)(2,1)}) fusion(pred[256,4096]{0,1:T(8,128)(4,1)S(1)} %copy-done.2, bf16[4096,2,128]{2,0,1:T(8,128)(2,1)} %bitcast.191, bf16[1024,8,64]{2,0,1:T(8,128)(2,1)} %get-tuple-element.6, bf16[1024,8,64]{2,0,1:T(8,128)(2,1)S(1)} %get-tuple-element.5), kind=kOutput, calls=%fused_computation.231 | convolution fusion | flops 4355788800 | bytes 29368320 | tf_op jit(solution)/shard_map/sub | solution.py:125
  661.2 14.7 %fusion.148 = (f32[8,256]{1,0:T(8,128)S(1)}, bf16[8,256,3072]{1,2,0:T(8,128)(2,1)}) fusion(pred[256,3072]{0,1:T(8,128)(4,1)} %iota_compare_fusion.1, bf16[4096,2,128]{2,0,1:T(8,128)(2,1)} %bitcast.192, bf16[1024,8,64]{2,0,1:T(8,128)(2,1)S(1)} %get-tuple-element.5, bf16[1024,8,64]{2,0,1:T(8,128)(2,1)} %get-tuple-element.6), kind=kOutput, calls=%fused_computation.232 | convolution fusion | flops 3267365888 | bytes 24125440 | tf_op jit(solution)/shard_map/sub | solution.py:125
  675.9 17.0 %fusion.153 = (f32[8,256]{1,0:T(8,128)S(1)}, bf16[8,256,2048]{1,2,0:T(8,128)(2,1)}) fusion(f32[2048,256,8]{1,0,2:T(8,128)} %fusion.67, pred[256,2048]{0,1:T(8,128)(4,1)S(1)} %copy-done.3), kind=kOutput, calls=%fused_computation.233 | output fusion | flops 29362176 | bytes 25698304 | tf_op jit(solution)/shard_map/sub | solution.py:125
  692.9 7.4 fusion.154
  700.2 0.0 copy-done.10
  700.2 0.0 copy-start.5
  700.2 0.0 copy-start.9
  700.2 16.9 %divide_convert_fusion = bf16[256,8,128]{0,2,1:T(8,128)(2,1)S(1)} fusion(bf16[4096,2,128]{2,0,1:T(8,128)(2,1)} %bitcast.194, bf16[8,256,4096]{1,2,0:T(8,128)(2,1)} %get-tuple-element.20, s32[4096]{0:T(1024)S(1)} %iota_multiply_fusion, s32[8,256]{1,0:T(8,128)S(1)} %copy-done.10, f32[256,8]{0,1:T(8,128)S(1)} %multiply_bitcast_fusion), kind=kOutput, calls=%fused_computation.99 | convolution fusion | flops 2248671232 | bytes 18382848 | tf_op jit(solution)/shard_map/hqk,ke->hqe/dot_general | solution.py:131
  717.1 0.0 copy-done.1
  717.1 0.0 copy-done.5
  717.2 0.0 copy-done.9
  717.2 0.0 copy-start.6
  717.2 0.0 copy-start.8
  717.2 0.0 copy-start.13
  717.2 13.2 %divide_convert_fusion.1 = bf16[256,8,128]{0,2,1:T(8,128)(2,1)S(1)} fusion(bf16[8,256,3072]{1,2,0:T(8,128)(2,1)} %get-tuple-element.22, s32[3072]{0:T(1024)S(1)} %copy-done.5, s32[8,256]{1,0:T(8,128)S(1)} %copy-done.9, bf16[4096,2,128]{2,0,1:T(8,128)(2,1)S(1)} %bitcast.195, f32[256,8]{0,1:T(8,128)S(1)} %multiply_bitcast_fusion.1), kind=kOutput, calls=%fused_computation.100 | convolution fusion | flops 1686634496 | bytes 13922304 | tf_op jit(solution)/shard_map/hqk,ke->hqe/dot_general | solution.py:131
  730.4 6.7 divide_convert_fusion.2
  737.2 3.5 divide_convert_fusion.3
  740.7 0.3 pad_maximum_fusion.1
  741.0 53.0 %all_to_all.30 = bf16[4,256,1024]{1,2,0:T(8,128)(2,1)S(1)} all-to-all(bf16[4,256,1024]{1,2,0:T(8,128)(2,1)S(1)} %pad_maximum_fusion.1), channel_id=1, replica_groups=mesh['cg'=4,'ct'=4,'fsdp'=2] {'cg'}, dimensions={0} | all-to-all | bytes 4194304 | tf_op jit(solution)/shard_map/all_to_all | solution.py:137
  794.0 2.8 copy.101
  (28 shorter events, 0.1 us)
Async XLA Ops:
  22.3 122.4 %all-to-all-start = ((bf16[512,4,1280]{0,2,1:T(8,128)(2,1)}), bf16[512,4,1280]{0,2,1:T(8,128)(2,1)}, u32[]{:S(2)}, u32[]{:S(2)}) async-start(bf16[512,4,1280]{0,2,1:T(8,128)(2,1)} %pad_maximum_fusion), calls=%async_computation | async-start | bytes 10485760 | tf_op jit(solution)/shard_map/all_to_all | solution.py:83
  28.6 124.1 %all-gather.7.cloned.1.call-start = ((), (), s32[]{:S(2)}) async-start(), calls=%async_computation.2 | async-start | bytes 6291456 | tf_op jit(solution)/shard_map/all_gather | solution.py:72
  29.3 254.2 %all-gather.11.cloned.1.call-start = ((), (), s32[]{:S(2)}) async-start(), calls=%async_computation.4 | async-start | bytes 26214400 | tf_op jit(solution)/shard_map/all_gather | solution.py:85
  152.6 419.4 %all-gather.9.cloned.1.call-start = ((), (), s32[]{:S(2)}) async-start(), calls=%async_computation.3 | async-start | bytes 20971520 | tf_op jit(solution)/shard_map/all_gather | solution.py:73
  153.4 471.0 %all-gather.13.cloned.1.call-start = ((), (), s32[]{:S(2)}) async-start(), calls=%async_computation.5 | async-start | bytes 2621440 | tf_op jit(solution)/shard_map/all_gather | solution.py:99
  599.1 2.3 copy-start
  603.4 4.8 slice-start
  633.6 9.5 %copy-start.2 = (pred[256,4096]{0,1:T(8,128)(4,1)S(1)}, pred[256,4096]{0,1:T(8,128)(4,1)}, u32[]{:S(2)}) copy-start(pred[256,4096]{0,1:T(8,128)(4,1)} %iota_compare_fusion) | copy-start | bytes 3145732
  661.1 14.7 %copy-start.3 = (pred[256,2048]{0,1:T(8,128)(4,1)S(1)}, pred[256,2048]{0,1:T(8,128)(4,1)}, u32[]{:S(2)}) copy-start(pred[256,2048]{0,1:T(8,128)(4,1)} %iota_compare_fusion.2) | copy-start | bytes 1572868
  675.8 17.0 %copy-start.4 = (pred[256,1024]{0,1:T(8,128)(4,1)S(1)}, pred[256,1024]{0,1:T(8,128)(4,1)}, u32[]{:S(2)}) copy-start(pred[256,1024]{0,1:T(8,128)(4,1)} %iota_compare_fusion.3) | copy-start | bytes 786436
  692.9 7.4 copy-start.10
  700.2 16.9 %copy-start.1 = (bf16[4,4,256,2,128]{4,2,1,0,3:T(8,128)(2,1)S(1)}, bf16[4,4,256,2,128]{4,2,1,0,3:T(8,128)(2,1)}, u32[]{:S(2)}) copy-start(bf16[4,4,256,2,128]{4,2,1,0,3:T(8,128)(2,1)} %copy.75) | copy-start | bytes 6291460
  700.2 16.9 %copy-start.5 = (s32[3072]{0:T(1024)S(1)}, s32[3072]{0:T(1024)}, u32[]{:S(2)}) copy-start(s32[3072]{0:T(1024)} %iota_multiply_fusion.1) | copy-start | bytes 36868
  700.2 16.9 %copy-start.9 = (s32[8,256]{1,0:T(8,128)S(1)}, s32[8,256]{1,0:T(8,128)}, u32[]{:S(2)}) copy-start(s32[8,256]{1,0:T(8,128)} %get-tuple-element.17) | copy-start | bytes 24580
  717.2 13.2 %copy-start.6 = (s32[2048]{0:T(1024)S(1)}, s32[2048]{0:T(1024)}, u32[]{:S(2)}) copy-start(s32[2048]{0:T(1024)} %iota_multiply_fusion.2) | copy-start | bytes 24580
  717.2 13.2 %copy-start.8 = (s32[8,256]{1,0:T(8,128)S(1)}, s32[8,256]{1,0:T(8,128)}, u32[]{:S(2)}) copy-start(s32[8,256]{1,0:T(8,128)} %get-tuple-element.16) | copy-start | bytes 24580
  717.2 13.2 %copy-start.13 = (bf16[8,256,2048]{1,2,0:T(8,128)(2,1)S(1)}, bf16[8,256,2048]{1,2,0:T(8,128)(2,1)}, u32[]{:S(2)}) copy-start(bf16[8,256,2048]{1,2,0:T(8,128)(2,1)} %get-tuple-element.24) | copy-start | bytes 25165828
  730.4 6.8 copy-start.7
  730.4 6.8 copy-start.11
  730.4 6.8 copy-start.12
Sparse Core Ops, SparseCore 0:
  31.0 58.3 all-gather.6
  152.7 130.7 all-gather.10
  285.1 286.8 all-gather.8
  603.5 20.7 all-gather.12

commit v2 on v1

v2 whole, which is shorter than its diff:
```python
import jax
import jax.numpy as jnp
import numpy as np
from jax import lax
from jax.sharding import Mesh
from jax.sharding import PartitionSpec as P

HQ = 64
KV = 8
HD = 128


golden = -1640531535
drop_rate = 0.1
drop_level = 1677722
rope_theta = 500000.0
masked_score = -1e30


def shift_down(values, amount):
    return lax.shift_right_logical(values, jnp.full(values.shape, amount, jnp.int32))


def scramble(values):
    values = jnp.bitwise_xor(values, shift_down(values, 16))
    values = values * jnp.int32(-2048144789)
    values = jnp.bitwise_xor(values, shift_down(values, 13))
    values = values * jnp.int32(-1028477387)
    return jnp.bitwise_xor(values, shift_down(values, 16))


def head_word(seed_words, stream_offset, layer_index, head_ids):
    inner = scramble(head_ids + stream_offset[0])
    middle = scramble(layer_index[0] * jnp.int32(golden) + inner)
    return scramble(seed_words[0] + middle)


def rotation(positions):
    half_width = HD // 2
    exponent = jnp.arange(half_width, dtype=jnp.float32) * 2.0 / HD
    frequency = rope_theta ** (-exponent)
    angles = positions.astype(jnp.float32)[:, None] * frequency[None, :]
    return jnp.cos(angles), jnp.sin(angles)


def rotate(values, cosine, sine_part):
    half_width = HD // 2
    first_half = values[..., :half_width]
    second_half = values[..., half_width:]
    return jnp.concatenate(
        [
            first_half * cosine - second_half * sine_part,
            second_half * cosine + first_half * sine_part,
        ],
        axis=-1,
    )


def attend(queries, keys, values, query_pos, words, spans):
    score_scale = HD ** (-0.5)
    pieces = []
    for first, count, span in spans:
        block_pos = query_pos[first : first + count]
        key_pos = jnp.arange(span, dtype=jnp.int32)
        scores = (
            jnp.einsum(
                "qhe,ke->hqk",
                queries[first : first + count],
                keys[:span],
                preferred_element_type=jnp.float32,
            )
            * score_scale
        )
        visible = key_pos[None, None, :] <= block_pos[None, :, None]
        highest = jnp.max(jnp.where(visible, scores, masked_score), axis=2, keepdims=True)
        weights = jnp.where(visible, jnp.exp(scores - highest), 0.0)
        summed = jnp.sum(weights, axis=2)
        row_words = scramble(jnp.bitwise_xor(words[:, None], block_pos[None, :]))
        mixed_bits = scramble(row_words[:, :, None] + (key_pos * jnp.int32(golden))[None, None, :])
        keep = shift_down(mixed_bits, 8) >= drop_level
        dropped = jnp.where(keep, weights, 0.0).astype(jnp.bfloat16)
        attended = jnp.einsum(
            "hqk,ke->qhe", dropped, values[:span], preferred_element_type=jnp.float32
        )
        pieces.append(
            (attended / (summed * (1.0 - drop_rate)).T[:, :, None]).astype(jnp.bfloat16)
        )
    return jnp.concatenate(pieces, axis=0)


def shards(activations, w_query, w_key, w_value, seed_words, stream_offset, layer_index):
    n_t = lax.axis_size("ct")
    n_g = lax.axis_size("cg")
    t = lax.axis_index("ct")
    g = lax.axis_index("cg")
    f = lax.axis_index("fsdp")
    tok = activations.shape[0]
    d_rows = w_query.shape[0]
    group_heads = HQ // KV
    local_heads = w_query.shape[1] // HD
    qcols = group_heads * HD
    width = qcols + 2 * HD
    rows = n_g * tok
    length = n_t * rows

    half_rows = lax.all_gather(activations, "cg", axis=0, tiled=True)
    grp_rows = lax.all_gather(half_rows, "fsdp", axis=1, tiled=True)

    local_w = jnp.concatenate(
        [
            w_query.reshape(d_rows, n_g, qcols),
            w_key.reshape(d_rows, n_g, HD),
            w_value.reshape(d_rows, n_g, HD),
        ],
        axis=2,
    )
    received = [lax.dynamic_index_in_dim(local_w, g, 1, keepdims=False)]
    for shift in range(1, n_g):
        outgoing = lax.dynamic_index_in_dim(local_w, (g + shift) % n_g, 1, keepdims=False)
        perm = [(i, (i + shift) % n_g) for i in range(n_g)]
        received.append(lax.ppermute(outgoing, "cg", perm))
    by_shift = jnp.stack(received, axis=0)
    mine = jnp.take(by_shift, (g - jnp.arange(n_g, dtype=jnp.int32)) % n_g, axis=0)
    every = lax.all_gather(mine, "ct", axis=0, tiled=False).reshape(n_t * n_g * d_rows, width)

    mixed = jnp.dot(grp_rows, every, preferred_element_type=jnp.float32)
    positions = t * rows + jnp.arange(rows, dtype=jnp.int32)
    cosine, sine_part = rotation(positions)
    queries = rotate(
        mixed[:, :qcols].reshape(rows, group_heads, HD), cosine[:, None, :], sine_part[:, None, :]
    ).astype(jnp.bfloat16)
    keys = rotate(mixed[:, qcols : qcols + HD], cosine, sine_part).astype(jnp.bfloat16)
    values = mixed[:, qcols + HD :].astype(jnp.bfloat16)

    pair = lax.all_gather(jnp.stack([keys, values], axis=1), "ct", axis=0, tiled=True)
    all_keys = pair[:, 0]
    all_values = pair[:, 1]

    if group_heads % n_t == 0:
        owned = group_heads // n_t
        spread = lax.all_to_all(
            queries.reshape(rows, n_t, owned, HD), "ct", split_axis=1, concat_axis=0, tiled=True
        ).reshape(length, owned, HD)
        head_local = g * group_heads + t * owned + jnp.arange(owned, dtype=jnp.int32)
        words = head_word(seed_words, stream_offset, layer_index, f * local_heads + head_local)
        block = min(length, 512)
        spans = [(i * block, block, (i + 1) * block) for i in range(length // block)]
        out = attend(
            spread, all_keys, all_values, jnp.arange(length, dtype=jnp.int32), words, spans
        )
        out = lax.all_to_all(
            out.reshape(n_t, rows, owned, HD), "ct", split_axis=0, concat_axis=2, tiled=True
        ).reshape(rows, qcols)
    else:
        head_local = g * group_heads + jnp.arange(group_heads, dtype=jnp.int32)
        words = head_word(seed_words, stream_offset, layer_index, f * local_heads + head_local)
        out = attend(queries, all_keys, all_values, positions, words, [(0, rows, length)])
        out = out.reshape(rows, qcols)
    returned = lax.all_to_all(
        out.reshape(n_g, tok, qcols), "cg", split_axis=0, concat_axis=2, tiled=True
    )
    return returned.reshape(tok, n_g * qcols)


def solution(mesh):
    ctx = mesh.shape["ctx"]
    fsdp = mesh.shape["fsdp"]
    n_g = KV // fsdp
    n_t = ctx // n_g
    order = [mesh.axis_names.index("ctx"), mesh.axis_names.index("fsdp")]
    devices = np.transpose(mesh.devices, order).reshape(n_t, n_g, fsdp)
    grid = Mesh(devices, ("ct", "cg", "fsdp"))
    spec = P(("ct", "cg"), "fsdp")
    placed = (spec, spec, spec, spec, P(), P(), P())
    return jax.shard_map(shards, mesh=grid, in_specs=placed, out_specs=spec, check_vma=False)
```

time: 807 us -> 960 us (1.19)
  waiting for transfers between devices: 514 us -> 636 us
  blocking collectives: 53 us -> 80.4 us
  local copies, waits for them, and re-layouts: 58 us -> 45.1 us
  other arithmetic: 39.6 us -> 50 us
    all_gather x4, waiting for transfers between devices: 397 us -> 519 us  [the longest x1 358 us: shards(): lax.all_gather(mine, 'ct', axis=0, tiled=False)]
    ppermute x0 -> x3, waiting for transfers between devices: none -> 50.8 us  [shards(): received.append(lax.ppermute(outgoing, 'cg', perm))]
    all_to_all x1, waiting for transfers between devices: 115 us -> 65.1 us  [shards(): lax.all_to_all(queries.reshape(rows, n_t, owned, HD), 'ct', split_axis=1,...]
    all_to_all x1 -> x2, blocking collectives: 53 us -> 80.4 us  [the longest x1 51.1 us: shards(): lax.all_to_all(out.reshape(n_t, rows, owned, HD), 'ct', split_axis=0, con...]
    transpose x2 -> x0, local copies, waits for them, and re-layouts: 22.7 us -> none  [the longest x1 17.9 us: shards(): every.transpose(1, 0, 2, 3).reshape(n_g * n_t * d_rows, qcols + 2 * HD)]
    sub x3 -> x6, matrix products: 40.1 us -> 53.4 us  [attend(): weights = jnp.where(visible, jnp.exp(scores - highest), 0.0)]
    sub x1 -> x2, other arithmetic: 17 us -> 5.83 us  [attend(): weights = jnp.where(visible, jnp.exp(scores - highest), 0.0)]
    unnamed x33 -> x55, local copies, waits for them, and re-layouts: 17.9 us -> 7.08 us
  transfers between devices with their start and end apart: 5 -> 8, of which waited for: 4 -> 7; matrix products, arithmetic and copies ran while one was open for 6% -> 7% of each run, Pallas kernels for 0% -> 0%
where the time goes in v2:
time: 960 us; the launch traced here: 953 us
  waiting for transfers between devices  636 us (66%)
  matrix products  120 us (12%)
  blocking collectives  80.4 us (8%)
  other arithmetic  50 us (5%)
  local copies, waits for them, and re-layouts  45.1 us (5%)
  between operations  15.8 us (2%)
    all_gather x1, waiting for transfers between devices, shards(): lax.all_gather(mine, 'ct', axis=0, tiled=False)  358 us
    all_gather x1, waiting for transfers between devices, shards(): grp_rows = lax.all_gather(half_rows, 'fsdp', axis=1, tiled=True)  97.9 us
    all_to_all x1, waiting for transfers between devices, shards(): lax.all_to_all(queries.reshape(rows, n_t, owned, HD), 'ct', split_axis=1,...  65.1 us
    all_gather x1, waiting for transfers between devices, shards(): half_rows = lax.all_gather(activations, 'cg', axis=0, tiled=True)  62.6 us
    sub x6, matrix products, attend(): weights = jnp.where(visible, jnp.exp(scores - highest), 0.0)  53.4 us
    all_to_all x1, blocking collectives, shards(): lax.all_to_all(out.reshape(n_t, rows, owned, HD), 'ct', split_axis=0, con...  51.1 us
    ppermute x3, waiting for transfers between devices, shards(): received.append(lax.ppermute(outgoing, 'cg', perm))  50.8 us
    dot_general x8, matrix products, attend(): jnp.einsum('hqk,ke->qhe', dropped, values[:span], preferred_element_type=...  36.3 us
  transfers between devices with their start and end apart: 8, of which 7 were waited for; matrix products, arithmetic and copies ran while one was open for 7% of the time, Pallas kernels for 0%

profile of v2, /device:TPU:0, one launch (start us, length us, event | category | flops | bytes accessed | tf_op | source)
XLA Modules:
  0.0 953.0 jit_solution(8433113393694348878)
XLA Ops:
  6.5 0.7 all-gather.7.cloned.1.call-update
  7.3 62.6 %all-gather.7.cloned.1.call-done = bf16[1024,4096]{1,0:T(8,128)(2,1)} async-done(((bf16[256,4096]{1,0:T(8,128)(2,1)}), bf16[1024,4096]{1,0:T(8,128)(2,1)}) %all-gather.7.cloned.1.call-update) | async-done | bytes 8388624 | tf_op jit(solution)/shard_map/all_gather | solution.py:106
  70.1 6.5 copy.73
  77.1 5.7 pad_maximum_fusion
  82.8 2.1 constant_dynamic-slice_fusion.3
  84.9 2.6 copy.77
  87.8 2.5 copy.78
  90.5 1.4 copy.79
  91.9 1.3 collective-permute-start.2
  93.2 0.6 copy.76
  93.9 21.6 %collective-permute-done = bf16[512,1280]{1,0:T(8,128)(2,1)} collective-permute-done((bf16[512,1280]{1,0:T(8,128)(2,1)}, bf16[512,1280]{1,0:T(8,128)(2,1)}, u32[]{:S(2)}, u32[]{:S(2)}) %collective-permute-start) | collective-permute-done | bytes 1310752 | tf_op jit(solution)/shard_map/ppermute | solution.py:121
  115.4 6.9 collective-permute-done.1
  122.3 22.3 %collective-permute-done.2 = bf16[512,1280]{1,0:T(8,128)(2,1)} collective-permute-done((bf16[512,1280]{1,0:T(8,128)(2,1)}, bf16[512,1280]{1,0:T(8,128)(2,1)}, u32[]{:S(2)}, u32[]{:S(2)}) %collective-permute-start.2) | collective-permute-done | bytes 1310752 | tf_op jit(solution)/shard_map/ppermute | solution.py:121
  144.7 5.2 pad_maximum_fusion.1
  149.9 5.7 gather_fusion
  155.5 5.3 bitcast_select_fusion.24
  163.6 0.6 iota_multiply_fusion.2
  165.5 0.7 shift-right-logical_xor_fusion.24
  166.2 0.8 iota_compare_fusion.7
  167.0 1.2 iota_compare_fusion.6
  168.2 1.8 iota_compare_fusion.4
  170.0 2.4 iota_compare_fusion.2
  172.5 97.9 %all-gather.9.cloned.1.call-done = bf16[1024,8192]{1,0:T(8,128)(2,1)} async-done(((bf16[1024,4096]{1,0:T(8,128)(2,1)}), bf16[1024,8192]{1,0:T(8,128)(2,1)}) %all-gather.9.cloned.1.call-update) | async-done | bytes 16777232 | tf_op jit(solution)/shard_map/all_gather | solution.py:107
  270.4 358.5 %all-gather.5.cloned.1.call-done = bf16[4,4,512,1280]{3,2,1,0:T(8,128)(2,1)} async-done(((bf16[1,4,512,1280]{3,2,1,0:T(8,128)(2,1)}), bf16[4,4,512,1280]{3,2,1,0:T(8,128)(2,1)}) %all-gather.5.cloned.1.call-update) | async-done | bytes 20971536 | tf_op jit(solution)/shard_map/all_gather | solution.py:124
  628.9 27.2 %convolution_bitcast_fusion = f32[1024,1280]{0,1:T(8,128)S(1)} fusion(bf16[8192,1280]{1,0:T(8,128)(2,1)} %bitcast.392, bf16[1024,8192]{1,0:T(8,128)(2,1)} %all-gather.9.cloned.1.call-done), kind=kOutput, calls=%fused_computation.119 | convolution fusion | flops 21474836480 | bytes 42991616 | tf_op jit(solution)/shard_map/dot_general | solution.py:126
  656.1 2.3 slice.265
  658.4 1.1 fusion.189
  659.5 0.8 pad_maximum_fusion.3
  660.4 3.9 subtract_convert_fusion
  664.3 2.0 copy.80
  666.3 1.8 copy.81
  668.1 4.1 pad_maximum_fusion.2
  672.2 3.8 all-to-all-start
  676.0 1.5 iota_compare_fusion.5
  677.5 1.0 iota_compare_fusion.3
  678.6 3.1 iota_compare_fusion
  681.7 2.7 iota_compare_fusion.1
  684.4 65.1 %all-to-all-done = bf16[1024,4,2,128]{3,0,2,1:T(8,128)(2,1)S(1)} async-done(((bf16[1024,4,2,128]{3,0,2,1:T(8,128)(2,1)}), bf16[1024,4,2,128]{3,0,2,1:T(8,128)(2,1)S(1)}, u32[]{:S(2)}, u32[]{:S(2)}) %all-to-all-start) | async-done | bytes 2097184 | tf_op jit(solution)/shard_map/all_to_all | solution.py:141
  749.5 1.5 copy.82
  750.9 13.2 %fusion.317 = (f32[2,512]{1,0:T(2,128)S(1)}, bf16[2,512,4096]{1,2,0:T(8,128)(2,1)}) fusion(pred[512,4096]{0,1:T(8,128)(4,1)} %iota_compare_fusion, bf16[4096,2,128]{0,2,1:T(8,128)(2,1)} %all-gather.11.cloned.1.call-done, bf16[4096,2,128]{2,0,1:T(8,128)(2,1)} %bitcast.379), kind=kOutput, calls=%fused_computation.439 | convolution fusion | flops 2176847872 | bytes 15208448 | tf_op jit(solution)/shard_map/sub | solution.py:76
  764.1 10.0 %fusion.312 = (f32[2,512]{1,0:T(2,128)S(1)}, bf16[2,512,3584]{1,2,0:T(8,128)(2,1)}) fusion(pred[512,3584]{0,1:T(8,128)(4,1)} %iota_compare_fusion.1, bf16[4096,2,128]{0,2,1:T(8,128)(2,1)} %all-gather.11.cloned.1.call-done, bf16[4096,2,128]{2,0,1:T(8,128)(2,1)S(1)} %bitcast.380), kind=kOutput, calls=%fused_computation.438 | convolution fusion | flops 1904741888 | bytes 13373440 | tf_op jit(solution)/shard_map/sub | solution.py:76
  774.2 10.2 %fusion.307 = (f32[2,512]{1,0:T(2,128)S(1)}, bf16[2,512,3072]{1,2,0:T(8,128)(2,1)}) fusion(pred[512,3072]{0,1:T(8,128)(4,1)} %iota_compare_fusion.2, bf16[4096,2,128]{0,2,1:T(8,128)(2,1)} %all-gather.11.cloned.1.call-done, bf16[4096,2,128]{2,0,1:T(8,128)(2,1)S(1)} %bitcast.381), kind=kOutput, calls=%fused_computation.437 | convolution fusion | flops 1632635904 | bytes 11538432 | tf_op jit(solution)/shard_map/sub | solution.py:76
  784.4 7.2 fusion.302
  791.6 8.3 fusion.297
  799.9 2.1 fusion.159
  802.0 4.6 fusion.296
  806.7 4.5 fusion.291
  811.2 1.5 fusion.162
  812.7 1.2 fusion.290
  813.9 1.7 fusion.117
  815.6 2.5 fusion.143
  818.1 3.3 fusion.137
  821.4 4.1 fusion.134
  825.6 5.3 fusion.131
  830.9 5.6 fusion.140
  836.6 6.6 fusion.149
  843.2 7.2 fusion.146
  850.4 4.7 copy.127
  855.1 51.1 %all_to_all.45 = bf16[4,1024,2,128]{3,2,1,0:T(2,128)(2,1)S(1)} all-to-all(bf16[4,1024,2,128]{3,2,1,0:T(2,128)(2,1)S(1)} %bitcast.374), channel_id=1, replica_groups=mesh['ct'=4,'cg'=4,'fsdp'=2] {'ct'}, dimensions={0} | all-to-all | bytes 4194304 | tf_op jit(solution)/shard_map/all_to_all | solution.py:151
  906.2 1.4 copy.100
  907.7 2.7 reshape_reshape.3
  910.4 29.3 %all_to_all.46 = bf16[4,256,1024]{2,1,0:T(8,128)(2,1)S(1)} all-to-all(bf16[4,256,1024]{2,1,0:T(8,128)(2,1)} %reshape_reshape.3), channel_id=1, replica_groups=mesh['ct'=4,'cg'=4,'fsdp'=2] {'cg'}, dimensions={0} | all-to-all | bytes 4194304 | tf_op jit(solution)/shard_map/all_to_all | solution.py:159
  939.6 2.6 copy.101
  942.3 4.1 copy.102
  (94 shorter events, 3.1 us)
Async XLA Ops:
  6.5 63.4 %all-gather.7.cloned.1.call-start = ((), (), s32[]{:S(2)}) async-start(), calls=%async_computation.4 | async-start | bytes 10485760 | tf_op jit(solution)/shard_map/all_gather | solution.py:106
  7.3 263.1 %all-gather.9.cloned.1.call-start = ((), (), s32[]{:S(2)}) async-start(), calls=%async_computation.5 | async-start | bytes 25165824 | tf_op jit(solution)/shard_map/all_gather | solution.py:107
  70.0 558.9 %all-gather.5.cloned.1.call-start = ((), (), s32[]{:S(2)}) async-start(), calls=%async_computation.3 | async-start | bytes 26214400 | tf_op jit(solution)/shard_map/all_gather | solution.py:124
  70.0 6.6 copy-start.2
  70.1 6.8 copy-start.3
  87.5 27.9 %collective-permute-start = (bf16[512,1280]{1,0:T(8,128)(2,1)}, bf16[512,1280]{1,0:T(8,128)(2,1)}, u32[]{:S(2)}, u32[]{:S(2)}) collective-permute-start(bf16[512,1280]{1,0:T(8,128)(2,1)} %bitcast.389), channel_id=1, source_target_pairs={{0,2},{2,4},{4,6},{6,0},{1,3},{3,5},{5,7},{7,1},{8,10},{10,12},{12... | collective-permute-start | bytes 3932168 | tf_op jit(solution)/shard_map/ppermute | solution.py:121
  90.3 32.0 %collective-permute-start.1 = (bf16[512,1280]{1,0:T(8,128)(2,1)}, bf16[512,1280]{1,0:T(8,128)(2,1)}, u32[]{:S(2)}, u32[]{:S(2)}) collective-permute-start(bf16[512,1280]{1,0:T(8,128)(2,1)} %bitcast.390), channel_id=1, source_target_pairs={{0,4},{2,6},{4,0},{6,2},{1,5},{3,7},{5,1},{7,3},{8,12},{10,14},{12... | collective-permute-start | bytes 3932168 | tf_op jit(solution)/shard_map/ppermute | solution.py:121
  91.9 52.8 %collective-permute-start.2 = (bf16[512,1280]{1,0:T(8,128)(2,1)}, bf16[512,1280]{1,0:T(8,128)(2,1)}, u32[]{:S(2)}, u32[]{:S(2)}) collective-permute-start(bf16[512,1280]{1,0:T(8,128)(2,1)} %bitcast.391), channel_id=1, source_target_pairs={{0,6},{2,0},{4,2},{6,4},{1,7},{3,1},{5,3},{7,5},{8,14},{10,8},{12,... | collective-permute-start | bytes 3932168 | tf_op jit(solution)/shard_map/ppermute | solution.py:121
  160.9 590.0 %all-gather.11.cloned.1.call-start = ((), (), s32[]{:S(2)}) async-start(), calls=%async_computation.6 | async-start | bytes 2621440 | tf_op jit(solution)/shard_map/all_gather | solution.py:135
  672.2 77.3 %all-to-all-start = ((bf16[1024,4,2,128]{3,0,2,1:T(8,128)(2,1)}), bf16[1024,4,2,128]{3,0,2,1:T(8,128)(2,1)S(1)}, u32[]{:S(2)}, u32[]{:S(2)}) async-start(bf16[1024,4,2,128]{3,0,2,1:T(8,128)(2,1)} %pad_maximum_fusion.2), calls=%async_computation | async-start | bytes 4194304 | tf_op jit(solution)/shard_map/all_to_all | solution.py:141
  750.9 13.2 %copy-start = (bf16[4,1024,1,2,128]{4,1,0,3,2:T(8,128)(2,1)S(1)}, bf16[4,1024,1,2,128]{4,1,0,3,2:T(8,128)(2,1)}, u32[]{:S(2)}) copy-start(bf16[4,1024,1,2,128]{4,1,0,3,2:T(8,128)(2,1)} %copy.82) | copy-start | bytes 6291460
  799.9 2.1 copy-start.1
  802.0 4.7 copy-start.4
  806.7 6.0 copy-start.5
  811.2 2.7 copy-start.6
  813.9 1.7 copy-start.16
  815.6 2.5 copy-start.15
  818.1 3.3 copy-start.17
  818.1 7.4 slice-start
  821.4 4.1 copy-start.10
  821.4 4.1 copy-start.14
  821.4 4.1 slice-start.1
  821.4 9.4 slice-start.2
  825.5 5.3 copy-start.9
  825.5 5.3 copy-start.13
  825.5 5.3 slice-start.3
  825.6 11.0 %slice-start.4 = ((s8[7340032]{0:T(1024)(128)(4,1)}), s8[4194304]{0:T(1024)(128)(4,1)S(1)}, s32[]{:S(2)}) async-start(s8[7340032]{0:T(1024)(128)(4,1)} %bitcast.397), calls=%async_computation.11 | async-start | bytes 8388608
  830.8 5.7 copy-start.8
  830.9 5.7 copy-start.12
  830.9 5.7 slice-start.5
  830.9 12.3 %slice-start.6 = ((s8[8388608]{0:T(1024)(128)(4,1)}), s8[4194304]{0:T(1024)(128)(4,1)S(1)}, s32[]{:S(2)}) async-start(s8[8388608]{0:T(1024)(128)(4,1)} %bitcast.399), calls=%async_computation.13 | async-start | bytes 8388608
  836.6 6.6 copy-start.7
  836.6 6.6 copy-start.11
  836.6 6.6 slice-start.7
Sparse Core Ops, SparseCore 0:
  8.9 60.9 all-gather.6
  71.5 198.8 all-gather.8
  272.0 356.8 all-gather.4
  660.5 79.2 all-gather.10

commit v3 on v1

--- a/solution.py
+++ b/solution.py
@@ -69,8 +69,20 @@
     qcols = group_heads * HD
     rows = n_g * tok
 
-    full_rows = lax.all_gather(activations, "fsdp", axis=1, tiled=True)
-    grp_rows = lax.all_gather(full_rows, "cg", axis=0, tiled=True)
+    own_half = [activations]
+    for shift in range(1, n_g):
+        perm = [(i, (i + shift) % n_g) for i in range(n_g)]
+        own_half.append(lax.ppermute(activations, "cg", perm))
+    own_half = jnp.concatenate(own_half, axis=0)
+    if lax.axis_size("fsdp") == 2:
+        other_half = lax.ppermute(own_half, "fsdp", [(0, 1), (1, 0)])
+        grp_rows = jnp.where(
+            f == 0,
+            jnp.concatenate([own_half, other_half], axis=1),
+            jnp.concatenate([other_half, own_half], axis=1),
+        )
+    else:
+        grp_rows = lax.all_gather(own_half, "fsdp", axis=1, tiled=True)
 
     local_w = jnp.concatenate(
         [
@@ -80,12 +92,19 @@
         ],
         axis=2,
     )
-    mine = lax.all_to_all(local_w, "cg", split_axis=1, concat_axis=0, tiled=True)
-    mine = mine.reshape(n_g, d_rows, qcols + 2 * HD)
+    received = [lax.dynamic_index_in_dim(local_w, g, 1, keepdims=False)]
+    for shift in range(1, n_g):
+        outgoing = lax.dynamic_index_in_dim(local_w, (g + shift) % n_g, 1, keepdims=False)
+        perm = [(i, (i + shift) % n_g) for i in range(n_g)]
+        received.append(lax.ppermute(outgoing, "cg", perm))
+    by_shift = jnp.stack(received, axis=0)
+    back = (g - jnp.arange(n_g, dtype=jnp.int32)) % n_g
+    mine = jnp.take(by_shift, back, axis=0)
     every = lax.all_gather(mine, "ct", axis=0, tiled=False)
     every = every.transpose(1, 0, 2, 3).reshape(n_g * n_t * d_rows, qcols + 2 * HD)
 
     mixed = jnp.dot(grp_rows, every, preferred_element_type=jnp.float32)
+    mixed = jnp.take(mixed.reshape(n_g, tok, -1), back, axis=0).reshape(rows, -1)
     chunk_of_row = n_t * (jnp.arange(rows, dtype=jnp.int32) // tok) + t
     positions = chunk_of_row * tok + jnp.arange(rows, dtype=jnp.int32) % tok
     cosine, sine_part = rotation(positions)

time: 807 us -> 781 us (0.968)
  waiting for transfers between devices: 514 us -> 416 us
  starting transfers between devices: 6.61 us -> 39.6 us
  local copies, waits for them, and re-layouts: 58 us -> 80.2 us
  other arithmetic: 39.6 us -> 51.6 us
    ppermute x0 -> x7, waiting for transfers between devices: none -> 368 us  [the longest x1 159 us: shards(): other_half = lax.ppermute(own_half, 'fsdp', [(0, 1), (1, 0)])]
    all_gather x2 -> x0, waiting for transfers between devices: 271 us -> none  [the longest x1 271 us: shards(): grp_rows = lax.all_gather(full_rows, 'cg', axis=0, tiled=True)]
    all_gather x1, waiting for transfers between devices: 125 us -> 0.01 us  [shards(): every = lax.all_gather(mine, 'ct', axis=0, tiled=False)]
    all_to_all x1 -> x0, waiting for transfers between devices: 115 us -> none  [shards(): lax.all_to_all(local_w, 'cg', split_axis=1, concat_axis=0, tiled=True)]
    all_gather x1, waiting for transfers between devices: 1.37 us -> 47.5 us  [shards(): pair = lax.all_gather(pair, 'ct', axis=0, tiled=False)]
    ppermute x0 -> x7, starting transfers between devices: none -> 39.5 us  [the longest x3 31 us: shards(): own_half.append(lax.ppermute(activations, 'cg', perm))]
    gather x0 -> x3, local copies, waits for them, and re-layouts: none -> 17.4 us  [the longest x2 11.7 us: shards(): jnp.take(mixed.reshape(n_g, tok, -1), back, axis=0).reshape(rows, -1)]
    dynamic_slice x0 -> x5, local copies, waits for them, and re-layouts: none -> 8.96 us  [the longest x3 6.34 us: shards(): lax.dynamic_index_in_dim(local_w, (g + shift) % n_g, 1, keepdims=False)]
  transfers between devices with their start and end apart: 5 -> 9, of which waited for: 4 -> 6; matrix products, arithmetic and copies ran while one was open for 6% -> 7% of each run, Pallas kernels for 0% -> 0%
where the time goes in v3:
time: 781 us; the launch traced here: 775 us
  waiting for transfers between devices  416 us (53%)
  matrix products  119 us (15%)
  local copies, waits for them, and re-layouts  80.2 us (10%)
  blocking collectives  53 us (7%)
  other arithmetic  51.6 us (7%)
  starting transfers between devices  39.6 us (5%)
  between operations  16.3 us (2%)
    ppermute x1, waiting for transfers between devices, shards(): other_half = lax.ppermute(own_half, 'fsdp', [(0, 1), (1, 0)])  159 us
    ppermute x3, waiting for transfers between devices, shards(): own_half.append(lax.ppermute(activations, 'cg', perm))  130 us
    ppermute x3, waiting for transfers between devices, shards(): received.append(lax.ppermute(outgoing, 'cg', perm))  78.9 us
    all_to_all x1, blocking collectives, shards(): lax.all_to_all(out_rows, 'cg', split_axis=0, concat_axis=2, tiled=True)  53 us
    all_gather x1, waiting for transfers between devices, shards(): pair = lax.all_gather(pair, 'ct', axis=0, tiled=False)  47.5 us
    sub x3, matrix products, shards(): weights = jnp.where(visible, jnp.exp(scores - highest), 0.0)  40.1 us
    dot_general x4, matrix products, shards(): jnp.einsum('hqk,ke->hqe', dropped, all_values[:span], preferred_element_t...  36.4 us
    dot_general x1, matrix products, shards(): mixed = jnp.dot(grp_rows, every, preferred_element_type=jnp.float32)  33.2 us
  transfers between devices with their start and end apart: 9, of which 6 were waited for; matrix products, arithmetic and copies ran while one was open for 7% of the time, Pallas kernels for 0%

profile of v3, /device:TPU:0, one launch (start us, length us, event | category | flops | bytes accessed | tf_op | source)
XLA Modules:
  0.0 775.3 jit_solution(7432776120720817894)
XLA Ops:
  6.5 6.6 copy.57
  13.1 0.2 copy.58
  13.3 0.2 copy.59
  13.6 5.2 pad_maximum_fusion
  18.8 2.0 constant_dynamic-slice_fusion.3
  20.8 2.5 copy.61
  23.3 3.0 collective-permute-start.4
  26.3 2.4 copy.62
  28.7 2.6 collective-permute-start.5
  31.3 1.4 copy.63
  32.8 1.3 collective-permute-start.6
  34.1 0.6 copy.60
  34.8 23.6 %collective-permute-done.4 = bf16[512,1280]{1,0:T(8,128)(2,1)} collective-permute-done((bf16[512,1280]{1,0:T(8,128)(2,1)}, bf16[512,1280]{1,0:T(8,128)(2,1)}, u32[]{:S(2)}, u32[]{:S(2)}) %collective-permute-start.4) | collective-permute-done | bytes 1310752 | tf_op jit(solution)/shard_map/ppermute | solution.py:99
  58.4 55.3 %collective-permute-done.5 = bf16[512,1280]{1,0:T(8,128)(2,1)} collective-permute-done((bf16[512,1280]{1,0:T(8,128)(2,1)}, bf16[512,1280]{1,0:T(8,128)(2,1)}, u32[]{:S(2)}, u32[]{:S(2)}) %collective-permute-start.5) | collective-permute-done | bytes 1310752 | tf_op jit(solution)/shard_map/ppermute | solution.py:99
  113.7 5.2 pad_maximum_fusion.1
  118.9 5.7 gather_fusion
  124.6 5.5 bitcast_select_fusion.16
  130.2 28.6 %collective-permute-start = (bf16[256,4096]{1,0:T(8,128)(2,1)S(1)}, bf16[256,4096]{1,0:T(8,128)(2,1)S(1)}, u32[]{:S(2)}, u32[]{:S(2)}) collective-permute-start(bf16[256,4096]{1,0:T(8,128)(2,1)S(1)} %copy-done.2), channel_id=1, source_target_pairs={{0,8},{8,16},{16,24},{24,0},{1,9},{9,17},{17,25},{25,1},{2,10},{10... | collective-permute-start | bytes 6291464 | tf_op jit(solution)/shard_map/ppermute | solution.py:75
  158.8 1.6 collective-permute-start.1
  160.4 0.8 collective-permute-start.2
  161.3 1.4 constant_dynamic-update-slice_fusion.3
  162.7 43.8 %collective-permute-done = bf16[256,4096]{1,0:T(8,128)(2,1)S(1)} collective-permute-done((bf16[256,4096]{1,0:T(8,128)(2,1)S(1)}, bf16[256,4096]{1,0:T(8,128)(2,1)S(1)}, u32[]{:S(2)}, u32[]{:S(2)}) %collective-permute-start) | collective-permute-done | bytes 2097184 | tf_op jit(solution)/shard_map/ppermute | solution.py:75
  206.6 1.5 constant_dynamic-update-slice_fusion.2
  208.1 86.6 %collective-permute-done.1 = bf16[256,4096]{1,0:T(8,128)(2,1)S(1)} collective-permute-done((bf16[256,4096]{1,0:T(8,128)(2,1)S(1)}, bf16[256,4096]{1,0:T(8,128)(2,1)S(1)}, u32[]{:S(2)}, u32[]{:S(2)}) %collective-permute-start.1) | collective-permute-done | bytes 2097184 | tf_op jit(solution)/shard_map/ppermute | solution.py:75
  294.7 1.4 constant_dynamic-update-slice_fusion.1
  296.1 1.5 constant_dynamic-update-slice_fusion
  297.6 1.5 collective-permute-start.3
  301.3 0.6 iota_multiply_fusion.2
  301.9 0.6 iota_multiply_fusion.1
  302.5 0.7 shift-right-logical_xor_fusion.21
  303.1 0.9 iota_compare_fusion.3
  304.0 17.6 %copy.64 = bf16[4,4,512,1280]{3,2,1,0:T(8,128)(2,1)} copy(bf16[4,4,512,1280]{3,2,0,1:T(8,128)(2,1)} %bitcast.193) | data formatting | bytes 41943040 | tf_op jit(solution)/shard_map/transpose | solution.py:104
  321.6 158.6 %collective-permute-done.3 = bf16[1024,4096]{1,0:T(8,128)(2,1)} collective-permute-done((bf16[1024,4096]{1,0:T(8,128)(2,1)}, bf16[1024,4096]{1,0:T(8,128)(2,1)}, u32[]{:S(2)}, u32[]{:S(2)}) %collective-permute-start.3) | collective-permute-done | bytes 8388640 | tf_op jit(solution)/shard_map/ppermute | solution.py:78
  480.2 33.2 %fusion.24 = f32[4,256,1280]{2,1,0:T(8,128)} fusion(bf16[8192,1280,1]{1,0,2:T(8,128)(2,1)} %bitcast.194, bf16[4,256,4096]{2,1,0:T(8,128)(2,1)} %bitcast.4, bf16[4,256,4096]{2,1,0:T(8,128)(2,1)} %bitcast.3, pred[]{:T(512)S(6)} %eq.11), kind=kOutput, calls=%fused_computation.42 | convolution fusion | flops 21550333952 | bytes 42991616 | tf_op jit(solution)/shard_map/dot_general | solution.py:106
  513.4 5.7 gather_fusion.1
  519.2 5.9 copy.65
  525.1 3.1 broadcast_select_fusion
  528.3 2.3 copy-done
  530.5 1.1 multiply_cosine_fusion
  531.7 0.8 pad_maximum_fusion.4
  532.6 0.6 iota_multiply_fusion
  533.2 1.2 iota_compare_fusion.2
  534.3 1.4 iota_compare_fusion.1
  535.7 1.7 iota_compare_fusion
  537.4 1.8 fusion.157
  539.2 3.9 copy.93
  543.1 2.7 copy.94
  546.0 0.2 copy.70
  546.2 6.0 subtract_convert_fusion
  552.2 47.5 %all-gather.6.cloned.1.call-done = bf16[4096,2,128]{0,2,1:T(8,128)(2,1)} async-done(((bf16[1024,2,128]{0,2,1:T(8,128)(2,1)}), bf16[4096,2,128]{0,2,1:T(8,128)(2,1)}) %all-gather.6.cloned.1.call-update) | async-done | bytes 2097168 | tf_op jit(solution)/shard_map/all_gather | solution.py:118
  599.7 4.5 reshape.546
  604.2 4.9 copy.66
  609.1 9.4 %fusion.74 = f32[2048,256,8]{1,0,2:T(8,128)} fusion(bf16[1024,8,64]{2,0,1:T(8,128)(2,1)S(1)} %get-tuple-element.5, bf16[1024,8,64]{2,0,1:T(8,128)(2,1)} %get-tuple-element.6, bf16[4096,2,128]{2,0,1:T(8,128)(2,1)} %bitcast.200), kind=kOutput, calls=%fused_computation.123 | convolution fusion | flops 1074790400 | bytes 20447232 | tf_op jit(solution)/shard_map/qhe,ke->hqk/dot_general | solution.py:134
  618.5 7.4 fusion.165
  625.9 16.6 %fusion.164 = (f32[8,256]{1,0:T(8,128)S(1)}, bf16[8,256,2048]{1,2,0:T(8,128)(2,1)}) fusion(f32[2048,256,8]{1,0,2:T(8,128)} %fusion.74, pred[256,2048]{0,1:T(8,128)(4,1)S(1)} %copy-done.6), kind=kOutput, calls=%fused_computation.267 | output fusion | flops 29362176 | bytes 25698304 | tf_op jit(solution)/shard_map/sub | solution.py:144
  642.5 14.7 %fusion.159 = (f32[8,256]{1,0:T(8,128)S(1)}, bf16[8,256,3072]{1,2,0:T(8,128)(2,1)}) fusion(pred[256,3072]{0,1:T(8,128)(4,1)} %iota_compare_fusion.1, bf16[4096,2,128]{2,0,1:T(8,128)(2,1)} %bitcast.202, bf16[1024,8,64]{2,0,1:T(8,128)(2,1)S(1)} %get-tuple-element.5, bf16[1024,8,64]{2,0,1:T(8,128)(2,1)} %get-tuple-element.6), kind=kOutput, calls=%fused_computation.266 | convolution fusion | flops 3267365888 | bytes 24125440 | tf_op jit(solution)/shard_map/sub | solution.py:144
  657.2 17.9 %fusion.158 = (f32[8,256]{1,0:T(8,128)S(1)}, bf16[8,256,4096]{1,2,0:T(8,128)(2,1)}) fusion(pred[256,4096]{0,1:T(8,128)(4,1)S(1)} %copy-done.3, bf16[4096,2,128]{2,0,1:T(8,128)(2,1)} %bitcast.203, bf16[1024,8,64]{2,0,1:T(8,128)(2,1)} %get-tuple-element.6, bf16[1024,8,64]{2,0,1:T(8,128)(2,1)S(1)} %get-tuple-element.5), kind=kOutput, calls=%fused_computation.265 | convolution fusion | flops 4355788800 | bytes 29368320 | tf_op jit(solution)/shard_map/sub | solution.py:144
  675.3 5.8 divide_convert_fusion.3
  681.2 6.7 divide_convert_fusion.2
  688.1 10.2 %divide_convert_fusion.1 = bf16[256,8,128]{0,2,1:T(8,128)(2,1)S(1)} fusion(bf16[8,256,3072]{1,2,0:T(8,128)(2,1)S(1)} %bitcast.220, s32[3072]{0:T(1024)S(1)} %copy-done.9, s32[8,256]{1,0:T(8,128)S(1)} %copy-done.12, bf16[4096,2,128]{2,0,1:T(8,128)(2,1)S(1)} %bitcast.206, f32[256,8]{0,1:T(8,128)S(1)} %multiply_bitcast_fusion.1), kind=kOutput, calls=%fused_computation.112 | convolution fusion | flops 1686634496 | bytes 13922304 | tf_op jit(solution)/shard_map/hqk,ke->hqe/dot_general | solution.py:150
  698.4 13.6 %divide_convert_fusion = bf16[256,8,128]{0,2,1:T(8,128)(2,1)S(1)} fusion(bf16[4096,2,128]{2,0,1:T(8,128)(2,1)S(1)} %bitcast.207, bf16[8,256,4096]{1,2,0:T(8,128)(2,1)S(1)} %bitcast.218, s32[4096]{0:T(1024)S(1)} %copy-done.8, s32[8,256]{1,0:T(8,128)S(1)} %copy-done.11, f32[256,8]{0,1:T(8,128)S(1)} %multiply_bitcast_fusion), kind=kOutput, calls=%fused_computation.111 | convolution fusion | flops 2248671232 | bytes 18382848 | tf_op jit(solution)/shard_map/hqk,ke->hqe/dot_general | solution.py:150
  711.9 0.3 pad_maximum_fusion.2
  712.2 53.0 %all_to_all.15 = bf16[4,256,1024]{1,2,0:T(8,128)(2,1)S(1)} all-to-all(bf16[4,256,1024]{1,2,0:T(8,128)(2,1)S(1)} %pad_maximum_fusion.2), channel_id=1, replica_groups=mesh['cg'=4,'ct'=4,'fsdp'=2] {'cg'}, dimensions={0} | all-to-all | bytes 4194304 | tf_op jit(solution)/shard_map/all_to_all | solution.py:156
  765.2 2.8 copy.92
  (74 shorter events, 0.6 us)
Async XLA Ops:
  6.5 6.6 copy-start.4
  6.5 6.8 copy-start.5
  6.5 297.5 %all-gather.4.cloned.1.call-start = ((), (), s32[]{:S(2)}) async-start(), calls=%async_computation.1 | async-start | bytes 26214400 | tf_op jit(solution)/shard_map/all_gather | solution.py:103
  23.3 35.1 %collective-permute-start.4 = (bf16[512,1280]{1,0:T(8,128)(2,1)}, bf16[512,1280]{1,0:T(8,128)(2,1)}, u32[]{:S(2)}, u32[]{:S(2)}) collective-permute-start(bf16[512,1280]{1,0:T(8,128)(2,1)} %bitcast.210), channel_id=1, source_target_pairs={{0,8},{8,16},{16,24},{24,0},{1,9},{9,17},{17,25},{25,1},{2,10},{10... | collective-permute-start | bytes 3932168 | tf_op jit(solution)/shard_map/ppermute | solution.py:99
  28.7 85.0 %collective-permute-start.5 = (bf16[512,1280]{1,0:T(8,128)(2,1)}, bf16[512,1280]{1,0:T(8,128)(2,1)}, u32[]{:S(2)}, u32[]{:S(2)}) collective-permute-start(bf16[512,1280]{1,0:T(8,128)(2,1)} %bitcast.211), channel_id=1, source_target_pairs={{0,16},{8,24},{16,0},{24,8},{1,17},{9,25},{17,1},{25,9},{2,18},{10... | collective-permute-start | bytes 3932168 | tf_op jit(solution)/shard_map/ppermute | solution.py:99
  32.8 81.0 %collective-permute-start.6 = (bf16[512,1280]{1,0:T(8,128)(2,1)}, bf16[512,1280]{1,0:T(8,128)(2,1)}, u32[]{:S(2)}, u32[]{:S(2)}) collective-permute-start(bf16[512,1280]{1,0:T(8,128)(2,1)} %bitcast.212), channel_id=1, source_target_pairs={{0,24},{8,0},{16,8},{24,16},{1,25},{9,1},{17,9},{25,17},{2,26},{10... | collective-permute-start | bytes 3932168 | tf_op jit(solution)/shard_map/ppermute | solution.py:99
  124.6 5.6 copy-start.2
  130.2 469.5 %all-gather.6.cloned.1.call-start = ((), (), s32[]{:S(2)}) async-start(), calls=%async_computation.2 | async-start | bytes 2621440 | tf_op jit(solution)/shard_map/all_gather | solution.py:118
  130.2 76.3 %collective-permute-start = (bf16[256,4096]{1,0:T(8,128)(2,1)S(1)}, bf16[256,4096]{1,0:T(8,128)(2,1)S(1)}, u32[]{:S(2)}, u32[]{:S(2)}) collective-permute-start(bf16[256,4096]{1,0:T(8,128)(2,1)S(1)} %copy-done.2), channel_id=1, source_target_pairs={{0,8},{8,16},{16,24},{24,0},{1,9},{9,17},{17,25},{25,1},{2,10},{10... | collective-permute-start | bytes 6291464 | tf_op jit(solution)/shard_map/ppermute | solution.py:75
  158.8 135.8 %collective-permute-start.1 = (bf16[256,4096]{1,0:T(8,128)(2,1)S(1)}, bf16[256,4096]{1,0:T(8,128)(2,1)S(1)}, u32[]{:S(2)}, u32[]{:S(2)}) collective-permute-start(bf16[256,4096]{1,0:T(8,128)(2,1)S(1)} %copy-done.2), channel_id=1, source_target_pairs={{0,16},{8,24},{16,0},{24,8},{1,17},{9,25},{17,1},{25,9},{2,18},{10... | collective-permute-start | bytes 6291464 | tf_op jit(solution)/shard_map/ppermute | solution.py:75
  160.4 135.6 %collective-permute-start.2 = (bf16[256,4096]{1,0:T(8,128)(2,1)S(1)}, bf16[256,4096]{1,0:T(8,128)(2,1)S(1)}, u32[]{:S(2)}, u32[]{:S(2)}) collective-permute-start(bf16[256,4096]{1,0:T(8,128)(2,1)S(1)} %copy-done.2), channel_id=1, source_target_pairs={{0,24},{8,0},{16,8},{24,16},{1,25},{9,1},{17,9},{25,17},{2,26},{10... | collective-permute-start | bytes 6291464 | tf_op jit(solution)/shard_map/ppermute | solution.py:75
  297.6 182.6 %collective-permute-start.3 = (bf16[1024,4096]{1,0:T(8,128)(2,1)}, bf16[1024,4096]{1,0:T(8,128)(2,1)}, u32[]{:S(2)}, u32[]{:S(2)}) collective-permute-start(bf16[1024,4096]{1,0:T(8,128)(2,1)} %constant_dynamic-update-slice_fusion), channel_id=1, source_target_pairs={{0,1},{1,0},{2,3},{3,2},{4,5},{5,4},{6,7},{7,6},{8,9},{9,8},{10,11... | collective-permute-start | bytes 25165832 | tf_op jit(solution)/shard_map/ppermute | solution.py:78
  528.2 2.3 copy-start
  532.6 4.9 slice-start
  609.1 9.4 %copy-start.7 = (pred[256,1024]{0,1:T(8,128)(4,1)S(1)}, pred[256,1024]{0,1:T(8,128)(4,1)}, u32[]{:S(2)}) copy-start(pred[256,1024]{0,1:T(8,128)(4,1)} %iota_compare_fusion.3) | copy-start | bytes 786436
  618.5 7.4 copy-start.6
  642.5 14.7 %copy-start.3 = (pred[256,4096]{0,1:T(8,128)(4,1)S(1)}, pred[256,4096]{0,1:T(8,128)(4,1)}, u32[]{:S(2)}) copy-start(pred[256,4096]{0,1:T(8,128)(4,1)} %iota_compare_fusion) | copy-start | bytes 3145732
  657.2 18.0 %copy-start.14 = (s32[8,256]{1,0:T(8,128)S(1)}, s32[8,256]{1,0:T(8,128)}, u32[]{:S(2)}) copy-start(s32[8,256]{1,0:T(8,128)} %get-tuple-element.19) | copy-start | bytes 24580
  675.2 5.9 copy-start.1
  675.2 5.9 copy-start.10
  675.2 5.9 copy-start.13
  675.2 5.9 copy-start.15
  675.3 12.7 %slice-start.5 = ((s8[12582912]{0:T(1024)(128)(4,1)}), s8[4194304]{0:T(1024)(128)(4,1)S(1)}, s32[]{:S(2)}) async-start(s8[12582912]{0:T(1024)(128)(4,1)} %bitcast.219), calls=%async_computation.8 | async-start | bytes 8388608
  681.2 6.8 copy-start.9
  681.2 6.8 copy-start.12
  681.2 6.8 slice-start.6
  681.2 6.8 slice-start.7
  681.2 17.1 %slice-start.1 = ((s8[16777216]{0:T(1024)(128)(4,1)}), s8[4194304]{0:T(1024)(128)(4,1)S(1)}, s32[]{:S(2)}) async-start(s8[16777216]{0:T(1024)(128)(4,1)} %bitcast.217), calls=%async_computation.4 | async-start | bytes 8388608
  681.2 17.1 %slice-start.2 = ((s8[16777216]{0:T(1024)(128)(4,1)}), s8[4194304]{0:T(1024)(128)(4,1)S(1)}, s32[]{:S(2)}) async-start(s8[16777216]{0:T(1024)(128)(4,1)} %bitcast.217), calls=%async_computation.5 | async-start | bytes 8388608
  688.0 10.3 %copy-start.8 = (s32[4096]{0:T(1024)S(1)}, s32[4096]{0:T(1024)}, u32[]{:S(2)}) copy-start(s32[4096]{0:T(1024)} %iota_multiply_fusion) | copy-start | bytes 49156
  688.0 10.3 %copy-start.11 = (s32[8,256]{1,0:T(8,128)S(1)}, s32[8,256]{1,0:T(8,128)}, u32[]{:S(2)}) copy-start(s32[8,256]{1,0:T(8,128)} %get-tuple-element.22) | copy-start | bytes 24580
  688.0 10.3 %slice-start.3 = ((s8[16777216]{0:T(1024)(128)(4,1)}), s8[4194304]{0:T(1024)(128)(4,1)S(1)}, s32[]{:S(2)}) async-start(s8[16777216]{0:T(1024)(128)(4,1)} %bitcast.217), calls=%async_computation.6 | async-start | bytes 8388608
  688.0 10.3 %slice-start.4 = ((s8[16777216]{0:T(1024)(128)(4,1)}), s8[4194304]{0:T(1024)(128)(4,1)S(1)}, s32[]{:S(2)}) async-start(s8[16777216]{0:T(1024)(128)(4,1)} %bitcast.217), calls=%async_computation.7 | async-start | bytes 8388608
Sparse Core Ops, SparseCore 0:
  130.3 158.8 all-gather.3
  532.7 66.9 all-gather.5

commit v4 on v3

--- a/solution.py
+++ b/solution.py
@@ -69,20 +69,20 @@
     qcols = group_heads * HD
     rows = n_g * tok
 
-    own_half = [activations]
+    if lax.axis_size("fsdp") == 2:
+        other_half = lax.ppermute(activations, "fsdp", [(0, 1), (1, 0)])
+        full_rows = jnp.where(
+            f == 0,
+            jnp.concatenate([activations, other_half], axis=1),
+            jnp.concatenate([other_half, activations], axis=1),
+        )
+    else:
+        full_rows = lax.all_gather(activations, "fsdp", axis=1, tiled=True)
+    grp_rows = [full_rows]
     for shift in range(1, n_g):
         perm = [(i, (i + shift) % n_g) for i in range(n_g)]
-        own_half.append(lax.ppermute(activations, "cg", perm))
-    own_half = jnp.concatenate(own_half, axis=0)
-    if lax.axis_size("fsdp") == 2:
-        other_half = lax.ppermute(own_half, "fsdp", [(0, 1), (1, 0)])
-        grp_rows = jnp.where(
-            f == 0,
-            jnp.concatenate([own_half, other_half], axis=1),
-            jnp.concatenate([other_half, own_half], axis=1),
-        )
-    else:
-        grp_rows = lax.all_gather(own_half, "fsdp", axis=1, tiled=True)
+        grp_rows.append(lax.ppermute(full_rows, "cg", perm))
+    grp_rows = jnp.concatenate(grp_rows, axis=0)
 
     local_w = jnp.concatenate(
         [

time: 781 us -> 848 us (1.086)
  waiting for transfers between devices: 416 us -> 481 us
  other arithmetic: 51.6 us -> 70 us
  local copies, waits for them, and re-layouts: 80.2 us -> 68.4 us
    all_gather x1, waiting for transfers between devices: 47.5 us -> 95.9 us  [shards(): pair = lax.all_gather(pair, 'ct', axis=0, tiled=False)]
    ppermute x4, waiting for transfers between devices: 289 us -> 304 us  [the longest x3 260 us: shards(): grp_rows.append(lax.ppermute(full_rows, 'cg', perm))]
    concatenate x0 -> x1, other arithmetic: none -> 13.8 us  [shards(): grp_rows = jnp.concatenate(grp_rows, axis=0)]
    unnamed x54 -> x51, local copies, waits for them, and re-layouts: 20.3 us -> 17.4 us
  transfers between devices with their start and end apart: 9 -> 9, of which waited for: 6 -> 7; matrix products, arithmetic and copies ran while one was open for 7% -> 5% of each run, Pallas kernels for 0% -> 0%
where the time goes in v4:
time: 848 us; the launch traced here: 841 us
  waiting for transfers between devices  481 us (57%)
  matrix products  112 us (13%)
  other arithmetic  70 us (8%)
  local copies, waits for them, and re-layouts  68.4 us (8%)
  blocking collectives  53 us (6%)
  starting transfers between devices  40.2 us (5%)
  between operations  16.3 us (2%)
    ppermute x3, waiting for transfers between devices, shards(): grp_rows.append(lax.ppermute(full_rows, 'cg', perm))  260 us
    all_gather x1, waiting for transfers between devices, shards(): pair = lax.all_gather(pair, 'ct', axis=0, tiled=False)  95.9 us
    ppermute x3, waiting for transfers between devices, shards(): received.append(lax.ppermute(outgoing, 'cg', perm))  81.4 us
    all_to_all x1, blocking collectives, shards(): lax.all_to_all(out_rows, 'cg', split_axis=0, concat_axis=2, tiled=True)  53 us
    ppermute x1, waiting for transfers between devices, shards(): other_half = lax.ppermute(activations, 'fsdp', [(0, 1), (1, 0)])  44.5 us
    sub x3, matrix products, shards(): weights = jnp.where(visible, jnp.exp(scores - highest), 0.0)  40 us
    dot_general x4, matrix products, shards(): jnp.einsum('hqk,ke->hqe', dropped, all_values[:span], preferred_element_t...  36.4 us
    ppermute x3, starting transfers between devices, shards(): grp_rows.append(lax.ppermute(full_rows, 'cg', perm))  32.5 us
  transfers between devices with their start and end apart: 9, of which 7 were waited for; matrix products, arithmetic and copies ran while one was open for 5% of the time, Pallas kernels for 0%

profile of v4, /device:TPU:0, one launch (start us, length us, event | category | flops | bytes accessed | tf_op | source)
XLA Modules:
  0.0 841.5 jit_solution(17099871883833585419)
XLA Ops:
  6.5 6.6 copy.57
  13.1 0.2 copy.58
  13.3 0.2 copy.59
  13.6 5.2 pad_maximum_fusion.1
  18.8 2.0 constant_dynamic-slice_fusion.3
  20.8 2.5 copy.62
  23.3 4.0 collective-permute-start.5
  27.3 2.4 copy.63
  29.7 1.3 collective-permute-start.6
  31.1 1.4 copy.61
  32.5 0.7 collective-permute-start.4
  33.2 0.6 copy.60
  33.9 52.3 %collective-permute-done.5 = bf16[512,1280]{1,0:T(8,128)(2,1)} collective-permute-done((bf16[512,1280]{1,0:T(8,128)(2,1)}, bf16[512,1280]{1,0:T(8,128)(2,1)}, u32[]{:S(2)}, u32[]{:S(2)}) %collective-permute-start.5) | collective-permute-done | bytes 1310752 | tf_op jit(solution)/shard_map/ppermute | solution.py:99
  86.2 29.1 %collective-permute-done.6 = bf16[512,1280]{1,0:T(8,128)(2,1)} collective-permute-done((bf16[512,1280]{1,0:T(8,128)(2,1)}, bf16[512,1280]{1,0:T(8,128)(2,1)}, u32[]{:S(2)}, u32[]{:S(2)}) %collective-permute-start.6) | collective-permute-done | bytes 1310752 | tf_op jit(solution)/shard_map/ppermute | solution.py:99
  115.3 5.2 pad_maximum_fusion.2
  120.5 5.7 gather_fusion
  126.2 5.3 bitcast_select_fusion.16
  131.6 1.5 copy-done.2
  133.1 1.6 collective-permute-start
  134.7 44.5 %collective-permute-done = bf16[256,4096]{1,0:T(8,128)(2,1)} collective-permute-done((bf16[256,4096]{1,0:T(8,128)(2,1)S(1)}, bf16[256,4096]{1,0:T(8,128)(2,1)}, u32[]{:S(2)}, u32[]{:S(2)}) %collective-permute-start) | collective-permute-done | bytes 2097184 | tf_op jit(solution)/shard_map/ppermute | solution.py:73
  179.2 4.8 maximum_select_fusion
  184.0 27.7 %collective-permute-start.1 = (bf16[256,8192]{1,0:T(8,128)(2,1)}, bf16[256,8192]{1,0:T(8,128)(2,1)}, u32[]{:S(2)}, u32[]{:S(2)}) collective-permute-start(bf16[256,8192]{1,0:T(8,128)(2,1)} %maximum_select_fusion), channel_id=1, source_target_pairs={{0,8},{8,16},{16,24},{24,0},{1,9},{9,17},{17,25},{25,1},{2,10},{10... | collective-permute-start | bytes 12582920 | tf_op jit(solution)/shard_map/ppermute | solution.py:84
  211.6 1.9 collective-permute-start.2
  213.5 2.9 collective-permute-start.3
  218.6 0.6 iota_multiply_fusion.2
  219.2 0.6 iota_multiply_fusion.1
  219.8 0.7 shift-right-logical_xor_fusion.21
  220.5 0.9 iota_compare_fusion.3
  221.4 81.6 %collective-permute-done.1 = bf16[256,8192]{1,0:T(8,128)(2,1)} collective-permute-done((bf16[256,8192]{1,0:T(8,128)(2,1)}, bf16[256,8192]{1,0:T(8,128)(2,1)}, u32[]{:S(2)}, u32[]{:S(2)}) %collective-permute-start.1) | collective-permute-done | bytes 4194336 | tf_op jit(solution)/shard_map/ppermute | solution.py:84
  303.0 154.8 %collective-permute-done.2 = bf16[256,8192]{1,0:T(8,128)(2,1)} collective-permute-done((bf16[256,8192]{1,0:T(8,128)(2,1)}, bf16[256,8192]{1,0:T(8,128)(2,1)}, u32[]{:S(2)}, u32[]{:S(2)}) %collective-permute-start.2) | collective-permute-done | bytes 4194336 | tf_op jit(solution)/shard_map/ppermute | solution.py:84
  457.8 23.1 %collective-permute-done.3 = bf16[256,8192]{1,0:T(8,128)(2,1)} collective-permute-done((bf16[256,8192]{1,0:T(8,128)(2,1)}, bf16[256,8192]{1,0:T(8,128)(2,1)}, u32[]{:S(2)}, u32[]{:S(2)}) %collective-permute-start.3) | collective-permute-done | bytes 4194336 | tf_op jit(solution)/shard_map/ppermute | solution.py:84
  480.9 13.8 %pad_maximum_fusion = bf16[1024,8192]{1,0:T(8,128)(2,1)} fusion(bf16[256,8192]{1,0:T(8,128)(2,1)} %collective-permute-done.3, bf16[256,8192]{1,0:T(8,128)(2,1)} %collective-permute-done.2, bf16[256,8192]{1,0:T(8,128)(2,1)} %collective-permute-done.1, bf16[256,8192]{1,0:T(8,128)(2,1)} %maximum_select_fusion), kind=kLoop, calls=%fused_computation.41 | loop fusion | flops 67108864 | bytes 33554432 | tf_op jit(solution)/shard_map/concatenate | solution.py:85
  494.8 10.1 %copy.64 = bf16[4,4,512,1280]{3,2,1,0:T(8,128)(2,1)S(1)} copy(bf16[4,4,512,1280]{3,2,0,1:T(8,128)(2,1)} %bitcast.193) | data formatting | bytes 41943040 | tf_op jit(solution)/shard_map/transpose | solution.py:104
  504.9 26.3 %fusion.162 = f32[4,256,1280]{2,1,0:T(8,128)} fusion(bf16[4,256,8192]{2,1,0:T(8,128)(2,1)} %bitcast.197, bf16[8192,1280,1]{1,0,2:T(8,128)(2,1)S(1)} %bitcast.194), kind=kOutput, calls=%fused_computation.258 | convolution fusion | flops 21474836480 | bytes 42991616 | tf_op jit(solution)/shard_map/dot_general | solution.py:106
  531.2 5.7 gather_fusion.1
  537.0 5.9 copy.65
  542.9 3.1 broadcast_select_fusion
  546.1 2.3 copy-done
  548.3 1.1 multiply_cosine_fusion
  549.5 0.8 pad_maximum_fusion.5
  550.4 0.6 iota_multiply_fusion
  551.0 1.2 iota_compare_fusion.2
  552.1 1.4 iota_compare_fusion.1
  553.5 1.7 iota_compare_fusion
  555.2 1.8 fusion.149
  557.0 3.9 copy.93
  560.8 2.7 copy.94
  563.8 0.2 copy.70
  564.0 6.0 subtract_convert_fusion
  570.0 95.9 %all-gather.6.cloned.1.call-done = bf16[4096,2,128]{0,2,1:T(8,128)(2,1)} async-done(((bf16[1024,2,128]{0,2,1:T(8,128)(2,1)}), bf16[4096,2,128]{0,2,1:T(8,128)(2,1)}) %all-gather.6.cloned.1.call-update) | async-done | bytes 2097168 | tf_op jit(solution)/shard_map/all_gather | solution.py:118
  665.9 4.5 reshape.542
  670.4 4.9 copy.66
  675.3 9.4 %fusion.67 = f32[2048,256,8]{1,0,2:T(8,128)} fusion(bf16[1024,8,64]{2,0,1:T(8,128)(2,1)S(1)} %get-tuple-element.5, bf16[1024,8,64]{2,0,1:T(8,128)(2,1)} %get-tuple-element.6, bf16[4096,2,128]{2,0,1:T(8,128)(2,1)} %bitcast.201), kind=kOutput, calls=%fused_computation.117 | convolution fusion | flops 1074790400 | bytes 20447232 | tf_op jit(solution)/shard_map/qhe,ke->hqk/dot_general | solution.py:134
  684.7 7.4 fusion.157
  692.1 16.6 %fusion.156 = (f32[8,256]{1,0:T(8,128)S(1)}, bf16[8,256,2048]{1,2,0:T(8,128)(2,1)}) fusion(f32[2048,256,8]{1,0,2:T(8,128)} %fusion.67, pred[256,2048]{0,1:T(8,128)(4,1)S(1)} %copy-done.6), kind=kOutput, calls=%fused_computation.256 | output fusion | flops 29362176 | bytes 25698304 | tf_op jit(solution)/shard_map/sub | solution.py:144
  708.7 14.7 %fusion.151 = (f32[8,256]{1,0:T(8,128)S(1)}, bf16[8,256,3072]{1,2,0:T(8,128)(2,1)}) fusion(pred[256,3072]{0,1:T(8,128)(4,1)} %iota_compare_fusion.1, bf16[4096,2,128]{2,0,1:T(8,128)(2,1)} %bitcast.203, bf16[1024,8,64]{2,0,1:T(8,128)(2,1)S(1)} %get-tuple-element.5, bf16[1024,8,64]{2,0,1:T(8,128)(2,1)} %get-tuple-element.6), kind=kOutput, calls=%fused_computation.255 | convolution fusion | flops 3267365888 | bytes 24125440 | tf_op jit(solution)/shard_map/sub | solution.py:144
  723.4 17.9 %fusion.150 = (f32[8,256]{1,0:T(8,128)S(1)}, bf16[8,256,4096]{1,2,0:T(8,128)(2,1)}) fusion(pred[256,4096]{0,1:T(8,128)(4,1)S(1)} %copy-done.3, bf16[4096,2,128]{2,0,1:T(8,128)(2,1)} %bitcast.204, bf16[1024,8,64]{2,0,1:T(8,128)(2,1)} %get-tuple-element.6, bf16[1024,8,64]{2,0,1:T(8,128)(2,1)S(1)} %get-tuple-element.5), kind=kOutput, calls=%fused_computation.254 | convolution fusion | flops 4355788800 | bytes 29368320 | tf_op jit(solution)/shard_map/sub | solution.py:144
  741.4 5.8 divide_convert_fusion.3
  747.4 6.7 divide_convert_fusion.2
  754.2 10.2 %divide_convert_fusion.1 = bf16[256,8,128]{0,2,1:T(8,128)(2,1)S(1)} fusion(bf16[8,256,3072]{1,2,0:T(8,128)(2,1)S(1)} %bitcast.221, s32[3072]{0:T(1024)S(1)} %copy-done.9, s32[8,256]{1,0:T(8,128)S(1)} %copy-done.12, bf16[4096,2,128]{2,0,1:T(8,128)(2,1)S(1)} %bitcast.207, f32[256,8]{0,1:T(8,128)S(1)} %multiply_bitcast_fusion.1), kind=kOutput, calls=%fused_computation.106 | convolution fusion | flops 1686634496 | bytes 13922304 | tf_op jit(solution)/shard_map/hqk,ke->hqe/dot_general | solution.py:150
  764.5 13.6 %divide_convert_fusion = bf16[256,8,128]{0,2,1:T(8,128)(2,1)S(1)} fusion(bf16[4096,2,128]{2,0,1:T(8,128)(2,1)S(1)} %bitcast.208, bf16[8,256,4096]{1,2,0:T(8,128)(2,1)S(1)} %bitcast.219, s32[4096]{0:T(1024)S(1)} %copy-done.8, s32[8,256]{1,0:T(8,128)S(1)} %copy-done.11, f32[256,8]{0,1:T(8,128)S(1)} %multiply_bitcast_fusion), kind=kOutput, calls=%fused_computation.105 | convolution fusion | flops 2248671232 | bytes 18382848 | tf_op jit(solution)/shard_map/hqk,ke->hqe/dot_general | solution.py:150
  778.1 0.3 pad_maximum_fusion.3
  778.4 53.0 %all_to_all.15 = bf16[4,256,1024]{1,2,0:T(8,128)(2,1)S(1)} all-to-all(bf16[4,256,1024]{1,2,0:T(8,128)(2,1)S(1)} %pad_maximum_fusion.3), channel_id=1, replica_groups=mesh['cg'=4,'ct'=4,'fsdp'=2] {'cg'}, dimensions={0} | all-to-all | bytes 4194304 | tf_op jit(solution)/shard_map/all_to_all | solution.py:156
  831.4 2.8 copy.92
  (72 shorter events, 0.6 us)
Async XLA Ops:
  6.5 6.6 copy-start.4
  6.5 6.8 copy-start.5
  6.5 488.2 %all-gather.4.cloned.1.call-start = ((), (), s32[]{:S(2)}) async-start(), calls=%async_computation.1 | async-start | bytes 26214400 | tf_op jit(solution)/shard_map/all_gather | solution.py:103
  23.3 63.0 %collective-permute-start.5 = (bf16[512,1280]{1,0:T(8,128)(2,1)}, bf16[512,1280]{1,0:T(8,128)(2,1)}, u32[]{:S(2)}, u32[]{:S(2)}) collective-permute-start(bf16[512,1280]{1,0:T(8,128)(2,1)} %bitcast.211), channel_id=1, source_target_pairs={{0,16},{8,24},{16,0},{24,8},{1,17},{9,25},{17,1},{25,9},{2,18},{10... | collective-permute-start | bytes 3932168 | tf_op jit(solution)/shard_map/ppermute | solution.py:99
  29.7 85.6 %collective-permute-start.6 = (bf16[512,1280]{1,0:T(8,128)(2,1)}, bf16[512,1280]{1,0:T(8,128)(2,1)}, u32[]{:S(2)}, u32[]{:S(2)}) collective-permute-start(bf16[512,1280]{1,0:T(8,128)(2,1)} %bitcast.212), channel_id=1, source_target_pairs={{0,24},{8,0},{16,8},{24,16},{1,25},{9,1},{17,9},{25,17},{2,26},{10... | collective-permute-start | bytes 3932168 | tf_op jit(solution)/shard_map/ppermute | solution.py:99
  32.5 82.8 %collective-permute-start.4 = (bf16[512,1280]{1,0:T(8,128)(2,1)}, bf16[512,1280]{1,0:T(8,128)(2,1)}, u32[]{:S(2)}, u32[]{:S(2)}) collective-permute-start(bf16[512,1280]{1,0:T(8,128)(2,1)} %bitcast.213), channel_id=1, source_target_pairs={{0,8},{8,16},{16,24},{24,0},{1,9},{9,17},{17,25},{25,1},{2,10},{10... | collective-permute-start | bytes 3932168 | tf_op jit(solution)/shard_map/ppermute | solution.py:99
  131.5 1.6 copy-start.2
  131.5 534.4 %all-gather.6.cloned.1.call-start = ((), (), s32[]{:S(2)}) async-start(), calls=%async_computation.2 | async-start | bytes 2621440 | tf_op jit(solution)/shard_map/all_gather | solution.py:118
  133.1 46.1 %collective-permute-start = (bf16[256,4096]{1,0:T(8,128)(2,1)S(1)}, bf16[256,4096]{1,0:T(8,128)(2,1)}, u32[]{:S(2)}, u32[]{:S(2)}) collective-permute-start(bf16[256,4096]{1,0:T(8,128)(2,1)S(1)} %copy-done.2), channel_id=1, source_target_pairs={{0,1},{1,0},{2,3},{3,2},{4,5},{5,4},{6,7},{7,6},{8,9},{9,8},{10,11... | collective-permute-start | bytes 6291464 | tf_op jit(solution)/shard_map/ppermute | solution.py:73
  184.0 119.0 %collective-permute-start.1 = (bf16[256,8192]{1,0:T(8,128)(2,1)}, bf16[256,8192]{1,0:T(8,128)(2,1)}, u32[]{:S(2)}, u32[]{:S(2)}) collective-permute-start(bf16[256,8192]{1,0:T(8,128)(2,1)} %maximum_select_fusion), channel_id=1, source_target_pairs={{0,8},{8,16},{16,24},{24,0},{1,9},{9,17},{17,25},{25,1},{2,10},{10... | collective-permute-start | bytes 12582920 | tf_op jit(solution)/shard_map/ppermute | solution.py:84
  211.6 246.2 %collective-permute-start.2 = (bf16[256,8192]{1,0:T(8,128)(2,1)}, bf16[256,8192]{1,0:T(8,128)(2,1)}, u32[]{:S(2)}, u32[]{:S(2)}) collective-permute-start(bf16[256,8192]{1,0:T(8,128)(2,1)} %maximum_select_fusion), channel_id=1, source_target_pairs={{0,16},{8,24},{16,0},{24,8},{1,17},{9,25},{17,1},{25,9},{2,18},{10... | collective-permute-start | bytes 12582920 | tf_op jit(solution)/shard_map/ppermute | solution.py:84
  213.5 267.4 %collective-permute-start.3 = (bf16[256,8192]{1,0:T(8,128)(2,1)}, bf16[256,8192]{1,0:T(8,128)(2,1)}, u32[]{:S(2)}, u32[]{:S(2)}) collective-permute-start(bf16[256,8192]{1,0:T(8,128)(2,1)} %maximum_select_fusion), channel_id=1, source_target_pairs={{0,24},{8,0},{16,8},{24,16},{1,25},{9,1},{17,9},{25,17},{2,26},{10... | collective-permute-start | bytes 12582920 | tf_op jit(solution)/shard_map/ppermute | solution.py:84
  546.0 2.3 copy-start
  552.1 3.1 slice-start
  675.3 9.4 %copy-start.7 = (pred[256,1024]{0,1:T(8,128)(4,1)S(1)}, pred[256,1024]{0,1:T(8,128)(4,1)}, u32[]{:S(2)}) copy-start(pred[256,1024]{0,1:T(8,128)(4,1)} %iota_compare_fusion.3) | copy-start | bytes 786436
  684.7 7.4 copy-start.6
  708.7 14.7 %copy-start.3 = (pred[256,4096]{0,1:T(8,128)(4,1)S(1)}, pred[256,4096]{0,1:T(8,128)(4,1)}, u32[]{:S(2)}) copy-start(pred[256,4096]{0,1:T(8,128)(4,1)} %iota_compare_fusion) | copy-start | bytes 3145732
  723.4 18.0 %copy-start.14 = (s32[8,256]{1,0:T(8,128)S(1)}, s32[8,256]{1,0:T(8,128)}, u32[]{:S(2)}) copy-start(s32[8,256]{1,0:T(8,128)} %get-tuple-element.19) | copy-start | bytes 24580
  741.4 5.9 copy-start.1
  741.4 5.9 copy-start.10
  741.4 5.9 copy-start.13
  741.4 5.9 copy-start.15
  741.4 12.7 %slice-start.5 = ((s8[12582912]{0:T(1024)(128)(4,1)}), s8[4194304]{0:T(1024)(128)(4,1)S(1)}, s32[]{:S(2)}) async-start(s8[12582912]{0:T(1024)(128)(4,1)} %bitcast.220), calls=%async_computation.8 | async-start | bytes 8388608
  747.3 6.8 copy-start.9
  747.3 6.8 copy-start.12
  747.3 6.8 slice-start.6
  747.3 6.8 slice-start.7
  747.4 17.1 %slice-start.1 = ((s8[16777216]{0:T(1024)(128)(4,1)}), s8[4194304]{0:T(1024)(128)(4,1)S(1)}, s32[]{:S(2)}) async-start(s8[16777216]{0:T(1024)(128)(4,1)} %bitcast.218), calls=%async_computation.4 | async-start | bytes 8388608
  747.4 17.1 %slice-start.2 = ((s8[16777216]{0:T(1024)(128)(4,1)}), s8[4194304]{0:T(1024)(128)(4,1)S(1)}, s32[]{:S(2)}) async-start(s8[16777216]{0:T(1024)(128)(4,1)} %bitcast.218), calls=%async_computation.5 | async-start | bytes 8388608
  754.2 10.3 %copy-start.8 = (s32[4096]{0:T(1024)S(1)}, s32[4096]{0:T(1024)}, u32[]{:S(2)}) copy-start(s32[4096]{0:T(1024)} %iota_multiply_fusion) | copy-start | bytes 49156
  754.2 10.3 %copy-start.11 = (s32[8,256]{1,0:T(8,128)S(1)}, s32[8,256]{1,0:T(8,128)}, u32[]{:S(2)}) copy-start(s32[8,256]{1,0:T(8,128)} %get-tuple-element.22) | copy-start | bytes 24580
  754.2 10.3 %slice-start.3 = ((s8[16777216]{0:T(1024)(128)(4,1)}), s8[4194304]{0:T(1024)(128)(4,1)S(1)}, s32[]{:S(2)}) async-start(s8[16777216]{0:T(1024)(128)(4,1)} %bitcast.218), calls=%async_computation.6 | async-start | bytes 8388608
  754.2 10.3 %slice-start.4 = ((s8[16777216]{0:T(1024)(128)(4,1)}), s8[4194304]{0:T(1024)(128)(4,1)S(1)}, s32[]{:S(2)}) async-start(s8[16777216]{0:T(1024)(128)(4,1)} %bitcast.218), calls=%async_computation.7 | async-start | bytes 8388608
Sparse Core Ops, SparseCore 0:
  131.6 157.2 all-gather.3
  550.5 115.3 all-gather.5

commit v5 on v1

--- a/solution.py
+++ b/solution.py
@@ -80,8 +80,15 @@
         ],
         axis=2,
     )
-    mine = lax.all_to_all(local_w, "cg", split_axis=1, concat_axis=0, tiled=True)
-    mine = mine.reshape(n_g, d_rows, qcols + 2 * HD)
+    received = [lax.dynamic_index_in_dim(local_w, g, 1, keepdims=False)]
+    for shift in range(1, n_g):
+        outgoing = lax.dynamic_index_in_dim(local_w, (g + shift) % n_g, 1, keepdims=False)
+        perm = [(i, (i + shift) % n_g) for i in range(n_g)]
+        received.append(lax.ppermute(outgoing, "cg", perm))
+    by_shift = jnp.stack(received, axis=0)
+    back = (g - jnp.arange(n_g, dtype=jnp.int32)) % n_g
+    mine = jnp.take(by_shift, back, axis=0)
+    grp_rows, mine = lax.optimization_barrier((grp_rows, mine))
     every = lax.all_gather(mine, "ct", axis=0, tiled=False)
     every = every.transpose(1, 0, 2, 3).reshape(n_g * n_t * d_rows, qcols + 2 * HD)
 

time: 807 us -> 841 us (1.042)
  waiting for transfers between devices: 514 us -> 556 us
  local copies, waits for them, and re-layouts: 58 us -> 45 us
  other arithmetic: 39.6 us -> 48.1 us
    ppermute x0 -> x3, waiting for transfers between devices: none -> 251 us  [shards(): received.append(lax.ppermute(outgoing, 'cg', perm))]
    all_gather x1, waiting for transfers between devices: 271 us -> 107 us  [shards(): grp_rows = lax.all_gather(full_rows, 'cg', axis=0, tiled=True)]
    all_to_all x1 -> x0, waiting for transfers between devices: 115 us -> none  [shards(): lax.all_to_all(local_w, 'cg', split_axis=1, concat_axis=0, tiled=True)]
    all_gather x1, waiting for transfers between devices: 0.02 us -> 61.1 us  [shards(): full_rows = lax.all_gather(activations, 'fsdp', axis=1, tiled=True)]
    all_gather x1, waiting for transfers between devices: 1.37 us -> 11.8 us  [shards(): pair = lax.all_gather(pair, 'ct', axis=0, tiled=False)]
    dynamic_slice x0 -> x5, local copies, waits for them, and re-layouts: none -> 9.08 us  [the longest x3 6.46 us: shards(): lax.dynamic_index_in_dim(local_w, (g + shift) % n_g, 1, keepdims=False)]
    unnamed x33 -> x43, local copies, waits for them, and re-layouts: 17.9 us -> 14 us
  transfers between devices with their start and end apart: 5 -> 7, of which waited for: 4 -> 6; matrix products, arithmetic and copies ran while one was open for 6% -> 6% of each run, Pallas kernels for 0% -> 0%
where the time goes in v5:
time: 841 us; the launch traced here: 836 us
  waiting for transfers between devices  556 us (66%)
  matrix products  114 us (14%)
  blocking collectives  53 us (6%)
  other arithmetic  48.1 us (6%)
  local copies, waits for them, and re-layouts  45 us (5%)
  between operations  15.8 us (2%)
    ppermute x3, waiting for transfers between devices, shards(): received.append(lax.ppermute(outgoing, 'cg', perm))  251 us
    all_gather x1, waiting for transfers between devices, shards(): every = lax.all_gather(mine, 'ct', axis=0, tiled=False)  124 us
    all_gather x1, waiting for transfers between devices, shards(): grp_rows = lax.all_gather(full_rows, 'cg', axis=0, tiled=True)  107 us
    all_gather x1, waiting for transfers between devices, shards(): full_rows = lax.all_gather(activations, 'fsdp', axis=1, tiled=True)  61.1 us
    all_to_all x1, blocking collectives, shards(): lax.all_to_all(out_rows, 'cg', split_axis=0, concat_axis=2, tiled=True)  53 us
    dot_general x4, matrix products, shards(): jnp.einsum('hqk,ke->hqe', dropped, all_values[:span], preferred_element_t...  40.4 us
    sub x3, matrix products, shards(): weights = jnp.where(visible, jnp.exp(scores - highest), 0.0)  39.9 us
    dot_general x1, matrix products, shards(): mixed = jnp.dot(grp_rows, every, preferred_element_type=jnp.float32)  25.2 us
  transfers between devices with their start and end apart: 7, of which 6 were waited for; matrix products, arithmetic and copies ran while one was open for 6% of the time, Pallas kernels for 0%

profile of v5, /device:TPU:0, one launch (start us, length us, event | category | flops | bytes accessed | tf_op | source)
XLA Modules:
  0.0 836.0 jit_solution(14705793955073860449)
XLA Ops:
  6.5 0.7 all-gather.7.cloned.1.call-update
  7.3 0.0 all-gather.9.cloned.1.call-start
  7.3 61.1 %all-gather.7.cloned.1.call-done = bf16[256,8192]{1,0:T(8,128)(2,1)} async-done(((bf16[256,4096]{1,0:T(8,128)(2,1)}), bf16[256,8192]{1,0:T(8,128)(2,1)}) %all-gather.7.cloned.1.call-update) | async-done | bytes 4194320 | tf_op jit(solution)/shard_map/all_gather | solution.py:72
  68.4 0.0 all-gather.9.cloned.1.call-update
  68.4 0.0 all-gather.11.cloned.1.call-start
  68.5 0.2 copy.74
  68.7 0.2 copy.73
  69.0 6.5 copy.72
  75.4 5.5 pad_maximum_fusion
  80.9 2.0 constant_dynamic-slice_fusion.3
  82.9 2.5 copy.78
  85.5 3.2 collective-permute-start.2
  88.6 2.5 copy.77
  91.1 0.0 collective-permute-start.1
  91.1 1.4 copy.76
  92.5 1.1 collective-permute-start
  93.7 0.6 copy.75
  94.3 75.2 %collective-permute-done.2 = bf16[512,1280]{1,0:T(8,128)(2,1)} collective-permute-done((bf16[512,1280]{1,0:T(8,128)(2,1)}, bf16[512,1280]{1,0:T(8,128)(2,1)}, u32[]{:S(2)}, u32[]{:S(2)}) %collective-permute-start.2) | collective-permute-done | bytes 1310752 | tf_op jit(solution)/shard_map/ppermute | solution.py:87
  169.5 175.6 %collective-permute-done.1 = bf16[512,1280]{1,0:T(8,128)(2,1)} collective-permute-done((bf16[512,1280]{1,0:T(8,128)(2,1)}, bf16[512,1280]{1,0:T(8,128)(2,1)}, u32[]{:S(2)}, u32[]{:S(2)}) %collective-permute-start.1) | collective-permute-done | bytes 1310752 | tf_op jit(solution)/shard_map/ppermute | solution.py:87
  345.1 0.0 collective-permute-done
  345.1 5.3 pad_maximum_fusion.1
  350.4 5.7 gather_fusion
  356.1 5.3 broadcast_select_fusion
  361.4 107.4 %all-gather.9.cloned.1.call-done = bf16[1024,8192]{1,0:T(8,128)(2,1)} async-done(((bf16[256,8192]{1,0:T(8,128)(2,1)}), bf16[1024,8192]{1,0:T(8,128)(2,1)}) %all-gather.9.cloned.1.call-update) | async-done | bytes 16777232 | tf_op jit(solution)/shard_map/all_gather | solution.py:73
  468.9 0.0 all-gather.11.cloned.1.call-update
  468.9 0.3 all-gather.13.cloned.1.call-start
  471.3 0.6 iota_multiply_fusion.3
  471.9 0.6 iota_multiply_fusion.2
  472.5 0.6 iota_multiply_fusion.1
  473.1 0.6 iota_multiply_fusion
  473.7 0.7 shift-right-logical_xor_fusion.21
  474.4 0.9 iota_compare_fusion.3
  475.3 1.2 iota_compare_fusion.2
  476.4 123.8 %all-gather.11.cloned.1.call-done = bf16[16,512,1280]{2,1,0:T(8,128)(2,1)} async-done(((bf16[4,512,1280]{2,1,0:T(8,128)(2,1)}), bf16[16,512,1280]{2,1,0:T(8,128)(2,1)}) %all-gather.11.cloned.1.call-update) | async-done | bytes 20971536 | tf_op jit(solution)/shard_map/all_gather | solution.py:92
  600.2 10.1 %copy.79 = bf16[4,4,512,1280]{3,2,1,0:T(8,128)(2,1)S(1)} copy(bf16[4,4,512,1280]{3,2,0,1:T(8,128)(2,1)} %bitcast.191) | data formatting | bytes 41943040 | tf_op jit(solution)/shard_map/transpose | solution.py:93
  610.4 25.2 %fusion.162 = f32[1024,1280]{1,0:T(8,128)S(1)} fusion(bf16[1024,8192]{1,0:T(8,128)(2,1)} %all-gather.9.cloned.1.call-done, bf16[8192,1280]{1,0:T(8,128)(2,1)S(1)} %bitcast.192), kind=kOutput, calls=%fused_computation.255 | convolution fusion | flops 21474836480 | bytes 42991616 | tf_op jit(solution)/shard_map/dot_general | solution.py:95
  635.6 0.0 copy-start.1
  635.6 2.3 copy-done.1
  637.9 2.7 multiply_cosine_fusion
  640.6 0.9 pad_maximum_fusion.4
  641.6 0.0 all-gather.13.cloned.1.call-update
  641.6 1.4 iota_compare_fusion.1
  643.0 1.7 iota_compare_fusion
  644.7 2.5 slice_bitcast_fusion
  647.2 1.0 copy.107
  648.2 1.3 fusion.149
  649.6 2.9 subtract_convert_fusion
  652.5 11.8 %all-gather.13.cloned.1.call-done = bf16[4096,2,128]{2,0,1:T(8,128)(2,1)} async-done(((bf16[1024,2,128]{2,0,1:T(8,128)(2,1)}), bf16[4096,2,128]{2,0,1:T(8,128)(2,1)}) %all-gather.13.cloned.1.call-update) | async-done | bytes 2097168 | tf_op jit(solution)/shard_map/all_gather | solution.py:106
  664.3 1.9 copy.80
  666.2 0.0 copy-start.2
  666.2 1.3 copy-done.2
  667.6 8.2 fusion.67
  675.7 17.9 %fusion.150 = (f32[8,256]{1,0:T(8,128)S(1)}, bf16[8,256,4096]{1,2,0:T(8,128)(2,1)}) fusion(pred[256,4096]{0,1:T(8,128)(4,1)S(1)} %copy-done.4, bf16[4096,2,128]{2,0,1:T(8,128)(2,1)} %bitcast.197, bf16[1024,8,64]{2,0,1:T(8,128)(2,1)} %get-tuple-element.10, bf16[1024,8,64]{2,0,1:T(8,128)(2,1)S(1)} %get-tuple-element.9), kind=kOutput, calls=%fused_computation.251 | convolution fusion | flops 4355788800 | bytes 29368320 | tf_op jit(solution)/shard_map/sub | solution.py:132
  693.7 14.6 %fusion.151 = (f32[8,256]{1,0:T(8,128)S(1)}, bf16[8,256,3072]{1,2,0:T(8,128)(2,1)}) fusion(pred[256,3072]{0,1:T(8,128)(4,1)} %iota_compare_fusion.1, bf16[4096,2,128]{2,0,1:T(8,128)(2,1)} %bitcast.198, bf16[1024,8,64]{2,0,1:T(8,128)(2,1)S(1)} %get-tuple-element.9, bf16[1024,8,64]{2,0,1:T(8,128)(2,1)} %get-tuple-element.10), kind=kOutput, calls=%fused_computation.252 | convolution fusion | flops 3267365888 | bytes 24125440 | tf_op jit(solution)/shard_map/sub | solution.py:132
  708.3 16.8 %fusion.156 = (f32[8,256]{1,0:T(8,128)S(1)}, bf16[8,256,2048]{1,2,0:T(8,128)(2,1)}) fusion(f32[2048,256,8]{1,0,2:T(8,128)} %fusion.67, pred[256,2048]{0,1:T(8,128)(4,1)S(1)} %copy-done.7), kind=kOutput, calls=%fused_computation.253 | output fusion | flops 29362176 | bytes 25698304 | tf_op jit(solution)/shard_map/sub | solution.py:132
  725.1 7.4 fusion.157
  732.5 0.0 copy-start.3
  732.5 16.9 %divide_convert_fusion = bf16[256,8,128]{0,2,1:T(8,128)(2,1)S(1)} fusion(bf16[4096,2,128]{2,0,1:T(8,128)(2,1)} %bitcast.200, bf16[8,256,4096]{1,2,0:T(8,128)(2,1)} %get-tuple-element.28, s32[4096]{0:T(1024)S(1)} %copy-done.9, s32[8,256]{1,0:T(8,128)S(1)} %copy-done.15, f32[256,8]{0,1:T(8,128)S(1)} %multiply_bitcast_fusion), kind=kOutput, calls=%fused_computation.102 | convolution fusion | flops 2248671232 | bytes 18382848 | tf_op jit(solution)/shard_map/hqk,ke->hqe/dot_general | solution.py:138
  749.5 13.3 %divide_convert_fusion.1 = bf16[256,8,128]{0,2,1:T(8,128)(2,1)S(1)} fusion(bf16[8,256,3072]{1,2,0:T(8,128)(2,1)} %get-tuple-element.30, s32[3072]{0:T(1024)S(1)} %copy-done.10, s32[8,256]{1,0:T(8,128)S(1)} %copy-done.14, bf16[4096,2,128]{2,0,1:T(8,128)(2,1)S(1)} %bitcast.201, f32[256,8]{0,1:T(8,128)S(1)} %multiply_bitcast_fusion.1), kind=kOutput, calls=%fused_computation.103 | convolution fusion | flops 1686634496 | bytes 13922304 | tf_op jit(solution)/shard_map/hqk,ke->hqe/dot_general | solution.py:138
  762.8 6.7 divide_convert_fusion.2
  769.6 3.5 divide_convert_fusion.3
  773.1 0.3 pad_maximum_fusion.2
  773.4 53.0 %all_to_all.15 = bf16[4,256,1024]{1,2,0:T(8,128)(2,1)S(1)} all-to-all(bf16[4,256,1024]{1,2,0:T(8,128)(2,1)S(1)} %pad_maximum_fusion.2), channel_id=1, replica_groups=mesh['cg'=4,'ct'=4,'fsdp'=2] {'cg'}, dimensions={0} | all-to-all | bytes 4194304 | tf_op jit(solution)/shard_map/all_to_all | solution.py:144
  826.4 2.8 copy.104
  (48 shorter events, 0.2 us)
Async XLA Ops:
  6.5 62.0 %copy-start.5 = (bf16[512,512]{1,0:T(8,128)(2,1)S(1)}, bf16[512,512]{1,0:T(8,128)(2,1)}, u32[]{:S(2)}) copy-start(bf16[512,512]{1,0:T(8,128)(2,1)} %param.10) | copy-start | bytes 1572868
  6.5 62.2 %copy-start.6 = (bf16[512,512]{1,0:T(8,128)(2,1)S(1)}, bf16[512,512]{1,0:T(8,128)(2,1)}, u32[]{:S(2)}) copy-start(bf16[512,512]{1,0:T(8,128)(2,1)} %param.9) | copy-start | bytes 1572868
  6.5 61.8 %all-gather.7.cloned.1.call-start = ((), (), s32[]{:S(2)}) async-start(), calls=%async_computation.1 | async-start | bytes 6291456 | tf_op jit(solution)/shard_map/all_gather | solution.py:72
  7.3 461.6 %all-gather.9.cloned.1.call-start = ((), (), s32[]{:S(2)}) async-start(), calls=%async_computation.2 | async-start | bytes 20971520 | tf_op jit(solution)/shard_map/all_gather | solution.py:73
  68.4 531.8 %all-gather.11.cloned.1.call-start = ((), (), s32[]{:S(2)}) async-start(), calls=%async_computation.3 | async-start | bytes 26214400 | tf_op jit(solution)/shard_map/all_gather | solution.py:92
  85.5 84.0 %collective-permute-start.2 = (bf16[512,1280]{1,0:T(8,128)(2,1)}, bf16[512,1280]{1,0:T(8,128)(2,1)}, u32[]{:S(2)}, u32[]{:S(2)}) collective-permute-start(bf16[512,1280]{1,0:T(8,128)(2,1)} %bitcast.207), channel_id=1, source_target_pairs={{0,24},{8,0},{16,8},{24,16},{1,25},{9,1},{17,9},{25,17},{2,26},{10... | collective-permute-start | bytes 3932168 | tf_op jit(solution)/shard_map/ppermute | solution.py:87
  91.1 254.0 %collective-permute-start.1 = (bf16[512,1280]{1,0:T(8,128)(2,1)}, bf16[512,1280]{1,0:T(8,128)(2,1)}, u32[]{:S(2)}, u32[]{:S(2)}) collective-permute-start(bf16[512,1280]{1,0:T(8,128)(2,1)} %bitcast.208), channel_id=1, source_target_pairs={{0,16},{8,24},{16,0},{24,8},{1,17},{9,25},{17,1},{25,9},{2,18},{10... | collective-permute-start | bytes 3932168 | tf_op jit(solution)/shard_map/ppermute | solution.py:87
  92.5 252.6 %collective-permute-start = (bf16[512,1280]{1,0:T(8,128)(2,1)}, bf16[512,1280]{1,0:T(8,128)(2,1)}, u32[]{:S(2)}, u32[]{:S(2)}) collective-permute-start(bf16[512,1280]{1,0:T(8,128)(2,1)} %bitcast.209), channel_id=1, source_target_pairs={{0,8},{8,16},{16,24},{24,0},{1,9},{9,17},{17,25},{25,1},{2,10},{10... | collective-permute-start | bytes 3932168 | tf_op jit(solution)/shard_map/ppermute | solution.py:87
  468.9 195.5 %all-gather.13.cloned.1.call-start = ((), (), s32[]{:S(2)}) async-start(), calls=%async_computation.4 | async-start | bytes 2621440 | tf_op jit(solution)/shard_map/all_gather | solution.py:106
  635.6 2.3 copy-start.1
  664.3 3.2 copy-start
  666.2 1.3 copy-start.2
  667.6 8.2 copy-start.4
  693.7 14.6 %copy-start.7 = (pred[256,2048]{0,1:T(8,128)(4,1)S(1)}, pred[256,2048]{0,1:T(8,128)(4,1)}, u32[]{:S(2)}) copy-start(pred[256,2048]{0,1:T(8,128)(4,1)} %iota_compare_fusion.2) | copy-start | bytes 1572868
  708.3 16.8 %copy-start.8 = (pred[256,1024]{0,1:T(8,128)(4,1)S(1)}, pred[256,1024]{0,1:T(8,128)(4,1)}, u32[]{:S(2)}) copy-start(pred[256,1024]{0,1:T(8,128)(4,1)} %iota_compare_fusion.3) | copy-start | bytes 786436
  725.1 7.4 copy-start.9
  725.1 7.4 copy-start.15
  732.5 16.9 %copy-start.3 = (bf16[4,4,256,2,128]{4,2,1,0,3:T(8,128)(2,1)S(1)}, bf16[4,4,256,2,128]{4,2,1,0,3:T(8,128)(2,1)}, u32[]{:S(2)}) copy-start(bf16[4,4,256,2,128]{4,2,1,0,3:T(8,128)(2,1)} %copy-done.2) | copy-start | bytes 6291460
  732.5 16.9 %copy-start.10 = (s32[3072]{0:T(1024)S(1)}, s32[3072]{0:T(1024)}, u32[]{:S(2)}) copy-start(s32[3072]{0:T(1024)} %iota_multiply_fusion.1) | copy-start | bytes 36868
  732.5 16.9 %copy-start.14 = (s32[8,256]{1,0:T(8,128)S(1)}, s32[8,256]{1,0:T(8,128)}, u32[]{:S(2)}) copy-start(s32[8,256]{1,0:T(8,128)} %get-tuple-element.25) | copy-start | bytes 24580
  749.4 13.3 %copy-start.11 = (s32[2048]{0:T(1024)S(1)}, s32[2048]{0:T(1024)}, u32[]{:S(2)}) copy-start(s32[2048]{0:T(1024)} %iota_multiply_fusion.2) | copy-start | bytes 24580
  749.5 13.3 %copy-start.13 = (s32[8,256]{1,0:T(8,128)S(1)}, s32[8,256]{1,0:T(8,128)}, u32[]{:S(2)}) copy-start(s32[8,256]{1,0:T(8,128)} %get-tuple-element.24) | copy-start | bytes 24580
  749.5 13.3 %copy-start.18 = (bf16[8,256,2048]{1,2,0:T(8,128)(2,1)S(1)}, bf16[8,256,2048]{1,2,0:T(8,128)(2,1)}, u32[]{:S(2)}) copy-start(bf16[8,256,2048]{1,2,0:T(8,128)(2,1)} %get-tuple-element.32) | copy-start | bytes 25165828
  762.8 6.8 copy-start.12
  762.8 6.8 copy-start.16
  762.8 6.8 copy-start.17
Sparse Core Ops, SparseCore 0:
  8.9 59.4 all-gather.6
  70.0 398.8 all-gather.8
  470.4 129.7 all-gather.10
  641.7 22.5 all-gather.12

commit v6 on v5

--- a/solution.py
+++ b/solution.py
@@ -70,7 +70,6 @@
     rows = n_g * tok
 
     full_rows = lax.all_gather(activations, "fsdp", axis=1, tiled=True)
-    grp_rows = lax.all_gather(full_rows, "cg", axis=0, tiled=True)
 
     local_w = jnp.concatenate(
         [
@@ -88,8 +87,10 @@
     by_shift = jnp.stack(received, axis=0)
     back = (g - jnp.arange(n_g, dtype=jnp.int32)) % n_g
     mine = jnp.take(by_shift, back, axis=0)
-    grp_rows, mine = lax.optimization_barrier((grp_rows, mine))
+    full_rows, mine = lax.optimization_barrier((full_rows, mine))
     every = lax.all_gather(mine, "ct", axis=0, tiled=False)
+    full_rows, every = lax.optimization_barrier((full_rows, every))
+    grp_rows = lax.all_gather(full_rows, "cg", axis=0, tiled=True)
     every = every.transpose(1, 0, 2, 3).reshape(n_g * n_t * d_rows, qcols + 2 * HD)
 
     mixed = jnp.dot(grp_rows, every, preferred_element_type=jnp.float32)

time: 841 us -> 809 us (0.962)
  waiting for transfers between devices: 556 us -> 513 us
    ppermute x3, waiting for transfers between devices: 251 us -> 81.4 us  [shards(): received.append(lax.ppermute(outgoing, 'cg', perm))]
    all_gather x1, waiting for transfers between devices: 107 us -> 264 us  [shards(): grp_rows = lax.all_gather(full_rows, 'cg', axis=0, tiled=True)]
    all_gather x1, waiting for transfers between devices: 61.1 us -> 0.01 us  [shards(): full_rows = lax.all_gather(activations, 'fsdp', axis=1, tiled=True)]
    all_gather x1, waiting for transfers between devices: 124 us -> 157 us  [shards(): every = lax.all_gather(mine, 'ct', axis=0, tiled=False)]
  transfers between devices with their start and end apart: 7 -> 7, of which waited for: 6 -> 5; matrix products, arithmetic and copies ran while one was open for 6% -> 9% of each run, Pallas kernels for 0% -> 0%
where the time goes in v6:
time: 809 us; the launch traced here: 800 us
  waiting for transfers between devices  513 us (63%)
  matrix products  111 us (14%)
  local copies, waits for them, and re-layouts  53.3 us (7%)
  blocking collectives  53 us (7%)
  other arithmetic  46.6 us (6%)
  between operations  16.1 us (2%)
    all_gather x1, waiting for transfers between devices, shards(): grp_rows = lax.all_gather(full_rows, 'cg', axis=0, tiled=True)  264 us
    all_gather x1, waiting for transfers between devices, shards(): every = lax.all_gather(mine, 'ct', axis=0, tiled=False)  157 us
    ppermute x3, waiting for transfers between devices, shards(): received.append(lax.ppermute(outgoing, 'cg', perm))  81.4 us
    all_to_all x1, blocking collectives, shards(): lax.all_to_all(out_rows, 'cg', split_axis=0, concat_axis=2, tiled=True)  53 us
    sub x3, matrix products, shards(): weights = jnp.where(visible, jnp.exp(scores - highest), 0.0)  40.4 us
    dot_general x4, matrix products, shards(): jnp.einsum('hqk,ke->hqe', dropped, all_values[:span], preferred_element_t...  36.4 us
    dot_general x1, matrix products, shards(): mixed = jnp.dot(grp_rows, every, preferred_element_type=jnp.float32)  26.5 us
    transpose x1, local copies, waits for them, and re-layouts, shards(): every.transpose(1, 0, 2, 3).reshape(n_g * n_t * d_rows, qcols + 2 * HD)  18.1 us
  transfers between devices with their start and end apart: 7, of which 5 were waited for; matrix products, arithmetic and copies ran while one was open for 9% of the time, Pallas kernels for 0%

profile of v6, /device:TPU:0, one launch (start us, length us, event | category | flops | bytes accessed | tf_op | source)
XLA Modules:
  0.0 799.6 jit_solution(16004522630029773506)
XLA Ops:
  6.5 0.7 all-gather.7.cloned.1.call-update
  7.3 0.0 all-gather.11.cloned.1.call-start
  7.4 6.5 copy.72
  13.9 0.2 copy.73
  14.1 0.2 copy.74
  14.4 5.2 pad_maximum_fusion
  19.6 2.0 constant_dynamic-slice_fusion.3
  21.6 2.5 copy.77
  24.1 4.0 collective-permute-start.1
  28.2 2.4 copy.78
  30.6 1.4 collective-permute-start.2
  32.0 1.4 copy.76
  33.4 0.7 collective-permute-start
  34.1 0.6 copy.75
  34.7 52.3 %collective-permute-done.1 = bf16[512,1280]{1,0:T(8,128)(2,1)} collective-permute-done((bf16[512,1280]{1,0:T(8,128)(2,1)}, bf16[512,1280]{1,0:T(8,128)(2,1)}, u32[]{:S(2)}, u32[]{:S(2)}) %collective-permute-start.1) | collective-permute-done | bytes 1310752 | tf_op jit(solution)/shard_map/ppermute | solution.py:86
  87.1 29.1 %collective-permute-done.2 = bf16[512,1280]{1,0:T(8,128)(2,1)} collective-permute-done((bf16[512,1280]{1,0:T(8,128)(2,1)}, bf16[512,1280]{1,0:T(8,128)(2,1)}, u32[]{:S(2)}, u32[]{:S(2)}) %collective-permute-start.2) | collective-permute-done | bytes 1310752 | tf_op jit(solution)/shard_map/ppermute | solution.py:86
  116.2 0.0 collective-permute-done
  116.2 5.2 pad_maximum_fusion.1
  121.4 5.7 gather_fusion
  127.1 5.4 broadcast_select_fusion
  132.5 0.0 all-gather.11.cloned.1.call-update
  132.5 0.0 all-gather.9.cloned.1.call-start
  132.5 157.4 %all-gather.11.cloned.1.call-done = bf16[16,512,1280]{2,1,0:T(8,128)(2,1)} async-done(((bf16[4,512,1280]{2,1,0:T(8,128)(2,1)}), bf16[16,512,1280]{2,1,0:T(8,128)(2,1)}) %all-gather.11.cloned.1.call-update) | async-done | bytes 20971536 | tf_op jit(solution)/shard_map/all_gather | solution.py:91
  289.9 0.0 all-gather.9.cloned.1.call-update
  290.0 0.0 all-gather.13.cloned.1.call-start
  292.1 0.6 iota_multiply_fusion.3
  292.7 0.6 iota_multiply_fusion.2
  293.3 0.6 iota_multiply_fusion.1
  293.9 0.6 iota_multiply_fusion
  294.5 0.7 shift-right-logical_xor_fusion.21
  295.2 0.2 iota_compare_fusion.3
  295.3 1.1 iota_compare_fusion.2
  296.5 18.1 %copy.79 = bf16[4,4,512,1280]{3,2,1,0:T(8,128)(2,1)} copy(bf16[4,4,512,1280]{3,2,0,1:T(8,128)(2,1)} %bitcast.190) | data formatting | bytes 41943040 | tf_op jit(solution)/shard_map/transpose | solution.py:94
  314.6 263.7 %all-gather.9.cloned.1.call-done = bf16[1024,8192]{1,0:T(8,128)(2,1)} async-done(((bf16[256,8192]{1,0:T(8,128)(2,1)}), bf16[1024,8192]{1,0:T(8,128)(2,1)}) %all-gather.9.cloned.1.call-update) | async-done | bytes 16777232 | tf_op jit(solution)/shard_map/all_gather | solution.py:93
  578.3 26.5 %fusion.162 = f32[1024,1280]{1,0:T(8,128)S(1)} fusion(bf16[1024,8192]{1,0:T(8,128)(2,1)} %all-gather.9.cloned.1.call-done, bf16[8192,1280]{1,0:T(8,128)(2,1)} %bitcast.191), kind=kOutput, calls=%fused_computation.255 | convolution fusion | flops 21474836480 | bytes 42991616 | tf_op jit(solution)/shard_map/dot_general | solution.py:96
  604.8 2.3 copy-done.1
  607.1 2.4 multiply_cosine_fusion
  609.5 0.9 pad_maximum_fusion.4
  610.5 0.0 all-gather.13.cloned.1.call-update
  610.5 1.4 iota_compare_fusion.1
  611.9 1.6 iota_compare_fusion
  613.5 2.7 slice_bitcast_fusion
  616.3 1.0 copy.107
  617.3 1.3 fusion.149
  618.6 3.0 subtract_convert_fusion
  621.6 9.8 %all-gather.13.cloned.1.call-done = bf16[4096,2,128]{2,0,1:T(8,128)(2,1)} async-done(((bf16[1024,2,128]{2,0,1:T(8,128)(2,1)}), bf16[4096,2,128]{2,0,1:T(8,128)(2,1)}) %all-gather.13.cloned.1.call-update) | async-done | bytes 2097168 | tf_op jit(solution)/shard_map/all_gather | solution.py:107
  631.4 1.9 copy.80
  633.3 0.0 copy-start.2
  633.3 1.3 copy-done.2
  634.6 8.2 %fusion.67 = f32[2048,256,8]{1,0,2:T(8,128)} fusion(bf16[1024,8,64]{2,0,1:T(8,128)(2,1)S(1)} %get-tuple-element.13, bf16[1024,8,64]{2,0,1:T(8,128)(2,1)S(1)} %copy-done, bf16[4096,2,128]{2,0,1:T(8,128)(2,1)S(1)} %bitcast.195), kind=kOutput, calls=%fused_computation.116 | convolution fusion | flops 1074790400 | bytes 21495808 | tf_op jit(solution)/shard_map/qhe,ke->hqk/dot_general | solution.py:123
  642.8 7.8 fusion.157
  650.6 16.6 %fusion.156 = (f32[8,256]{1,0:T(8,128)S(1)}, bf16[8,256,2048]{1,2,0:T(8,128)(2,1)}) fusion(f32[2048,256,8]{1,0,2:T(8,128)} %fusion.67, pred[256,2048]{0,1:T(8,128)(4,1)S(1)} %copy-done.7), kind=kOutput, calls=%fused_computation.253 | output fusion | flops 29362176 | bytes 25698304 | tf_op jit(solution)/shard_map/sub | solution.py:133
  667.2 14.6 %fusion.151 = (f32[8,256]{1,0:T(8,128)S(1)}, bf16[8,256,3072]{1,2,0:T(8,128)(2,1)}) fusion(pred[256,3072]{0,1:T(8,128)(4,1)} %iota_compare_fusion.1, bf16[4096,2,128]{2,0,1:T(8,128)(2,1)} %bitcast.197, bf16[1024,8,64]{2,0,1:T(8,128)(2,1)S(1)} %get-tuple-element.13, bf16[1024,8,64]{2,0,1:T(8,128)(2,1)} %get-tuple-element.14), kind=kOutput, calls=%fused_computation.252 | convolution fusion | flops 3267365888 | bytes 24125440 | tf_op jit(solution)/shard_map/sub | solution.py:133
  681.8 17.9 %fusion.150 = (f32[8,256]{1,0:T(8,128)S(1)}, bf16[8,256,4096]{1,2,0:T(8,128)(2,1)}) fusion(pred[256,4096]{0,1:T(8,128)(4,1)S(1)} %copy-done.4, bf16[4096,2,128]{2,0,1:T(8,128)(2,1)} %bitcast.198, bf16[1024,8,64]{2,0,1:T(8,128)(2,1)} %get-tuple-element.14, bf16[1024,8,64]{2,0,1:T(8,128)(2,1)S(1)} %get-tuple-element.13), kind=kOutput, calls=%fused_computation.251 | convolution fusion | flops 4355788800 | bytes 29368320 | tf_op jit(solution)/shard_map/sub | solution.py:133
  699.8 0.0 copy-start.3
  699.9 0.0 slice-start.4
  699.9 5.8 divide_convert_fusion.3
  705.8 0.0 slice-start.5
  705.8 6.7 divide_convert_fusion.2
  712.7 10.2 %divide_convert_fusion.1 = bf16[256,8,128]{0,2,1:T(8,128)(2,1)S(1)} fusion(bf16[8,256,3072]{1,2,0:T(8,128)(2,1)S(1)} %bitcast.216, s32[3072]{0:T(1024)S(1)} %copy-done.9, s32[8,256]{1,0:T(8,128)S(1)} %copy-done.12, bf16[4096,2,128]{2,0,1:T(8,128)(2,1)S(1)} %bitcast.201, f32[256,8]{0,1:T(8,128)S(1)} %multiply_bitcast_fusion.1), kind=kOutput, calls=%fused_computation.103 | convolution fusion | flops 1686634496 | bytes 13922304 | tf_op jit(solution)/shard_map/hqk,ke->hqe/dot_general | solution.py:139
  723.0 13.6 %divide_convert_fusion = bf16[256,8,128]{0,2,1:T(8,128)(2,1)S(1)} fusion(bf16[4096,2,128]{2,0,1:T(8,128)(2,1)S(1)} %bitcast.202, bf16[8,256,4096]{1,2,0:T(8,128)(2,1)S(1)} %bitcast.214, s32[4096]{0:T(1024)S(1)} %copy-done.8, s32[8,256]{1,0:T(8,128)S(1)} %copy-done.11, f32[256,8]{0,1:T(8,128)S(1)} %multiply_bitcast_fusion), kind=kOutput, calls=%fused_computation.102 | convolution fusion | flops 2248671232 | bytes 18382848 | tf_op jit(solution)/shard_map/hqk,ke->hqe/dot_general | solution.py:139
  736.6 0.3 pad_maximum_fusion.2
  736.8 53.0 %all_to_all.15 = bf16[4,256,1024]{1,2,0:T(8,128)(2,1)S(1)} all-to-all(bf16[4,256,1024]{1,2,0:T(8,128)(2,1)S(1)} %pad_maximum_fusion.2), channel_id=1, replica_groups=mesh['cg'=4,'ct'=4,'fsdp'=2] {'cg'}, dimensions={0} | all-to-all | bytes 4194304 | tf_op jit(solution)/shard_map/all_to_all | solution.py:145
  789.8 2.8 copy.104
  (60 shorter events, 0.2 us)
Async XLA Ops:
  6.5 7.4 copy-start.5
  6.5 125.9 %all-gather.7.cloned.1.call-start = ((), (), s32[]{:S(2)}) async-start(), calls=%async_computation.1 | async-start | bytes 6291456 | tf_op jit(solution)/shard_map/all_gather | solution.py:72
  7.3 6.9 copy-start.6
  7.3 282.7 %all-gather.11.cloned.1.call-start = ((), (), s32[]{:S(2)}) async-start(), calls=%async_computation.3 | async-start | bytes 26214400 | tf_op jit(solution)/shard_map/all_gather | solution.py:91
  24.1 62.9 %collective-permute-start.1 = (bf16[512,1280]{1,0:T(8,128)(2,1)}, bf16[512,1280]{1,0:T(8,128)(2,1)}, u32[]{:S(2)}, u32[]{:S(2)}) collective-permute-start(bf16[512,1280]{1,0:T(8,128)(2,1)} %bitcast.206), channel_id=1, source_target_pairs={{0,16},{8,24},{16,0},{24,8},{1,17},{9,25},{17,1},{25,9},{2,18},{10... | collective-permute-start | bytes 3932168 | tf_op jit(solution)/shard_map/ppermute | solution.py:86
  30.6 85.6 %collective-permute-start.2 = (bf16[512,1280]{1,0:T(8,128)(2,1)}, bf16[512,1280]{1,0:T(8,128)(2,1)}, u32[]{:S(2)}, u32[]{:S(2)}) collective-permute-start(bf16[512,1280]{1,0:T(8,128)(2,1)} %bitcast.207), channel_id=1, source_target_pairs={{0,24},{8,0},{16,8},{24,16},{1,25},{9,1},{17,9},{25,17},{2,26},{10... | collective-permute-start | bytes 3932168 | tf_op jit(solution)/shard_map/ppermute | solution.py:86
  33.4 82.8 %collective-permute-start = (bf16[512,1280]{1,0:T(8,128)(2,1)}, bf16[512,1280]{1,0:T(8,128)(2,1)}, u32[]{:S(2)}, u32[]{:S(2)}) collective-permute-start(bf16[512,1280]{1,0:T(8,128)(2,1)} %bitcast.208), channel_id=1, source_target_pairs={{0,8},{8,16},{16,24},{24,0},{1,9},{9,17},{17,25},{25,1},{2,10},{10... | collective-permute-start | bytes 3932168 | tf_op jit(solution)/shard_map/ppermute | solution.py:86
  132.5 445.8 %all-gather.9.cloned.1.call-start = ((), (), s32[]{:S(2)}) async-start(), calls=%async_computation.2 | async-start | bytes 20971520 | tf_op jit(solution)/shard_map/all_gather | solution.py:93
  290.0 341.5 %all-gather.13.cloned.1.call-start = ((), (), s32[]{:S(2)}) async-start(), calls=%async_computation.4 | async-start | bytes 2621440 | tf_op jit(solution)/shard_map/all_gather | solution.py:107
  604.8 2.3 copy-start.1
  631.4 3.2 copy-start
  633.3 1.3 copy-start.2
  642.8 7.8 copy-start.7
  667.2 14.6 %copy-start.4 = (pred[256,4096]{0,1:T(8,128)(4,1)S(1)}, pred[256,4096]{0,1:T(8,128)(4,1)}, u32[]{:S(2)}) copy-start(pred[256,4096]{0,1:T(8,128)(4,1)} %iota_compare_fusion) | copy-start | bytes 3145732
  681.8 18.0 %copy-start.14 = (s32[8,256]{1,0:T(8,128)S(1)}, s32[8,256]{1,0:T(8,128)}, u32[]{:S(2)}) copy-start(s32[8,256]{1,0:T(8,128)} %get-tuple-element.27) | copy-start | bytes 24580
  681.8 18.0 %copy-start.15 = (s32[1024]{0:T(1024)S(1)}, s32[1024]{0:T(1024)}, u32[]{:S(2)}) copy-start(s32[1024]{0:T(1024)} %iota_multiply_fusion.3) | copy-start | bytes 12292
  699.8 5.9 copy-start.3
  699.8 5.9 copy-start.10
  699.9 5.9 copy-start.13
  699.9 5.9 copy-start.16
  699.9 12.7 %slice-start.4 = ((s8[12582912]{0:T(1024)(128)(4,1)}), s8[4194304]{0:T(1024)(128)(4,1)S(1)}, s32[]{:S(2)}) async-start(s8[12582912]{0:T(1024)(128)(4,1)} %bitcast.215), calls=%async_computation.9 | async-start | bytes 8388608
  705.8 6.8 copy-start.9
  705.8 6.8 copy-start.12
  705.8 6.8 slice-start.5
  705.8 6.8 slice-start.6
  705.8 17.1 %slice-start = ((s8[16777216]{0:T(1024)(128)(4,1)}), s8[4194304]{0:T(1024)(128)(4,1)S(1)}, s32[]{:S(2)}) async-start(s8[16777216]{0:T(1024)(128)(4,1)} %bitcast.213), calls=%async_computation.5 | async-start | bytes 8388608
  705.8 17.1 %slice-start.1 = ((s8[16777216]{0:T(1024)(128)(4,1)}), s8[4194304]{0:T(1024)(128)(4,1)S(1)}, s32[]{:S(2)}) async-start(s8[16777216]{0:T(1024)(128)(4,1)} %bitcast.213), calls=%async_computation.6 | async-start | bytes 8388608
  712.6 10.3 %copy-start.8 = (s32[4096]{0:T(1024)S(1)}, s32[4096]{0:T(1024)}, u32[]{:S(2)}) copy-start(s32[4096]{0:T(1024)} %iota_multiply_fusion) | copy-start | bytes 49156
  712.6 10.3 %copy-start.11 = (s32[8,256]{1,0:T(8,128)S(1)}, s32[8,256]{1,0:T(8,128)}, u32[]{:S(2)}) copy-start(s32[8,256]{1,0:T(8,128)} %get-tuple-element.30) | copy-start | bytes 24580
  712.7 10.3 %slice-start.2 = ((s8[16777216]{0:T(1024)(128)(4,1)}), s8[4194304]{0:T(1024)(128)(4,1)S(1)}, s32[]{:S(2)}) async-start(s8[16777216]{0:T(1024)(128)(4,1)} %bitcast.213), calls=%async_computation.7 | async-start | bytes 8388608
  712.7 10.3 %slice-start.3 = ((s8[16777216]{0:T(1024)(128)(4,1)}), s8[4194304]{0:T(1024)(128)(4,1)S(1)}, s32[]{:S(2)}) async-start(s8[16777216]{0:T(1024)(128)(4,1)} %bitcast.213), calls=%async_computation.8 | async-start | bytes 8388608
Sparse Core Ops, SparseCore 0:
  8.9 59.4 all-gather.6
  132.6 157.2 all-gather.10
  291.5 286.7 all-gather.8
  610.6 20.7 all-gather.12

commit v7 on v6

--- a/solution.py
+++ b/solution.py
@@ -69,8 +69,6 @@
     qcols = group_heads * HD
     rows = n_g * tok
 
-    full_rows = lax.all_gather(activations, "fsdp", axis=1, tiled=True)
-
     local_w = jnp.concatenate(
         [
             w_query.reshape(d_rows, n_g, qcols),
@@ -87,13 +85,32 @@
     by_shift = jnp.stack(received, axis=0)
     back = (g - jnp.arange(n_g, dtype=jnp.int32)) % n_g
     mine = jnp.take(by_shift, back, axis=0)
+
+    if lax.axis_size("fsdp") == 2:
+        other_half = lax.ppermute(activations, "fsdp", [(0, 1), (1, 0)])
+        full_rows = jnp.where(
+            f == 0,
+            jnp.concatenate([activations, other_half], axis=1),
+            jnp.concatenate([other_half, activations], axis=1),
+        )
+    else:
+        full_rows = lax.all_gather(activations, "fsdp", axis=1, tiled=True)
+    grp_rows = [full_rows]
     full_rows, mine = lax.optimization_barrier((full_rows, mine))
+    for shift in range(1, n_g):
+        perm = [(i, (i + shift) % n_g) for i in range(n_g)]
+        grp_rows.append(lax.ppermute(full_rows, "cg", perm))
+    grp_rows = jnp.concatenate(grp_rows, axis=0)
+
     every = lax.all_gather(mine, "ct", axis=0, tiled=False)
-    full_rows, every = lax.optimization_barrier((full_rows, every))
-    grp_rows = lax.all_gather(full_rows, "cg", axis=0, tiled=True)
-    every = every.transpose(1, 0, 2, 3).reshape(n_g * n_t * d_rows, qcols + 2 * HD)
 
-    mixed = jnp.dot(grp_rows, every, preferred_element_type=jnp.float32)
+    mixed = jnp.einsum(
+        "rgtd,tgdc->rc",
+        grp_rows.reshape(rows, n_g, n_t, d_rows),
+        every,
+        preferred_element_type=jnp.float32,
+    )
+    mixed = jnp.take(mixed.reshape(n_g, tok, -1), back, axis=0).reshape(rows, -1)
     chunk_of_row = n_t * (jnp.arange(rows, dtype=jnp.int32) // tok) + t
     positions = chunk_of_row * tok + jnp.arange(rows, dtype=jnp.int32) % tok
     cosine, sine_part = rotation(positions)

time: 809 us -> 898 us (1.11)
  starting transfers between devices: 6.17 us -> 127 us
  waiting for transfers between devices: 513 us -> 429 us
  local copies, waits for them, and re-layouts: 53.3 us -> 81.7 us
  other arithmetic: 46.6 us -> 69.7 us
    all_gather x2 -> x0, waiting for transfers between devices: 264 us -> none  [the longest x1 264 us: shards(): grp_rows = lax.all_gather(full_rows, 'cg', axis=0, tiled=True)]
    ppermute x0 -> x4, waiting for transfers between devices: none -> 262 us  [the longest x3 262 us: shards(): grp_rows.append(lax.ppermute(full_rows, 'cg', perm))]
    all_gather x1, waiting for transfers between devices: 157 us -> 0.01 us  [shards(): every = lax.all_gather(mine, 'ct', axis=0, tiled=False)]
    ppermute x0 -> x4, starting transfers between devices: none -> 121 us  [the longest x3 120 us: shards(): grp_rows.append(lax.ppermute(full_rows, 'cg', perm))]
    all_gather x1, waiting for transfers between devices: 9.8 us -> 91.8 us  [shards(): pair = lax.all_gather(pair, 'ct', axis=0, tiled=False)]
    dot_general x0 -> x1, local copies, waits for them, and re-layouts: none -> 21.6 us  [shards(): jnp.einsum('rgtd,tgdc->rc', grp_rows.reshape(rows, n_g, n_t, d_rows), eve...]
    transpose x2 -> x0, local copies, waits for them, and re-layouts: 20 us -> none  [the longest x1 18.1 us: shards(): every.transpose(1, 0, 2, 3).reshape(n_g * n_t * d_rows, qcols + 2 * HD)]
    concatenate x0 -> x1, other arithmetic: none -> 14.1 us  [shards(): grp_rows = jnp.concatenate(grp_rows, axis=0)]
  transfers between devices with their start and end apart: 7 -> 9, of which waited for: 5 -> 6; matrix products, arithmetic and copies ran while one was open for 9% -> 9% of each run, Pallas kernels for 0% -> 0%
where the time goes in v7:
time: 898 us; the launch traced here: 892 us
  waiting for transfers between devices  429 us (48%)
  starting transfers between devices  127 us (14%)
  matrix products  114 us (13%)
  local copies, waits for them, and re-layouts  81.7 us (9%)
  other arithmetic  69.7 us (8%)
  blocking collectives  53 us (6%)
  between operations  16.3 us (2%)
    ppermute x3, waiting for transfers between devices, shards(): grp_rows.append(lax.ppermute(full_rows, 'cg', perm))  262 us
    ppermute x3, starting transfers between devices, shards(): grp_rows.append(lax.ppermute(full_rows, 'cg', perm))  120 us
    all_gather x1, waiting for transfers between devices, shards(): pair = lax.all_gather(pair, 'ct', axis=0, tiled=False)  91.8 us
    ppermute x3, waiting for transfers between devices, shards(): received.append(lax.ppermute(outgoing, 'cg', perm))  75.6 us
    all_to_all x1, blocking collectives, shards(): lax.all_to_all(out_rows, 'cg', split_axis=0, concat_axis=2, tiled=True)  53 us
    sub x3, matrix products, shards(): weights = jnp.where(visible, jnp.exp(scores - highest), 0.0)  40.1 us
    dot_general x4, matrix products, shards(): jnp.einsum('hqk,ke->hqe', dropped, all_values[:span], preferred_element_t...  36.4 us
    dot_general x1, matrix products, shards(): jnp.einsum('rgtd,tgdc->rc', grp_rows.reshape(rows, n_g, n_t, d_rows), eve...  28.6 us
  transfers between devices with their start and end apart: 9, of which 6 were waited for; matrix products, arithmetic and copies ran while one was open for 9% of the time, Pallas kernels for 0%

profile of v7, /device:TPU:0, one launch (start us, length us, event | category | flops | bytes accessed | tf_op | source)
XLA Modules:
  0.0 891.7 jit_solution(4499141345315585566)
XLA Ops:
  6.5 6.6 copy.65
  13.1 0.2 copy.66
  13.3 0.2 copy.67
  13.6 5.2 pad_maximum_fusion.1
  18.8 2.0 constant_dynamic-slice_fusion.3
  20.8 2.5 copy.70
  23.3 4.0 collective-permute-start.2
  27.3 1.5 copy.71
  28.8 1.3 collective-permute-start.3
  30.1 1.4 copy.69
  31.6 0.7 collective-permute-start.1
  32.2 3.3 copy.63
  35.5 1.6 collective-permute-start
  37.1 1.6 copy.68
  38.8 47.5 %collective-permute-done.2 = bf16[512,1280]{1,0:T(8,128)(2,1)} collective-permute-done((bf16[512,1280]{1,0:T(8,128)(2,1)}, bf16[512,1280]{1,0:T(8,128)(2,1)}, u32[]{:S(2)}, u32[]{:S(2)}) %collective-permute-start.2) | collective-permute-done | bytes 1310752 | tf_op jit(solution)/shard_map/ppermute | solution.py:84
  86.2 28.1 %collective-permute-done.3 = bf16[512,1280]{1,0:T(8,128)(2,1)} collective-permute-done((bf16[512,1280]{1,0:T(8,128)(2,1)}, bf16[512,1280]{1,0:T(8,128)(2,1)}, u32[]{:S(2)}, u32[]{:S(2)}) %collective-permute-start.3) | collective-permute-done | bytes 1310752 | tf_op jit(solution)/shard_map/ppermute | solution.py:84
  114.3 5.2 pad_maximum_fusion.2
  119.5 5.7 gather_fusion
  125.2 5.3 broadcast_select_fusion
  130.5 4.2 maximum_select_fusion
  134.8 116.9 %collective-permute-start.4 = (bf16[256,8192]{0,1:T(8,128)(2,1)}, bf16[256,8192]{0,1:T(8,128)(2,1)}, u32[]{:S(2)}, u32[]{:S(2)}) collective-permute-start(bf16[256,8192]{0,1:T(8,128)(2,1)} %maximum_select_fusion), channel_id=1, source_target_pairs={{0,8},{8,16},{16,24},{24,0},{1,9},{9,17},{17,25},{25,1},{2,10},{10... | collective-permute-start | bytes 12582920 | tf_op jit(solution)/shard_map/ppermute | solution.py:102
  251.7 2.6 collective-permute-start.6
  254.3 0.1 broadcast_in_dim.167
  256.5 0.6 iota_multiply_fusion.2
  257.1 0.6 iota_multiply_fusion.1
  257.7 0.7 shift-right-logical_xor_fusion.21
  258.3 0.9 iota_compare_fusion.3
  259.2 83.8 %collective-permute-done.4 = bf16[256,8192]{0,1:T(8,128)(2,1)} collective-permute-done((bf16[256,8192]{0,1:T(8,128)(2,1)}, bf16[256,8192]{0,1:T(8,128)(2,1)}, u32[]{:S(2)}, u32[]{:S(2)}) %collective-permute-start.4) | collective-permute-done | bytes 4194336 | tf_op jit(solution)/shard_map/ppermute | solution.py:102
  343.0 91.1 %collective-permute-done.5 = bf16[256,8192]{0,1:T(8,128)(2,1)} collective-permute-done((bf16[256,8192]{0,1:T(8,128)(2,1)}, bf16[256,8192]{0,1:T(8,128)(2,1)}, u32[]{:S(2)}, u32[]{:S(2)}) %collective-permute-start.5) | collective-permute-done | bytes 4194336 | tf_op jit(solution)/shard_map/ppermute | solution.py:102
  434.2 86.9 %collective-permute-done.6 = bf16[256,8192]{0,1:T(8,128)(2,1)} collective-permute-done((bf16[256,8192]{0,1:T(8,128)(2,1)}, bf16[256,8192]{0,1:T(8,128)(2,1)}, u32[]{:S(2)}, u32[]{:S(2)}) %collective-permute-start.6) | collective-permute-done | bytes 4194336 | tf_op jit(solution)/shard_map/ppermute | solution.py:102
  521.1 14.1 %pad_maximum_fusion = bf16[1024,8192]{0,1:T(8,128)(2,1)} fusion(bf16[256,8192]{0,1:T(8,128)(2,1)} %collective-permute-done.6, bf16[256,8192]{0,1:T(8,128)(2,1)} %collective-permute-done.5, bf16[256,8192]{0,1:T(8,128)(2,1)} %collective-permute-done.4, bf16[256,8192]{0,1:T(8,128)(2,1)} %maximum_select_fusion), kind=kLoop, calls=%fused_computation.43 | loop fusion | flops 67108864 | bytes 33554432 | tf_op jit(solution)/shard_map/concatenate | solution.py:103
  535.2 21.6 %copy.72 = bf16[1024,512,4,4]{1,0,3,2:T(8,128)(2,1)} copy(bf16[1024,512,4,4]{0,1,3,2:T(8,128)(2,1)} %bitcast.196) | data formatting | bytes 33554432 | tf_op jit(solution)/shard_map/rgtd,tgdc->rc/dot_general | solution.py:107
  556.8 28.6 %fusion.50 = f32[4,256,1280]{2,1,0:T(8,128)} fusion(bf16[4,256,512,4,4]{2,1,0,4,3:T(8,128)(2,1)} %bitcast.199, bf16[4,4,512,1280,1]{3,2,1,0,4:T(8,128)(2,1)} %bitcast.219), kind=kOutput, calls=%fused_computation.80 | convolution fusion | flops 21474836480 | bytes 42991616 | tf_op jit(solution)/shard_map/rgtd,tgdc->rc/dot_general | solution.py:107
  585.4 5.7 gather_fusion.1
  591.1 6.0 copy.74
  597.1 3.1 broadcast_select_fusion.1
  600.3 2.3 copy-done
  602.6 1.1 multiply_cosine_fusion
  603.7 0.8 pad_maximum_fusion.5
  604.6 0.6 iota_multiply_fusion
  605.2 1.2 iota_compare_fusion.2
  606.3 1.4 iota_compare_fusion.1
  607.7 1.7 iota_compare_fusion
  609.4 1.8 fusion.154
  611.2 3.9 copy.106
  615.1 2.7 copy.107
  617.8 0.2 copy.77
  618.0 0.2 copy.79
  618.2 6.0 subtract_convert_fusion
  624.2 91.8 %all-gather.7.cloned.1.call-done = bf16[4096,2,128]{0,2,1:T(8,128)(2,1)} async-done(((bf16[1024,2,128]{0,2,1:T(8,128)(2,1)}), bf16[4096,2,128]{0,2,1:T(8,128)(2,1)}) %all-gather.7.cloned.1.call-update) | async-done | bytes 2097168 | tf_op jit(solution)/shard_map/all_gather | solution.py:124
  716.0 4.5 reshape.535
  720.5 4.9 copy.75
  725.5 9.4 %fusion.72 = f32[2048,256,8]{1,0,2:T(8,128)} fusion(bf16[1024,8,64]{2,0,1:T(8,128)(2,1)S(1)} %get-tuple-element.9, bf16[1024,8,64]{2,0,1:T(8,128)(2,1)} %get-tuple-element.10, bf16[4096,2,128]{2,0,1:T(8,128)(2,1)} %bitcast.203), kind=kOutput, calls=%fused_computation.120 | convolution fusion | flops 1074790400 | bytes 20447232 | tf_op jit(solution)/shard_map/qhe,ke->hqk/dot_general | solution.py:140
  734.8 7.4 fusion.162
  742.2 16.6 %fusion.161 = (f32[8,256]{1,0:T(8,128)S(1)}, bf16[8,256,2048]{1,2,0:T(8,128)(2,1)}) fusion(f32[2048,256,8]{1,0,2:T(8,128)} %fusion.72, pred[256,2048]{0,1:T(8,128)(4,1)S(1)} %copy-done.5), kind=kOutput, calls=%fused_computation.259 | output fusion | flops 29362176 | bytes 25698304 | tf_op jit(solution)/shard_map/sub | solution.py:150
  758.8 14.7 %fusion.156 = (f32[8,256]{1,0:T(8,128)S(1)}, bf16[8,256,3072]{1,2,0:T(8,128)(2,1)}) fusion(pred[256,3072]{0,1:T(8,128)(4,1)} %iota_compare_fusion.1, bf16[4096,2,128]{2,0,1:T(8,128)(2,1)} %bitcast.205, bf16[1024,8,64]{2,0,1:T(8,128)(2,1)S(1)} %get-tuple-element.9, bf16[1024,8,64]{2,0,1:T(8,128)(2,1)} %get-tuple-element.10), kind=kOutput, calls=%fused_computation.258 | convolution fusion | flops 3267365888 | bytes 24125440 | tf_op jit(solution)/shard_map/sub | solution.py:150
  773.5 18.0 %fusion.155 = (f32[8,256]{1,0:T(8,128)S(1)}, bf16[8,256,4096]{1,2,0:T(8,128)(2,1)}) fusion(pred[256,4096]{0,1:T(8,128)(4,1)S(1)} %copy-done.2, bf16[4096,2,128]{2,0,1:T(8,128)(2,1)} %bitcast.206, bf16[1024,8,64]{2,0,1:T(8,128)(2,1)} %get-tuple-element.10, bf16[1024,8,64]{2,0,1:T(8,128)(2,1)S(1)} %get-tuple-element.9), kind=kOutput, calls=%fused_computation.257 | convolution fusion | flops 4355788800 | bytes 29368320 | tf_op jit(solution)/shard_map/sub | solution.py:150
  791.6 5.8 divide_convert_fusion.3
  797.6 6.7 divide_convert_fusion.2
  804.4 10.2 %divide_convert_fusion.1 = bf16[256,8,128]{0,2,1:T(8,128)(2,1)S(1)} fusion(bf16[8,256,3072]{1,2,0:T(8,128)(2,1)S(1)} %bitcast.223, s32[3072]{0:T(1024)S(1)} %copy-done.8, s32[8,256]{1,0:T(8,128)S(1)} %copy-done.11, bf16[4096,2,128]{2,0,1:T(8,128)(2,1)S(1)} %bitcast.209, f32[256,8]{0,1:T(8,128)S(1)} %multiply_bitcast_fusion.1), kind=kOutput, calls=%fused_computation.109 | convolution fusion | flops 1686634496 | bytes 13922304 | tf_op jit(solution)/shard_map/hqk,ke->hqe/dot_general | solution.py:156
  814.7 13.6 %divide_convert_fusion = bf16[256,8,128]{0,2,1:T(8,128)(2,1)S(1)} fusion(bf16[4096,2,128]{2,0,1:T(8,128)(2,1)S(1)} %bitcast.210, bf16[8,256,4096]{1,2,0:T(8,128)(2,1)S(1)} %bitcast.221, s32[4096]{0:T(1024)S(1)} %copy-done.7, s32[8,256]{1,0:T(8,128)S(1)} %copy-done.10, f32[256,8]{0,1:T(8,128)S(1)} %multiply_bitcast_fusion), kind=kOutput, calls=%fused_computation.108 | convolution fusion | flops 2248671232 | bytes 18382848 | tf_op jit(solution)/shard_map/hqk,ke->hqe/dot_general | solution.py:156
  828.3 0.3 pad_maximum_fusion.3
  828.6 53.0 %all_to_all.15 = bf16[4,256,1024]{1,2,0:T(8,128)(2,1)S(1)} all-to-all(bf16[4,256,1024]{1,2,0:T(8,128)(2,1)S(1)} %pad_maximum_fusion.3), channel_id=1, replica_groups=mesh['cg'=4,'ct'=4,'fsdp'=2] {'cg'}, dimensions={0} | all-to-all | bytes 4194304 | tf_op jit(solution)/shard_map/all_to_all | solution.py:162
  881.6 2.8 copy.105
  (71 shorter events, 0.3 us)
Async XLA Ops:
  6.5 6.6 copy-start.3
  6.5 6.8 copy-start.4
  6.5 550.3 %all-gather.5.cloned.1.call-start = ((), (), s32[]{:S(2)}) async-start(), calls=%async_computation.1 | async-start | bytes 26214400 | tf_op jit(solution)/shard_map/all_gather | solution.py:105
  23.3 62.9 %collective-permute-start.2 = (bf16[512,1280]{1,0:T(8,128)(2,1)}, bf16[512,1280]{1,0:T(8,128)(2,1)}, u32[]{:S(2)}, u32[]{:S(2)}) collective-permute-start(bf16[512,1280]{1,0:T(8,128)(2,1)} %bitcast.213), channel_id=1, source_target_pairs={{0,16},{8,24},{16,0},{24,8},{1,17},{9,25},{17,1},{25,9},{2,18},{10... | collective-permute-start | bytes 3932168 | tf_op jit(solution)/shard_map/ppermute | solution.py:84
  28.8 85.6 %collective-permute-start.3 = (bf16[512,1280]{1,0:T(8,128)(2,1)}, bf16[512,1280]{1,0:T(8,128)(2,1)}, u32[]{:S(2)}, u32[]{:S(2)}) collective-permute-start(bf16[512,1280]{1,0:T(8,128)(2,1)} %bitcast.214), channel_id=1, source_target_pairs={{0,24},{8,0},{16,8},{24,16},{1,25},{9,1},{17,9},{25,17},{2,26},{10... | collective-permute-start | bytes 3932168 | tf_op jit(solution)/shard_map/ppermute | solution.py:84
  31.6 82.8 %collective-permute-start.1 = (bf16[512,1280]{1,0:T(8,128)(2,1)}, bf16[512,1280]{1,0:T(8,128)(2,1)}, u32[]{:S(2)}, u32[]{:S(2)}) collective-permute-start(bf16[512,1280]{1,0:T(8,128)(2,1)} %bitcast.7), channel_id=1, source_target_pairs={{0,8},{8,16},{16,24},{24,0},{1,9},{9,17},{17,25},{25,1},{2,10},{10... | collective-permute-start | bytes 3932168 | tf_op jit(solution)/shard_map/ppermute | solution.py:84
  35.5 95.0 %collective-permute-start = (bf16[256,4096]{0,1:T(8,128)(2,1)S(1)}, bf16[256,4096]{0,1:T(8,128)(2,1)}, u32[]{:S(2)}, u32[]{:S(2)}) collective-permute-start(bf16[256,4096]{0,1:T(8,128)(2,1)S(1)} %copy.63), channel_id=1, source_target_pairs={{0,1},{1,0},{2,3},{3,2},{4,5},{5,4},{6,7},{7,6},{8,9},{9,8},{10,11... | collective-permute-start | bytes 6291464 | tf_op jit(solution)/shard_map/ppermute | solution.py:90
  134.8 581.2 %all-gather.7.cloned.1.call-start = ((), (), s32[]{:S(2)}) async-start(), calls=%async_computation.2 | async-start | bytes 2621440 | tf_op jit(solution)/shard_map/all_gather | solution.py:124
  134.8 208.2 %collective-permute-start.4 = (bf16[256,8192]{0,1:T(8,128)(2,1)}, bf16[256,8192]{0,1:T(8,128)(2,1)}, u32[]{:S(2)}, u32[]{:S(2)}) collective-permute-start(bf16[256,8192]{0,1:T(8,128)(2,1)} %maximum_select_fusion), channel_id=1, source_target_pairs={{0,8},{8,16},{16,24},{24,0},{1,9},{9,17},{17,25},{25,1},{2,10},{10... | collective-permute-start | bytes 12582920 | tf_op jit(solution)/shard_map/ppermute | solution.py:102
  251.7 182.5 %collective-permute-start.5 = (bf16[256,8192]{0,1:T(8,128)(2,1)}, bf16[256,8192]{0,1:T(8,128)(2,1)}, u32[]{:S(2)}, u32[]{:S(2)}) collective-permute-start(bf16[256,8192]{0,1:T(8,128)(2,1)} %maximum_select_fusion), channel_id=1, source_target_pairs={{0,16},{8,24},{16,0},{24,8},{1,17},{9,25},{17,1},{25,9},{2,18},{10... | collective-permute-start | bytes 12582920 | tf_op jit(solution)/shard_map/ppermute | solution.py:102
  251.7 269.4 %collective-permute-start.6 = (bf16[256,8192]{0,1:T(8,128)(2,1)}, bf16[256,8192]{0,1:T(8,128)(2,1)}, u32[]{:S(2)}, u32[]{:S(2)}) collective-permute-start(bf16[256,8192]{0,1:T(8,128)(2,1)} %maximum_select_fusion), channel_id=1, source_target_pairs={{0,24},{8,0},{16,8},{24,16},{1,25},{9,1},{17,9},{25,17},{2,26},{10... | collective-permute-start | bytes 12582920 | tf_op jit(solution)/shard_map/ppermute | solution.py:102
  600.2 2.3 copy-start
  606.3 3.1 slice-start
  725.4 9.4 %copy-start.6 = (pred[256,1024]{0,1:T(8,128)(4,1)S(1)}, pred[256,1024]{0,1:T(8,128)(4,1)}, u32[]{:S(2)}) copy-start(pred[256,1024]{0,1:T(8,128)(4,1)} %iota_compare_fusion.3) | copy-start | bytes 786436
  734.8 7.4 copy-start.5
  758.8 14.7 %copy-start.2 = (pred[256,4096]{0,1:T(8,128)(4,1)S(1)}, pred[256,4096]{0,1:T(8,128)(4,1)}, u32[]{:S(2)}) copy-start(pred[256,4096]{0,1:T(8,128)(4,1)} %iota_compare_fusion) | copy-start | bytes 3145732
  773.5 18.0 %copy-start.13 = (s32[8,256]{1,0:T(8,128)S(1)}, s32[8,256]{1,0:T(8,128)}, u32[]{:S(2)}) copy-start(s32[8,256]{1,0:T(8,128)} %get-tuple-element.23) | copy-start | bytes 24580
  791.6 5.9 copy-start.1
  791.6 5.9 copy-start.9
  791.6 5.9 copy-start.12
  791.6 5.9 copy-start.14
  791.6 12.7 %slice-start.5 = ((s8[12582912]{0:T(1024)(128)(4,1)}), s8[4194304]{0:T(1024)(128)(4,1)S(1)}, s32[]{:S(2)}) async-start(s8[12582912]{0:T(1024)(128)(4,1)} %bitcast.222), calls=%async_computation.8 | async-start | bytes 8388608
  797.5 6.8 copy-start.8
  797.5 6.8 copy-start.11
  797.5 6.8 slice-start.6
  797.5 6.8 slice-start.7
  797.6 17.1 %slice-start.1 = ((s8[16777216]{0:T(1024)(128)(4,1)}), s8[4194304]{0:T(1024)(128)(4,1)S(1)}, s32[]{:S(2)}) async-start(s8[16777216]{0:T(1024)(128)(4,1)} %bitcast.220), calls=%async_computation.4 | async-start | bytes 8388608
  797.6 17.1 %slice-start.2 = ((s8[16777216]{0:T(1024)(128)(4,1)}), s8[4194304]{0:T(1024)(128)(4,1)S(1)}, s32[]{:S(2)}) async-start(s8[16777216]{0:T(1024)(128)(4,1)} %bitcast.220), calls=%async_computation.5 | async-start | bytes 8388608
  804.4 10.3 %copy-start.7 = (s32[4096]{0:T(1024)S(1)}, s32[4096]{0:T(1024)}, u32[]{:S(2)}) copy-start(s32[4096]{0:T(1024)} %iota_multiply_fusion) | copy-start | bytes 49156
  804.4 10.3 %copy-start.10 = (s32[8,256]{1,0:T(8,128)S(1)}, s32[8,256]{1,0:T(8,128)}, u32[]{:S(2)}) copy-start(s32[8,256]{1,0:T(8,128)} %get-tuple-element.26) | copy-start | bytes 24580
  804.4 10.3 %slice-start.3 = ((s8[16777216]{0:T(1024)(128)(4,1)}), s8[4194304]{0:T(1024)(128)(4,1)S(1)}, s32[]{:S(2)}) async-start(s8[16777216]{0:T(1024)(128)(4,1)} %bitcast.220), calls=%async_computation.6 | async-start | bytes 8388608
  804.4 10.3 %slice-start.4 = ((s8[16777216]{0:T(1024)(128)(4,1)}), s8[4194304]{0:T(1024)(128)(4,1)S(1)}, s32[]{:S(2)}) async-start(s8[16777216]{0:T(1024)(128)(4,1)} %bitcast.220), calls=%async_computation.7 | async-start | bytes 8388608
Sparse Core Ops, SparseCore 0:
  134.9 292.0 all-gather.4
  604.7 111.2 all-gather.6

commit v8 on v5

--- a/solution.py
+++ b/solution.py
@@ -69,8 +69,29 @@
     qcols = group_heads * HD
     rows = n_g * tok
 
-    full_rows = lax.all_gather(activations, "fsdp", axis=1, tiled=True)
-    grp_rows = lax.all_gather(full_rows, "cg", axis=0, tiled=True)
+    if lax.axis_size("fsdp") == 2:
+        pieces = []
+        for shift in range(n_g):
+            if shift:
+                perm = [(i, (i + shift) % n_g) for i in range(n_g)]
+                mine_half = lax.ppermute(activations, "cg", perm)
+            else:
+                mine_half = activations
+            other_half = lax.ppermute(mine_half, "fsdp", [(0, 1), (1, 0)])
+            pieces.append(
+                jnp.where(
+                    f == 0,
+                    jnp.concatenate([mine_half, other_half], axis=1),
+                    jnp.concatenate([other_half, mine_half], axis=1),
+                )
+            )
+        grp_rows = jnp.concatenate(pieces, axis=0)
+    else:
+        own_half = [activations]
+        for shift in range(1, n_g):
+            perm = [(i, (i + shift) % n_g) for i in range(n_g)]
+            own_half.append(lax.ppermute(activations, "cg", perm))
+        grp_rows = lax.all_gather(jnp.concatenate(own_half, axis=0), "fsdp", axis=1, tiled=True)
 
     local_w = jnp.concatenate(
         [
@@ -88,11 +109,11 @@
     by_shift = jnp.stack(received, axis=0)
     back = (g - jnp.arange(n_g, dtype=jnp.int32)) % n_g
     mine = jnp.take(by_shift, back, axis=0)
-    grp_rows, mine = lax.optimization_barrier((grp_rows, mine))
     every = lax.all_gather(mine, "ct", axis=0, tiled=False)
     every = every.transpose(1, 0, 2, 3).reshape(n_g * n_t * d_rows, qcols + 2 * HD)
 
     mixed = jnp.dot(grp_rows, every, preferred_element_type=jnp.float32)
+    mixed = jnp.take(mixed.reshape(n_g, tok, -1), back, axis=0).reshape(rows, -1)
     chunk_of_row = n_t * (jnp.arange(rows, dtype=jnp.int32) // tok) + t
     positions = chunk_of_row * tok + jnp.arange(rows, dtype=jnp.int32) % tok
     cosine, sine_part = rotation(positions)

time: 841 us -> 745 us (0.89)
  waiting for transfers between devices: 556 us -> 332 us
  starting transfers between devices: 4.69 us -> 85.1 us
  other arithmetic: 48.1 us -> 72.2 us
  local copies, waits for them, and re-layouts: 45 us -> 68.2 us
    ppermute x3, waiting for transfers between devices: 251 us -> 81.4 us  [shards(): received.append(lax.ppermute(outgoing, 'cg', perm))]
    all_gather x2 -> x0, waiting for transfers between devices: 169 us -> none  [the longest x1 107 us: shards(): grp_rows = lax.all_gather(full_rows, 'cg', axis=0, tiled=True)]
    ppermute x0 -> x7, waiting for transfers between devices: none -> 162 us  [the longest x3 123 us: shards(): mine_half = lax.ppermute(activations, 'cg', perm)]
    all_gather x1, waiting for transfers between devices: 124 us -> 0.01 us  [shards(): every = lax.all_gather(mine, 'ct', axis=0, tiled=False)]
    ppermute x0 -> x7, starting transfers between devices: none -> 79 us  [the longest x3 73.3 us: shards(): mine_half = lax.ppermute(activations, 'cg', perm)]
    all_gather x1, waiting for transfers between devices: 11.8 us -> 88.8 us  [shards(): pair = lax.all_gather(pair, 'ct', axis=0, tiled=False)]
    select_n x0 -> x6, other arithmetic: none -> 16.3 us  [the longest x4 13.2 us: shards(): jnp.where(f == 0, jnp.concatenate([mine_half, other_half], axis=1), jnp.c...]
    gather x0 -> x2, local copies, waits for them, and re-layouts: none -> 11.7 us  [shards(): jnp.take(mixed.reshape(n_g, tok, -1), back, axis=0).reshape(rows, -1)]
  transfers between devices with their start and end apart: 7 -> 12, of which waited for: 6 -> 7; matrix products, arithmetic and copies ran while one was open for 6% -> 6% of each run, Pallas kernels for 0% -> 0%
where the time goes in v8:
time: 745 us; the launch traced here: 739 us
  waiting for transfers between devices  332 us (45%)
  matrix products  112 us (15%)
  starting transfers between devices  85.1 us (11%)
  other arithmetic  72.2 us (10%)
  local copies, waits for them, and re-layouts  68.2 us (9%)
  blocking collectives  53 us (7%)
  between operations  16.4 us (2%)
    ppermute x3, waiting for transfers between devices, shards(): mine_half = lax.ppermute(activations, 'cg', perm)  123 us
    all_gather x1, waiting for transfers between devices, shards(): pair = lax.all_gather(pair, 'ct', axis=0, tiled=False)  88.8 us
    ppermute x3, waiting for transfers between devices, shards(): received.append(lax.ppermute(outgoing, 'cg', perm))  81.4 us
    ppermute x3, starting transfers between devices, shards(): mine_half = lax.ppermute(activations, 'cg', perm)  73.3 us
    all_to_all x1, blocking collectives, shards(): lax.all_to_all(out_rows, 'cg', split_axis=0, concat_axis=2, tiled=True)  53 us
    sub x3, matrix products, shards(): weights = jnp.where(visible, jnp.exp(scores - highest), 0.0)  40.1 us
    ppermute x4, waiting for transfers between devices, shards(): other_half = lax.ppermute(mine_half, 'fsdp', [(0, 1), (1, 0)])  39.5 us
    dot_general x4, matrix products, shards(): jnp.einsum('hqk,ke->hqe', dropped, all_values[:span], preferred_element_t...  36.4 us
  transfers between devices with their start and end apart: 12, of which 7 were waited for; matrix products, arithmetic and copies ran while one was open for 6% of the time, Pallas kernels for 0%

profile of v8, /device:TPU:0, one launch (start us, length us, event | category | flops | bytes accessed | tf_op | source)
XLA Modules:
  0.0 739.4 jit_solution(1218337516951923487)
XLA Ops:
  6.5 6.6 copy.57
  13.6 5.2 pad_maximum_fusion.1
  18.8 2.0 constant_dynamic-slice_fusion.3
  20.8 2.5 copy.62
  23.3 4.0 collective-permute-start.8
  27.3 2.4 copy.63
  29.8 1.3 collective-permute-start.9
  31.1 1.4 copy.61
  32.5 0.7 collective-permute-start.7
  33.2 0.6 copy.60
  33.9 52.4 %collective-permute-done.8 = bf16[512,1280]{1,0:T(8,128)(2,1)} collective-permute-done((bf16[512,1280]{1,0:T(8,128)(2,1)}, bf16[512,1280]{1,0:T(8,128)(2,1)}, u32[]{:S(2)}, u32[]{:S(2)}) %collective-permute-start.8) | collective-permute-done | bytes 1310752 | tf_op jit(solution)/shard_map/ppermute | solution.py:108
  86.3 29.1 %collective-permute-done.9 = bf16[512,1280]{1,0:T(8,128)(2,1)} collective-permute-done((bf16[512,1280]{1,0:T(8,128)(2,1)}, bf16[512,1280]{1,0:T(8,128)(2,1)}, u32[]{:S(2)}, u32[]{:S(2)}) %collective-permute-start.9) | collective-permute-done | bytes 1310752 | tf_op jit(solution)/shard_map/ppermute | solution.py:108
  115.3 5.2 pad_maximum_fusion.2
  120.6 5.7 gather_fusion
  126.2 5.3 bitcast_select_fusion.16
  131.6 1.5 copy-done.2
  133.1 70.9 %collective-permute-start.1 = (bf16[256,4096]{1,0:T(8,128)(2,1)S(1)}, bf16[256,4096]{1,0:T(8,128)(2,1)}, u32[]{:S(2)}, u32[]{:S(2)}) collective-permute-start(bf16[256,4096]{1,0:T(8,128)(2,1)S(1)} %copy-done.2), channel_id=1, source_target_pairs={{0,8},{8,16},{16,24},{24,0},{1,9},{9,17},{17,25},{25,1},{2,10},{10... | collective-permute-start | bytes 6291464 | tf_op jit(solution)/shard_map/ppermute | solution.py:77
  204.1 2.4 collective-permute-start.5
  206.4 1.6 collective-permute-start
  210.1 40.1 %collective-permute-done.1 = bf16[256,4096]{1,0:T(8,128)(2,1)} collective-permute-done((bf16[256,4096]{1,0:T(8,128)(2,1)S(1)}, bf16[256,4096]{1,0:T(8,128)(2,1)}, u32[]{:S(2)}, u32[]{:S(2)}) %collective-permute-start.1) | collective-permute-done | bytes 2097184 | tf_op jit(solution)/shard_map/ppermute | solution.py:77
  250.1 1.6 collective-permute-start.2
  252.4 0.6 iota_multiply_fusion.1
  253.0 0.7 shift-right-logical_xor_fusion.21
  253.6 0.9 iota_compare_fusion.3
  254.5 41.8 %collective-permute-done.3 = bf16[256,4096]{1,0:T(8,128)(2,1)} collective-permute-done((bf16[256,4096]{1,0:T(8,128)(2,1)S(1)}, bf16[256,4096]{1,0:T(8,128)(2,1)}, u32[]{:S(2)}, u32[]{:S(2)}) %collective-permute-start.3) | collective-permute-done | bytes 2097184 | tf_op jit(solution)/shard_map/ppermute | solution.py:77
  296.3 1.3 collective-permute-start.4
  297.6 40.7 %collective-permute-done.5 = bf16[256,4096]{1,0:T(8,128)(2,1)} collective-permute-done((bf16[256,4096]{1,0:T(8,128)(2,1)S(1)}, bf16[256,4096]{1,0:T(8,128)(2,1)}, u32[]{:S(2)}, u32[]{:S(2)}) %collective-permute-start.5) | collective-permute-done | bytes 2097184 | tf_op jit(solution)/shard_map/ppermute | solution.py:77
  338.3 1.3 collective-permute-start.6
  339.6 3.3 maximum_select_fusion
  342.9 3.3 maximum_select_fusion.1
  346.3 3.2 maximum_select_fusion.2
  349.5 39.5 %collective-permute-done.6 = bf16[256,4096]{1,0:T(8,128)(2,1)S(1)} collective-permute-done((bf16[256,4096]{1,0:T(8,128)(2,1)}, bf16[256,4096]{1,0:T(8,128)(2,1)S(1)}, u32[]{:S(2)}, u32[]{:S(2)}) %collective-permute-start.6) | collective-permute-done | bytes 2097184 | tf_op jit(solution)/shard_map/ppermute | solution.py:80
  389.0 3.3 maximum_select_fusion.3
  392.3 7.3 pad_maximum_fusion
  399.5 10.1 %copy.64 = bf16[4,4,512,1280]{3,2,1,0:T(8,128)(2,1)S(1)} copy(bf16[4,4,512,1280]{3,2,0,1:T(8,128)(2,1)} %bitcast.193) | data formatting | bytes 41943040 | tf_op jit(solution)/shard_map/transpose | solution.py:113
  409.7 26.3 %fusion.162 = f32[4,256,1280]{2,1,0:T(8,128)} fusion(bf16[4,256,8192]{2,1,0:T(8,128)(2,1)} %bitcast.197, bf16[8192,1280,1]{1,0,2:T(8,128)(2,1)S(1)} %bitcast.194), kind=kOutput, calls=%fused_computation.261 | convolution fusion | flops 21474836480 | bytes 42991616 | tf_op jit(solution)/shard_map/dot_general | solution.py:115
  436.0 5.7 gather_fusion.1
  441.8 6.0 copy.65
  447.7 3.1 broadcast_select_fusion
  450.9 2.3 copy-done
  453.2 1.1 multiply_cosine_fusion
  454.4 0.8 pad_maximum_fusion.5
  455.2 0.6 iota_multiply_fusion
  455.8 1.1 iota_compare_fusion.2
  457.0 1.4 iota_compare_fusion.1
  458.4 1.7 iota_compare_fusion
  460.1 1.8 fusion.149
  461.8 3.9 copy.93
  465.7 2.9 copy.94
  469.0 6.0 subtract_convert_fusion
  475.0 88.8 %all-gather.6.cloned.1.call-done = bf16[4096,2,128]{0,2,1:T(8,128)(2,1)} async-done(((bf16[1024,2,128]{0,2,1:T(8,128)(2,1)}), bf16[4096,2,128]{0,2,1:T(8,128)(2,1)}) %all-gather.6.cloned.1.call-update) | async-done | bytes 2097168 | tf_op jit(solution)/shard_map/all_gather | solution.py:127
  563.8 4.5 reshape.542
  568.3 4.5 copy.66
  572.8 9.4 %fusion.67 = f32[2048,256,8]{1,0,2:T(8,128)} fusion(bf16[1024,8,64]{2,0,1:T(8,128)(2,1)S(1)} %get-tuple-element.5, bf16[1024,8,64]{2,0,1:T(8,128)(2,1)} %get-tuple-element.6, bf16[4096,2,128]{2,0,1:T(8,128)(2,1)} %bitcast.201), kind=kOutput, calls=%fused_computation.120 | convolution fusion | flops 1074790400 | bytes 20447232 | tf_op jit(solution)/shard_map/qhe,ke->hqk/dot_general | solution.py:143
  582.2 7.4 fusion.157
  589.6 17.0 %fusion.156 = (f32[8,256]{1,0:T(8,128)S(1)}, bf16[8,256,2048]{1,2,0:T(8,128)(2,1)}) fusion(f32[2048,256,8]{1,0,2:T(8,128)} %fusion.67, pred[256,2048]{0,1:T(8,128)(4,1)S(1)} %copy-done.6), kind=kOutput, calls=%fused_computation.259 | output fusion | flops 29362176 | bytes 25698304 | tf_op jit(solution)/shard_map/sub | solution.py:153
  606.6 14.7 %fusion.151 = (f32[8,256]{1,0:T(8,128)S(1)}, bf16[8,256,3072]{1,2,0:T(8,128)(2,1)}) fusion(pred[256,3072]{0,1:T(8,128)(4,1)} %iota_compare_fusion.1, bf16[4096,2,128]{2,0,1:T(8,128)(2,1)} %bitcast.203, bf16[1024,8,64]{2,0,1:T(8,128)(2,1)S(1)} %get-tuple-element.5, bf16[1024,8,64]{2,0,1:T(8,128)(2,1)} %get-tuple-element.6), kind=kOutput, calls=%fused_computation.258 | convolution fusion | flops 3267365888 | bytes 24125440 | tf_op jit(solution)/shard_map/sub | solution.py:153
  621.3 18.0 %fusion.150 = (f32[8,256]{1,0:T(8,128)S(1)}, bf16[8,256,4096]{1,2,0:T(8,128)(2,1)}) fusion(pred[256,4096]{0,1:T(8,128)(4,1)S(1)} %copy-done.3, bf16[4096,2,128]{2,0,1:T(8,128)(2,1)} %bitcast.204, bf16[1024,8,64]{2,0,1:T(8,128)(2,1)} %get-tuple-element.6, bf16[1024,8,64]{2,0,1:T(8,128)(2,1)S(1)} %get-tuple-element.5), kind=kOutput, calls=%fused_computation.257 | convolution fusion | flops 4355788800 | bytes 29368320 | tf_op jit(solution)/shard_map/sub | solution.py:153
  639.4 5.8 divide_convert_fusion.3
  645.3 6.7 divide_convert_fusion.2
  652.2 10.2 %divide_convert_fusion.1 = bf16[256,8,128]{0,2,1:T(8,128)(2,1)S(1)} fusion(bf16[8,256,3072]{1,2,0:T(8,128)(2,1)S(1)} %bitcast.221, s32[3072]{0:T(1024)S(1)} %copy-done.9, s32[8,256]{1,0:T(8,128)S(1)} %copy-done.12, bf16[4096,2,128]{2,0,1:T(8,128)(2,1)S(1)} %bitcast.207, f32[256,8]{0,1:T(8,128)S(1)} %multiply_bitcast_fusion.1), kind=kOutput, calls=%fused_computation.109 | convolution fusion | flops 1686634496 | bytes 13922304 | tf_op jit(solution)/shard_map/hqk,ke->hqe/dot_general | solution.py:159
  662.5 13.6 %divide_convert_fusion = bf16[256,8,128]{0,2,1:T(8,128)(2,1)S(1)} fusion(bf16[4096,2,128]{2,0,1:T(8,128)(2,1)S(1)} %bitcast.208, bf16[8,256,4096]{1,2,0:T(8,128)(2,1)S(1)} %bitcast.219, s32[4096]{0:T(1024)S(1)} %copy-done.8, s32[8,256]{1,0:T(8,128)S(1)} %copy-done.11, f32[256,8]{0,1:T(8,128)S(1)} %multiply_bitcast_fusion), kind=kOutput, calls=%fused_computation.108 | convolution fusion | flops 2248671232 | bytes 18382848 | tf_op jit(solution)/shard_map/hqk,ke->hqe/dot_general | solution.py:159
  676.3 53.0 %all_to_all.15 = bf16[4,256,1024]{1,2,0:T(8,128)(2,1)S(1)} all-to-all(bf16[4,256,1024]{1,2,0:T(8,128)(2,1)S(1)} %pad_maximum_fusion.3), channel_id=1, replica_groups=mesh['cg'=4,'ct'=4,'fsdp'=2] {'cg'}, dimensions={0} | all-to-all | bytes 4194304 | tf_op jit(solution)/shard_map/all_to_all | solution.py:165
  729.3 2.8 copy.92
  (81 shorter events, 2.1 us)
Async XLA Ops:
  6.5 6.6 copy-start.4
  6.5 6.8 copy-start.5
  6.5 393.0 %all-gather.4.cloned.1.call-start = ((), (), s32[]{:S(2)}) async-start(), calls=%async_computation.1 | async-start | bytes 26214400 | tf_op jit(solution)/shard_map/all_gather | solution.py:112
  23.3 63.0 %collective-permute-start.8 = (bf16[512,1280]{1,0:T(8,128)(2,1)}, bf16[512,1280]{1,0:T(8,128)(2,1)}, u32[]{:S(2)}, u32[]{:S(2)}) collective-permute-start(bf16[512,1280]{1,0:T(8,128)(2,1)} %bitcast.211), channel_id=1, source_target_pairs={{0,16},{8,24},{16,0},{24,8},{1,17},{9,25},{17,1},{25,9},{2,18},{10... | collective-permute-start | bytes 3932168 | tf_op jit(solution)/shard_map/ppermute | solution.py:108
  29.8 85.6 %collective-permute-start.9 = (bf16[512,1280]{1,0:T(8,128)(2,1)}, bf16[512,1280]{1,0:T(8,128)(2,1)}, u32[]{:S(2)}, u32[]{:S(2)}) collective-permute-start(bf16[512,1280]{1,0:T(8,128)(2,1)} %bitcast.212), channel_id=1, source_target_pairs={{0,24},{8,0},{16,8},{24,16},{1,25},{9,1},{17,9},{25,17},{2,26},{10... | collective-permute-start | bytes 3932168 | tf_op jit(solution)/shard_map/ppermute | solution.py:108
  32.5 82.8 %collective-permute-start.7 = (bf16[512,1280]{1,0:T(8,128)(2,1)}, bf16[512,1280]{1,0:T(8,128)(2,1)}, u32[]{:S(2)}, u32[]{:S(2)}) collective-permute-start(bf16[512,1280]{1,0:T(8,128)(2,1)} %bitcast.213), channel_id=1, source_target_pairs={{0,8},{8,16},{16,24},{24,0},{1,9},{9,17},{17,25},{25,1},{2,10},{10... | collective-permute-start | bytes 3932168 | tf_op jit(solution)/shard_map/ppermute | solution.py:108
  131.5 1.6 copy-start.2
  131.6 432.3 %all-gather.6.cloned.1.call-start = ((), (), s32[]{:S(2)}) async-start(), calls=%async_computation.2 | async-start | bytes 2621440 | tf_op jit(solution)/shard_map/all_gather | solution.py:127
  133.1 117.0 %collective-permute-start.1 = (bf16[256,4096]{1,0:T(8,128)(2,1)S(1)}, bf16[256,4096]{1,0:T(8,128)(2,1)}, u32[]{:S(2)}, u32[]{:S(2)}) collective-permute-start(bf16[256,4096]{1,0:T(8,128)(2,1)S(1)} %copy-done.2), channel_id=1, source_target_pairs={{0,8},{8,16},{16,24},{24,0},{1,9},{9,17},{17,25},{25,1},{2,10},{10... | collective-permute-start | bytes 6291464 | tf_op jit(solution)/shard_map/ppermute | solution.py:77
  204.1 92.3 %collective-permute-start.3 = (bf16[256,4096]{1,0:T(8,128)(2,1)S(1)}, bf16[256,4096]{1,0:T(8,128)(2,1)}, u32[]{:S(2)}, u32[]{:S(2)}) collective-permute-start(bf16[256,4096]{1,0:T(8,128)(2,1)S(1)} %copy-done.2), channel_id=1, source_target_pairs={{0,16},{8,24},{16,0},{24,8},{1,17},{9,25},{17,1},{25,9},{2,18},{10... | collective-permute-start | bytes 6291464 | tf_op jit(solution)/shard_map/ppermute | solution.py:77
  204.1 134.3 %collective-permute-start.5 = (bf16[256,4096]{1,0:T(8,128)(2,1)S(1)}, bf16[256,4096]{1,0:T(8,128)(2,1)}, u32[]{:S(2)}, u32[]{:S(2)}) collective-permute-start(bf16[256,4096]{1,0:T(8,128)(2,1)S(1)} %copy-done.2), channel_id=1, source_target_pairs={{0,24},{8,0},{16,8},{24,16},{1,25},{9,1},{17,9},{25,17},{2,26},{10... | collective-permute-start | bytes 6291464 | tf_op jit(solution)/shard_map/ppermute | solution.py:77
  206.4 133.2 %collective-permute-start = (bf16[256,4096]{1,0:T(8,128)(2,1)S(1)}, bf16[256,4096]{1,0:T(8,128)(2,1)}, u32[]{:S(2)}, u32[]{:S(2)}) collective-permute-start(bf16[256,4096]{1,0:T(8,128)(2,1)S(1)} %copy-done.2), channel_id=1, source_target_pairs={{0,1},{1,0},{2,3},{3,2},{4,5},{5,4},{6,7},{7,6},{8,9},{9,8},{10,11... | collective-permute-start | bytes 6291464 | tf_op jit(solution)/shard_map/ppermute | solution.py:80
  250.1 92.8 %collective-permute-start.2 = (bf16[256,4096]{1,0:T(8,128)(2,1)}, bf16[256,4096]{1,0:T(8,128)(2,1)S(1)}, u32[]{:S(2)}, u32[]{:S(2)}) collective-permute-start(bf16[256,4096]{1,0:T(8,128)(2,1)} %collective-permute-done.1), channel_id=1, source_target_pairs={{0,1},{1,0},{2,3},{3,2},{4,5},{5,4},{6,7},{7,6},{8,9},{9,8},{10,11... | collective-permute-start | bytes 6291464 | tf_op jit(solution)/shard_map/ppermute | solution.py:80
  296.3 49.9 %collective-permute-start.4 = (bf16[256,4096]{1,0:T(8,128)(2,1)}, bf16[256,4096]{1,0:T(8,128)(2,1)S(1)}, u32[]{:S(2)}, u32[]{:S(2)}) collective-permute-start(bf16[256,4096]{1,0:T(8,128)(2,1)} %collective-permute-done.3), channel_id=1, source_target_pairs={{0,1},{1,0},{2,3},{3,2},{4,5},{5,4},{6,7},{7,6},{8,9},{9,8},{10,11... | collective-permute-start | bytes 6291464 | tf_op jit(solution)/shard_map/ppermute | solution.py:80
  338.3 50.6 %collective-permute-start.6 = (bf16[256,4096]{1,0:T(8,128)(2,1)}, bf16[256,4096]{1,0:T(8,128)(2,1)S(1)}, u32[]{:S(2)}, u32[]{:S(2)}) collective-permute-start(bf16[256,4096]{1,0:T(8,128)(2,1)} %collective-permute-done.5), channel_id=1, source_target_pairs={{0,1},{1,0},{2,3},{3,2},{4,5},{5,4},{6,7},{7,6},{8,9},{9,8},{10,11... | collective-permute-start | bytes 6291464 | tf_op jit(solution)/shard_map/ppermute | solution.py:80
  450.8 2.3 copy-start
  457.0 3.1 slice-start
  572.8 9.4 %copy-start.7 = (pred[256,1024]{0,1:T(8,128)(4,1)S(1)}, pred[256,1024]{0,1:T(8,128)(4,1)}, u32[]{:S(2)}) copy-start(pred[256,1024]{0,1:T(8,128)(4,1)} %iota_compare_fusion.3) | copy-start | bytes 786436
  582.2 7.4 copy-start.6
  606.6 14.7 %copy-start.3 = (pred[256,4096]{0,1:T(8,128)(4,1)S(1)}, pred[256,4096]{0,1:T(8,128)(4,1)}, u32[]{:S(2)}) copy-start(pred[256,4096]{0,1:T(8,128)(4,1)} %iota_compare_fusion) | copy-start | bytes 3145732
  621.3 18.0 %copy-start.14 = (s32[8,256]{1,0:T(8,128)S(1)}, s32[8,256]{1,0:T(8,128)}, u32[]{:S(2)}) copy-start(s32[8,256]{1,0:T(8,128)} %get-tuple-element.19) | copy-start | bytes 24580
  639.3 5.9 copy-start.1
  639.3 5.9 copy-start.10
  639.3 5.9 copy-start.13
  639.4 5.9 copy-start.15
  639.4 12.7 %slice-start.5 = ((s8[12582912]{0:T(1024)(128)(4,1)}), s8[4194304]{0:T(1024)(128)(4,1)S(1)}, s32[]{:S(2)}) async-start(s8[12582912]{0:T(1024)(128)(4,1)} %bitcast.220), calls=%async_computation.8 | async-start | bytes 8388608
  645.3 6.8 copy-start.9
  645.3 6.8 copy-start.12
  645.3 6.8 slice-start.6
  645.3 6.8 slice-start.7
  645.3 17.1 %slice-start.1 = ((s8[16777216]{0:T(1024)(128)(4,1)}), s8[4194304]{0:T(1024)(128)(4,1)S(1)}, s32[]{:S(2)}) async-start(s8[16777216]{0:T(1024)(128)(4,1)} %bitcast.218), calls=%async_computation.4 | async-start | bytes 8388608
  645.3 17.1 %slice-start.2 = ((s8[16777216]{0:T(1024)(128)(4,1)}), s8[4194304]{0:T(1024)(128)(4,1)S(1)}, s32[]{:S(2)}) async-start(s8[16777216]{0:T(1024)(128)(4,1)} %bitcast.218), calls=%async_computation.5 | async-start | bytes 8388608
  652.1 10.3 %copy-start.8 = (s32[4096]{0:T(1024)S(1)}, s32[4096]{0:T(1024)}, u32[]{:S(2)}) copy-start(s32[4096]{0:T(1024)} %iota_multiply_fusion) | copy-start | bytes 49156
  652.1 10.3 %copy-start.11 = (s32[8,256]{1,0:T(8,128)S(1)}, s32[8,256]{1,0:T(8,128)}, u32[]{:S(2)}) copy-start(s32[8,256]{1,0:T(8,128)} %get-tuple-element.22) | copy-start | bytes 24580
  652.1 10.3 %slice-start.3 = ((s8[16777216]{0:T(1024)(128)(4,1)}), s8[4194304]{0:T(1024)(128)(4,1)S(1)}, s32[]{:S(2)}) async-start(s8[16777216]{0:T(1024)(128)(4,1)} %bitcast.218), calls=%async_computation.6 | async-start | bytes 8388608
  652.2 10.3 %slice-start.4 = ((s8[16777216]{0:T(1024)(128)(4,1)}), s8[4194304]{0:T(1024)(128)(4,1)S(1)}, s32[]{:S(2)}) async-start(s8[16777216]{0:T(1024)(128)(4,1)} %bitcast.218), calls=%async_computation.7 | async-start | bytes 8388608
Sparse Core Ops, SparseCore 0:
  131.7 200.2 all-gather.3
  455.3 108.4 all-gather.5

commit v9 on v8

--- a/solution.py
+++ b/solution.py
@@ -71,12 +71,18 @@
 
     if lax.axis_size("fsdp") == 2:
         pieces = []
-        for shift in range(n_g):
-            if shift:
+        halves = [activations]
+        if n_g == 4:
+            right = [(i, (i + 1) % n_g) for i in range(n_g)]
+            left = [(i, (i - 1) % n_g) for i in range(n_g)]
+            from_left = lax.ppermute(activations, "cg", right)
+            from_right = lax.ppermute(activations, "cg", left)
+            halves += [from_left, lax.ppermute(from_left, "cg", right), from_right]
+        else:
+            for shift in range(1, n_g):
                 perm = [(i, (i + shift) % n_g) for i in range(n_g)]
-                mine_half = lax.ppermute(activations, "cg", perm)
-            else:
-                mine_half = activations
+                halves.append(lax.ppermute(activations, "cg", perm))
+        for mine_half in halves:
             other_half = lax.ppermute(mine_half, "fsdp", [(0, 1), (1, 0)])
             pieces.append(
                 jnp.where(

time: 745 us -> 700 us (0.940)
  waiting for transfers between devices: 332 us -> 288 us
    all_gather x1, waiting for transfers between devices: 88.8 us -> 1.25 us  [shards(): pair = lax.all_gather(pair, 'ct', axis=0, tiled=False)]
    ppermute x4, waiting for transfers between devices: 39.5 us -> 81.9 us  [shards(): other_half = lax.ppermute(mine_half, 'fsdp', [(0, 1), (1, 0)])]
  transfers between devices with their start and end apart: 12 -> 12, of which waited for: 7 -> 9; matrix products, arithmetic and copies ran while one was open for 6% -> 7% of each run, Pallas kernels for 0% -> 0%
where the time goes in v9:
time: 700 us; the launch traced here: 694 us
  waiting for transfers between devices  288 us (41%)
  matrix products  112 us (16%)
  starting transfers between devices  84.5 us (12%)
  other arithmetic  72.3 us (10%)
  local copies, waits for them, and re-layouts  68.2 us (10%)
  blocking collectives  53 us (8%)
  between operations  16.3 us (2%)
    ppermute x4, waiting for transfers between devices, shards(): other_half = lax.ppermute(mine_half, 'fsdp', [(0, 1), (1, 0)])  81.9 us
    ppermute x3, waiting for transfers between devices, shards(): received.append(lax.ppermute(outgoing, 'cg', perm))  81.4 us
    ppermute x1, starting transfers between devices, shards(): from_left = lax.ppermute(activations, 'cg', right)  70.9 us
    all_to_all x1, blocking collectives, shards(): lax.all_to_all(out_rows, 'cg', split_axis=0, concat_axis=2, tiled=True)  53 us
    ppermute x1, waiting for transfers between devices, shards(): from_left = lax.ppermute(activations, 'cg', right)  46.1 us
    ppermute x1, waiting for transfers between devices, shards(): halves += [from_left, lax.ppermute(from_left, 'cg', right), from_right]  41.7 us
    sub x3, matrix products, shards(): weights = jnp.where(visible, jnp.exp(scores - highest), 0.0)  40.1 us
    dot_general x4, matrix products, shards(): jnp.einsum('hqk,ke->hqe', dropped, all_values[:span], preferred_element_t...  36.4 us
  transfers between devices with their start and end apart: 12, of which 9 were waited for; matrix products, arithmetic and copies ran while one was open for 7% of the time, Pallas kernels for 0%

profile of v9, /device:TPU:0, one launch (start us, length us, event | category | flops | bytes accessed | tf_op | source)
XLA Modules:
  0.0 694.4 jit_solution(11898111536271823225)
XLA Ops:
  6.5 6.6 copy.57
  13.6 5.2 pad_maximum_fusion.1
  18.8 2.0 constant_dynamic-slice_fusion.3
  20.8 2.5 copy.62
  23.3 4.0 collective-permute-start.8
  27.3 2.4 copy.63
  29.8 1.3 collective-permute-start.9
  31.1 1.4 copy.61
  32.5 0.7 collective-permute-start.7
  33.2 0.6 copy.60
  33.9 52.4 %collective-permute-done.8 = bf16[512,1280]{1,0:T(8,128)(2,1)} collective-permute-done((bf16[512,1280]{1,0:T(8,128)(2,1)}, bf16[512,1280]{1,0:T(8,128)(2,1)}, u32[]{:S(2)}, u32[]{:S(2)}) %collective-permute-start.8) | collective-permute-done | bytes 1310752 | tf_op jit(solution)/shard_map/ppermute | solution.py:114
  86.3 29.1 %collective-permute-done.9 = bf16[512,1280]{1,0:T(8,128)(2,1)} collective-permute-done((bf16[512,1280]{1,0:T(8,128)(2,1)}, bf16[512,1280]{1,0:T(8,128)(2,1)}, u32[]{:S(2)}, u32[]{:S(2)}) %collective-permute-start.9) | collective-permute-done | bytes 1310752 | tf_op jit(solution)/shard_map/ppermute | solution.py:114
  115.3 5.2 pad_maximum_fusion.2
  120.6 5.7 gather_fusion
  126.2 5.3 bitcast_select_fusion.16
  131.6 1.5 copy-done.2
  133.1 70.9 %collective-permute-start.1 = (bf16[256,4096]{1,0:T(8,128)(2,1)S(1)}, bf16[256,4096]{1,0:T(8,128)(2,1)}, u32[]{:S(2)}, u32[]{:S(2)}) collective-permute-start(bf16[256,4096]{1,0:T(8,128)(2,1)S(1)} %copy-done.2), channel_id=1, source_target_pairs={{0,8},{8,16},{16,24},{24,0},{1,9},{9,17},{17,25},{25,1},{2,10},{10... | collective-permute-start | bytes 6291464 | tf_op jit(solution)/shard_map/ppermute | solution.py:78
  204.1 46.1 %collective-permute-done.1 = bf16[256,4096]{1,0:T(8,128)(2,1)} collective-permute-done((bf16[256,4096]{1,0:T(8,128)(2,1)S(1)}, bf16[256,4096]{1,0:T(8,128)(2,1)}, u32[]{:S(2)}, u32[]{:S(2)}) %collective-permute-start.1) | collective-permute-done | bytes 2097184 | tf_op jit(solution)/shard_map/ppermute | solution.py:78
  250.1 2.6 collective-permute-start.3
  252.7 1.6 collective-permute-start
  258.1 0.7 shift-right-logical_xor_fusion.21
  258.8 0.9 iota_compare_fusion.3
  259.7 35.4 %collective-permute-done.5 = bf16[256,4096]{1,0:T(8,128)(2,1)} collective-permute-done((bf16[256,4096]{1,0:T(8,128)(2,1)S(1)}, bf16[256,4096]{1,0:T(8,128)(2,1)}, u32[]{:S(2)}, u32[]{:S(2)}) %collective-permute-start.5) | collective-permute-done | bytes 2097184 | tf_op jit(solution)/shard_map/ppermute | solution.py:79
  295.1 1.6 collective-permute-start.6
  296.7 41.7 %collective-permute-done.3 = bf16[256,4096]{1,0:T(8,128)(2,1)} collective-permute-done((bf16[256,4096]{1,0:T(8,128)(2,1)}, bf16[256,4096]{1,0:T(8,128)(2,1)}, u32[]{:S(2)}, u32[]{:S(2)}) %collective-permute-start.3) | collective-permute-done | bytes 2097184 | tf_op jit(solution)/shard_map/ppermute | solution.py:80
  338.4 1.3 collective-permute-start.4
  339.7 3.3 maximum_select_fusion
  343.0 3.2 collective-permute-done.2
  346.2 3.2 maximum_select_fusion.1
  349.5 41.7 %collective-permute-done.6 = bf16[256,4096]{1,0:T(8,128)(2,1)S(1)} collective-permute-done((bf16[256,4096]{1,0:T(8,128)(2,1)}, bf16[256,4096]{1,0:T(8,128)(2,1)S(1)}, u32[]{:S(2)}, u32[]{:S(2)}) %collective-permute-start.6) | collective-permute-done | bytes 2097184 | tf_op jit(solution)/shard_map/ppermute | solution.py:86
  391.2 3.3 maximum_select_fusion.3
  394.5 36.9 %collective-permute-done.4 = bf16[256,4096]{1,0:T(8,128)(2,1)S(1)} collective-permute-done((bf16[256,4096]{1,0:T(8,128)(2,1)}, bf16[256,4096]{1,0:T(8,128)(2,1)S(1)}, u32[]{:S(2)}, u32[]{:S(2)}) %collective-permute-start.4) | collective-permute-done | bytes 2097184 | tf_op jit(solution)/shard_map/ppermute | solution.py:86
  431.4 3.3 maximum_select_fusion.2
  434.7 7.3 %pad_maximum_fusion = bf16[1024,8192]{1,0:T(8,128)(2,1)} fusion(bf16[256,8192]{1,0:T(8,128)(2,1)S(1)} %maximum_select_fusion.3, bf16[256,8192]{1,0:T(8,128)(2,1)S(1)} %maximum_select_fusion.2, bf16[256,8192]{1,0:T(8,128)(2,1)S(1)} %maximum_select_fusion.1, bf16[256,8192]{1,0:T(8,128)(2,1)S(1)} %maximum_select_fusion), kind=kLoop, calls=%fused_computation.41 | loop fusion | flops 67108864 | bytes 33554432 | tf_op jit(solution)/shard_map/concatenate | solution.py:94
  442.0 10.1 %copy.64 = bf16[4,4,512,1280]{3,2,1,0:T(8,128)(2,1)S(1)} copy(bf16[4,4,512,1280]{3,2,0,1:T(8,128)(2,1)} %bitcast.193) | data formatting | bytes 41943040 | tf_op jit(solution)/shard_map/transpose | solution.py:119
  452.1 26.3 %fusion.162 = f32[4,256,1280]{2,1,0:T(8,128)} fusion(bf16[4,256,8192]{2,1,0:T(8,128)(2,1)} %bitcast.197, bf16[8192,1280,1]{1,0,2:T(8,128)(2,1)S(1)} %bitcast.194), kind=kOutput, calls=%fused_computation.261 | convolution fusion | flops 21474836480 | bytes 42991616 | tf_op jit(solution)/shard_map/dot_general | solution.py:121
  478.5 5.7 gather_fusion.1
  484.2 6.0 copy.65
  490.2 3.1 broadcast_select_fusion
  493.4 2.3 copy-done
  495.7 1.1 multiply_cosine_fusion
  496.8 0.8 pad_maximum_fusion.5
  497.7 0.6 iota_multiply_fusion
  498.3 1.1 iota_compare_fusion.2
  499.4 1.4 iota_compare_fusion.1
  500.8 1.7 iota_compare_fusion
  502.5 1.8 fusion.149
  504.3 3.9 copy.93
  508.2 2.9 copy.94
  511.5 6.0 subtract_convert_fusion
  517.5 1.3 all-gather.6.cloned.1.call-done
  518.8 4.5 reshape.542
  523.2 4.5 copy.66
  527.7 9.4 %fusion.67 = f32[2048,256,8]{1,0,2:T(8,128)} fusion(bf16[1024,8,64]{2,0,1:T(8,128)(2,1)S(1)} %get-tuple-element.5, bf16[1024,8,64]{2,0,1:T(8,128)(2,1)} %get-tuple-element.6, bf16[4096,2,128]{2,0,1:T(8,128)(2,1)} %bitcast.201), kind=kOutput, calls=%fused_computation.120 | convolution fusion | flops 1074790400 | bytes 20447232 | tf_op jit(solution)/shard_map/qhe,ke->hqk/dot_general | solution.py:149
  537.2 7.4 %fusion.157 = (f32[8,256]{1,0:T(8,128)S(1)}, bf16[8,256,1024]{1,2,0:T(8,128)(2,1)}) fusion(pred[256,1024]{0,1:T(8,128)(4,1)S(1)} %copy-done.7, bf16[4096,2,128]{2,0,1:T(8,128)(2,1)} %bitcast.202, bf16[1024,8,64]{2,0,1:T(8,128)(2,1)S(1)} %get-tuple-element.5, bf16[1024,8,64]{2,0,1:T(8,128)(2,1)} %get-tuple-element.6), kind=kOutput, calls=%fused_computation.260 | convolution fusion | flops 1090520064 | bytes 13639680 | tf_op jit(solution)/shard_map/sub | solution.py:159
  544.5 17.0 %fusion.156 = (f32[8,256]{1,0:T(8,128)S(1)}, bf16[8,256,2048]{1,2,0:T(8,128)(2,1)}) fusion(f32[2048,256,8]{1,0,2:T(8,128)} %fusion.67, pred[256,2048]{0,1:T(8,128)(4,1)S(1)} %copy-done.6), kind=kOutput, calls=%fused_computation.259 | output fusion | flops 29362176 | bytes 25698304 | tf_op jit(solution)/shard_map/sub | solution.py:159
  561.5 14.7 %fusion.151 = (f32[8,256]{1,0:T(8,128)S(1)}, bf16[8,256,3072]{1,2,0:T(8,128)(2,1)}) fusion(pred[256,3072]{0,1:T(8,128)(4,1)} %iota_compare_fusion.1, bf16[4096,2,128]{2,0,1:T(8,128)(2,1)} %bitcast.203, bf16[1024,8,64]{2,0,1:T(8,128)(2,1)S(1)} %get-tuple-element.5, bf16[1024,8,64]{2,0,1:T(8,128)(2,1)} %get-tuple-element.6), kind=kOutput, calls=%fused_computation.258 | convolution fusion | flops 3267365888 | bytes 24125440 | tf_op jit(solution)/shard_map/sub | solution.py:159
  576.3 18.0 %fusion.150 = (f32[8,256]{1,0:T(8,128)S(1)}, bf16[8,256,4096]{1,2,0:T(8,128)(2,1)}) fusion(pred[256,4096]{0,1:T(8,128)(4,1)S(1)} %copy-done.3, bf16[4096,2,128]{2,0,1:T(8,128)(2,1)} %bitcast.204, bf16[1024,8,64]{2,0,1:T(8,128)(2,1)} %get-tuple-element.6, bf16[1024,8,64]{2,0,1:T(8,128)(2,1)S(1)} %get-tuple-element.5), kind=kOutput, calls=%fused_computation.257 | convolution fusion | flops 4355788800 | bytes 29368320 | tf_op jit(solution)/shard_map/sub | solution.py:159
  594.3 5.8 divide_convert_fusion.3
  600.2 6.7 divide_convert_fusion.2
  607.1 10.2 %divide_convert_fusion.1 = bf16[256,8,128]{0,2,1:T(8,128)(2,1)S(1)} fusion(bf16[8,256,3072]{1,2,0:T(8,128)(2,1)S(1)} %bitcast.221, s32[3072]{0:T(1024)S(1)} %copy-done.9, s32[8,256]{1,0:T(8,128)S(1)} %copy-done.12, bf16[4096,2,128]{2,0,1:T(8,128)(2,1)S(1)} %bitcast.207, f32[256,8]{0,1:T(8,128)S(1)} %multiply_bitcast_fusion.1), kind=kOutput, calls=%fused_computation.109 | convolution fusion | flops 1686634496 | bytes 13922304 | tf_op jit(solution)/shard_map/hqk,ke->hqe/dot_general | solution.py:165
  617.4 13.6 %divide_convert_fusion = bf16[256,8,128]{0,2,1:T(8,128)(2,1)S(1)} fusion(bf16[4096,2,128]{2,0,1:T(8,128)(2,1)S(1)} %bitcast.208, bf16[8,256,4096]{1,2,0:T(8,128)(2,1)S(1)} %bitcast.219, s32[4096]{0:T(1024)S(1)} %copy-done.8, s32[8,256]{1,0:T(8,128)S(1)} %copy-done.11, f32[256,8]{0,1:T(8,128)S(1)} %multiply_bitcast_fusion), kind=kOutput, calls=%fused_computation.108 | convolution fusion | flops 2248671232 | bytes 18382848 | tf_op jit(solution)/shard_map/hqk,ke->hqe/dot_general | solution.py:165
  631.2 53.0 %all_to_all.15 = bf16[4,256,1024]{1,2,0:T(8,128)(2,1)S(1)} all-to-all(bf16[4,256,1024]{1,2,0:T(8,128)(2,1)S(1)} %pad_maximum_fusion.3), channel_id=1, replica_groups=mesh['cg'=4,'ct'=4,'fsdp'=2] {'cg'}, dimensions={0} | all-to-all | bytes 4194304 | tf_op jit(solution)/shard_map/all_to_all | solution.py:171
  684.2 2.8 copy.92
  (81 shorter events, 3.2 us)
Async XLA Ops:
  6.5 6.6 copy-start.4
  6.5 6.8 copy-start.5
  6.5 435.5 %all-gather.4.cloned.1.call-start = ((), (), s32[]{:S(2)}) async-start(), calls=%async_computation.1 | async-start | bytes 26214400 | tf_op jit(solution)/shard_map/all_gather | solution.py:118
  23.3 63.0 %collective-permute-start.8 = (bf16[512,1280]{1,0:T(8,128)(2,1)}, bf16[512,1280]{1,0:T(8,128)(2,1)}, u32[]{:S(2)}, u32[]{:S(2)}) collective-permute-start(bf16[512,1280]{1,0:T(8,128)(2,1)} %bitcast.211), channel_id=1, source_target_pairs={{0,16},{8,24},{16,0},{24,8},{1,17},{9,25},{17,1},{25,9},{2,18},{10... | collective-permute-start | bytes 3932168 | tf_op jit(solution)/shard_map/ppermute | solution.py:114
  29.8 85.6 %collective-permute-start.9 = (bf16[512,1280]{1,0:T(8,128)(2,1)}, bf16[512,1280]{1,0:T(8,128)(2,1)}, u32[]{:S(2)}, u32[]{:S(2)}) collective-permute-start(bf16[512,1280]{1,0:T(8,128)(2,1)} %bitcast.212), channel_id=1, source_target_pairs={{0,24},{8,0},{16,8},{24,16},{1,25},{9,1},{17,9},{25,17},{2,26},{10... | collective-permute-start | bytes 3932168 | tf_op jit(solution)/shard_map/ppermute | solution.py:114
  32.5 82.8 %collective-permute-start.7 = (bf16[512,1280]{1,0:T(8,128)(2,1)}, bf16[512,1280]{1,0:T(8,128)(2,1)}, u32[]{:S(2)}, u32[]{:S(2)}) collective-permute-start(bf16[512,1280]{1,0:T(8,128)(2,1)} %bitcast.213), channel_id=1, source_target_pairs={{0,8},{8,16},{16,24},{24,0},{1,9},{9,17},{17,25},{25,1},{2,10},{10... | collective-permute-start | bytes 3932168 | tf_op jit(solution)/shard_map/ppermute | solution.py:114
  131.5 1.6 copy-start.2
  131.6 387.2 %all-gather.6.cloned.1.call-start = ((), (), s32[]{:S(2)}) async-start(), calls=%async_computation.2 | async-start | bytes 2621440 | tf_op jit(solution)/shard_map/all_gather | solution.py:133
  133.1 117.0 %collective-permute-start.1 = (bf16[256,4096]{1,0:T(8,128)(2,1)S(1)}, bf16[256,4096]{1,0:T(8,128)(2,1)}, u32[]{:S(2)}, u32[]{:S(2)}) collective-permute-start(bf16[256,4096]{1,0:T(8,128)(2,1)S(1)} %copy-done.2), channel_id=1, source_target_pairs={{0,8},{8,16},{16,24},{24,0},{1,9},{9,17},{17,25},{25,1},{2,10},{10... | collective-permute-start | bytes 6291464 | tf_op jit(solution)/shard_map/ppermute | solution.py:78
  204.1 91.1 %collective-permute-start.5 = (bf16[256,4096]{1,0:T(8,128)(2,1)S(1)}, bf16[256,4096]{1,0:T(8,128)(2,1)}, u32[]{:S(2)}, u32[]{:S(2)}) collective-permute-start(bf16[256,4096]{1,0:T(8,128)(2,1)S(1)} %copy-done.2), channel_id=1, source_target_pairs={{0,24},{8,0},{16,8},{24,16},{1,25},{9,1},{17,9},{25,17},{2,26},{10... | collective-permute-start | bytes 6291464 | tf_op jit(solution)/shard_map/ppermute | solution.py:79
  250.1 88.3 %collective-permute-start.3 = (bf16[256,4096]{1,0:T(8,128)(2,1)}, bf16[256,4096]{1,0:T(8,128)(2,1)}, u32[]{:S(2)}, u32[]{:S(2)}) collective-permute-start(bf16[256,4096]{1,0:T(8,128)(2,1)} %collective-permute-done.1), channel_id=1, source_target_pairs={{0,8},{8,16},{16,24},{24,0},{1,9},{9,17},{17,25},{25,1},{2,10},{10... | collective-permute-start | bytes 6291464 | tf_op jit(solution)/shard_map/ppermute | solution.py:80
  252.7 87.0 %collective-permute-start = (bf16[256,4096]{1,0:T(8,128)(2,1)S(1)}, bf16[256,4096]{1,0:T(8,128)(2,1)}, u32[]{:S(2)}, u32[]{:S(2)}) collective-permute-start(bf16[256,4096]{1,0:T(8,128)(2,1)S(1)} %copy-done.2), channel_id=1, source_target_pairs={{0,1},{1,0},{2,3},{3,2},{4,5},{5,4},{6,7},{7,6},{8,9},{9,8},{10,11... | collective-permute-start | bytes 6291464 | tf_op jit(solution)/shard_map/ppermute | solution.py:86
  256.4 89.9 %collective-permute-start.2 = (bf16[256,4096]{1,0:T(8,128)(2,1)}, bf16[256,4096]{1,0:T(8,128)(2,1)S(1)}, u32[]{:S(2)}, u32[]{:S(2)}) collective-permute-start(bf16[256,4096]{1,0:T(8,128)(2,1)} %collective-permute-done.1), channel_id=1, source_target_pairs={{0,1},{1,0},{2,3},{3,2},{4,5},{5,4},{6,7},{7,6},{8,9},{9,8},{10,11... | collective-permute-start | bytes 6291464 | tf_op jit(solution)/shard_map/ppermute | solution.py:86
  295.1 96.1 %collective-permute-start.6 = (bf16[256,4096]{1,0:T(8,128)(2,1)}, bf16[256,4096]{1,0:T(8,128)(2,1)S(1)}, u32[]{:S(2)}, u32[]{:S(2)}) collective-permute-start(bf16[256,4096]{1,0:T(8,128)(2,1)} %collective-permute-done.5), channel_id=1, source_target_pairs={{0,1},{1,0},{2,3},{3,2},{4,5},{5,4},{6,7},{7,6},{8,9},{9,8},{10,11... | collective-permute-start | bytes 6291464 | tf_op jit(solution)/shard_map/ppermute | solution.py:86
  338.4 93.0 %collective-permute-start.4 = (bf16[256,4096]{1,0:T(8,128)(2,1)}, bf16[256,4096]{1,0:T(8,128)(2,1)S(1)}, u32[]{:S(2)}, u32[]{:S(2)}) collective-permute-start(bf16[256,4096]{1,0:T(8,128)(2,1)} %collective-permute-done.3), channel_id=1, source_target_pairs={{0,1},{1,0},{2,3},{3,2},{4,5},{5,4},{6,7},{7,6},{8,9},{9,8},{10,11... | collective-permute-start | bytes 6291464 | tf_op jit(solution)/shard_map/ppermute | solution.py:86
  493.3 2.3 copy-start
  499.4 3.1 slice-start
  527.7 9.4 %copy-start.7 = (pred[256,1024]{0,1:T(8,128)(4,1)S(1)}, pred[256,1024]{0,1:T(8,128)(4,1)}, u32[]{:S(2)}) copy-start(pred[256,1024]{0,1:T(8,128)(4,1)} %iota_compare_fusion.3) | copy-start | bytes 786436
  537.2 7.4 %copy-start.6 = (pred[256,2048]{0,1:T(8,128)(4,1)S(1)}, pred[256,2048]{0,1:T(8,128)(4,1)}, u32[]{:S(2)}) copy-start(pred[256,2048]{0,1:T(8,128)(4,1)} %iota_compare_fusion.2) | copy-start | bytes 1572868
  561.5 14.7 %copy-start.3 = (pred[256,4096]{0,1:T(8,128)(4,1)S(1)}, pred[256,4096]{0,1:T(8,128)(4,1)}, u32[]{:S(2)}) copy-start(pred[256,4096]{0,1:T(8,128)(4,1)} %iota_compare_fusion) | copy-start | bytes 3145732
  576.2 18.0 %copy-start.14 = (s32[8,256]{1,0:T(8,128)S(1)}, s32[8,256]{1,0:T(8,128)}, u32[]{:S(2)}) copy-start(s32[8,256]{1,0:T(8,128)} %get-tuple-element.19) | copy-start | bytes 24580
  594.2 5.9 copy-start.1
  594.3 5.9 copy-start.10
  594.3 5.9 copy-start.13
  594.3 5.9 copy-start.15
  594.3 12.7 %slice-start.5 = ((s8[12582912]{0:T(1024)(128)(4,1)}), s8[4194304]{0:T(1024)(128)(4,1)S(1)}, s32[]{:S(2)}) async-start(s8[12582912]{0:T(1024)(128)(4,1)} %bitcast.220), calls=%async_computation.8 | async-start | bytes 8388608
  600.2 6.8 copy-start.9
  600.2 6.8 copy-start.12
  600.2 6.8 slice-start.6
  600.2 6.8 slice-start.7
  600.2 17.1 %slice-start.1 = ((s8[16777216]{0:T(1024)(128)(4,1)}), s8[4194304]{0:T(1024)(128)(4,1)S(1)}, s32[]{:S(2)}) async-start(s8[16777216]{0:T(1024)(128)(4,1)} %bitcast.218), calls=%async_computation.4 | async-start | bytes 8388608
  600.2 17.1 %slice-start.2 = ((s8[16777216]{0:T(1024)(128)(4,1)}), s8[4194304]{0:T(1024)(128)(4,1)S(1)}, s32[]{:S(2)}) async-start(s8[16777216]{0:T(1024)(128)(4,1)} %bitcast.218), calls=%async_computation.5 | async-start | bytes 8388608
  607.0 10.3 %copy-start.8 = (s32[4096]{0:T(1024)S(1)}, s32[4096]{0:T(1024)}, u32[]{:S(2)}) copy-start(s32[4096]{0:T(1024)} %iota_multiply_fusion) | copy-start | bytes 49156
  607.1 10.3 %copy-start.11 = (s32[8,256]{1,0:T(8,128)S(1)}, s32[8,256]{1,0:T(8,128)}, u32[]{:S(2)}) copy-start(s32[8,256]{1,0:T(8,128)} %get-tuple-element.22) | copy-start | bytes 24580
  607.1 10.3 %slice-start.3 = ((s8[16777216]{0:T(1024)(128)(4,1)}), s8[4194304]{0:T(1024)(128)(4,1)S(1)}, s32[]{:S(2)}) async-start(s8[16777216]{0:T(1024)(128)(4,1)} %bitcast.218), calls=%async_computation.6 | async-start | bytes 8388608
  607.1 10.3 %slice-start.4 = ((s8[16777216]{0:T(1024)(128)(4,1)}), s8[4194304]{0:T(1024)(128)(4,1)S(1)}, s32[]{:S(2)}) async-start(s8[16777216]{0:T(1024)(128)(4,1)} %bitcast.218), calls=%async_computation.7 | async-start | bytes 8388608
Sparse Core Ops, SparseCore 0:
  131.7 200.2 all-gather.3
  497.8 20.9 all-gather.5

commit v10 on v9

--- a/solution.py
+++ b/solution.py
@@ -91,13 +91,13 @@
                     jnp.concatenate([other_half, mine_half], axis=1),
                 )
             )
-        grp_rows = jnp.concatenate(pieces, axis=0)
     else:
         own_half = [activations]
         for shift in range(1, n_g):
             perm = [(i, (i + shift) % n_g) for i in range(n_g)]
             own_half.append(lax.ppermute(activations, "cg", perm))
         grp_rows = lax.all_gather(jnp.concatenate(own_half, axis=0), "fsdp", axis=1, tiled=True)
+        pieces = [grp_rows[i * tok : (i + 1) * tok] for i in range(n_g)]
 
     local_w = jnp.concatenate(
         [
@@ -118,8 +118,10 @@
     every = lax.all_gather(mine, "ct", axis=0, tiled=False)
     every = every.transpose(1, 0, 2, 3).reshape(n_g * n_t * d_rows, qcols + 2 * HD)
 
-    mixed = jnp.dot(grp_rows, every, preferred_element_type=jnp.float32)
-    mixed = jnp.take(mixed.reshape(n_g, tok, -1), back, axis=0).reshape(rows, -1)
+    mixed = jnp.stack(
+        [jnp.dot(piece, every, preferred_element_type=jnp.float32) for piece in pieces], axis=0
+    )
+    mixed = jnp.take(mixed, back, axis=0).reshape(rows, -1)
     chunk_of_row = n_t * (jnp.arange(rows, dtype=jnp.int32) // tok) + t
     positions = chunk_of_row * tok + jnp.arange(rows, dtype=jnp.int32) % tok
     cosine, sine_part = rotation(positions)

time: 700 us -> 729 us (1.041)
  matrix products: 112 us -> 143 us
  other arithmetic: 72.3 us -> 54.4 us
  waiting for transfers between devices: 288 us -> 296 us
  local copies, waits for them, and re-layouts: 68.2 us -> 75.5 us
    dot_general x1 -> x4, matrix products: 26.3 us -> 56.7 us  [shards(): jnp.dot(piece, every, preferred_element_type=jnp.float32)]
    all_gather x0 -> x1, local copies, waits for them, and re-layouts: none -> 17.4 us  [shards(): every = lax.all_gather(mine, 'ct', axis=0, tiled=False)]
    select_n x6 -> x2, other arithmetic: 16.3 us -> 3.13 us  [shards(): mixed = jnp.take(mixed, back, axis=0).reshape(rows, -1)]
    transpose x1 -> x0, local copies, waits for them, and re-layouts: 10.1 us -> none  [shards(): every.transpose(1, 0, 2, 3).reshape(n_g * n_t * d_rows, qcols + 2 * HD)]
    unnamed x51 -> x55, local copies, waits for them, and re-layouts: 17.7 us -> 17.5 us
  transfers between devices with their start and end apart: 12 -> 12, of which waited for: 9 -> 8; matrix products, arithmetic and copies ran while one was open for 7% -> 12% of each run, Pallas kernels for 0% -> 0%
where the time goes in v10:
time: 729 us; the launch traced here: 723 us
  waiting for transfers between devices  296 us (41%)
  matrix products  143 us (20%)
  starting transfers between devices  85.3 us (12%)
  local copies, waits for them, and re-layouts  75.5 us (10%)
  other arithmetic  54.4 us (7%)
  blocking collectives  53 us (7%)
  between operations  16.1 us (2%)
    ppermute x4, waiting for transfers between devices, shards(): other_half = lax.ppermute(mine_half, 'fsdp', [(0, 1), (1, 0)])  88.7 us
    ppermute x3, waiting for transfers between devices, shards(): received.append(lax.ppermute(outgoing, 'cg', perm))  81.4 us
    ppermute x1, starting transfers between devices, shards(): from_left = lax.ppermute(activations, 'cg', right)  70.9 us
    dot_general x4, matrix products, shards(): jnp.dot(piece, every, preferred_element_type=jnp.float32)  56.7 us
    all_to_all x1, blocking collectives, shards(): lax.all_to_all(out_rows, 'cg', split_axis=0, concat_axis=2, tiled=True)  53 us
    ppermute x1, waiting for transfers between devices, shards(): halves += [from_left, lax.ppermute(from_left, 'cg', right), from_right]  46.5 us
    ppermute x1, waiting for transfers between devices, shards(): from_left = lax.ppermute(activations, 'cg', right)  44.3 us
    sub x3, matrix products, shards(): weights = jnp.where(visible, jnp.exp(scores - highest), 0.0)  40.4 us
  transfers between devices with their start and end apart: 12, of which 8 were waited for; matrix products, arithmetic and copies ran while one was open for 12% of the time, Pallas kernels for 0%

profile of v10, /device:TPU:0, one launch (start us, length us, event | category | flops | bytes accessed | tf_op | source)
XLA Modules:
  0.0 723.3 jit_solution(12505204595712421221)
XLA Ops:
  6.5 6.6 copy.57
  13.6 5.2 pad_maximum_fusion
  18.8 2.0 constant_dynamic-slice_fusion.3
  20.8 2.5 copy.62
  23.3 4.0 collective-permute-start.2
  27.3 2.4 copy.63
  29.7 1.3 collective-permute-start.3
  31.1 1.4 copy.61
  32.5 0.7 collective-permute-start.1
  33.2 0.6 copy.60
  33.9 52.4 %collective-permute-done.2 = bf16[512,1280]{1,0:T(8,128)(2,1)} collective-permute-done((bf16[512,1280]{1,0:T(8,128)(2,1)}, bf16[512,1280]{1,0:T(8,128)(2,1)}, u32[]{:S(2)}, u32[]{:S(2)}) %collective-permute-start.2) | collective-permute-done | bytes 1310752 | tf_op jit(solution)/shard_map/ppermute | solution.py:114
  86.2 29.1 %collective-permute-done.3 = bf16[512,1280]{1,0:T(8,128)(2,1)} collective-permute-done((bf16[512,1280]{1,0:T(8,128)(2,1)}, bf16[512,1280]{1,0:T(8,128)(2,1)}, u32[]{:S(2)}, u32[]{:S(2)}) %collective-permute-start.3) | collective-permute-done | bytes 1310752 | tf_op jit(solution)/shard_map/ppermute | solution.py:114
  115.3 5.2 pad_maximum_fusion.1
  120.5 5.7 gather_fusion
  126.2 5.4 bitcast_select_fusion.16
  131.7 1.5 copy-done.14
  133.2 70.9 %collective-permute-start.4 = (bf16[256,4096]{1,0:T(8,128)(2,1)S(1)}, bf16[256,4096]{1,0:T(8,128)(2,1)S(1)}, u32[]{:S(2)}, u32[]{:S(2)}) collective-permute-start(bf16[256,4096]{1,0:T(8,128)(2,1)S(1)} %copy-done.14), channel_id=1, source_target_pairs={{0,8},{8,16},{16,24},{24,0},{1,9},{9,17},{17,25},{25,1},{2,10},{10... | collective-permute-start | bytes 6291464 | tf_op jit(solution)/shard_map/ppermute | solution.py:78
  204.1 44.3 %collective-permute-done.4 = bf16[256,4096]{1,0:T(8,128)(2,1)S(1)} collective-permute-done((bf16[256,4096]{1,0:T(8,128)(2,1)S(1)}, bf16[256,4096]{1,0:T(8,128)(2,1)S(1)}, u32[]{:S(2)}, u32[]{:S(2)}) %collective-permute-start.4) | collective-permute-done | bytes 2097184 | tf_op jit(solution)/shard_map/ppermute | solution.py:78
  248.5 2.5 collective-permute-start.6
  250.9 1.5 collective-permute-start.8
  252.4 46.5 %collective-permute-done.6 = bf16[256,4096]{1,0:T(8,128)(2,1)} collective-permute-done((bf16[256,4096]{1,0:T(8,128)(2,1)S(1)}, bf16[256,4096]{1,0:T(8,128)(2,1)}, u32[]{:S(2)}, u32[]{:S(2)}) %collective-permute-start.6) | collective-permute-done | bytes 2097184 | tf_op jit(solution)/shard_map/ppermute | solution.py:80
  298.9 1.3 collective-permute-start.7
  300.2 0.7 collective-permute-start
  304.3 0.7 shift-right-logical_xor_fusion.21
  305.0 0.9 iota_compare_fusion.3
  305.9 1.3 collective-permute-start.5
  307.2 34.1 %collective-permute-done.8 = bf16[256,4096]{1,0:T(8,128)(2,1)} collective-permute-done((bf16[256,4096]{1,0:T(8,128)(2,1)S(1)}, bf16[256,4096]{1,0:T(8,128)(2,1)}, u32[]{:S(2)}, u32[]{:S(2)}) %collective-permute-start.8) | collective-permute-done | bytes 2097184 | tf_op jit(solution)/shard_map/ppermute | solution.py:79
  341.2 1.0 collective-permute-start.9
  342.2 17.4 %copy.64 = bf16[4,4,512,1280]{3,2,0,1:T(8,128)(2,1)} copy(bf16[4,4,512,1280]{3,2,1,0:T(8,128)(2,1)} %all-gather.4.cloned.1.call-done) | data formatting | bytes 41943040 | tf_op jit(solution)/shard_map/all_gather | solution.py:118
  359.6 14.4 %fusion.83 = f32[1,256,1280]{2,1,0:T(8,128)S(1)} fusion(bf16[8192,1280]{1,0:T(8,128)(2,1)} %bitcast.201, bf16[256,4096]{1,0:T(8,128)(2,1)} %collective-permute-done.7, bf16[256,4096]{1,0:T(8,128)(2,1)} %collective-permute-done.6, pred[]{:T(512)S(6)} %eq.14), kind=kOutput, calls=%fused_computation.120 | convolution fusion | flops 5387583488 | bytes 26476544 | tf_op jit(solution)/shard_map/dot_general | solution.py:122
  374.0 63.7 %collective-permute-done.5 = bf16[256,4096]{1,0:T(8,128)(2,1)} collective-permute-done((bf16[256,4096]{1,0:T(8,128)(2,1)}, bf16[256,4096]{1,0:T(8,128)(2,1)}, u32[]{:S(2)}, u32[]{:S(2)}) %collective-permute-start.5) | collective-permute-done | bytes 2097184 | tf_op jit(solution)/shard_map/ppermute | solution.py:86
  437.7 13.8 %fusion.84 = f32[1,256,1280]{2,1,0:T(8,128)S(1)} fusion(bf16[8192,1280]{1,0:T(8,128)(2,1)} %bitcast.202, bf16[256,4096]{1,0:T(8,128)(2,1)} %collective-permute-done.5, bf16[256,4096]{1,0:T(8,128)(2,1)S(1)} %copy-done.16, pred[]{:T(512)S(6)} %eq.14), kind=kOutput, calls=%fused_computation.121 | convolution fusion | flops 5387583488 | bytes 26476544 | tf_op jit(solution)/shard_map/dot_general | solution.py:122
  451.5 25.0 %collective-permute-done.9 = bf16[256,4096]{1,0:T(8,128)(2,1)} collective-permute-done((bf16[256,4096]{1,0:T(8,128)(2,1)}, bf16[256,4096]{1,0:T(8,128)(2,1)}, u32[]{:S(2)}, u32[]{:S(2)}) %collective-permute-start.9) | collective-permute-done | bytes 2097184 | tf_op jit(solution)/shard_map/ppermute | solution.py:86
  476.5 14.7 %fusion.82 = f32[1,256,1280]{2,1,0:T(8,128)S(1)} fusion(bf16[8192,1280]{1,0:T(8,128)(2,1)} %bitcast.203, bf16[256,4096]{1,0:T(8,128)(2,1)} %collective-permute-done.9, bf16[256,4096]{1,0:T(8,128)(2,1)} %collective-permute-done.8, pred[]{:T(512)S(6)} %eq.14), kind=kOutput, calls=%fused_computation.119 | convolution fusion | flops 5387583488 | bytes 26476544 | tf_op jit(solution)/shard_map/dot_general | solution.py:122
  491.2 13.9 %fusion.85 = f32[1,256,1280]{2,1,0:T(8,128)S(1)} fusion(bf16[8192,1280]{1,0:T(8,128)(2,1)} %bitcast.204, bf16[256,4096]{1,0:T(8,128)(2,1)} %collective-permute-done, bf16[256,4096]{1,0:T(8,128)(2,1)S(1)} %copy-done.14, pred[]{:T(512)S(6)} %eq.14), kind=kOutput, calls=%fused_computation.122 | convolution fusion | flops 5387583488 | bytes 26476544 | tf_op jit(solution)/shard_map/dot_general | solution.py:122
  505.0 2.9 pad_maximum_fusion.2
  508.0 5.7 gather_fusion.1
  513.7 6.0 copy.65
  519.6 3.1 broadcast_select_fusion
  522.8 2.3 copy-done
  525.1 1.1 multiply_cosine_fusion
  526.3 0.8 pad_maximum_fusion.5
  527.1 0.6 iota_multiply_fusion
  527.7 1.1 iota_compare_fusion.2
  528.9 1.4 iota_compare_fusion.1
  530.3 1.7 iota_compare_fusion
  532.0 1.8 fusion.185
  533.8 3.9 copy.93
  537.6 2.7 copy.94
  540.7 6.0 subtract_convert_fusion
  546.8 1.0 all-gather.6.cloned.1.call-done
  547.8 4.5 reshape.540
  552.2 4.7 copy.66
  557.0 9.4 %fusion.99 = f32[2048,256,8]{1,0,2:T(8,128)} fusion(bf16[1024,8,64]{2,0,1:T(8,128)(2,1)S(1)} %get-tuple-element.5, bf16[1024,8,64]{2,0,1:T(8,128)(2,1)} %get-tuple-element.6, bf16[4096,2,128]{2,0,1:T(8,128)(2,1)} %bitcast.210), kind=kOutput, calls=%fused_computation.152 | convolution fusion | flops 1074790400 | bytes 20447232 | tf_op jit(solution)/shard_map/qhe,ke->hqk/dot_general | solution.py:151
  566.4 7.4 %fusion.193 = (f32[8,256]{1,0:T(8,128)S(1)}, bf16[8,256,1024]{1,2,0:T(8,128)(2,1)}) fusion(pred[256,1024]{0,1:T(8,128)(4,1)S(1)} %copy-done.6, bf16[4096,2,128]{2,0,1:T(8,128)(2,1)} %bitcast.211, bf16[1024,8,64]{2,0,1:T(8,128)(2,1)S(1)} %get-tuple-element.5, bf16[1024,8,64]{2,0,1:T(8,128)(2,1)} %get-tuple-element.6), kind=kOutput, calls=%fused_computation.296 | convolution fusion | flops 1090520064 | bytes 13639680 | tf_op jit(solution)/shard_map/sub | solution.py:161
  573.8 16.6 %fusion.192 = (f32[8,256]{1,0:T(8,128)S(1)}, bf16[8,256,2048]{1,2,0:T(8,128)(2,1)}) fusion(f32[2048,256,8]{1,0,2:T(8,128)} %fusion.99, pred[256,2048]{0,1:T(8,128)(4,1)S(1)} %copy-done.5), kind=kOutput, calls=%fused_computation.295 | output fusion | flops 29362176 | bytes 25698304 | tf_op jit(solution)/shard_map/sub | solution.py:161
  590.4 14.8 %fusion.187 = (f32[8,256]{1,0:T(8,128)S(1)}, bf16[8,256,3072]{1,2,0:T(8,128)(2,1)}) fusion(pred[256,3072]{0,1:T(8,128)(4,1)} %iota_compare_fusion.1, bf16[4096,2,128]{2,0,1:T(8,128)(2,1)} %bitcast.212, bf16[1024,8,64]{2,0,1:T(8,128)(2,1)S(1)} %get-tuple-element.5, bf16[1024,8,64]{2,0,1:T(8,128)(2,1)} %get-tuple-element.6), kind=kOutput, calls=%fused_computation.294 | convolution fusion | flops 3267365888 | bytes 24125440 | tf_op jit(solution)/shard_map/sub | solution.py:161
  605.2 18.2 %fusion.186 = (f32[8,256]{1,0:T(8,128)S(1)}, bf16[8,256,4096]{1,2,0:T(8,128)(2,1)}) fusion(pred[256,4096]{0,1:T(8,128)(4,1)S(1)} %copy-done.2, bf16[4096,2,128]{2,0,1:T(8,128)(2,1)} %bitcast.213, bf16[1024,8,64]{2,0,1:T(8,128)(2,1)} %get-tuple-element.6, bf16[1024,8,64]{2,0,1:T(8,128)(2,1)S(1)} %get-tuple-element.5), kind=kOutput, calls=%fused_computation.293 | convolution fusion | flops 4355788800 | bytes 29368320 | tf_op jit(solution)/shard_map/sub | solution.py:161
  623.5 5.8 divide_convert_fusion.3
  629.4 6.7 divide_convert_fusion.2
  636.3 10.2 %divide_convert_fusion.1 = bf16[256,8,128]{0,2,1:T(8,128)(2,1)S(1)} fusion(bf16[8,256,3072]{1,2,0:T(8,128)(2,1)S(1)} %bitcast.230, s32[3072]{0:T(1024)S(1)} %copy-done.8, s32[8,256]{1,0:T(8,128)S(1)} %copy-done.11, bf16[4096,2,128]{2,0,1:T(8,128)(2,1)S(1)} %bitcast.216, f32[256,8]{0,1:T(8,128)S(1)} %multiply_bitcast_fusion.1), kind=kOutput, calls=%fused_computation.141 | convolution fusion | flops 1686634496 | bytes 13922304 | tf_op jit(solution)/shard_map/hqk,ke->hqe/dot_general | solution.py:167
  646.5 13.5 %divide_convert_fusion = bf16[256,8,128]{0,2,1:T(8,128)(2,1)S(1)} fusion(bf16[4096,2,128]{2,0,1:T(8,128)(2,1)S(1)} %bitcast.217, bf16[8,256,4096]{1,2,0:T(8,128)(2,1)S(1)} %bitcast.228, s32[4096]{0:T(1024)S(1)} %copy-done.7, s32[8,256]{1,0:T(8,128)S(1)} %copy-done.10, f32[256,8]{0,1:T(8,128)S(1)} %multiply_bitcast_fusion), kind=kOutput, calls=%fused_computation.140 | convolution fusion | flops 2248671232 | bytes 18382848 | tf_op jit(solution)/shard_map/hqk,ke->hqe/dot_general | solution.py:167
  660.3 53.0 %all_to_all.15 = bf16[4,256,1024]{1,2,0:T(8,128)(2,1)S(1)} all-to-all(bf16[4,256,1024]{1,2,0:T(8,128)(2,1)S(1)} %pad_maximum_fusion.3), channel_id=1, replica_groups=mesh['cg'=4,'ct'=4,'fsdp'=2] {'cg'}, dimensions={0} | all-to-all | bytes 4194304 | tf_op jit(solution)/shard_map/all_to_all | solution.py:173
  713.4 2.8 copy.92
  (84 shorter events, 2.7 us)
Async XLA Ops:
  6.5 6.6 copy-start.3
  6.5 6.8 copy-start.4
  6.5 335.7 %all-gather.4.cloned.1.call-start = ((), (), s32[]{:S(2)}) async-start(), calls=%async_computation.1 | async-start | bytes 26214400 | tf_op jit(solution)/shard_map/all_gather | solution.py:118
  23.3 63.0 %collective-permute-start.2 = (bf16[512,1280]{1,0:T(8,128)(2,1)}, bf16[512,1280]{1,0:T(8,128)(2,1)}, u32[]{:S(2)}, u32[]{:S(2)}) collective-permute-start(bf16[512,1280]{1,0:T(8,128)(2,1)} %bitcast.220), channel_id=1, source_target_pairs={{0,16},{8,24},{16,0},{24,8},{1,17},{9,25},{17,1},{25,9},{2,18},{10... | collective-permute-start | bytes 3932168 | tf_op jit(solution)/shard_map/ppermute | solution.py:114
  29.7 85.6 %collective-permute-start.3 = (bf16[512,1280]{1,0:T(8,128)(2,1)}, bf16[512,1280]{1,0:T(8,128)(2,1)}, u32[]{:S(2)}, u32[]{:S(2)}) collective-permute-start(bf16[512,1280]{1,0:T(8,128)(2,1)} %bitcast.221), channel_id=1, source_target_pairs={{0,24},{8,0},{16,8},{24,16},{1,25},{9,1},{17,9},{25,17},{2,26},{10... | collective-permute-start | bytes 3932168 | tf_op jit(solution)/shard_map/ppermute | solution.py:114
  32.5 82.8 %collective-permute-start.1 = (bf16[512,1280]{1,0:T(8,128)(2,1)}, bf16[512,1280]{1,0:T(8,128)(2,1)}, u32[]{:S(2)}, u32[]{:S(2)}) collective-permute-start(bf16[512,1280]{1,0:T(8,128)(2,1)} %bitcast.222), channel_id=1, source_target_pairs={{0,8},{8,16},{16,24},{24,0},{1,9},{9,17},{17,25},{25,1},{2,10},{10... | collective-permute-start | bytes 3932168 | tf_op jit(solution)/shard_map/ppermute | solution.py:114
  131.6 1.6 copy-start.14
  131.6 416.1 %all-gather.6.cloned.1.call-start = ((), (), s32[]{:S(2)}) async-start(), calls=%async_computation.2 | async-start | bytes 2621440 | tf_op jit(solution)/shard_map/all_gather | solution.py:135
  133.2 115.3 %collective-permute-start.4 = (bf16[256,4096]{1,0:T(8,128)(2,1)S(1)}, bf16[256,4096]{1,0:T(8,128)(2,1)S(1)}, u32[]{:S(2)}, u32[]{:S(2)}) collective-permute-start(bf16[256,4096]{1,0:T(8,128)(2,1)S(1)} %copy-done.14), channel_id=1, source_target_pairs={{0,8},{8,16},{16,24},{24,0},{1,9},{9,17},{17,25},{25,1},{2,10},{10... | collective-permute-start | bytes 6291464 | tf_op jit(solution)/shard_map/ppermute | solution.py:78
  248.5 50.5 %copy-start.15 = (bf16[256,4096]{1,0:T(8,128)(2,1)}, bf16[256,4096]{1,0:T(8,128)(2,1)S(1)}, u32[]{:S(2)}) copy-start(bf16[256,4096]{1,0:T(8,128)(2,1)S(1)} %collective-permute-done.4) | copy-start | bytes 6291460
  248.5 50.5 %collective-permute-start.6 = (bf16[256,4096]{1,0:T(8,128)(2,1)S(1)}, bf16[256,4096]{1,0:T(8,128)(2,1)}, u32[]{:S(2)}, u32[]{:S(2)}) collective-permute-start(bf16[256,4096]{1,0:T(8,128)(2,1)S(1)} %collective-permute-done.4), channel_id=1, source_target_pairs={{0,8},{8,16},{16,24},{24,0},{1,9},{9,17},{17,25},{25,1},{2,10},{10... | collective-permute-start | bytes 6291464 | tf_op jit(solution)/shard_map/ppermute | solution.py:80
  250.9 90.3 %collective-permute-start.8 = (bf16[256,4096]{1,0:T(8,128)(2,1)S(1)}, bf16[256,4096]{1,0:T(8,128)(2,1)}, u32[]{:S(2)}, u32[]{:S(2)}) collective-permute-start(bf16[256,4096]{1,0:T(8,128)(2,1)S(1)} %copy-done.14), channel_id=1, source_target_pairs={{0,24},{8,0},{16,8},{24,16},{1,25},{9,1},{17,9},{25,17},{2,26},{10... | collective-permute-start | bytes 6291464 | tf_op jit(solution)/shard_map/ppermute | solution.py:79
  298.9 60.6 %collective-permute-start.7 = (bf16[256,4096]{1,0:T(8,128)(2,1)}, bf16[256,4096]{1,0:T(8,128)(2,1)}, u32[]{:S(2)}, u32[]{:S(2)}) collective-permute-start(bf16[256,4096]{1,0:T(8,128)(2,1)} %collective-permute-done.6), channel_id=1, source_target_pairs={{0,1},{1,0},{2,3},{3,2},{4,5},{5,4},{6,7},{7,6},{8,9},{9,8},{10,11... | collective-permute-start | bytes 6291464 | tf_op jit(solution)/shard_map/ppermute | solution.py:86
  300.2 190.9 %collective-permute-start = (bf16[256,4096]{1,0:T(8,128)(2,1)S(1)}, bf16[256,4096]{1,0:T(8,128)(2,1)}, u32[]{:S(2)}, u32[]{:S(2)}) collective-permute-start(bf16[256,4096]{1,0:T(8,128)(2,1)S(1)} %copy-done.14), channel_id=1, source_target_pairs={{0,1},{1,0},{2,3},{3,2},{4,5},{5,4},{6,7},{7,6},{8,9},{9,8},{10,11... | collective-permute-start | bytes 6291464 | tf_op jit(solution)/shard_map/ppermute | solution.py:86
  305.9 131.8 %collective-permute-start.5 = (bf16[256,4096]{1,0:T(8,128)(2,1)}, bf16[256,4096]{1,0:T(8,128)(2,1)}, u32[]{:S(2)}, u32[]{:S(2)}) collective-permute-start(bf16[256,4096]{1,0:T(8,128)(2,1)} %copy-done.15), channel_id=1, source_target_pairs={{0,1},{1,0},{2,3},{3,2},{4,5},{5,4},{6,7},{7,6},{8,9},{9,8},{10,11... | collective-permute-start | bytes 6291464 | tf_op jit(solution)/shard_map/ppermute | solution.py:86
  341.2 135.3 %collective-permute-start.9 = (bf16[256,4096]{1,0:T(8,128)(2,1)}, bf16[256,4096]{1,0:T(8,128)(2,1)}, u32[]{:S(2)}, u32[]{:S(2)}) collective-permute-start(bf16[256,4096]{1,0:T(8,128)(2,1)} %collective-permute-done.8), channel_id=1, source_target_pairs={{0,1},{1,0},{2,3},{3,2},{4,5},{5,4},{6,7},{7,6},{8,9},{9,8},{10,11... | collective-permute-start | bytes 6291464 | tf_op jit(solution)/shard_map/ppermute | solution.py:86
  359.6 78.1 %copy-start.16 = (bf16[256,4096]{1,0:T(8,128)(2,1)S(1)}, bf16[256,4096]{1,0:T(8,128)(2,1)}, u32[]{:S(2)}) copy-start(bf16[256,4096]{1,0:T(8,128)(2,1)} %copy-done.15) | copy-start | bytes 6291460
  522.8 2.3 copy-start
  528.9 3.1 slice-start
  556.9 9.4 %copy-start.6 = (pred[256,1024]{0,1:T(8,128)(4,1)S(1)}, pred[256,1024]{0,1:T(8,128)(4,1)}, u32[]{:S(2)}) copy-start(pred[256,1024]{0,1:T(8,128)(4,1)} %iota_compare_fusion.3) | copy-start | bytes 786436
  566.4 7.4 %copy-start.5 = (pred[256,2048]{0,1:T(8,128)(4,1)S(1)}, pred[256,2048]{0,1:T(8,128)(4,1)}, u32[]{:S(2)}) copy-start(pred[256,2048]{0,1:T(8,128)(4,1)} %iota_compare_fusion.2) | copy-start | bytes 1572868
  590.4 14.8 %copy-start.2 = (pred[256,4096]{0,1:T(8,128)(4,1)S(1)}, pred[256,4096]{0,1:T(8,128)(4,1)}, u32[]{:S(2)}) copy-start(pred[256,4096]{0,1:T(8,128)(4,1)} %iota_compare_fusion) | copy-start | bytes 3145732
  605.2 18.2 %copy-start.13 = (s32[8,256]{1,0:T(8,128)S(1)}, s32[8,256]{1,0:T(8,128)}, u32[]{:S(2)}) copy-start(s32[8,256]{1,0:T(8,128)} %get-tuple-element.19) | copy-start | bytes 24580
  623.4 5.9 copy-start.1
  623.4 5.9 copy-start.9
  623.5 5.9 copy-start.12
  623.5 5.9 copy-start.17
  623.5 12.7 %slice-start.5 = ((s8[12582912]{0:T(1024)(128)(4,1)}), s8[4194304]{0:T(1024)(128)(4,1)S(1)}, s32[]{:S(2)}) async-start(s8[12582912]{0:T(1024)(128)(4,1)} %bitcast.229), calls=%async_computation.8 | async-start | bytes 8388608
  629.4 6.8 copy-start.8
  629.4 6.8 copy-start.11
  629.4 6.8 slice-start.6
  629.4 6.8 slice-start.7
  629.4 17.1 %slice-start.1 = ((s8[16777216]{0:T(1024)(128)(4,1)}), s8[4194304]{0:T(1024)(128)(4,1)S(1)}, s32[]{:S(2)}) async-start(s8[16777216]{0:T(1024)(128)(4,1)} %bitcast.227), calls=%async_computation.4 | async-start | bytes 8388608
  629.4 17.1 %slice-start.2 = ((s8[16777216]{0:T(1024)(128)(4,1)}), s8[4194304]{0:T(1024)(128)(4,1)S(1)}, s32[]{:S(2)}) async-start(s8[16777216]{0:T(1024)(128)(4,1)} %bitcast.227), calls=%async_computation.5 | async-start | bytes 8388608
  636.2 10.3 %copy-start.7 = (s32[4096]{0:T(1024)S(1)}, s32[4096]{0:T(1024)}, u32[]{:S(2)}) copy-start(s32[4096]{0:T(1024)} %iota_multiply_fusion) | copy-start | bytes 49156
  636.2 10.3 %copy-start.10 = (s32[8,256]{1,0:T(8,128)S(1)}, s32[8,256]{1,0:T(8,128)}, u32[]{:S(2)}) copy-start(s32[8,256]{1,0:T(8,128)} %get-tuple-element.22) | copy-start | bytes 24580
  636.2 10.3 %slice-start.3 = ((s8[16777216]{0:T(1024)(128)(4,1)}), s8[4194304]{0:T(1024)(128)(4,1)S(1)}, s32[]{:S(2)}) async-start(s8[16777216]{0:T(1024)(128)(4,1)} %bitcast.227), calls=%async_computation.6 | async-start | bytes 8388608
  636.3 10.3 %slice-start.4 = ((s8[16777216]{0:T(1024)(128)(4,1)}), s8[4194304]{0:T(1024)(128)(4,1)S(1)}, s32[]{:S(2)}) async-start(s8[16777216]{0:T(1024)(128)(4,1)} %bitcast.227), calls=%async_computation.7 | async-start | bytes 8388608
Sparse Core Ops, SparseCore 0:
  131.8 200.2 all-gather.3
  527.2 20.4 all-gather.5

commit v11 on v5

--- a/solution.py
+++ b/solution.py
@@ -69,9 +69,6 @@
     qcols = group_heads * HD
     rows = n_g * tok
 
-    full_rows = lax.all_gather(activations, "fsdp", axis=1, tiled=True)
-    grp_rows = lax.all_gather(full_rows, "cg", axis=0, tiled=True)
-
     local_w = jnp.concatenate(
         [
             w_query.reshape(d_rows, n_g, qcols),
@@ -80,6 +77,9 @@
         ],
         axis=2,
     )
+    if lax.axis_size("fsdp") == 2:
+        own_other = lax.ppermute(activations, "fsdp", [(0, 1), (1, 0)])
+        own_other, local_w = lax.optimization_barrier((own_other, local_w))
     received = [lax.dynamic_index_in_dim(local_w, g, 1, keepdims=False)]
     for shift in range(1, n_g):
         outgoing = lax.dynamic_index_in_dim(local_w, (g + shift) % n_g, 1, keepdims=False)
@@ -88,11 +88,44 @@
     by_shift = jnp.stack(received, axis=0)
     back = (g - jnp.arange(n_g, dtype=jnp.int32)) % n_g
     mine = jnp.take(by_shift, back, axis=0)
-    grp_rows, mine = lax.optimization_barrier((grp_rows, mine))
+    if lax.axis_size("fsdp") == 2:
+        pieces = []
+        halves = [activations]
+        if n_g == 4:
+            right = [(i, (i + 1) % n_g) for i in range(n_g)]
+            left = [(i, (i - 1) % n_g) for i in range(n_g)]
+            from_left = lax.ppermute(activations, "cg", right)
+            from_right = lax.ppermute(activations, "cg", left)
+            halves += [from_left, lax.ppermute(from_left, "cg", right), from_right]
+        else:
+            for shift in range(1, n_g):
+                perm = [(i, (i + shift) % n_g) for i in range(n_g)]
+                halves.append(lax.ppermute(activations, "cg", perm))
+        for index, mine_half in enumerate(halves):
+            if index:
+                other_half = lax.ppermute(mine_half, "fsdp", [(0, 1), (1, 0)])
+            else:
+                other_half = own_other
+            pieces.append(
+                jnp.where(
+                    f == 0,
+                    jnp.concatenate([mine_half, other_half], axis=1),
+                    jnp.concatenate([other_half, mine_half], axis=1),
+                )
+            )
+        grp_rows = jnp.concatenate(pieces, axis=0)
+    else:
+        own_half = [activations]
+        for shift in range(1, n_g):
+            perm = [(i, (i + shift) % n_g) for i in range(n_g)]
+            own_half.append(lax.ppermute(activations, "cg", perm))
+        grp_rows = lax.all_gather(jnp.concatenate(own_half, axis=0), "fsdp", axis=1, tiled=True)
+
     every = lax.all_gather(mine, "ct", axis=0, tiled=False)
     every = every.transpose(1, 0, 2, 3).reshape(n_g * n_t * d_rows, qcols + 2 * HD)
 
     mixed = jnp.dot(grp_rows, every, preferred_element_type=jnp.float32)
+    mixed = jnp.take(mixed.reshape(n_g, tok, -1), back, axis=0).reshape(rows, -1)
     chunk_of_row = n_t * (jnp.arange(rows, dtype=jnp.int32) // tok) + t
     positions = chunk_of_row * tok + jnp.arange(rows, dtype=jnp.int32) % tok
     cosine, sine_part = rotation(positions)

time: 841 us -> 692 us (0.82)
  waiting for transfers between devices: 556 us -> 279 us
  starting transfers between devices: 4.69 us -> 85.6 us
  other arithmetic: 48.1 us -> 72.3 us
  local copies, waits for them, and re-layouts: 45 us -> 68.2 us
    ppermute x0 -> x7, waiting for transfers between devices: none -> 196 us  [the longest x1 46.1 us: shards(): from_left = lax.ppermute(activations, 'cg', right)]
    ppermute x3, waiting for transfers between devices: 251 us -> 80.7 us  [shards(): received.append(lax.ppermute(outgoing, 'cg', perm))]
    all_gather x2 -> x0, waiting for transfers between devices: 169 us -> none  [the longest x1 107 us: shards(): grp_rows = lax.all_gather(full_rows, 'cg', axis=0, tiled=True)]
    all_gather x1, waiting for transfers between devices: 124 us -> 0.01 us  [shards(): every = lax.all_gather(mine, 'ct', axis=0, tiled=False)]
    ppermute x0 -> x7, starting transfers between devices: none -> 80.7 us  [the longest x1 70.9 us: shards(): from_left = lax.ppermute(activations, 'cg', right)]
    select_n x0 -> x6, other arithmetic: none -> 16.3 us  [the longest x4 13.1 us: shards(): jnp.where(f == 0, jnp.concatenate([mine_half, other_half], axis=1), jnp.c...]
    gather x0 -> x2, local copies, waits for them, and re-layouts: none -> 11.7 us  [shards(): jnp.take(mixed.reshape(n_g, tok, -1), back, axis=0).reshape(rows, -1)]
    all_gather x1, waiting for transfers between devices: 11.8 us -> 1.46 us  [shards(): pair = lax.all_gather(pair, 'ct', axis=0, tiled=False)]
  transfers between devices with their start and end apart: 7 -> 12, of which waited for: 6 -> 9; matrix products, arithmetic and copies ran while one was open for 6% -> 9% of each run, Pallas kernels for 0% -> 0%
where the time goes in v11:
time: 692 us; the launch traced here: 686 us
  waiting for transfers between devices  279 us (40%)
  matrix products  112 us (16%)
  starting transfers between devices  85.6 us (12%)
  other arithmetic  72.3 us (10%)
  local copies, waits for them, and re-layouts  68.2 us (10%)
  blocking collectives  53 us (8%)
  between operations  16.3 us (2%)
    ppermute x3, waiting for transfers between devices, shards(): received.append(lax.ppermute(outgoing, 'cg', perm))  80.7 us
    ppermute x1, starting transfers between devices, shards(): from_left = lax.ppermute(activations, 'cg', right)  70.9 us
    all_to_all x1, blocking collectives, shards(): lax.all_to_all(out_rows, 'cg', split_axis=0, concat_axis=2, tiled=True)  53 us
    ppermute x1, waiting for transfers between devices, shards(): from_left = lax.ppermute(activations, 'cg', right)  46.1 us
    ppermute x1, waiting for transfers between devices, shards(): halves += [from_left, lax.ppermute(from_left, 'cg', right), from_right]  41.6 us
    sub x3, matrix products, shards(): weights = jnp.where(visible, jnp.exp(scores - highest), 0.0)  40.1 us
    ppermute x3, waiting for transfers between devices, shards(): other_half = lax.ppermute(mine_half, 'fsdp', [(0, 1), (1, 0)])  38.8 us
    dot_general x4, matrix products, shards(): jnp.einsum('hqk,ke->hqe', dropped, all_values[:span], preferred_element_t...  36.4 us
  transfers between devices with their start and end apart: 12, of which 9 were waited for; matrix products, arithmetic and copies ran while one was open for 9% of the time, Pallas kernels for 0%

profile of v11, /device:TPU:0, one launch (start us, length us, event | category | flops | bytes accessed | tf_op | source)
XLA Modules:
  0.0 686.1 jit_solution(13348802402459643296)
XLA Ops:
  6.5 3.0 collective-permute-start
  9.5 6.5 copy.57
  16.5 5.2 pad_maximum_fusion.1
  21.7 33.8 %collective-permute-done = bf16[256,4096]{1,0:T(8,128)(2,1)} collective-permute-done((bf16[256,4096]{1,0:T(8,128)(2,1)}, bf16[256,4096]{1,0:T(8,128)(2,1)}, u32[]{:S(2)}, u32[]{:S(2)}) %collective-permute-start) | collective-permute-done | bytes 2097184 | tf_op jit(solution)/shard_map/ppermute | solution.py:81
  55.5 2.0 constant_dynamic-slice_fusion.3
  57.5 2.5 copy.62
  59.9 2.8 collective-permute-start.8
  62.7 2.4 copy.63
  65.2 1.3 collective-permute-start.9
  66.5 1.4 copy.61
  67.9 0.7 collective-permute-start.7
  68.7 0.6 copy.60
  69.3 79.1 %collective-permute-done.8 = bf16[512,1280]{1,0:T(8,128)(2,1)} collective-permute-done((bf16[512,1280]{1,0:T(8,128)(2,1)}, bf16[512,1280]{1,0:T(8,128)(2,1)}, u32[]{:S(2)}, u32[]{:S(2)}) %collective-permute-start.8) | collective-permute-done | bytes 1310752 | tf_op jit(solution)/shard_map/ppermute | solution.py:87
  148.4 1.6 collective-permute-done.9
  150.0 5.2 pad_maximum_fusion.2
  155.2 5.7 gather_fusion
  160.9 5.3 bitcast_select_fusion.16
  166.3 1.5 copy-done.2
  167.8 70.9 %collective-permute-start.1 = (bf16[256,4096]{1,0:T(8,128)(2,1)S(1)}, bf16[256,4096]{1,0:T(8,128)(2,1)}, u32[]{:S(2)}, u32[]{:S(2)}) collective-permute-start(bf16[256,4096]{1,0:T(8,128)(2,1)S(1)} %copy-done.2), channel_id=1, source_target_pairs={{0,8},{8,16},{16,24},{24,0},{1,9},{9,17},{17,25},{25,1},{2,10},{10... | collective-permute-start | bytes 6291464 | tf_op jit(solution)/shard_map/ppermute | solution.py:97
  238.7 46.1 %collective-permute-done.1 = bf16[256,4096]{1,0:T(8,128)(2,1)} collective-permute-done((bf16[256,4096]{1,0:T(8,128)(2,1)S(1)}, bf16[256,4096]{1,0:T(8,128)(2,1)}, u32[]{:S(2)}, u32[]{:S(2)}) %collective-permute-start.1) | collective-permute-done | bytes 2097184 | tf_op jit(solution)/shard_map/ppermute | solution.py:97
  284.8 2.6 collective-permute-start.3
  289.5 1.5 collective-permute-start.2
  292.2 0.7 shift-right-logical_xor_fusion.21
  292.9 0.9 iota_compare_fusion.3
  293.8 36.0 %collective-permute-done.5 = bf16[256,4096]{1,0:T(8,128)(2,1)} collective-permute-done((bf16[256,4096]{1,0:T(8,128)(2,1)S(1)}, bf16[256,4096]{1,0:T(8,128)(2,1)}, u32[]{:S(2)}, u32[]{:S(2)}) %collective-permute-start.5) | collective-permute-done | bytes 2097184 | tf_op jit(solution)/shard_map/ppermute | solution.py:98
  329.8 1.4 collective-permute-start.6
  331.2 41.6 %collective-permute-done.3 = bf16[256,4096]{1,0:T(8,128)(2,1)} collective-permute-done((bf16[256,4096]{1,0:T(8,128)(2,1)}, bf16[256,4096]{1,0:T(8,128)(2,1)}, u32[]{:S(2)}, u32[]{:S(2)}) %collective-permute-start.3) | collective-permute-done | bytes 2097184 | tf_op jit(solution)/shard_map/ppermute | solution.py:99
  372.8 1.3 collective-permute-start.4
  374.2 3.4 maximum_select_fusion
  377.6 3.3 maximum_select_fusion.1
  380.9 1.3 collective-permute-done.6
  382.3 3.2 maximum_select_fusion.3
  385.5 37.5 %collective-permute-done.4 = bf16[256,4096]{1,0:T(8,128)(2,1)S(1)} collective-permute-done((bf16[256,4096]{1,0:T(8,128)(2,1)}, bf16[256,4096]{1,0:T(8,128)(2,1)S(1)}, u32[]{:S(2)}, u32[]{:S(2)}) %collective-permute-start.4) | collective-permute-done | bytes 2097184 | tf_op jit(solution)/shard_map/ppermute | solution.py:106
  423.0 3.2 maximum_select_fusion.2
  426.2 7.3 %pad_maximum_fusion = bf16[1024,8192]{1,0:T(8,128)(2,1)} fusion(bf16[256,8192]{1,0:T(8,128)(2,1)S(1)} %maximum_select_fusion.3, bf16[256,8192]{1,0:T(8,128)(2,1)S(1)} %maximum_select_fusion.2, bf16[256,8192]{1,0:T(8,128)(2,1)S(1)} %maximum_select_fusion.1, bf16[256,8192]{1,0:T(8,128)(2,1)S(1)} %maximum_select_fusion), kind=kLoop, calls=%fused_computation.41 | loop fusion | flops 67108864 | bytes 33554432 | tf_op jit(solution)/shard_map/concatenate | solution.py:116
  433.5 10.1 %copy.64 = bf16[4,4,512,1280]{3,2,1,0:T(8,128)(2,1)S(1)} copy(bf16[4,4,512,1280]{3,2,0,1:T(8,128)(2,1)} %bitcast.193) | data formatting | bytes 41943040 | tf_op jit(solution)/shard_map/transpose | solution.py:125
  443.6 26.3 %fusion.162 = f32[4,256,1280]{2,1,0:T(8,128)} fusion(bf16[4,256,8192]{2,1,0:T(8,128)(2,1)} %bitcast.197, bf16[8192,1280,1]{1,0,2:T(8,128)(2,1)S(1)} %bitcast.194), kind=kOutput, calls=%fused_computation.261 | convolution fusion | flops 21474836480 | bytes 42991616 | tf_op jit(solution)/shard_map/dot_general | solution.py:127
  469.9 5.7 gather_fusion.1
  475.7 6.0 copy.65
  481.6 3.1 broadcast_select_fusion
  484.8 2.3 copy-done
  487.1 1.1 multiply_cosine_fusion
  488.3 0.8 pad_maximum_fusion.5
  489.7 1.1 iota_compare_fusion.2
  490.9 1.4 iota_compare_fusion.1
  492.3 1.7 iota_compare_fusion
  494.0 1.8 fusion.149
  495.7 3.9 copy.93
  499.6 2.9 copy.94
  503.0 6.0 subtract_convert_fusion
  509.0 1.5 all-gather.6.cloned.1.call-done
  510.5 4.5 reshape.542
  515.0 4.5 copy.66
  519.4 9.4 %fusion.67 = f32[2048,256,8]{1,0,2:T(8,128)} fusion(bf16[1024,8,64]{2,0,1:T(8,128)(2,1)S(1)} %get-tuple-element.9, bf16[1024,8,64]{2,0,1:T(8,128)(2,1)} %get-tuple-element.10, bf16[4096,2,128]{2,0,1:T(8,128)(2,1)} %bitcast.201), kind=kOutput, calls=%fused_computation.120 | convolution fusion | flops 1074790400 | bytes 20447232 | tf_op jit(solution)/shard_map/qhe,ke->hqk/dot_general | solution.py:155
  528.9 7.4 %fusion.157 = (f32[8,256]{1,0:T(8,128)S(1)}, bf16[8,256,1024]{1,2,0:T(8,128)(2,1)}) fusion(pred[256,1024]{0,1:T(8,128)(4,1)S(1)} %copy-done.7, bf16[4096,2,128]{2,0,1:T(8,128)(2,1)} %bitcast.202, bf16[1024,8,64]{2,0,1:T(8,128)(2,1)S(1)} %get-tuple-element.9, bf16[1024,8,64]{2,0,1:T(8,128)(2,1)} %get-tuple-element.10), kind=kOutput, calls=%fused_computation.260 | convolution fusion | flops 1090520064 | bytes 13639680 | tf_op jit(solution)/shard_map/sub | solution.py:165
  536.3 17.0 %fusion.156 = (f32[8,256]{1,0:T(8,128)S(1)}, bf16[8,256,2048]{1,2,0:T(8,128)(2,1)}) fusion(f32[2048,256,8]{1,0,2:T(8,128)} %fusion.67, pred[256,2048]{0,1:T(8,128)(4,1)S(1)} %copy-done.6), kind=kOutput, calls=%fused_computation.259 | output fusion | flops 29362176 | bytes 25698304 | tf_op jit(solution)/shard_map/sub | solution.py:165
  553.2 14.7 %fusion.151 = (f32[8,256]{1,0:T(8,128)S(1)}, bf16[8,256,3072]{1,2,0:T(8,128)(2,1)}) fusion(pred[256,3072]{0,1:T(8,128)(4,1)} %iota_compare_fusion.1, bf16[4096,2,128]{2,0,1:T(8,128)(2,1)} %bitcast.203, bf16[1024,8,64]{2,0,1:T(8,128)(2,1)S(1)} %get-tuple-element.9, bf16[1024,8,64]{2,0,1:T(8,128)(2,1)} %get-tuple-element.10), kind=kOutput, calls=%fused_computation.258 | convolution fusion | flops 3267365888 | bytes 24125440 | tf_op jit(solution)/shard_map/sub | solution.py:165
  568.0 18.0 %fusion.150 = (f32[8,256]{1,0:T(8,128)S(1)}, bf16[8,256,4096]{1,2,0:T(8,128)(2,1)}) fusion(pred[256,4096]{0,1:T(8,128)(4,1)S(1)} %copy-done.3, bf16[4096,2,128]{2,0,1:T(8,128)(2,1)} %bitcast.204, bf16[1024,8,64]{2,0,1:T(8,128)(2,1)} %get-tuple-element.10, bf16[1024,8,64]{2,0,1:T(8,128)(2,1)S(1)} %get-tuple-element.9), kind=kOutput, calls=%fused_computation.257 | convolution fusion | flops 4355788800 | bytes 29368320 | tf_op jit(solution)/shard_map/sub | solution.py:165
  586.0 5.8 divide_convert_fusion.3
  592.0 6.7 divide_convert_fusion.2
  598.8 10.2 %divide_convert_fusion.1 = bf16[256,8,128]{0,2,1:T(8,128)(2,1)S(1)} fusion(bf16[8,256,3072]{1,2,0:T(8,128)(2,1)S(1)} %bitcast.221, s32[3072]{0:T(1024)S(1)} %copy-done.9, s32[8,256]{1,0:T(8,128)S(1)} %copy-done.12, bf16[4096,2,128]{2,0,1:T(8,128)(2,1)S(1)} %bitcast.207, f32[256,8]{0,1:T(8,128)S(1)} %multiply_bitcast_fusion.1), kind=kOutput, calls=%fused_computation.109 | convolution fusion | flops 1686634496 | bytes 13922304 | tf_op jit(solution)/shard_map/hqk,ke->hqe/dot_general | solution.py:171
  609.1 13.6 %divide_convert_fusion = bf16[256,8,128]{0,2,1:T(8,128)(2,1)S(1)} fusion(bf16[4096,2,128]{2,0,1:T(8,128)(2,1)S(1)} %bitcast.208, bf16[8,256,4096]{1,2,0:T(8,128)(2,1)S(1)} %bitcast.219, s32[4096]{0:T(1024)S(1)} %copy-done.8, s32[8,256]{1,0:T(8,128)S(1)} %copy-done.11, f32[256,8]{0,1:T(8,128)S(1)} %multiply_bitcast_fusion), kind=kOutput, calls=%fused_computation.108 | convolution fusion | flops 2248671232 | bytes 18382848 | tf_op jit(solution)/shard_map/hqk,ke->hqe/dot_general | solution.py:171
  622.9 53.0 %all_to_all.15 = bf16[4,256,1024]{1,2,0:T(8,128)(2,1)S(1)} all-to-all(bf16[4,256,1024]{1,2,0:T(8,128)(2,1)S(1)} %pad_maximum_fusion.3), channel_id=1, replica_groups=mesh['cg'=4,'ct'=4,'fsdp'=2] {'cg'}, dimensions={0} | all-to-all | bytes 4194304 | tf_op jit(solution)/shard_map/all_to_all | solution.py:177
  675.9 2.8 copy.92
  (81 shorter events, 3.3 us)
Async XLA Ops:
  6.5 9.5 %copy-start.4 = (bf16[512,512]{1,0:T(8,128)(2,1)S(1)}, bf16[512,512]{1,0:T(8,128)(2,1)}, u32[]{:S(2)}) copy-start(bf16[512,512]{1,0:T(8,128)(2,1)} %param.9) | copy-start | bytes 1572868
  6.5 9.7 %copy-start.5 = (bf16[512,512]{1,0:T(8,128)(2,1)S(1)}, bf16[512,512]{1,0:T(8,128)(2,1)}, u32[]{:S(2)}) copy-start(bf16[512,512]{1,0:T(8,128)(2,1)} %param.10) | copy-start | bytes 1572868
  6.5 426.9 %all-gather.4.cloned.1.call-start = ((), (), s32[]{:S(2)}) async-start(), calls=%async_computation.1 | async-start | bytes 26214400 | tf_op jit(solution)/shard_map/all_gather | solution.py:124
  6.5 48.9 %collective-permute-start = (bf16[256,4096]{1,0:T(8,128)(2,1)}, bf16[256,4096]{1,0:T(8,128)(2,1)}, u32[]{:S(2)}, u32[]{:S(2)}) collective-permute-start(bf16[256,4096]{1,0:T(8,128)(2,1)} %param.7), channel_id=1, source_target_pairs={{0,1},{1,0},{2,3},{3,2},{4,5},{5,4},{6,7},{7,6},{8,9},{9,8},{10,11... | collective-permute-start | bytes 6291464 | tf_op jit(solution)/shard_map/ppermute | solution.py:81
  59.9 88.5 %collective-permute-start.8 = (bf16[512,1280]{1,0:T(8,128)(2,1)}, bf16[512,1280]{1,0:T(8,128)(2,1)}, u32[]{:S(2)}, u32[]{:S(2)}) collective-permute-start(bf16[512,1280]{1,0:T(8,128)(2,1)} %bitcast.211), channel_id=1, source_target_pairs={{0,16},{8,24},{16,0},{24,8},{1,17},{9,25},{17,1},{25,9},{2,18},{10... | collective-permute-start | bytes 3932168 | tf_op jit(solution)/shard_map/ppermute | solution.py:87
  65.2 84.8 %collective-permute-start.9 = (bf16[512,1280]{1,0:T(8,128)(2,1)}, bf16[512,1280]{1,0:T(8,128)(2,1)}, u32[]{:S(2)}, u32[]{:S(2)}) collective-permute-start(bf16[512,1280]{1,0:T(8,128)(2,1)} %bitcast.212), channel_id=1, source_target_pairs={{0,24},{8,0},{16,8},{24,16},{1,25},{9,1},{17,9},{25,17},{2,26},{10... | collective-permute-start | bytes 3932168 | tf_op jit(solution)/shard_map/ppermute | solution.py:87
  67.9 82.1 %collective-permute-start.7 = (bf16[512,1280]{1,0:T(8,128)(2,1)}, bf16[512,1280]{1,0:T(8,128)(2,1)}, u32[]{:S(2)}, u32[]{:S(2)}) collective-permute-start(bf16[512,1280]{1,0:T(8,128)(2,1)} %bitcast.213), channel_id=1, source_target_pairs={{0,8},{8,16},{16,24},{24,0},{1,9},{9,17},{17,25},{25,1},{2,10},{10... | collective-permute-start | bytes 3932168 | tf_op jit(solution)/shard_map/ppermute | solution.py:87
  166.2 1.6 copy-start.2
  166.2 344.2 %all-gather.6.cloned.1.call-start = ((), (), s32[]{:S(2)}) async-start(), calls=%async_computation.2 | async-start | bytes 2621440 | tf_op jit(solution)/shard_map/all_gather | solution.py:139
  167.8 117.0 %collective-permute-start.1 = (bf16[256,4096]{1,0:T(8,128)(2,1)S(1)}, bf16[256,4096]{1,0:T(8,128)(2,1)}, u32[]{:S(2)}, u32[]{:S(2)}) collective-permute-start(bf16[256,4096]{1,0:T(8,128)(2,1)S(1)} %copy-done.2), channel_id=1, source_target_pairs={{0,8},{8,16},{16,24},{24,0},{1,9},{9,17},{17,25},{25,1},{2,10},{10... | collective-permute-start | bytes 6291464 | tf_op jit(solution)/shard_map/ppermute | solution.py:97
  238.7 91.1 %collective-permute-start.5 = (bf16[256,4096]{1,0:T(8,128)(2,1)S(1)}, bf16[256,4096]{1,0:T(8,128)(2,1)}, u32[]{:S(2)}, u32[]{:S(2)}) collective-permute-start(bf16[256,4096]{1,0:T(8,128)(2,1)S(1)} %copy-done.2), channel_id=1, source_target_pairs={{0,24},{8,0},{16,8},{24,16},{1,25},{9,1},{17,9},{25,17},{2,26},{10... | collective-permute-start | bytes 6291464 | tf_op jit(solution)/shard_map/ppermute | solution.py:98
  284.8 88.0 %collective-permute-start.3 = (bf16[256,4096]{1,0:T(8,128)(2,1)}, bf16[256,4096]{1,0:T(8,128)(2,1)}, u32[]{:S(2)}, u32[]{:S(2)}) collective-permute-start(bf16[256,4096]{1,0:T(8,128)(2,1)} %collective-permute-done.1), channel_id=1, source_target_pairs={{0,8},{8,16},{16,24},{24,0},{1,9},{9,17},{17,25},{25,1},{2,10},{10... | collective-permute-start | bytes 6291464 | tf_op jit(solution)/shard_map/ppermute | solution.py:99
  289.5 88.1 %collective-permute-start.2 = (bf16[256,4096]{1,0:T(8,128)(2,1)}, bf16[256,4096]{1,0:T(8,128)(2,1)S(1)}, u32[]{:S(2)}, u32[]{:S(2)}) collective-permute-start(bf16[256,4096]{1,0:T(8,128)(2,1)} %collective-permute-done.1), channel_id=1, source_target_pairs={{0,1},{1,0},{2,3},{3,2},{4,5},{5,4},{6,7},{7,6},{8,9},{9,8},{10,11... | collective-permute-start | bytes 6291464 | tf_op jit(solution)/shard_map/ppermute | solution.py:106
  329.8 52.5 %collective-permute-start.6 = (bf16[256,4096]{1,0:T(8,128)(2,1)}, bf16[256,4096]{1,0:T(8,128)(2,1)S(1)}, u32[]{:S(2)}, u32[]{:S(2)}) collective-permute-start(bf16[256,4096]{1,0:T(8,128)(2,1)} %collective-permute-done.5), channel_id=1, source_target_pairs={{0,1},{1,0},{2,3},{3,2},{4,5},{5,4},{6,7},{7,6},{8,9},{9,8},{10,11... | collective-permute-start | bytes 6291464 | tf_op jit(solution)/shard_map/ppermute | solution.py:106
  372.8 50.1 %collective-permute-start.4 = (bf16[256,4096]{1,0:T(8,128)(2,1)}, bf16[256,4096]{1,0:T(8,128)(2,1)S(1)}, u32[]{:S(2)}, u32[]{:S(2)}) collective-permute-start(bf16[256,4096]{1,0:T(8,128)(2,1)} %collective-permute-done.3), channel_id=1, source_target_pairs={{0,1},{1,0},{2,3},{3,2},{4,5},{5,4},{6,7},{7,6},{8,9},{9,8},{10,11... | collective-permute-start | bytes 6291464 | tf_op jit(solution)/shard_map/ppermute | solution.py:106
  484.8 2.3 copy-start
  490.9 3.1 slice-start
  519.4 9.4 %copy-start.7 = (pred[256,1024]{0,1:T(8,128)(4,1)S(1)}, pred[256,1024]{0,1:T(8,128)(4,1)}, u32[]{:S(2)}) copy-start(pred[256,1024]{0,1:T(8,128)(4,1)} %iota_compare_fusion.3) | copy-start | bytes 786436
  528.9 7.4 %copy-start.6 = (pred[256,2048]{0,1:T(8,128)(4,1)S(1)}, pred[256,2048]{0,1:T(8,128)(4,1)}, u32[]{:S(2)}) copy-start(pred[256,2048]{0,1:T(8,128)(4,1)} %iota_compare_fusion.2) | copy-start | bytes 1572868
  553.2 14.7 %copy-start.3 = (pred[256,4096]{0,1:T(8,128)(4,1)S(1)}, pred[256,4096]{0,1:T(8,128)(4,1)}, u32[]{:S(2)}) copy-start(pred[256,4096]{0,1:T(8,128)(4,1)} %iota_compare_fusion) | copy-start | bytes 3145732
  568.0 18.0 %copy-start.14 = (s32[8,256]{1,0:T(8,128)S(1)}, s32[8,256]{1,0:T(8,128)}, u32[]{:S(2)}) copy-start(s32[8,256]{1,0:T(8,128)} %get-tuple-element.23) | copy-start | bytes 24580
  586.0 5.9 copy-start.1
  586.0 5.9 copy-start.10
  586.0 5.9 copy-start.13
  586.0 5.9 copy-start.15
  586.0 12.7 %slice-start.5 = ((s8[12582912]{0:T(1024)(128)(4,1)}), s8[4194304]{0:T(1024)(128)(4,1)S(1)}, s32[]{:S(2)}) async-start(s8[12582912]{0:T(1024)(128)(4,1)} %bitcast.220), calls=%async_computation.8 | async-start | bytes 8388608
  591.9 6.8 copy-start.9
  591.9 6.8 copy-start.12
  591.9 6.8 slice-start.6
  591.9 6.8 slice-start.7
  591.9 17.1 %slice-start.1 = ((s8[16777216]{0:T(1024)(128)(4,1)}), s8[4194304]{0:T(1024)(128)(4,1)S(1)}, s32[]{:S(2)}) async-start(s8[16777216]{0:T(1024)(128)(4,1)} %bitcast.218), calls=%async_computation.4 | async-start | bytes 8388608
  591.9 17.1 %slice-start.2 = ((s8[16777216]{0:T(1024)(128)(4,1)}), s8[4194304]{0:T(1024)(128)(4,1)S(1)}, s32[]{:S(2)}) async-start(s8[16777216]{0:T(1024)(128)(4,1)} %bitcast.218), calls=%async_computation.5 | async-start | bytes 8388608
  598.8 10.3 %copy-start.8 = (s32[4096]{0:T(1024)S(1)}, s32[4096]{0:T(1024)}, u32[]{:S(2)}) copy-start(s32[4096]{0:T(1024)} %iota_multiply_fusion) | copy-start | bytes 49156
  598.8 10.3 %copy-start.11 = (s32[8,256]{1,0:T(8,128)S(1)}, s32[8,256]{1,0:T(8,128)}, u32[]{:S(2)}) copy-start(s32[8,256]{1,0:T(8,128)} %get-tuple-element.26) | copy-start | bytes 24580
  598.8 10.3 %slice-start.3 = ((s8[16777216]{0:T(1024)(128)(4,1)}), s8[4194304]{0:T(1024)(128)(4,1)S(1)}, s32[]{:S(2)}) async-start(s8[16777216]{0:T(1024)(128)(4,1)} %bitcast.218), calls=%async_computation.6 | async-start | bytes 8388608
  598.8 10.3 %slice-start.4 = ((s8[16777216]{0:T(1024)(128)(4,1)}), s8[4194304]{0:T(1024)(128)(4,1)S(1)}, s32[]{:S(2)}) async-start(s8[16777216]{0:T(1024)(128)(4,1)} %bitcast.218), calls=%async_computation.7 | async-start | bytes 8388608
Sparse Core Ops, SparseCore 0:
  166.4 200.0 all-gather.3
  489.2 21.1 all-gather.5

commit v12 on v11

--- a/solution.py
+++ b/solution.py
@@ -101,30 +101,30 @@
             for shift in range(1, n_g):
                 perm = [(i, (i + shift) % n_g) for i in range(n_g)]
                 halves.append(lax.ppermute(activations, "cg", perm))
-        for index, mine_half in enumerate(halves):
-            if index:
-                other_half = lax.ppermute(mine_half, "fsdp", [(0, 1), (1, 0)])
-            else:
-                other_half = own_other
-            pieces.append(
-                jnp.where(
-                    f == 0,
-                    jnp.concatenate([mine_half, other_half], axis=1),
-                    jnp.concatenate([other_half, mine_half], axis=1),
-                )
-            )
-        grp_rows = jnp.concatenate(pieces, axis=0)
+        others = [own_other] + [
+            lax.ppermute(half, "fsdp", [(0, 1), (1, 0)]) for half in halves[1:]
+        ]
+        split_rows = (jnp.concatenate(halves, axis=0), jnp.concatenate(others, axis=0))
     else:
         own_half = [activations]
         for shift in range(1, n_g):
             perm = [(i, (i + shift) % n_g) for i in range(n_g)]
             own_half.append(lax.ppermute(activations, "cg", perm))
         grp_rows = lax.all_gather(jnp.concatenate(own_half, axis=0), "fsdp", axis=1, tiled=True)
+        split_rows = None
 
     every = lax.all_gather(mine, "ct", axis=0, tiled=False)
     every = every.transpose(1, 0, 2, 3).reshape(n_g * n_t * d_rows, qcols + 2 * HD)
 
-    mixed = jnp.dot(grp_rows, every, preferred_element_type=jnp.float32)
+    if split_rows is None:
+        mixed = jnp.dot(grp_rows, every, preferred_element_type=jnp.float32)
+    else:
+        halves_w = every.reshape(2, every.shape[0] // 2, every.shape[1])
+        mine_w = lax.dynamic_index_in_dim(halves_w, f, 0, keepdims=False)
+        other_w = lax.dynamic_index_in_dim(halves_w, 1 - f, 0, keepdims=False)
+        mixed = jnp.dot(split_rows[0], mine_w, preferred_element_type=jnp.float32) + jnp.dot(
+            split_rows[1], other_w, preferred_element_type=jnp.float32
+        )
     mixed = jnp.take(mixed.reshape(n_g, tok, -1), back, axis=0).reshape(rows, -1)
     chunk_of_row = n_t * (jnp.arange(rows, dtype=jnp.int32) // tok) + t
     positions = chunk_of_row * tok + jnp.arange(rows, dtype=jnp.int32) % tok

time: 692 us -> 670 us (0.968)
  waiting for transfers between devices: 279 us -> 253 us
  other arithmetic: 72.3 us -> 51.9 us
  matrix products: 112 us -> 129 us
  local copies, waits for them, and re-layouts: 68.2 us -> 75.5 us
    ppermute x3, waiting for transfers between devices: 38.8 us -> 14.2 us  [shards(): lax.ppermute(half, 'fsdp', [(0, 1), (1, 0)])]
    all_gather x0 -> x1, local copies, waits for them, and re-layouts: none -> 17.4 us  [shards(): every = lax.all_gather(mine, 'ct', axis=0, tiled=False)]
    dot_general x1 -> x2, matrix products: 26.3 us -> 42.7 us  [the longest x1 22.2 us: shards(): jnp.dot(split_rows[1], other_w, preferred_element_type=jnp.float32)]
    select_n x4 -> x0, other arithmetic: 13.1 us -> none  [shards(): jnp.where(f == 0, jnp.concatenate([mine_half, other_half], axis=1), jnp.c...]
    transpose x1 -> x0, local copies, waits for them, and re-layouts: 10.1 us -> none  [shards(): every.transpose(1, 0, 2, 3).reshape(n_g * n_t * d_rows, qcols + 2 * HD)]
    concatenate x1 -> x0, other arithmetic: 7.27 us -> none  [shards(): grp_rows = jnp.concatenate(pieces, axis=0)]
  transfers between devices with their start and end apart: 12 -> 12, of which waited for: 9 -> 8; matrix products, arithmetic and copies ran while one was open for 9% -> 12% of each run, Pallas kernels for 0% -> 0%
where the time goes in v12:
time: 670 us; the launch traced here: 665 us
  waiting for transfers between devices  253 us (38%)
  matrix products  129 us (19%)
  starting transfers between devices  86 us (13%)
  local copies, waits for them, and re-layouts  75.5 us (11%)
  blocking collectives  53 us (8%)
  other arithmetic  51.9 us (8%)
  between operations  16.3 us (2%)
    ppermute x3, waiting for transfers between devices, shards(): received.append(lax.ppermute(outgoing, 'cg', perm))  80.7 us
    ppermute x1, starting transfers between devices, shards(): from_left = lax.ppermute(activations, 'cg', right)  70.9 us
    all_to_all x1, blocking collectives, shards(): lax.all_to_all(out_rows, 'cg', split_axis=0, concat_axis=2, tiled=True)  53 us
    ppermute x1, waiting for transfers between devices, shards(): from_left = lax.ppermute(activations, 'cg', right)  46.1 us
    ppermute x1, waiting for transfers between devices, shards(): halves += [from_left, lax.ppermute(from_left, 'cg', right), from_right]  41.6 us
    sub x3, matrix products, shards(): weights = jnp.where(visible, jnp.exp(scores - highest), 0.0)  40.1 us
    dot_general x4, matrix products, shards(): jnp.einsum('hqk,ke->hqe', dropped, all_values[:span], preferred_element_t...  36.4 us
    ppermute x1, waiting for transfers between devices, shards(): from_right = lax.ppermute(activations, 'cg', left)  35.6 us
  transfers between devices with their start and end apart: 12, of which 8 were waited for; matrix products, arithmetic and copies ran while one was open for 12% of the time, Pallas kernels for 0%

profile of v12, /device:TPU:0, one launch (start us, length us, event | category | flops | bytes accessed | tf_op | source)
XLA Modules:
  0.0 664.8 jit_solution(15791033604339523203)
XLA Ops:
  6.5 3.0 collective-permute-start.3
  9.5 6.5 copy.57
  16.2 0.2 copy.59
  16.5 5.2 pad_maximum_fusion
  21.7 33.8 %collective-permute-done.3 = bf16[256,4096]{1,0:T(8,128)(2,1)} collective-permute-done((bf16[256,4096]{1,0:T(8,128)(2,1)}, bf16[256,4096]{1,0:T(8,128)(2,1)}, u32[]{:S(2)}, u32[]{:S(2)}) %collective-permute-start.3) | collective-permute-done | bytes 2097184 | tf_op jit(solution)/shard_map/ppermute | solution.py:81
  55.5 2.0 constant_dynamic-slice_fusion.3
  57.5 2.5 copy.62
  59.9 2.8 collective-permute-start.5
  62.7 2.4 copy.63
  65.2 1.3 collective-permute-start.6
  66.5 1.4 copy.61
  67.9 0.7 collective-permute-start.4
  68.7 0.6 copy.60
  69.3 79.1 %collective-permute-done.5 = bf16[512,1280]{1,0:T(8,128)(2,1)} collective-permute-done((bf16[512,1280]{1,0:T(8,128)(2,1)}, bf16[512,1280]{1,0:T(8,128)(2,1)}, u32[]{:S(2)}, u32[]{:S(2)}) %collective-permute-start.5) | collective-permute-done | bytes 1310752 | tf_op jit(solution)/shard_map/ppermute | solution.py:87
  148.4 1.6 collective-permute-done.6
  150.0 5.2 pad_maximum_fusion.1
  155.2 5.7 gather_fusion
  161.0 5.4 bitcast_select_fusion.16
  166.4 1.5 copy-done.14
  167.9 70.9 %collective-permute-start = (bf16[256,4096]{1,0:T(8,128)(2,1)S(1)}, bf16[256,4096]{1,0:T(8,128)(2,1)}, u32[]{:S(2)}, u32[]{:S(2)}) collective-permute-start(bf16[256,4096]{1,0:T(8,128)(2,1)S(1)} %copy-done.14), channel_id=1, source_target_pairs={{0,8},{8,16},{16,24},{24,0},{1,9},{9,17},{17,25},{25,1},{2,10},{10... | collective-permute-start | bytes 6291464 | tf_op jit(solution)/shard_map/ppermute | solution.py:97
  238.9 46.1 %collective-permute-done = bf16[256,4096]{1,0:T(8,128)(2,1)} collective-permute-done((bf16[256,4096]{1,0:T(8,128)(2,1)S(1)}, bf16[256,4096]{1,0:T(8,128)(2,1)}, u32[]{:S(2)}, u32[]{:S(2)}) %collective-permute-start) | collective-permute-done | bytes 2097184 | tf_op jit(solution)/shard_map/ppermute | solution.py:97
  284.9 3.1 collective-permute-start.1
  290.2 0.6 iota_multiply_fusion.2
  290.8 0.6 iota_multiply_fusion.1
  291.4 0.7 shift-right-logical_xor_fusion.21
  292.1 0.9 iota_compare_fusion.3
  292.9 1.4 collective-permute-start.7
  294.4 35.6 %collective-permute-done.2 = bf16[256,4096]{1,0:T(8,128)(2,1)} collective-permute-done((bf16[256,4096]{1,0:T(8,128)(2,1)S(1)}, bf16[256,4096]{1,0:T(8,128)(2,1)}, u32[]{:S(2)}, u32[]{:S(2)}) %collective-permute-start.2) | collective-permute-done | bytes 2097184 | tf_op jit(solution)/shard_map/ppermute | solution.py:98
  329.9 1.4 collective-permute-start.9
  331.4 41.6 %collective-permute-done.1 = bf16[256,4096]{1,0:T(8,128)(2,1)} collective-permute-done((bf16[256,4096]{1,0:T(8,128)(2,1)}, bf16[256,4096]{1,0:T(8,128)(2,1)}, u32[]{:S(2)}, u32[]{:S(2)}) %collective-permute-start.1) | collective-permute-done | bytes 2097184 | tf_op jit(solution)/shard_map/ppermute | solution.py:99
  373.0 1.3 collective-permute-start.8
  374.3 17.4 %copy.64 = bf16[4,4,512,1280]{3,2,0,1:T(8,128)(2,1)} copy(bf16[4,4,512,1280]{3,2,1,0:T(8,128)(2,1)} %all-gather.4.cloned.1.call-done) | data formatting | bytes 41943040 | tf_op jit(solution)/shard_map/all_gather | solution.py:116
  391.7 20.6 %fusion.38 = f32[1024,1280]{1,0:T(8,128)} fusion(bf16[2,4096,1280]{2,1,0:T(8,128)(2,1)} %bitcast.198, s32[]{:T(128)S(6)} %select_n.161, bf16[256,4096]{1,0:T(8,128)(2,1)} %collective-permute-done.2, bf16[256,4096]{1,0:T(8,128)(2,1)} %collective-permute-done.1, bf16[256,4096]{1,0:T(8,128)(2,1)} %collective-permute-done, bf16[256,4096]{1,0:T(8,128)(2,1)S(1)} %copy-done.14), kind=kOutput, calls=%fused_computation.61 | convolution fusion | flops 10770972672 | bytes 24117252 | tf_op jit(solution)/shard_map/dot_general | solution.py:125
  412.3 14.2 %collective-permute-done.8 = bf16[256,4096]{1,0:T(8,128)(2,1)} collective-permute-done((bf16[256,4096]{1,0:T(8,128)(2,1)}, bf16[256,4096]{1,0:T(8,128)(2,1)}, u32[]{:S(2)}, u32[]{:S(2)}) %collective-permute-start.8) | collective-permute-done | bytes 2097184 | tf_op jit(solution)/shard_map/ppermute | solution.py:105
  426.5 22.2 %fusion.72 = f32[1024,1280]{1,0:T(8,128)} fusion(f32[1024,1280]{1,0:T(8,128)} %fusion.38, bf16[2,4096,1280]{2,1,0:T(8,128)(2,1)} %bitcast.199, s32[]{:T(128)S(6)} %select_n.162, bf16[256,4096]{1,0:T(8,128)(2,1)} %collective-permute-done.9, bf16[256,4096]{1,0:T(8,128)(2,1)} %collective-permute-done.8, bf16[256,4096]{1,0:T(8,128)(2,1)} %collective-permute-done.7, ...), kind=kOutput, calls=%fused_computation.104 | convolution fusion | flops 10772283392 | bytes 29360132 | tf_op jit(solution)/shard_map/dot_general | solution.py:125
  448.7 5.7 gather_fusion.1
  454.4 6.0 copy.88
  460.4 3.1 broadcast_select_fusion
  463.5 2.3 copy-done
  465.8 1.1 multiply_cosine_fusion
  467.0 0.8 pad_maximum_fusion.4
  467.9 0.6 iota_multiply_fusion
  468.5 1.1 iota_compare_fusion.2
  469.6 1.4 iota_compare_fusion.1
  471.0 1.7 iota_compare_fusion
  472.7 1.8 fusion.178
  474.5 3.9 copy.94
  478.4 2.9 copy.95
  481.7 6.0 subtract_convert_fusion
  487.7 1.5 all-gather.6.cloned.1.call-done
  489.2 4.5 reshape.540
  493.7 4.5 copy.66
  498.2 9.4 %fusion.92 = f32[2048,256,8]{1,0,2:T(8,128)} fusion(bf16[1024,8,64]{2,0,1:T(8,128)(2,1)S(1)} %get-tuple-element.9, bf16[1024,8,64]{2,0,1:T(8,128)(2,1)} %get-tuple-element.10, bf16[4096,2,128]{2,0,1:T(8,128)(2,1)} %bitcast.206), kind=kOutput, calls=%fused_computation.136 | convolution fusion | flops 1074790400 | bytes 20447232 | tf_op jit(solution)/shard_map/qhe,ke->hqk/dot_general | solution.py:155
  507.6 7.4 %fusion.186 = (f32[8,256]{1,0:T(8,128)S(1)}, bf16[8,256,1024]{1,2,0:T(8,128)(2,1)}) fusion(pred[256,1024]{0,1:T(8,128)(4,1)S(1)} %copy-done.6, bf16[4096,2,128]{2,0,1:T(8,128)(2,1)} %bitcast.207, bf16[1024,8,64]{2,0,1:T(8,128)(2,1)S(1)} %get-tuple-element.9, bf16[1024,8,64]{2,0,1:T(8,128)(2,1)} %get-tuple-element.10), kind=kOutput, calls=%fused_computation.280 | convolution fusion | flops 1090520064 | bytes 13639680 | tf_op jit(solution)/shard_map/sub | solution.py:165
  515.0 17.0 %fusion.185 = (f32[8,256]{1,0:T(8,128)S(1)}, bf16[8,256,2048]{1,2,0:T(8,128)(2,1)}) fusion(f32[2048,256,8]{1,0,2:T(8,128)} %fusion.92, pred[256,2048]{0,1:T(8,128)(4,1)S(1)} %copy-done.5), kind=kOutput, calls=%fused_computation.279 | output fusion | flops 29362176 | bytes 25698304 | tf_op jit(solution)/shard_map/sub | solution.py:165
  532.0 14.7 %fusion.180 = (f32[8,256]{1,0:T(8,128)S(1)}, bf16[8,256,3072]{1,2,0:T(8,128)(2,1)}) fusion(pred[256,3072]{0,1:T(8,128)(4,1)} %iota_compare_fusion.1, bf16[4096,2,128]{2,0,1:T(8,128)(2,1)} %bitcast.208, bf16[1024,8,64]{2,0,1:T(8,128)(2,1)S(1)} %get-tuple-element.9, bf16[1024,8,64]{2,0,1:T(8,128)(2,1)} %get-tuple-element.10), kind=kOutput, calls=%fused_computation.278 | convolution fusion | flops 3267365888 | bytes 24125440 | tf_op jit(solution)/shard_map/sub | solution.py:165
  546.7 18.0 %fusion.179 = (f32[8,256]{1,0:T(8,128)S(1)}, bf16[8,256,4096]{1,2,0:T(8,128)(2,1)}) fusion(pred[256,4096]{0,1:T(8,128)(4,1)S(1)} %copy-done.2, bf16[4096,2,128]{2,0,1:T(8,128)(2,1)} %bitcast.209, bf16[1024,8,64]{2,0,1:T(8,128)(2,1)} %get-tuple-element.10, bf16[1024,8,64]{2,0,1:T(8,128)(2,1)S(1)} %get-tuple-element.9), kind=kOutput, calls=%fused_computation.277 | convolution fusion | flops 4355788800 | bytes 29368320 | tf_op jit(solution)/shard_map/sub | solution.py:165
  564.8 5.8 divide_convert_fusion.3
  570.7 6.7 %divide_convert_fusion.2 = bf16[256,8,128]{0,2,1:T(8,128)(2,1)S(1)} fusion(bf16[8,256,2048]{1,2,0:T(8,128)(2,1)S(1)} %copy-done.15, s32[2048]{0:T(1024)S(1)} %copy-done.9, s32[8,256]{1,0:T(8,128)S(1)} %copy-done.12, bf16[4096,2,128]{2,0,1:T(8,128)(2,1)S(1)} %bitcast.211, f32[256,8]{0,1:T(8,128)S(1)} %multiply_bitcast_fusion.2), kind=kOutput, calls=%fused_computation.126 | convolution fusion | flops 1124597760 | bytes 9461760 | tf_op jit(solution)/shard_map/hqk,ke->hqe/dot_general | solution.py:171
  577.6 10.2 %divide_convert_fusion.1 = bf16[256,8,128]{0,2,1:T(8,128)(2,1)S(1)} fusion(bf16[8,256,3072]{1,2,0:T(8,128)(2,1)S(1)} %bitcast.226, s32[3072]{0:T(1024)S(1)} %copy-done.8, s32[8,256]{1,0:T(8,128)S(1)} %copy-done.11, bf16[4096,2,128]{2,0,1:T(8,128)(2,1)S(1)} %bitcast.212, f32[256,8]{0,1:T(8,128)S(1)} %multiply_bitcast_fusion.1), kind=kOutput, calls=%fused_computation.125 | convolution fusion | flops 1686634496 | bytes 13922304 | tf_op jit(solution)/shard_map/hqk,ke->hqe/dot_general | solution.py:171
  587.9 13.6 %divide_convert_fusion = bf16[256,8,128]{0,2,1:T(8,128)(2,1)S(1)} fusion(bf16[4096,2,128]{2,0,1:T(8,128)(2,1)S(1)} %bitcast.213, bf16[8,256,4096]{1,2,0:T(8,128)(2,1)S(1)} %bitcast.224, s32[4096]{0:T(1024)S(1)} %copy-done.7, s32[8,256]{1,0:T(8,128)S(1)} %copy-done.10, f32[256,8]{0,1:T(8,128)S(1)} %multiply_bitcast_fusion), kind=kOutput, calls=%fused_computation.124 | convolution fusion | flops 2248671232 | bytes 18382848 | tf_op jit(solution)/shard_map/hqk,ke->hqe/dot_general | solution.py:171
  601.5 0.3 pad_maximum_fusion.2
  601.7 53.0 %all_to_all.15 = bf16[4,256,1024]{1,2,0:T(8,128)(2,1)S(1)} all-to-all(bf16[4,256,1024]{1,2,0:T(8,128)(2,1)S(1)} %pad_maximum_fusion.2), channel_id=1, replica_groups=mesh['cg'=4,'ct'=4,'fsdp'=2] {'cg'}, dimensions={0} | all-to-all | bytes 4194304 | tf_op jit(solution)/shard_map/all_to_all | solution.py:177
  654.7 2.8 copy.93
  (77 shorter events, 1.0 us)
Async XLA Ops:
  6.5 9.5 %copy-start.3 = (bf16[512,512]{1,0:T(8,128)(2,1)S(1)}, bf16[512,512]{1,0:T(8,128)(2,1)}, u32[]{:S(2)}) copy-start(bf16[512,512]{1,0:T(8,128)(2,1)} %param.9) | copy-start | bytes 1572868
  6.5 9.7 %copy-start.4 = (bf16[512,512]{1,0:T(8,128)(2,1)S(1)}, bf16[512,512]{1,0:T(8,128)(2,1)}, u32[]{:S(2)}) copy-start(bf16[512,512]{1,0:T(8,128)(2,1)} %param.10) | copy-start | bytes 1572868
  6.5 367.8 %all-gather.4.cloned.1.call-start = ((), (), s32[]{:S(2)}) async-start(), calls=%async_computation.1 | async-start | bytes 26214400 | tf_op jit(solution)/shard_map/all_gather | solution.py:116
  6.5 48.9 %collective-permute-start.3 = (bf16[256,4096]{1,0:T(8,128)(2,1)}, bf16[256,4096]{1,0:T(8,128)(2,1)}, u32[]{:S(2)}, u32[]{:S(2)}) collective-permute-start(bf16[256,4096]{1,0:T(8,128)(2,1)} %param.7), channel_id=1, source_target_pairs={{0,1},{1,0},{2,3},{3,2},{4,5},{5,4},{6,7},{7,6},{8,9},{9,8},{10,11... | collective-permute-start | bytes 6291464 | tf_op jit(solution)/shard_map/ppermute | solution.py:81
  59.9 88.5 %collective-permute-start.5 = (bf16[512,1280]{1,0:T(8,128)(2,1)}, bf16[512,1280]{1,0:T(8,128)(2,1)}, u32[]{:S(2)}, u32[]{:S(2)}) collective-permute-start(bf16[512,1280]{1,0:T(8,128)(2,1)} %bitcast.216), channel_id=1, source_target_pairs={{0,16},{8,24},{16,0},{24,8},{1,17},{9,25},{17,1},{25,9},{2,18},{10... | collective-permute-start | bytes 3932168 | tf_op jit(solution)/shard_map/ppermute | solution.py:87
  65.2 84.8 %collective-permute-start.6 = (bf16[512,1280]{1,0:T(8,128)(2,1)}, bf16[512,1280]{1,0:T(8,128)(2,1)}, u32[]{:S(2)}, u32[]{:S(2)}) collective-permute-start(bf16[512,1280]{1,0:T(8,128)(2,1)} %bitcast.217), channel_id=1, source_target_pairs={{0,24},{8,0},{16,8},{24,16},{1,25},{9,1},{17,9},{25,17},{2,26},{10... | collective-permute-start | bytes 3932168 | tf_op jit(solution)/shard_map/ppermute | solution.py:87
  67.9 82.1 %collective-permute-start.4 = (bf16[512,1280]{1,0:T(8,128)(2,1)}, bf16[512,1280]{1,0:T(8,128)(2,1)}, u32[]{:S(2)}, u32[]{:S(2)}) collective-permute-start(bf16[512,1280]{1,0:T(8,128)(2,1)} %bitcast.218), channel_id=1, source_target_pairs={{0,8},{8,16},{16,24},{24,0},{1,9},{9,17},{17,25},{25,1},{2,10},{10... | collective-permute-start | bytes 3932168 | tf_op jit(solution)/shard_map/ppermute | solution.py:87
  166.4 1.6 copy-start.14
  166.4 322.8 %all-gather.6.cloned.1.call-start = ((), (), s32[]{:S(2)}) async-start(), calls=%async_computation.2 | async-start | bytes 2621440 | tf_op jit(solution)/shard_map/all_gather | solution.py:139
  167.9 117.0 %collective-permute-start = (bf16[256,4096]{1,0:T(8,128)(2,1)S(1)}, bf16[256,4096]{1,0:T(8,128)(2,1)}, u32[]{:S(2)}, u32[]{:S(2)}) collective-permute-start(bf16[256,4096]{1,0:T(8,128)(2,1)S(1)} %copy-done.14), channel_id=1, source_target_pairs={{0,8},{8,16},{16,24},{24,0},{1,9},{9,17},{17,25},{25,1},{2,10},{10... | collective-permute-start | bytes 6291464 | tf_op jit(solution)/shard_map/ppermute | solution.py:97
  238.9 91.1 %collective-permute-start.2 = (bf16[256,4096]{1,0:T(8,128)(2,1)S(1)}, bf16[256,4096]{1,0:T(8,128)(2,1)}, u32[]{:S(2)}, u32[]{:S(2)}) collective-permute-start(bf16[256,4096]{1,0:T(8,128)(2,1)S(1)} %copy-done.14), channel_id=1, source_target_pairs={{0,24},{8,0},{16,8},{24,16},{1,25},{9,1},{17,9},{25,17},{2,26},{10... | collective-permute-start | bytes 6291464 | tf_op jit(solution)/shard_map/ppermute | solution.py:98
  284.9 88.0 %collective-permute-start.1 = (bf16[256,4096]{1,0:T(8,128)(2,1)}, bf16[256,4096]{1,0:T(8,128)(2,1)}, u32[]{:S(2)}, u32[]{:S(2)}) collective-permute-start(bf16[256,4096]{1,0:T(8,128)(2,1)} %collective-permute-done), channel_id=1, source_target_pairs={{0,8},{8,16},{16,24},{24,0},{1,9},{9,17},{17,25},{25,1},{2,10},{10... | collective-permute-start | bytes 6291464 | tf_op jit(solution)/shard_map/ppermute | solution.py:99
  292.9 119.3 %collective-permute-start.7 = (bf16[256,4096]{1,0:T(8,128)(2,1)}, bf16[256,4096]{1,0:T(8,128)(2,1)}, u32[]{:S(2)}, u32[]{:S(2)}) collective-permute-start(bf16[256,4096]{1,0:T(8,128)(2,1)} %collective-permute-done), channel_id=1, source_target_pairs={{0,1},{1,0},{2,3},{3,2},{4,5},{5,4},{6,7},{7,6},{8,9},{9,8},{10,11... | collective-permute-start | bytes 6291464 | tf_op jit(solution)/shard_map/ppermute | solution.py:105
  329.9 82.4 %collective-permute-start.9 = (bf16[256,4096]{1,0:T(8,128)(2,1)}, bf16[256,4096]{1,0:T(8,128)(2,1)}, u32[]{:S(2)}, u32[]{:S(2)}) collective-permute-start(bf16[256,4096]{1,0:T(8,128)(2,1)} %collective-permute-done.2), channel_id=1, source_target_pairs={{0,1},{1,0},{2,3},{3,2},{4,5},{5,4},{6,7},{7,6},{8,9},{9,8},{10,11... | collective-permute-start | bytes 6291464 | tf_op jit(solution)/shard_map/ppermute | solution.py:105
  373.0 53.5 %collective-permute-start.8 = (bf16[256,4096]{1,0:T(8,128)(2,1)}, bf16[256,4096]{1,0:T(8,128)(2,1)}, u32[]{:S(2)}, u32[]{:S(2)}) collective-permute-start(bf16[256,4096]{1,0:T(8,128)(2,1)} %collective-permute-done.1), channel_id=1, source_target_pairs={{0,1},{1,0},{2,3},{3,2},{4,5},{5,4},{6,7},{7,6},{8,9},{9,8},{10,11... | collective-permute-start | bytes 6291464 | tf_op jit(solution)/shard_map/ppermute | solution.py:105
  463.5 2.3 copy-start
  469.6 3.1 slice-start
  498.2 9.4 %copy-start.6 = (pred[256,1024]{0,1:T(8,128)(4,1)S(1)}, pred[256,1024]{0,1:T(8,128)(4,1)}, u32[]{:S(2)}) copy-start(pred[256,1024]{0,1:T(8,128)(4,1)} %iota_compare_fusion.3) | copy-start | bytes 786436
  507.6 7.4 %copy-start.5 = (pred[256,2048]{0,1:T(8,128)(4,1)S(1)}, pred[256,2048]{0,1:T(8,128)(4,1)}, u32[]{:S(2)}) copy-start(pred[256,2048]{0,1:T(8,128)(4,1)} %iota_compare_fusion.2) | copy-start | bytes 1572868
  532.0 14.7 %copy-start.2 = (pred[256,4096]{0,1:T(8,128)(4,1)S(1)}, pred[256,4096]{0,1:T(8,128)(4,1)}, u32[]{:S(2)}) copy-start(pred[256,4096]{0,1:T(8,128)(4,1)} %iota_compare_fusion) | copy-start | bytes 3145732
  546.7 18.0 %copy-start.13 = (s32[8,256]{1,0:T(8,128)S(1)}, s32[8,256]{1,0:T(8,128)}, u32[]{:S(2)}) copy-start(s32[8,256]{1,0:T(8,128)} %get-tuple-element.23) | copy-start | bytes 24580
  564.7 5.9 copy-start.1
  564.7 5.9 copy-start.9
  564.8 5.9 copy-start.12
  564.8 5.9 copy-start.15
  564.8 12.7 %slice-start.5 = ((s8[12582912]{0:T(1024)(128)(4,1)}), s8[4194304]{0:T(1024)(128)(4,1)S(1)}, s32[]{:S(2)}) async-start(s8[12582912]{0:T(1024)(128)(4,1)} %bitcast.225), calls=%async_computation.8 | async-start | bytes 8388608
  570.7 6.8 %copy-start.8 = (s32[3072]{0:T(1024)S(1)}, s32[3072]{0:T(1024)}, u32[]{:S(2)}) copy-start(s32[3072]{0:T(1024)} %iota_multiply_fusion.1) | copy-start | bytes 36868
  570.7 6.8 %copy-start.11 = (s32[8,256]{1,0:T(8,128)S(1)}, s32[8,256]{1,0:T(8,128)}, u32[]{:S(2)}) copy-start(s32[8,256]{1,0:T(8,128)} %get-tuple-element.25) | copy-start | bytes 24580
  570.7 6.8 %slice-start.6 = ((s8[12582912]{0:T(1024)(128)(4,1)}), s8[4194304]{0:T(1024)(128)(4,1)S(1)}, s32[]{:S(2)}) async-start(s8[12582912]{0:T(1024)(128)(4,1)} %bitcast.225), calls=%async_computation.9 | async-start | bytes 8388608
  570.7 6.8 %slice-start.7 = ((s8[12582912]{0:T(1024)(128)(4,1)}), s8[4194304]{0:T(1024)(128)(4,1)S(1)}, s32[]{:S(2)}) async-start(s8[12582912]{0:T(1024)(128)(4,1)} %bitcast.225), calls=%async_computation.10 | async-start | bytes 8388608
  570.7 17.1 %slice-start.1 = ((s8[16777216]{0:T(1024)(128)(4,1)}), s8[4194304]{0:T(1024)(128)(4,1)S(1)}, s32[]{:S(2)}) async-start(s8[16777216]{0:T(1024)(128)(4,1)} %bitcast.223), calls=%async_computation.4 | async-start | bytes 8388608
  570.7 17.1 %slice-start.2 = ((s8[16777216]{0:T(1024)(128)(4,1)}), s8[4194304]{0:T(1024)(128)(4,1)S(1)}, s32[]{:S(2)}) async-start(s8[16777216]{0:T(1024)(128)(4,1)} %bitcast.223), calls=%async_computation.5 | async-start | bytes 8388608
  577.5 10.3 %copy-start.7 = (s32[4096]{0:T(1024)S(1)}, s32[4096]{0:T(1024)}, u32[]{:S(2)}) copy-start(s32[4096]{0:T(1024)} %iota_multiply_fusion) | copy-start | bytes 49156
  577.5 10.3 %copy-start.10 = (s32[8,256]{1,0:T(8,128)S(1)}, s32[8,256]{1,0:T(8,128)}, u32[]{:S(2)}) copy-start(s32[8,256]{1,0:T(8,128)} %get-tuple-element.26) | copy-start | bytes 24580
  577.6 10.3 %slice-start.3 = ((s8[16777216]{0:T(1024)(128)(4,1)}), s8[4194304]{0:T(1024)(128)(4,1)S(1)}, s32[]{:S(2)}) async-start(s8[16777216]{0:T(1024)(128)(4,1)} %bitcast.223), calls=%async_computation.6 | async-start | bytes 8388608
  577.6 10.3 %slice-start.4 = ((s8[16777216]{0:T(1024)(128)(4,1)}), s8[4194304]{0:T(1024)(128)(4,1)S(1)}, s32[]{:S(2)}) async-start(s8[16777216]{0:T(1024)(128)(4,1)} %bitcast.223), calls=%async_computation.7 | async-start | bytes 8388608
Sparse Core Ops, SparseCore 0:
  166.5 200.0 all-gather.3
  468.0 21.1 all-gather.5

commit v13 on v12

--- a/solution.py
+++ b/solution.py
@@ -87,7 +87,6 @@
         received.append(lax.ppermute(outgoing, "cg", perm))
     by_shift = jnp.stack(received, axis=0)
     back = (g - jnp.arange(n_g, dtype=jnp.int32)) % n_g
-    mine = jnp.take(by_shift, back, axis=0)
     if lax.axis_size("fsdp") == 2:
         pieces = []
         halves = [activations]
@@ -113,8 +112,9 @@
         grp_rows = lax.all_gather(jnp.concatenate(own_half, axis=0), "fsdp", axis=1, tiled=True)
         split_rows = None
 
-    every = lax.all_gather(mine, "ct", axis=0, tiled=False)
-    every = every.transpose(1, 0, 2, 3).reshape(n_g * n_t * d_rows, qcols + 2 * HD)
+    every = lax.all_gather(by_shift, "ct", axis=0, tiled=False)
+    every = jnp.take(every, back, axis=1).transpose(1, 0, 2, 3)
+    every = every.reshape(n_g * n_t * d_rows, qcols + 2 * HD)
 
     if split_rows is None:
         mixed = jnp.dot(grp_rows, every, preferred_element_type=jnp.float32)
@@ -125,8 +125,8 @@
         mixed = jnp.dot(split_rows[0], mine_w, preferred_element_type=jnp.float32) + jnp.dot(
             split_rows[1], other_w, preferred_element_type=jnp.float32
         )
-    mixed = jnp.take(mixed.reshape(n_g, tok, -1), back, axis=0).reshape(rows, -1)
-    chunk_of_row = n_t * (jnp.arange(rows, dtype=jnp.int32) // tok) + t
+    shift_of_row = jnp.arange(rows, dtype=jnp.int32) // tok
+    chunk_of_row = n_t * ((g - shift_of_row) % n_g) + t
     positions = chunk_of_row * tok + jnp.arange(rows, dtype=jnp.int32) % tok
     cosine, sine_part = rotation(positions)
     queries = rotate(
@@ -134,6 +134,10 @@
     ).astype(jnp.bfloat16)
     keys = rotate(mixed[:, qcols : qcols + HD], cosine, sine_part).astype(jnp.bfloat16)
     values = mixed[:, qcols + HD :].astype(jnp.bfloat16)
+    queries = jnp.take(queries.reshape(n_g, tok, group_heads, HD), back, axis=0)
+    queries = queries.reshape(rows, group_heads, HD)
+    keys = jnp.take(keys.reshape(n_g, tok, HD), back, axis=0).reshape(rows, HD)
+    values = jnp.take(values.reshape(n_g, tok, HD), back, axis=0).reshape(rows, HD)
 
     pair = jnp.stack([keys, values], axis=1)
     pair = lax.all_gather(pair, "ct", axis=0, tiled=False)

time: 670 us -> 652 us (0.973)
  starting transfers between devices: 86 us -> 60 us
  waiting for transfers between devices: 253 us -> 229 us
  local copies, waits for them, and re-layouts: 75.5 us -> 96.2 us
  other arithmetic: 51.9 us -> 62.9 us
    ppermute x1, starting transfers between devices: 70.9 us -> 1.66 us  [shards(): from_left = lax.ppermute(activations, 'cg', right)]
    gather x3 -> x22, local copies, waits for them, and re-layouts: 17.4 us -> 59.6 us  [the longest x2 11.7 us: shards(): jnp.take(mixed.reshape(n_g, tok, -1), back, axis=0).reshape(rows, -1)]
    ppermute x1, starting transfers between devices: 3.09 us -> 44.7 us  [shards(): halves += [from_left, lax.ppermute(from_left, 'cg', right), from_right]]
    ppermute x1, waiting for transfers between devices: 35.6 us -> 0.01 us  [shards(): from_right = lax.ppermute(activations, 'cg', left)]
    ppermute x3, waiting for transfers between devices: 80.7 us -> 106 us  [shards(): received.append(lax.ppermute(outgoing, 'cg', perm))]
    all_gather x1 -> x0, local copies, waits for them, and re-layouts: 17.4 us -> none  [shards(): every = lax.all_gather(mine, 'ct', axis=0, tiled=False)]
    ppermute x3, waiting for transfers between devices: 14.2 us -> 0.01 us  [shards(): lax.ppermute(half, 'fsdp', [(0, 1), (1, 0)])]
    select_n x3 -> x6, other arithmetic: 8.53 us -> 20.8 us  [the longest x3 18.7 us: shards(): every = jnp.take(every, back, axis=1).transpose(1, 0, 2, 3)]
  transfers between devices with their start and end apart: 12 -> 12, of which waited for: 8 -> 6; matrix products, arithmetic and copies ran while one was open for 12% -> 22% of each run, Pallas kernels for 0% -> 0%
where the time goes in v13:
time: 652 us; the launch traced here: 646 us
  waiting for transfers between devices  229 us (35%)
  matrix products  129 us (20%)
  local copies, waits for them, and re-layouts  96.2 us (15%)
  other arithmetic  62.9 us (10%)
  starting transfers between devices  60 us (9%)
  blocking collectives  53 us (8%)
  between operations  16.2 us (2%)
    ppermute x3, waiting for transfers between devices, shards(): received.append(lax.ppermute(outgoing, 'cg', perm))  106 us
    all_to_all x1, blocking collectives, shards(): lax.all_to_all(out_rows, 'cg', split_axis=0, concat_axis=2, tiled=True)  53 us
    ppermute x1, waiting for transfers between devices, shards(): from_left = lax.ppermute(activations, 'cg', right)  44.9 us
    ppermute x1, starting transfers between devices, shards(): halves += [from_left, lax.ppermute(from_left, 'cg', right), from_right]  44.7 us
    dot_general x4, matrix products, shards(): jnp.einsum('hqk,ke->hqe', dropped, all_values[:span], preferred_element_t...  40.4 us
    sub x3, matrix products, shards(): weights = jnp.where(visible, jnp.exp(scores - highest), 0.0)  37.1 us
    ppermute x1, waiting for transfers between devices, shards(): halves += [from_left, lax.ppermute(from_left, 'cg', right), from_right]  36 us
    gather x16, local copies, waits for them, and re-layouts  35.3 us
  transfers between devices with their start and end apart: 12, of which 6 were waited for; matrix products, arithmetic and copies ran while one was open for 22% of the time, Pallas kernels for 0%

profile of v13, /device:TPU:0, one launch (start us, length us, event | category | flops | bytes accessed | tf_op | source)
XLA Modules:
  0.0 646.2 jit_solution(13105186843186562240)
XLA Ops:
  6.5 3.0 collective-permute-start.3
  9.5 1.3 copy.48
  10.8 1.3 copy.47
  12.0 6.5 %copy.46 = bf16[512,4096]{0,1:T(8,128)(2,1)} copy(bf16[512,4096]{1,0:T(8,128)(2,1)} %param.10) | data formatting | bytes 8388608 | tf_op args[1]
  18.5 5.2 pad_maximum_fusion
  23.7 31.7 %collective-permute-done.3 = bf16[256,4096]{1,0:T(8,128)(2,1)} collective-permute-done((bf16[256,4096]{1,0:T(8,128)(2,1)}, bf16[256,4096]{1,0:T(8,128)(2,1)}, u32[]{:S(2)}, u32[]{:S(2)}) %collective-permute-start.3) | collective-permute-done | bytes 2097184 | tf_op jit(solution)/shard_map/ppermute | solution.py:81
  55.4 2.0 constant_dynamic-slice_fusion.5
  57.5 2.4 copy.52
  59.9 3.8 collective-permute-start.6
  63.7 2.4 copy.51
  66.1 1.4 copy.50
  67.6 1.0 collective-permute-start.4
  69.2 24.1 %collective-permute-done.6 = bf16[512,1280]{1,0:T(8,128)(2,1)} collective-permute-done((bf16[512,1280]{1,0:T(8,128)(2,1)}, bf16[512,1280]{1,0:T(8,128)(2,1)}, u32[]{:S(2)}, u32[]{:S(2)}) %collective-permute-start.6) | collective-permute-done | bytes 1310752 | tf_op jit(solution)/shard_map/ppermute | solution.py:87
  93.3 82.0 %collective-permute-done.5 = bf16[512,1280]{1,0:T(8,128)(2,1)} collective-permute-done((bf16[512,1280]{1,0:T(8,128)(2,1)}, bf16[512,1280]{1,0:T(8,128)(2,1)}, u32[]{:S(2)}, u32[]{:S(2)}) %collective-permute-start.5) | collective-permute-done | bytes 1310752 | tf_op jit(solution)/shard_map/ppermute | solution.py:87
  175.3 5.3 pad_maximum_fusion.1
  180.7 1.7 collective-permute-start
  182.3 2.2 collective-permute-start.2
  186.5 44.9 %collective-permute-done = bf16[256,4096]{1,0:T(8,128)(2,1)} collective-permute-done((bf16[256,4096]{1,0:T(8,128)(2,1)}, bf16[256,4096]{1,0:T(8,128)(2,1)}, u32[]{:S(2)}, u32[]{:S(2)}) %collective-permute-start) | collective-permute-done | bytes 2097184 | tf_op jit(solution)/shard_map/ppermute | solution.py:96
  231.4 44.7 %collective-permute-start.1 = (bf16[256,4096]{1,0:T(8,128)(2,1)}, bf16[256,4096]{1,0:T(8,128)(2,1)}, u32[]{:S(2)}, u32[]{:S(2)}) collective-permute-start(bf16[256,4096]{1,0:T(8,128)(2,1)} %collective-permute-done), channel_id=1, source_target_pairs={{0,8},{8,16},{16,24},{24,0},{1,9},{9,17},{17,25},{25,1},{2,10},{10... | collective-permute-start | bytes 6291464 | tf_op jit(solution)/shard_map/ppermute | solution.py:98
  279.1 1.1 iota_compare_fusion.2
  280.3 1.5 collective-permute-start.7
  282.3 36.0 %collective-permute-done.1 = bf16[256,4096]{1,0:T(8,128)(2,1)} collective-permute-done((bf16[256,4096]{1,0:T(8,128)(2,1)}, bf16[256,4096]{1,0:T(8,128)(2,1)}, u32[]{:S(2)}, u32[]{:S(2)}) %collective-permute-start.1) | collective-permute-done | bytes 2097184 | tf_op jit(solution)/shard_map/ppermute | solution.py:98
  318.3 1.5 collective-permute-start.8
  319.9 4.5 mini-gather-slice.5
  324.4 11.5 %fusion.164 = (bf16[4,4,512,512]{3,2,1,0:T(8,128)(2,1)}, bf16[4,4,512,512]{3,2,1,0:T(8,128)(2,1)}) fusion(bf16[4,4,512,1280]{3,2,1,0:T(8,128)(2,1)} %bitcast.251), kind=kLoop, calls=%fused_computation.283 | loop fusion | bytes 33554432 | tf_op jit(solution)/shard_map/jit(_take)/gather | solution.py:116
  335.8 4.0 broadcast.681.clone
  339.9 17.7 %while.3 = (s32[]{:T(128)}, bf16[4,4,512,512]{3,2,1,0:T(8,128)(2,1)}, s32[4,1]{0,1:T(1,128)S(1)}, bf16[4,4,512,512]{3,2,1,0:T(8,128)(2,1)}, s32[]{:T(128)}) while((s32[]{:T(128)}, bf16[4,4,512,512]{3,2,1,0:T(8,128)(2,1)}, s32[4,1]{0,1:T(1,128)S(1)}, bf16[4,4,512,512]{3,2,1,0:T(8,128)(2,1)}, s32[]{:T(128)}) %tuple.52), condition=%wide.while_cond.1, body=%wide.while_body.1.sunk | while | flops 2 | bytes 4194901 | solution.py:116
  340.5 3.7 bitcast_dynamic-update-slice_fusion.5
  344.9 3.8 bitcast_dynamic-update-slice_fusion.5
  349.3 3.8 bitcast_dynamic-update-slice_fusion.5
  353.8 3.7 bitcast_dynamic-update-slice_fusion.5
  357.5 4.2 broadcast.681.clone.1
  361.7 17.7 %while.2 = (s32[]{:T(128)}, bf16[4,4,512,512]{3,2,1,0:T(8,128)(2,1)}, s32[4,1]{0,1:T(1,128)S(1)}, bf16[4,4,512,512]{3,2,1,0:T(8,128)(2,1)}, s32[]{:T(128)}) while((s32[]{:T(128)}, bf16[4,4,512,512]{3,2,1,0:T(8,128)(2,1)}, s32[4,1]{0,1:T(1,128)S(1)}, bf16[4,4,512,512]{3,2,1,0:T(8,128)(2,1)}, s32[]{:T(128)}) %tuple.62), condition=%wide.while_cond, body=%wide.while_body.sunk | while | flops 2 | bytes 4194901 | solution.py:116
  362.3 3.8 bitcast_dynamic-update-slice_fusion.4
  366.8 3.7 bitcast_dynamic-update-slice_fusion.4
  371.2 3.7 bitcast_dynamic-update-slice_fusion.4
  375.5 3.8 bitcast_dynamic-update-slice_fusion.4
  379.4 5.0 gather_fusion.1
  384.3 18.7 %maximum_select_fusion = bf16[4,4,512,1280]{3,2,0,1:T(8,128)(2,1)} fusion(bf16[4,4,512,256]{3,2,0,1:T(8,128)(2,1)} %bitcast.255, bf16[4,4,512,512]{3,2,0,1:T(8,128)(2,1)} %bitcast.249, bf16[4,4,512,512]{3,2,0,1:T(8,128)(2,1)} %bitcast.248, pred[4]{0:T(512)(128)(4,1)S(1)} %compare_and_fusion), kind=kLoop, calls=%fused_computation.43 | loop fusion | flops 73400320 | bytes 41943044 | tf_op jit(solution)/shard_map/jit(_take)/select_n | solution.py:116
  403.0 21.3 %fusion.38 = f32[1024,1280]{1,0:T(8,128)} fusion(bf16[2,4096,1280]{2,1,0:T(8,128)(2,1)} %bitcast.252, s32[]{:T(128)S(6)} %select_n.172, bf16[256,4096]{1,0:T(8,128)(2,1)} %collective-permute-done.2, bf16[256,4096]{1,0:T(8,128)(2,1)} %collective-permute-done.1, bf16[256,4096]{1,0:T(8,128)(2,1)} %collective-permute-done, bf16[256,4096]{1,0:T(8,128)(2,1)} %param.9), kind=kOutput, calls=%fused_computation.68 | convolution fusion | flops 10770972672 | bytes 24117252 | tf_op jit(solution)/shard_map/dot_general | solution.py:125
  424.4 22.5 %fusion.72 = f32[1024,1280]{1,0:T(8,128)} fusion(f32[1024,1280]{1,0:T(8,128)} %fusion.38, bf16[2,4096,1280]{2,1,0:T(8,128)(2,1)} %bitcast.253, s32[]{:T(128)S(6)} %select_n.173, bf16[256,4096]{1,0:T(8,128)(2,1)} %collective-permute-done.9, bf16[256,4096]{1,0:T(8,128)(2,1)} %collective-permute-done.8, bf16[256,4096]{1,0:T(8,128)(2,1)} %collective-permute-done.7, ...), kind=kOutput, calls=%fused_computation.111 | convolution fusion | flops 10772283392 | bytes 29360132 | tf_op jit(solution)/shard_map/dot_general | solution.py:125
  446.8 1.1 slice.230
  447.9 3.8 multiply_cosine_fusion
  454.7 1.4 iota_compare_fusion.1
  456.8 2.5 slice_bitcast_fusion
  459.3 1.0 copy.77
  460.3 2.0 subtract_convert_fusion
  462.3 1.2 pad_maximum_fusion.2
  463.4 2.1 gather_fusion
  465.6 1.9 copy_select_fusion
  467.5 9.7 %all-gather.7.cloned.1.call-done = bf16[4096,2,128]{2,0,1:T(8,128)(2,1)} async-done(((bf16[1024,2,128]{2,0,1:T(8,128)(2,1)}), bf16[4096,2,128]{2,0,1:T(8,128)(2,1)}) %all-gather.7.cloned.1.call-update) | async-done | bytes 2097168 | tf_op jit(solution)/shard_map/all_gather | solution.py:143
  477.2 1.7 copy.53
  478.9 1.3 copy-done
  480.2 8.1 %fusion.89 = f32[2048,256,8]{1,0,2:T(8,128)} fusion(bf16[4,256,8,128]{3,1,2,0:T(8,128)(2,1)S(1)} %copy_select_fusion, bf16[4096,2,128]{2,0,1:T(8,128)(2,1)S(1)} %bitcast.260), kind=kOutput, calls=%fused_computation.141 | convolution fusion | flops 1073741824 | bytes 17825792 | tf_op jit(solution)/shard_map/qhe,ke->hqk/dot_general | solution.py:159
  488.3 16.9 %fusion.165 = (f32[8,256]{1,0:T(8,128)S(1)}, bf16[8,256,4096]{1,2,0:T(8,128)(2,1)}) fusion(pred[256,4096]{0,1:T(8,128)(4,1)S(1)} %iota_compare_fusion, bf16[4096,2,128]{2,0,1:T(8,128)(2,1)} %bitcast.261, bf16[4,256,8,128]{3,1,2,0:T(8,128)(2,1)S(1)} %copy_select_fusion), kind=kOutput, calls=%fused_computation.284 | convolution fusion | flops 4353691648 | bytes 22028288 | tf_op jit(solution)/shard_map/sub | solution.py:169
  505.2 13.8 %fusion.166 = (f32[8,256]{1,0:T(8,128)S(1)}, bf16[8,256,3072]{1,2,0:T(8,128)(2,1)}) fusion(pred[256,3072]{0,1:T(8,128)(4,1)} %iota_compare_fusion.1, bf16[4096,2,128]{2,0,1:T(8,128)(2,1)} %bitcast.262, bf16[4,256,8,128]{3,1,2,0:T(8,128)(2,1)S(1)} %copy_select_fusion), kind=kOutput, calls=%fused_computation.285 | convolution fusion | flops 3265268736 | bytes 16785408 | tf_op jit(solution)/shard_map/sub | solution.py:169
  519.0 16.8 %fusion.167 = (f32[8,256]{1,0:T(8,128)S(1)}, bf16[8,256,2048]{1,2,0:T(8,128)(2,1)}) fusion(f32[2048,256,8]{1,0,2:T(8,128)} %fusion.89, pred[256,2048]{0,1:T(8,128)(4,1)S(1)} %copy-done.2), kind=kOutput, calls=%fused_computation.286 | output fusion | flops 29362176 | bytes 25698304 | tf_op jit(solution)/shard_map/sub | solution.py:169
  535.8 6.4 fusion.168
  542.2 16.9 %divide_convert_fusion = bf16[256,8,128]{0,2,1:T(8,128)(2,1)S(1)} fusion(bf16[4096,2,128]{2,0,1:T(8,128)(2,1)} %bitcast.264, bf16[8,256,4096]{1,2,0:T(8,128)(2,1)} %get-tuple-element.63, s32[4096]{0:T(1024)S(1)} %iota_multiply_fusion, s32[8,256]{1,0:T(8,128)S(1)} %copy-done.9, f32[256,8]{0,1:T(8,128)S(1)} %multiply_bitcast_fusion), kind=kOutput, calls=%fused_computation.126 | convolution fusion | flops 2248671232 | bytes 18382848 | tf_op jit(solution)/shard_map/hqk,ke->hqe/dot_general | solution.py:175
  559.2 13.3 %divide_convert_fusion.1 = bf16[256,8,128]{0,2,1:T(8,128)(2,1)S(1)} fusion(bf16[8,256,3072]{1,2,0:T(8,128)(2,1)} %get-tuple-element.65, s32[3072]{0:T(1024)S(1)} %copy-done.4, s32[8,256]{1,0:T(8,128)S(1)} %copy-done.8, bf16[4096,2,128]{2,0,1:T(8,128)(2,1)S(1)} %bitcast.265, f32[256,8]{0,1:T(8,128)S(1)} %multiply_bitcast_fusion.1), kind=kOutput, calls=%fused_computation.127 | convolution fusion | flops 1686634496 | bytes 13922304 | tf_op jit(solution)/shard_map/hqk,ke->hqe/dot_general | solution.py:175
  572.5 6.7 %divide_convert_fusion.2 = bf16[256,8,128]{0,2,1:T(8,128)(2,1)S(1)} fusion(bf16[8,256,2048]{1,2,0:T(8,128)(2,1)S(1)} %copy-done.11, s32[2048]{0:T(1024)S(1)} %copy-done.5, s32[8,256]{1,0:T(8,128)S(1)} %copy-done.7, bf16[4096,2,128]{2,0,1:T(8,128)(2,1)S(1)} %bitcast.266, f32[256,8]{0,1:T(8,128)S(1)} %multiply_bitcast_fusion.2), kind=kOutput, calls=%fused_computation.128 | convolution fusion | flops 1124597760 | bytes 9461760 | tf_op jit(solution)/shard_map/hqk,ke->hqe/dot_general | solution.py:175
  579.3 3.5 divide_convert_fusion.3
  583.1 53.0 %all_to_all.15 = bf16[4,256,1024]{1,2,0:T(8,128)(2,1)S(1)} all-to-all(bf16[4,256,1024]{1,2,0:T(8,128)(2,1)S(1)} %pad_maximum_fusion.3), channel_id=1, replica_groups=mesh['cg'=4,'ct'=4,'fsdp'=2] {'cg'}, dimensions={0} | all-to-all | bytes 4194304 | tf_op jit(solution)/shard_map/all_to_all | solution.py:181
  636.1 2.8 copy.76
  (75 shorter events, 13.3 us)
Async XLA Ops:
  6.5 313.3 %all-gather.5.cloned.1.call-start = ((), (), s32[]{:S(2)}) async-start(), calls=%async_computation.1 | async-start | bytes 26214400 | tf_op jit(solution)/shard_map/all_gather | solution.py:115
  6.5 48.9 %collective-permute-start.3 = (bf16[256,4096]{1,0:T(8,128)(2,1)}, bf16[256,4096]{1,0:T(8,128)(2,1)}, u32[]{:S(2)}, u32[]{:S(2)}) collective-permute-start(bf16[256,4096]{1,0:T(8,128)(2,1)} %param.9), channel_id=1, source_target_pairs={{0,1},{1,0},{2,3},{3,2},{4,5},{5,4},{6,7},{7,6},{8,9},{9,8},{10,11... | collective-permute-start | bytes 6291464 | tf_op jit(solution)/shard_map/ppermute | solution.py:81
  59.9 33.5 %collective-permute-start.6 = (bf16[512,1280]{1,0:T(8,128)(2,1)}, bf16[512,1280]{1,0:T(8,128)(2,1)}, u32[]{:S(2)}, u32[]{:S(2)}) collective-permute-start(bf16[512,1280]{1,0:T(8,128)(2,1)} %bitcast.271), channel_id=1, source_target_pairs={{0,24},{8,0},{16,8},{24,16},{1,25},{9,1},{17,9},{25,17},{2,26},{10... | collective-permute-start | bytes 3932168 | tf_op jit(solution)/shard_map/ppermute | solution.py:87
  66.1 109.2 %collective-permute-start.5 = (bf16[512,1280]{1,0:T(8,128)(2,1)}, bf16[512,1280]{1,0:T(8,128)(2,1)}, u32[]{:S(2)}, u32[]{:S(2)}) collective-permute-start(bf16[512,1280]{1,0:T(8,128)(2,1)} %bitcast.272), channel_id=1, source_target_pairs={{0,16},{8,24},{16,0},{24,8},{1,17},{9,25},{17,1},{25,9},{2,18},{10... | collective-permute-start | bytes 3932168 | tf_op jit(solution)/shard_map/ppermute | solution.py:87
  67.6 107.8 %collective-permute-start.4 = (bf16[512,1280]{1,0:T(8,128)(2,1)}, bf16[512,1280]{1,0:T(8,128)(2,1)}, u32[]{:S(2)}, u32[]{:S(2)}) collective-permute-start(bf16[512,1280]{1,0:T(8,128)(2,1)} %bitcast.273), channel_id=1, source_target_pairs={{0,8},{8,16},{16,24},{24,0},{1,9},{9,17},{17,25},{25,1},{2,10},{10... | collective-permute-start | bytes 3932168 | tf_op jit(solution)/shard_map/ppermute | solution.py:87
  180.6 296.6 %all-gather.7.cloned.1.call-start = ((), (), s32[]{:S(2)}) async-start(), calls=%async_computation.2 | async-start | bytes 2621440 | tf_op jit(solution)/shard_map/all_gather | solution.py:143
  180.7 50.8 %collective-permute-start = (bf16[256,4096]{1,0:T(8,128)(2,1)}, bf16[256,4096]{1,0:T(8,128)(2,1)}, u32[]{:S(2)}, u32[]{:S(2)}) collective-permute-start(bf16[256,4096]{1,0:T(8,128)(2,1)} %param.9), channel_id=1, source_target_pairs={{0,8},{8,16},{16,24},{24,0},{1,9},{9,17},{17,25},{25,1},{2,10},{10... | collective-permute-start | bytes 6291464 | tf_op jit(solution)/shard_map/ppermute | solution.py:96
  182.3 99.5 %collective-permute-start.2 = (bf16[256,4096]{1,0:T(8,128)(2,1)}, bf16[256,4096]{1,0:T(8,128)(2,1)}, u32[]{:S(2)}, u32[]{:S(2)}) collective-permute-start(bf16[256,4096]{1,0:T(8,128)(2,1)} %param.9), channel_id=1, source_target_pairs={{0,24},{8,0},{16,8},{24,16},{1,25},{9,1},{17,9},{25,17},{2,26},{10... | collective-permute-start | bytes 6291464 | tf_op jit(solution)/shard_map/ppermute | solution.py:97
  231.4 86.9 %collective-permute-start.1 = (bf16[256,4096]{1,0:T(8,128)(2,1)}, bf16[256,4096]{1,0:T(8,128)(2,1)}, u32[]{:S(2)}, u32[]{:S(2)}) collective-permute-start(bf16[256,4096]{1,0:T(8,128)(2,1)} %collective-permute-done), channel_id=1, source_target_pairs={{0,8},{8,16},{16,24},{24,0},{1,9},{9,17},{17,25},{25,1},{2,10},{10... | collective-permute-start | bytes 6291464 | tf_op jit(solution)/shard_map/ppermute | solution.py:98
  280.3 144.1 %collective-permute-start.7 = (bf16[256,4096]{1,0:T(8,128)(2,1)}, bf16[256,4096]{1,0:T(8,128)(2,1)}, u32[]{:S(2)}, u32[]{:S(2)}) collective-permute-start(bf16[256,4096]{1,0:T(8,128)(2,1)} %collective-permute-done), channel_id=1, source_target_pairs={{0,1},{1,0},{2,3},{3,2},{4,5},{5,4},{6,7},{7,6},{8,9},{9,8},{10,11... | collective-permute-start | bytes 6291464 | tf_op jit(solution)/shard_map/ppermute | solution.py:104
  281.8 142.5 %collective-permute-start.9 = (bf16[256,4096]{1,0:T(8,128)(2,1)}, bf16[256,4096]{1,0:T(8,128)(2,1)}, u32[]{:S(2)}, u32[]{:S(2)}) collective-permute-start(bf16[256,4096]{1,0:T(8,128)(2,1)} %collective-permute-done.2), channel_id=1, source_target_pairs={{0,1},{1,0},{2,3},{3,2},{4,5},{5,4},{6,7},{7,6},{8,9},{9,8},{10,11... | collective-permute-start | bytes 6291464 | tf_op jit(solution)/shard_map/ppermute | solution.py:104
  318.3 106.0 %collective-permute-start.8 = (bf16[256,4096]{1,0:T(8,128)(2,1)}, bf16[256,4096]{1,0:T(8,128)(2,1)}, u32[]{:S(2)}, u32[]{:S(2)}) collective-permute-start(bf16[256,4096]{1,0:T(8,128)(2,1)} %collective-permute-done.1), channel_id=1, source_target_pairs={{0,1},{1,0},{2,3},{3,2},{4,5},{5,4},{6,7},{7,6},{8,9},{9,8},{10,11... | collective-permute-start | bytes 6291464 | tf_op jit(solution)/shard_map/ppermute | solution.py:104
  478.9 1.3 copy-start
  505.2 13.8 %copy-start.2 = (pred[256,2048]{0,1:T(8,128)(4,1)S(1)}, pred[256,2048]{0,1:T(8,128)(4,1)}, u32[]{:S(2)}) copy-start(pred[256,2048]{0,1:T(8,128)(4,1)} %iota_compare_fusion.2) | copy-start | bytes 1572868
  519.0 16.8 %copy-start.3 = (pred[256,1024]{0,1:T(8,128)(4,1)S(1)}, pred[256,1024]{0,1:T(8,128)(4,1)}, u32[]{:S(2)}) copy-start(pred[256,1024]{0,1:T(8,128)(4,1)} %iota_compare_fusion.3) | copy-start | bytes 786436
  535.8 6.4 copy-start.9
  542.2 16.9 %copy-start.1 = (bf16[4,4,256,2,128]{4,2,1,0,3:T(8,128)(2,1)S(1)}, bf16[4,4,256,2,128]{4,2,1,0,3:T(8,128)(2,1)}, u32[]{:S(2)}) copy-start(bf16[4,4,256,2,128]{4,2,1,0,3:T(8,128)(2,1)} %copy-done) | copy-start | bytes 6291460
  542.2 16.9 %copy-start.4 = (s32[3072]{0:T(1024)S(1)}, s32[3072]{0:T(1024)}, u32[]{:S(2)}) copy-start(s32[3072]{0:T(1024)} %iota_multiply_fusion.1) | copy-start | bytes 36868
  542.2 16.9 %copy-start.8 = (s32[8,256]{1,0:T(8,128)S(1)}, s32[8,256]{1,0:T(8,128)}, u32[]{:S(2)}) copy-start(s32[8,256]{1,0:T(8,128)} %get-tuple-element.58) | copy-start | bytes 24580
  559.2 13.3 %copy-start.5 = (s32[2048]{0:T(1024)S(1)}, s32[2048]{0:T(1024)}, u32[]{:S(2)}) copy-start(s32[2048]{0:T(1024)} %iota_multiply_fusion.2) | copy-start | bytes 24580
  559.2 13.3 %copy-start.7 = (s32[8,256]{1,0:T(8,128)S(1)}, s32[8,256]{1,0:T(8,128)}, u32[]{:S(2)}) copy-start(s32[8,256]{1,0:T(8,128)} %get-tuple-element.57) | copy-start | bytes 24580
  559.2 13.3 %copy-start.11 = (bf16[8,256,2048]{1,2,0:T(8,128)(2,1)S(1)}, bf16[8,256,2048]{1,2,0:T(8,128)(2,1)}, u32[]{:S(2)}) copy-start(bf16[8,256,2048]{1,2,0:T(8,128)(2,1)} %get-tuple-element.67) | copy-start | bytes 25165828
  572.5 6.8 %copy-start.6 = (s32[8,256]{1,0:T(8,128)S(1)}, s32[8,256]{1,0:T(8,128)}, u32[]{:S(2)}) copy-start(s32[8,256]{1,0:T(8,128)} %get-tuple-element.56) | copy-start | bytes 24580
  572.5 6.8 %copy-start.10 = (s32[1024]{0:T(1024)S(1)}, s32[1024]{0:T(1024)}, u32[]{:S(2)}) copy-start(s32[1024]{0:T(1024)} %iota_multiply_fusion.3) | copy-start | bytes 12292
  572.5 6.8 %copy-start.12 = (bf16[8,256,1024]{1,2,0:T(8,128)(2,1)S(1)}, bf16[8,256,1024]{1,2,0:T(8,128)(2,1)}, u32[]{:S(2)}) copy-start(bf16[8,256,1024]{1,2,0:T(8,128)(2,1)} %get-tuple-element.69) | copy-start | bytes 12582916
Sparse Core Ops, SparseCore 0:
  180.7 132.7 all-gather.4
  454.2 22.9 all-gather.6

commit v14 on v13

--- a/solution.py
+++ b/solution.py
@@ -87,6 +87,7 @@
         received.append(lax.ppermute(outgoing, "cg", perm))
     by_shift = jnp.stack(received, axis=0)
     back = (g - jnp.arange(n_g, dtype=jnp.int32)) % n_g
+    mine = jnp.take(by_shift, back, axis=0)
     if lax.axis_size("fsdp") == 2:
         pieces = []
         halves = [activations]
@@ -112,18 +113,17 @@
         grp_rows = lax.all_gather(jnp.concatenate(own_half, axis=0), "fsdp", axis=1, tiled=True)
         split_rows = None
 
-    every = lax.all_gather(by_shift, "ct", axis=0, tiled=False)
-    every = jnp.take(every, back, axis=1).transpose(1, 0, 2, 3)
-    every = every.reshape(n_g * n_t * d_rows, qcols + 2 * HD)
+    every = lax.all_gather(mine, "ct", axis=0, tiled=False)
+    every = every.transpose(1, 0, 2, 3).reshape(n_g * n_t * d_rows, qcols + 2 * HD)
 
     if split_rows is None:
         mixed = jnp.dot(grp_rows, every, preferred_element_type=jnp.float32)
     else:
-        halves_w = every.reshape(2, every.shape[0] // 2, every.shape[1])
-        mine_w = lax.dynamic_index_in_dim(halves_w, f, 0, keepdims=False)
-        other_w = lax.dynamic_index_in_dim(halves_w, 1 - f, 0, keepdims=False)
-        mixed = jnp.dot(split_rows[0], mine_w, preferred_element_type=jnp.float32) + jnp.dot(
-            split_rows[1], other_w, preferred_element_type=jnp.float32
+        half = every.shape[0] // 2
+        low_rows = jnp.where(f == 0, split_rows[0], split_rows[1])
+        high_rows = jnp.where(f == 0, split_rows[1], split_rows[0])
+        mixed = jnp.dot(low_rows, every[:half], preferred_element_type=jnp.float32) + jnp.dot(
+            high_rows, every[half:], preferred_element_type=jnp.float32
         )
     shift_of_row = jnp.arange(rows, dtype=jnp.int32) // tok
     chunk_of_row = n_t * ((g - shift_of_row) % n_g) + t

time: 652 us -> 716 us (1.098)
  waiting for transfers between devices: 229 us -> 327 us
  local copies, waits for them, and re-layouts: 96.2 us -> 63.8 us
  starting transfers between devices: 60 us -> 85.1 us
  other arithmetic: 62.9 us -> 49.4 us
  matrix products: 129 us -> 116 us
    ppermute x3, waiting for transfers between devices: 0.01 us -> 77.4 us  [shards(): lax.ppermute(half, 'fsdp', [(0, 1), (1, 0)])]
    ppermute x1, starting transfers between devices: 1.66 us -> 71 us  [shards(): from_left = lax.ppermute(activations, 'cg', right)]
    gather x19 -> x1, local copies, waits for them, and re-layouts: 56.3 us -> 5.65 us  [shards(): mine = jnp.take(by_shift, back, axis=0)]
    ppermute x1, waiting for transfers between devices: 36 us -> 78.4 us  [shards(): halves += [from_left, lax.ppermute(from_left, 'cg', right), from_right]]
    ppermute x1, starting transfers between devices: 44.7 us -> 2.74 us  [shards(): halves += [from_left, lax.ppermute(from_left, 'cg', right), from_right]]
    ppermute x3, waiting for transfers between devices: 106 us -> 80.7 us  [shards(): received.append(lax.ppermute(outgoing, 'cg', perm))]
    select_n x3 -> x2, other arithmetic: 18.7 us -> 5.49 us  [shards(): mine = jnp.take(by_shift, back, axis=0)]
    all_gather x0 -> x1, local copies, waits for them, and re-layouts: none -> 10.1 us  [shards(): every = lax.all_gather(mine, 'ct', axis=0, tiled=False)]
  transfers between devices with their start and end apart: 12 -> 12, of which waited for: 6 -> 8; matrix products, arithmetic and copies ran while one was open for 22% -> 6% of each run, Pallas kernels for 0% -> 0%
where the time goes in v14:
time: 716 us; the launch traced here: 711 us
  waiting for transfers between devices  327 us (46%)
  matrix products  116 us (16%)
  starting transfers between devices  85.1 us (12%)
  local copies, waits for them, and re-layouts  63.8 us (9%)
  blocking collectives  53 us (7%)
  other arithmetic  49.4 us (7%)
  between operations  16.4 us (2%)
    ppermute x3, waiting for transfers between devices, shards(): received.append(lax.ppermute(outgoing, 'cg', perm))  80.7 us
    ppermute x1, waiting for transfers between devices, shards(): halves += [from_left, lax.ppermute(from_left, 'cg', right), from_right]  78.4 us
    ppermute x3, waiting for transfers between devices, shards(): lax.ppermute(half, 'fsdp', [(0, 1), (1, 0)])  77.4 us
    ppermute x1, starting transfers between devices, shards(): from_left = lax.ppermute(activations, 'cg', right)  71 us
    all_to_all x1, blocking collectives, shards(): lax.all_to_all(out_rows, 'cg', split_axis=0, concat_axis=2, tiled=True)  53 us
    ppermute x1, waiting for transfers between devices, shards(): from_left = lax.ppermute(activations, 'cg', right)  46.1 us
    sub x3, matrix products, shards(): weights = jnp.where(visible, jnp.exp(scores - highest), 0.0)  37.4 us
    dot_general x4, matrix products, shards(): jnp.einsum('hqk,ke->hqe', dropped, all_values[:span], preferred_element_t...  36.4 us
  transfers between devices with their start and end apart: 12, of which 8 were waited for; matrix products, arithmetic and copies ran while one was open for 6% of the time, Pallas kernels for 0%

profile of v14, /device:TPU:0, one launch (start us, length us, event | category | flops | bytes accessed | tf_op | source)
XLA Modules:
  0.0 710.5 jit_solution(17651858658041938238)
XLA Ops:
  6.5 3.0 collective-permute-start.3
  9.5 6.5 copy.50
  16.4 5.2 pad_maximum_fusion
  21.7 33.8 %collective-permute-done.3 = bf16[256,4096]{1,0:T(8,128)(2,1)} collective-permute-done((bf16[256,4096]{1,0:T(8,128)(2,1)}, bf16[256,4096]{1,0:T(8,128)(2,1)}, u32[]{:S(2)}, u32[]{:S(2)}) %collective-permute-start.3) | collective-permute-done | bytes 2097184 | tf_op jit(solution)/shard_map/ppermute | solution.py:81
  55.5 2.0 constant_dynamic-slice_fusion.3
  57.4 2.5 copy.55
  59.9 2.8 collective-permute-start.8
  62.7 2.4 copy.56
  65.2 1.3 collective-permute-start.9
  66.5 1.4 copy.54
  68.0 0.7 collective-permute-start.7
  68.7 0.6 copy.53
  69.3 79.1 %collective-permute-done.8 = bf16[512,1280]{1,0:T(8,128)(2,1)} collective-permute-done((bf16[512,1280]{1,0:T(8,128)(2,1)}, bf16[512,1280]{1,0:T(8,128)(2,1)}, u32[]{:S(2)}, u32[]{:S(2)}) %collective-permute-start.8) | collective-permute-done | bytes 1310752 | tf_op jit(solution)/shard_map/ppermute | solution.py:87
  148.4 1.6 collective-permute-done.9
  150.0 5.2 pad_maximum_fusion.1
  155.2 5.7 gather_fusion
  160.9 5.5 bitcast_select_fusion.16
  166.4 71.0 %collective-permute-start = (bf16[256,4096]{1,0:T(8,128)(2,1)S(1)}, bf16[256,4096]{1,0:T(8,128)(2,1)}, u32[]{:S(2)}, u32[]{:S(2)}) collective-permute-start(bf16[256,4096]{1,0:T(8,128)(2,1)S(1)} %copy-done.2), channel_id=1, source_target_pairs={{0,8},{8,16},{16,24},{24,0},{1,9},{9,17},{17,25},{25,1},{2,10},{10... | collective-permute-start | bytes 6291464 | tf_op jit(solution)/shard_map/ppermute | solution.py:97
  237.4 46.1 %collective-permute-done = bf16[256,4096]{1,0:T(8,128)(2,1)} collective-permute-done((bf16[256,4096]{1,0:T(8,128)(2,1)S(1)}, bf16[256,4096]{1,0:T(8,128)(2,1)}, u32[]{:S(2)}, u32[]{:S(2)}) %collective-permute-start) | collective-permute-done | bytes 2097184 | tf_op jit(solution)/shard_map/ppermute | solution.py:97
  283.5 2.7 collective-permute-start.1
  289.4 0.7 shift-right-logical_xor_fusion.21
  290.3 1.1 iota_compare_fusion.2
  291.6 1.5 collective-permute-start.4
  293.1 78.4 %collective-permute-done.1 = bf16[256,4096]{1,0:T(8,128)(2,1)} collective-permute-done((bf16[256,4096]{1,0:T(8,128)(2,1)}, bf16[256,4096]{1,0:T(8,128)(2,1)}, u32[]{:S(2)}, u32[]{:S(2)}) %collective-permute-start.1) | collective-permute-done | bytes 2097184 | tf_op jit(solution)/shard_map/ppermute | solution.py:99
  371.5 1.3 collective-permute-start.5
  372.8 3.1 constant_dynamic-update-slice_fusion.7
  376.0 0.7 collective-permute-start.6
  376.7 1.7 constant_dynamic-update-slice_fusion.2
  378.4 1.7 constant_dynamic-update-slice_fusion.1
  380.1 1.7 constant_dynamic-update-slice_fusion
  381.9 1.6 constant_dynamic-update-slice_fusion.6
  383.4 36.9 %collective-permute-done.5 = bf16[256,4096]{1,0:T(8,128)(2,1)S(1)} collective-permute-done((bf16[256,4096]{1,0:T(8,128)(2,1)}, bf16[256,4096]{1,0:T(8,128)(2,1)S(1)}, u32[]{:S(2)}, u32[]{:S(2)}) %collective-permute-start.5) | collective-permute-done | bytes 2097184 | tf_op jit(solution)/shard_map/ppermute | solution.py:105
  420.3 1.4 constant_dynamic-update-slice_fusion.5
  421.7 40.6 %collective-permute-done.6 = bf16[256,4096]{1,0:T(8,128)(2,1)S(1)} collective-permute-done((bf16[256,4096]{1,0:T(8,128)(2,1)}, bf16[256,4096]{1,0:T(8,128)(2,1)S(1)}, u32[]{:S(2)}, u32[]{:S(2)}) %collective-permute-start.6) | collective-permute-done | bytes 2097184 | tf_op jit(solution)/shard_map/ppermute | solution.py:105
  462.3 1.5 constant_dynamic-update-slice_fusion.4
  463.8 10.1 %copy.85 = bf16[4,4,512,1280]{3,2,0,1:T(8,128)(2,1)S(1)} copy(bf16[4,4,512,1280]{3,2,1,0:T(8,128)(2,1)} %all-gather.4.cloned.1.call-done) | data formatting | bytes 41943040 | tf_op jit(solution)/shard_map/all_gather | solution.py:116
  473.9 5.4 fusion.144
  479.4 18.2 %fusion.44 = f32[1024,1280]{1,0:T(8,128)} fusion(bf16[4096,1280]{1,0:T(8,128)(2,1)} %bitcast.231, bf16[1024,4096]{1,0:T(8,128)(2,1)} %constant_dynamic-update-slice_fusion.4, bf16[1024,4096]{1,0:T(8,128)(2,1)} %copy-done.3, pred[]{:T(512)S(6)} %eq.13), kind=kOutput, calls=%fused_computation.73 | convolution fusion | flops 10741612544 | bytes 32505856 | tf_op jit(solution)/shard_map/dot_general | solution.py:125
  497.6 16.1 %fusion.54 = f32[1024,1280]{1,0:T(8,128)} fusion(f32[1024,1280]{1,0:T(8,128)} %fusion.44, bf16[4096,1280]{1,0:T(8,128)(2,1)S(1)} %bitcast.230, bf16[1024,4096]{1,0:T(8,128)(2,1)} %copy-done.3, bf16[1024,4096]{1,0:T(8,128)(2,1)} %constant_dynamic-update-slice_fusion.4, pred[]{:T(512)S(6)} %eq.13), kind=kOutput, calls=%fused_computation.86 | convolution fusion | flops 10742923264 | bytes 37748736 | tf_op jit(solution)/shard_map/dot_general | solution.py:125
  513.7 1.1 slice.226
  514.8 4.0 multiply_cosine_fusion
  520.3 0.9 pad_maximum_fusion.4
  521.8 1.4 iota_compare_fusion.1
  523.2 0.7 iota_compare_fusion
  523.9 2.5 slice_bitcast_fusion
  526.4 1.0 copy.82
  527.4 1.8 subtract_convert_fusion
  529.2 1.2 pad_maximum_fusion.2
  530.4 2.1 gather_fusion.1
  532.5 1.9 copy_select_fusion
  534.4 10.2 %all-gather.6.cloned.1.call-done = bf16[4096,2,128]{2,0,1:T(8,128)(2,1)} async-done(((bf16[1024,2,128]{2,0,1:T(8,128)(2,1)}), bf16[4096,2,128]{2,0,1:T(8,128)(2,1)}) %all-gather.6.cloned.1.call-update) | async-done | bytes 2097168 | tf_op jit(solution)/shard_map/all_gather | solution.py:143
  544.6 1.7 copy.58
  546.4 1.3 copy-done
  547.7 8.1 %fusion.73 = f32[2048,256,8]{1,0,2:T(8,128)} fusion(bf16[4,256,8,128]{3,1,2,0:T(8,128)(2,1)S(1)} %copy_select_fusion, bf16[4096,2,128]{2,0,1:T(8,128)(2,1)S(1)} %bitcast.236), kind=kOutput, calls=%fused_computation.124 | convolution fusion | flops 1073741824 | bytes 17825792 | tf_op jit(solution)/shard_map/qhe,ke->hqk/dot_general | solution.py:159
  555.8 6.5 fusion.148
  562.3 17.2 %fusion.147 = (f32[8,256]{1,0:T(8,128)S(1)}, bf16[8,256,2048]{1,2,0:T(8,128)(2,1)}) fusion(f32[2048,256,8]{1,0,2:T(8,128)} %fusion.73, pred[256,2048]{0,1:T(8,128)(4,1)} %iota_compare_fusion.2), kind=kOutput, calls=%fused_computation.273 | output fusion | flops 29362176 | bytes 25698304 | tf_op jit(solution)/shard_map/sub | solution.py:169
  579.4 13.9 %fusion.146 = (f32[8,256]{1,0:T(8,128)S(1)}, bf16[8,256,3072]{1,2,0:T(8,128)(2,1)}) fusion(pred[256,3072]{0,1:T(8,128)(4,1)} %iota_compare_fusion.1, bf16[4096,2,128]{2,0,1:T(8,128)(2,1)} %bitcast.238, bf16[4,256,8,128]{3,1,2,0:T(8,128)(2,1)S(1)} %copy_select_fusion), kind=kOutput, calls=%fused_computation.272 | convolution fusion | flops 3265268736 | bytes 16785408 | tf_op jit(solution)/shard_map/sub | solution.py:169
  593.3 17.0 %fusion.145 = (f32[8,256]{1,0:T(8,128)S(1)}, bf16[8,256,4096]{1,2,0:T(8,128)(2,1)}) fusion(pred[256,4096]{0,1:T(8,128)(4,1)S(1)} %iota_compare_fusion, bf16[4096,2,128]{2,0,1:T(8,128)(2,1)} %bitcast.239, bf16[4,256,8,128]{3,1,2,0:T(8,128)(2,1)S(1)} %copy_select_fusion), kind=kOutput, calls=%fused_computation.271 | convolution fusion | flops 4353691648 | bytes 22028288 | tf_op jit(solution)/shard_map/sub | solution.py:169
  610.5 5.8 divide_convert_fusion.3
  616.4 6.7 divide_convert_fusion.2
  623.3 10.2 %divide_convert_fusion.1 = bf16[256,8,128]{0,2,1:T(8,128)(2,1)S(1)} fusion(bf16[8,256,3072]{1,2,0:T(8,128)(2,1)S(1)} %bitcast.262, s32[3072]{0:T(1024)S(1)} %copy-done.7, s32[8,256]{1,0:T(8,128)S(1)} %copy-done.10, bf16[4096,2,128]{2,0,1:T(8,128)(2,1)S(1)} %bitcast.242, f32[256,8]{0,1:T(8,128)S(1)} %multiply_bitcast_fusion.1), kind=kOutput, calls=%fused_computation.110 | convolution fusion | flops 1686634496 | bytes 13922304 | tf_op jit(solution)/shard_map/hqk,ke->hqe/dot_general | solution.py:175
  633.6 13.6 %divide_convert_fusion = bf16[256,8,128]{0,2,1:T(8,128)(2,1)S(1)} fusion(bf16[4096,2,128]{2,0,1:T(8,128)(2,1)S(1)} %bitcast.243, bf16[8,256,4096]{1,2,0:T(8,128)(2,1)S(1)} %bitcast.260, s32[4096]{0:T(1024)S(1)} %copy-done.6, s32[8,256]{1,0:T(8,128)S(1)} %copy-done.9, f32[256,8]{0,1:T(8,128)S(1)} %multiply_bitcast_fusion), kind=kOutput, calls=%fused_computation.109 | convolution fusion | flops 2248671232 | bytes 18382848 | tf_op jit(solution)/shard_map/hqk,ke->hqe/dot_general | solution.py:175
  647.4 53.0 %all_to_all.15 = bf16[4,256,1024]{1,2,0:T(8,128)(2,1)S(1)} all-to-all(bf16[4,256,1024]{1,2,0:T(8,128)(2,1)S(1)} %pad_maximum_fusion.3), channel_id=1, replica_groups=mesh['cg'=4,'ct'=4,'fsdp'=2] {'cg'}, dimensions={0} | all-to-all | bytes 4194304 | tf_op jit(solution)/shard_map/all_to_all | solution.py:181
  700.4 2.8 copy.81
  (80 shorter events, 4.6 us)
Async XLA Ops:
  6.5 9.4 %copy-start.4 = (bf16[512,512]{1,0:T(8,128)(2,1)S(1)}, bf16[512,512]{1,0:T(8,128)(2,1)}, u32[]{:S(2)}) copy-start(bf16[512,512]{1,0:T(8,128)(2,1)} %param.11) | copy-start | bytes 1572868
  6.5 9.7 %copy-start.5 = (bf16[512,512]{1,0:T(8,128)(2,1)S(1)}, bf16[512,512]{1,0:T(8,128)(2,1)}, u32[]{:S(2)}) copy-start(bf16[512,512]{1,0:T(8,128)(2,1)} %param.12) | copy-start | bytes 1572868
  6.5 457.3 %all-gather.4.cloned.1.call-start = ((), (), s32[]{:S(2)}) async-start(), calls=%async_computation.1 | async-start | bytes 26214400 | tf_op jit(solution)/shard_map/all_gather | solution.py:116
  6.5 48.9 %collective-permute-start.3 = (bf16[256,4096]{1,0:T(8,128)(2,1)}, bf16[256,4096]{1,0:T(8,128)(2,1)}, u32[]{:S(2)}, u32[]{:S(2)}) collective-permute-start(bf16[256,4096]{1,0:T(8,128)(2,1)} %param.9), channel_id=1, source_target_pairs={{0,1},{1,0},{2,3},{3,2},{4,5},{5,4},{6,7},{7,6},{8,9},{9,8},{10,11... | collective-permute-start | bytes 6291464 | tf_op jit(solution)/shard_map/ppermute | solution.py:81
  59.9 88.5 %collective-permute-start.8 = (bf16[512,1280]{1,0:T(8,128)(2,1)}, bf16[512,1280]{1,0:T(8,128)(2,1)}, u32[]{:S(2)}, u32[]{:S(2)}) collective-permute-start(bf16[512,1280]{1,0:T(8,128)(2,1)} %bitcast.247), channel_id=1, source_target_pairs={{0,16},{8,24},{16,0},{24,8},{1,17},{9,25},{17,1},{25,9},{2,18},{10... | collective-permute-start | bytes 3932168 | tf_op jit(solution)/shard_map/ppermute | solution.py:87
  65.2 84.8 %collective-permute-start.9 = (bf16[512,1280]{1,0:T(8,128)(2,1)}, bf16[512,1280]{1,0:T(8,128)(2,1)}, u32[]{:S(2)}, u32[]{:S(2)}) collective-permute-start(bf16[512,1280]{1,0:T(8,128)(2,1)} %bitcast.248), channel_id=1, source_target_pairs={{0,24},{8,0},{16,8},{24,16},{1,25},{9,1},{17,9},{25,17},{2,26},{10... | collective-permute-start | bytes 3932168 | tf_op jit(solution)/shard_map/ppermute | solution.py:87
  68.0 82.1 %collective-permute-start.7 = (bf16[512,1280]{1,0:T(8,128)(2,1)}, bf16[512,1280]{1,0:T(8,128)(2,1)}, u32[]{:S(2)}, u32[]{:S(2)}) collective-permute-start(bf16[512,1280]{1,0:T(8,128)(2,1)} %bitcast.249), channel_id=1, source_target_pairs={{0,8},{8,16},{16,24},{24,0},{1,9},{9,17},{17,25},{25,1},{2,10},{10... | collective-permute-start | bytes 3932168 | tf_op jit(solution)/shard_map/ppermute | solution.py:87
  160.9 5.6 copy-start.2
  166.4 378.3 %all-gather.6.cloned.1.call-start = ((), (), s32[]{:S(2)}) async-start(), calls=%async_computation.2 | async-start | bytes 2621440 | tf_op jit(solution)/shard_map/all_gather | solution.py:143
  166.4 117.0 %collective-permute-start = (bf16[256,4096]{1,0:T(8,128)(2,1)S(1)}, bf16[256,4096]{1,0:T(8,128)(2,1)}, u32[]{:S(2)}, u32[]{:S(2)}) collective-permute-start(bf16[256,4096]{1,0:T(8,128)(2,1)S(1)} %copy-done.2), channel_id=1, source_target_pairs={{0,8},{8,16},{16,24},{24,0},{1,9},{9,17},{17,25},{25,1},{2,10},{10... | collective-permute-start | bytes 6291464 | tf_op jit(solution)/shard_map/ppermute | solution.py:97
  237.4 138.6 %collective-permute-start.2 = (bf16[256,4096]{1,0:T(8,128)(2,1)S(1)}, bf16[256,4096]{1,0:T(8,128)(2,1)}, u32[]{:S(2)}, u32[]{:S(2)}) collective-permute-start(bf16[256,4096]{1,0:T(8,128)(2,1)S(1)} %copy-done.2), channel_id=1, source_target_pairs={{0,24},{8,0},{16,8},{24,16},{1,25},{9,1},{17,9},{25,17},{2,26},{10... | collective-permute-start | bytes 6291464 | tf_op jit(solution)/shard_map/ppermute | solution.py:98
  283.5 88.0 %collective-permute-start.1 = (bf16[256,4096]{1,0:T(8,128)(2,1)}, bf16[256,4096]{1,0:T(8,128)(2,1)}, u32[]{:S(2)}, u32[]{:S(2)}) collective-permute-start(bf16[256,4096]{1,0:T(8,128)(2,1)} %collective-permute-done), channel_id=1, source_target_pairs={{0,8},{8,16},{16,24},{24,0},{1,9},{9,17},{17,25},{25,1},{2,10},{10... | collective-permute-start | bytes 6291464 | tf_op jit(solution)/shard_map/ppermute | solution.py:99
  291.6 90.3 %collective-permute-start.4 = (bf16[256,4096]{1,0:T(8,128)(2,1)}, bf16[256,4096]{1,0:T(8,128)(2,1)S(1)}, u32[]{:S(2)}, u32[]{:S(2)}) collective-permute-start(bf16[256,4096]{1,0:T(8,128)(2,1)} %collective-permute-done), channel_id=1, source_target_pairs={{0,1},{1,0},{2,3},{3,2},{4,5},{5,4},{6,7},{7,6},{8,9},{9,8},{10,11... | collective-permute-start | bytes 6291464 | tf_op jit(solution)/shard_map/ppermute | solution.py:105
  371.5 48.8 %collective-permute-start.5 = (bf16[256,4096]{1,0:T(8,128)(2,1)}, bf16[256,4096]{1,0:T(8,128)(2,1)S(1)}, u32[]{:S(2)}, u32[]{:S(2)}) collective-permute-start(bf16[256,4096]{1,0:T(8,128)(2,1)} %collective-permute-done.1), channel_id=1, source_target_pairs={{0,1},{1,0},{2,3},{3,2},{4,5},{5,4},{6,7},{7,6},{8,9},{9,8},{10,11... | collective-permute-start | bytes 6291464 | tf_op jit(solution)/shard_map/ppermute | solution.py:105
  376.0 86.3 %collective-permute-start.6 = (bf16[256,4096]{1,0:T(8,128)(2,1)}, bf16[256,4096]{1,0:T(8,128)(2,1)S(1)}, u32[]{:S(2)}, u32[]{:S(2)}) collective-permute-start(bf16[256,4096]{1,0:T(8,128)(2,1)} %collective-permute-done.2), channel_id=1, source_target_pairs={{0,1},{1,0},{2,3},{3,2},{4,5},{5,4},{6,7},{7,6},{8,9},{9,8},{10,11... | collective-permute-start | bytes 6291464 | tf_op jit(solution)/shard_map/ppermute | solution.py:105
  381.9 80.4 %copy-start.3 = (bf16[1024,4096]{1,0:T(8,128)(2,1)}, bf16[1024,4096]{1,0:T(8,128)(2,1)S(1)}, u32[]{:S(2)}) copy-start(bf16[1024,4096]{1,0:T(8,128)(2,1)S(1)} %constant_dynamic-update-slice_fusion) | copy-start | bytes 25165828
  546.4 1.3 copy-start
  593.3 17.1 %copy-start.12 = (s32[8,256]{1,0:T(8,128)S(1)}, s32[8,256]{1,0:T(8,128)}, u32[]{:S(2)}) copy-start(s32[8,256]{1,0:T(8,128)} %get-tuple-element.24) | copy-start | bytes 24580
  610.4 5.9 copy-start.1
  610.4 5.9 copy-start.8
  610.4 5.9 copy-start.11
  610.4 5.9 copy-start.13
  610.5 12.7 %slice-start.4 = ((s8[12582912]{0:T(1024)(128)(4,1)}), s8[4194304]{0:T(1024)(128)(4,1)S(1)}, s32[]{:S(2)}) async-start(s8[12582912]{0:T(1024)(128)(4,1)} %bitcast.261), calls=%async_computation.7 | async-start | bytes 8388608
  616.4 6.8 copy-start.7
  616.4 6.8 copy-start.10
  616.4 6.8 slice-start.5
  616.4 6.8 slice-start.6
  616.4 17.1 %slice-start = ((s8[16777216]{0:T(1024)(128)(4,1)}), s8[4194304]{0:T(1024)(128)(4,1)S(1)}, s32[]{:S(2)}) async-start(s8[16777216]{0:T(1024)(128)(4,1)} %bitcast.259), calls=%async_computation.3 | async-start | bytes 8388608
  616.4 17.1 %slice-start.1 = ((s8[16777216]{0:T(1024)(128)(4,1)}), s8[4194304]{0:T(1024)(128)(4,1)S(1)}, s32[]{:S(2)}) async-start(s8[16777216]{0:T(1024)(128)(4,1)} %bitcast.259), calls=%async_computation.4 | async-start | bytes 8388608
  623.2 10.3 %copy-start.6 = (s32[4096]{0:T(1024)S(1)}, s32[4096]{0:T(1024)}, u32[]{:S(2)}) copy-start(s32[4096]{0:T(1024)} %iota_multiply_fusion) | copy-start | bytes 49156
  623.2 10.3 %copy-start.9 = (s32[8,256]{1,0:T(8,128)S(1)}, s32[8,256]{1,0:T(8,128)}, u32[]{:S(2)}) copy-start(s32[8,256]{1,0:T(8,128)} %get-tuple-element.27) | copy-start | bytes 24580
  623.2 10.3 %slice-start.2 = ((s8[16777216]{0:T(1024)(128)(4,1)}), s8[4194304]{0:T(1024)(128)(4,1)S(1)}, s32[]{:S(2)}) async-start(s8[16777216]{0:T(1024)(128)(4,1)} %bitcast.259), calls=%async_computation.5 | async-start | bytes 8388608
  623.2 10.3 %slice-start.3 = ((s8[16777216]{0:T(1024)(128)(4,1)}), s8[4194304]{0:T(1024)(128)(4,1)S(1)}, s32[]{:S(2)}) async-start(s8[16777216]{0:T(1024)(128)(4,1)} %bitcast.259), calls=%async_computation.6 | async-start | bytes 8388608
Sparse Core Ops, SparseCore 0:
  166.5 200.0 all-gather.3
  521.3 23.3 all-gather.5

commit v15 on v14

--- a/solution.py
+++ b/solution.py
@@ -87,7 +87,6 @@
         received.append(lax.ppermute(outgoing, "cg", perm))
     by_shift = jnp.stack(received, axis=0)
     back = (g - jnp.arange(n_g, dtype=jnp.int32)) % n_g
-    mine = jnp.take(by_shift, back, axis=0)
     if lax.axis_size("fsdp") == 2:
         pieces = []
         halves = [activations]
@@ -113,8 +112,9 @@
         grp_rows = lax.all_gather(jnp.concatenate(own_half, axis=0), "fsdp", axis=1, tiled=True)
         split_rows = None
 
-    every = lax.all_gather(mine, "ct", axis=0, tiled=False)
-    every = every.transpose(1, 0, 2, 3).reshape(n_g * n_t * d_rows, qcols + 2 * HD)
+    every = lax.all_gather(by_shift, "ct", axis=0, tiled=False)
+    every = jnp.take(every.transpose(1, 0, 2, 3), back, axis=0)
+    every = every.reshape(n_g * n_t * d_rows, qcols + 2 * HD)
 
     if split_rows is None:
         mixed = jnp.dot(grp_rows, every, preferred_element_type=jnp.float32)

time: 716 us -> 747 us (1.043)
  local copies, waits for them, and re-layouts: 63.8 us -> 121 us
  starting transfers between devices: 85.1 us -> 59.8 us
  waiting for transfers between devices: 327 us -> 305 us
  other arithmetic: 49.4 us -> 63.3 us
    ppermute x1, starting transfers between devices: 71 us -> 1.66 us  [shards(): from_left = lax.ppermute(activations, 'cg', right)]
    gather x1 -> x19, local copies, waits for them, and re-layouts: 5.65 us -> 55.9 us  [shards(): mine = jnp.take(by_shift, back, axis=0)]
    ppermute x1, waiting for transfers between devices: 78.4 us -> 34.8 us  [shards(): halves += [from_left, lax.ppermute(from_left, 'cg', right), from_right]]
    ppermute x1, starting transfers between devices: 2.74 us -> 44.4 us  [shards(): halves += [from_left, lax.ppermute(from_left, 'cg', right), from_right]]
    ppermute x3, waiting for transfers between devices: 80.7 us -> 106 us  [shards(): received.append(lax.ppermute(outgoing, 'cg', perm))]
    select_n x2 -> x3, other arithmetic: 5.49 us -> 18.7 us  [shards(): every = jnp.take(every.transpose(1, 0, 2, 3), back, axis=0)]
    unnamed x53 -> x43, local copies, waits for them, and re-layouts: 21.5 us -> 32 us
    all_gather x1 -> x0, local copies, waits for them, and re-layouts: 10.1 us -> none  [shards(): every = lax.all_gather(mine, 'ct', axis=0, tiled=False)]
  transfers between devices with their start and end apart: 12 -> 12, of which waited for: 8 -> 8; matrix products, arithmetic and copies ran while one was open for 6% -> 7% of each run, Pallas kernels for 0% -> 0%
where the time goes in v15:
time: 747 us; the launch traced here: 739 us
  waiting for transfers between devices  305 us (41%)
  local copies, waits for them, and re-layouts  121 us (16%)
  matrix products  121 us (16%)
  other arithmetic  63.3 us (8%)
  starting transfers between devices  59.8 us (8%)
  blocking collectives  53 us (7%)
  between operations  16.2 us (2%)
    ppermute x3, waiting for transfers between devices, shards(): received.append(lax.ppermute(outgoing, 'cg', perm))  106 us
    ppermute x3, waiting for transfers between devices, shards(): lax.ppermute(half, 'fsdp', [(0, 1), (1, 0)])  76.3 us
    all_to_all x1, blocking collectives, shards(): lax.all_to_all(out_rows, 'cg', split_axis=0, concat_axis=2, tiled=True)  53 us
    ppermute x1, waiting for transfers between devices, shards(): from_left = lax.ppermute(activations, 'cg', right)  46.6 us
    ppermute x1, starting transfers between devices, shards(): halves += [from_left, lax.ppermute(from_left, 'cg', right), from_right]  44.4 us
    dot_general x4, matrix products, shards(): jnp.einsum('hqk,ke->hqe', dropped, all_values[:span], preferred_element_t...  40.4 us
    sub x3, matrix products, shards(): weights = jnp.where(visible, jnp.exp(scores - highest), 0.0)  37.7 us
    ppermute x1, waiting for transfers between devices, shards(): halves += [from_left, lax.ppermute(from_left, 'cg', right), from_right]  34.8 us
  transfers between devices with their start and end apart: 12, of which 8 were waited for; matrix products, arithmetic and copies ran while one was open for 7% of the time, Pallas kernels for 0%

profile of v15, /device:TPU:0, one launch (start us, length us, event | category | flops | bytes accessed | tf_op | source)
XLA Modules:
  0.0 739.5 jit_solution(16773772976338741412)
XLA Ops:
  6.5 3.0 collective-permute-start.3
  12.0 6.5 copy.50
  18.5 5.2 pad_maximum_fusion
  23.7 31.7 %collective-permute-done.3 = bf16[256,4096]{1,0:T(8,128)(2,1)} collective-permute-done((bf16[256,4096]{1,0:T(8,128)(2,1)}, bf16[256,4096]{1,0:T(8,128)(2,1)}, u32[]{:S(2)}, u32[]{:S(2)}) %collective-permute-start.3) | collective-permute-done | bytes 2097184 | tf_op jit(solution)/shard_map/ppermute | solution.py:81
  55.4 2.0 constant_dynamic-slice_fusion.5
  57.5 2.4 copy.56
  59.9 3.8 collective-permute-start.9
  63.7 2.4 copy.55
  69.2 24.1 %collective-permute-done.9 = bf16[512,1280]{1,0:T(8,128)(2,1)} collective-permute-done((bf16[512,1280]{1,0:T(8,128)(2,1)}, bf16[512,1280]{1,0:T(8,128)(2,1)}, u32[]{:S(2)}, u32[]{:S(2)}) %collective-permute-start.9) | collective-permute-done | bytes 1310752 | tf_op jit(solution)/shard_map/ppermute | solution.py:87
  93.3 82.0 %collective-permute-done.8 = bf16[512,1280]{1,0:T(8,128)(2,1)} collective-permute-done((bf16[512,1280]{1,0:T(8,128)(2,1)}, bf16[512,1280]{1,0:T(8,128)(2,1)}, u32[]{:S(2)}, u32[]{:S(2)}) %collective-permute-start.8) | collective-permute-done | bytes 1310752 | tf_op jit(solution)/shard_map/ppermute | solution.py:87
  175.3 5.2 pad_maximum_fusion.1
  180.7 1.7 collective-permute-start
  182.3 2.2 collective-permute-start.2
  184.6 46.6 %collective-permute-done = bf16[256,4096]{1,0:T(8,128)(2,1)} collective-permute-done((bf16[256,4096]{1,0:T(8,128)(2,1)S(1)}, bf16[256,4096]{1,0:T(8,128)(2,1)}, u32[]{:S(2)}, u32[]{:S(2)}) %collective-permute-start) | collective-permute-done | bytes 2097184 | tf_op jit(solution)/shard_map/ppermute | solution.py:96
  231.2 44.4 %collective-permute-start.1 = (bf16[256,4096]{1,0:T(8,128)(2,1)}, bf16[256,4096]{1,0:T(8,128)(2,1)}, u32[]{:S(2)}, u32[]{:S(2)}) collective-permute-start(bf16[256,4096]{1,0:T(8,128)(2,1)} %collective-permute-done), channel_id=1, source_target_pairs={{0,8},{8,16},{16,24},{24,0},{1,9},{9,17},{17,25},{25,1},{2,10},{10... | collective-permute-start | bytes 6291464 | tf_op jit(solution)/shard_map/ppermute | solution.py:98
  281.7 1.6 collective-permute-start.4
  283.3 34.8 %collective-permute-done.1 = bf16[256,4096]{1,0:T(8,128)(2,1)} collective-permute-done((bf16[256,4096]{1,0:T(8,128)(2,1)}, bf16[256,4096]{1,0:T(8,128)(2,1)}, u32[]{:S(2)}, u32[]{:S(2)}) %collective-permute-start.1) | collective-permute-done | bytes 2097184 | tf_op jit(solution)/shard_map/ppermute | solution.py:98
  318.1 1.5 collective-permute-start.5
  319.6 3.1 constant_dynamic-update-slice_fusion.7
  323.3 1.7 constant_dynamic-update-slice_fusion.2
  325.0 1.7 constant_dynamic-update-slice_fusion.1
  326.7 1.7 constant_dynamic-update-slice_fusion
  328.5 1.6 constant_dynamic-update-slice_fusion.6
  330.1 36.8 %collective-permute-done.5 = bf16[256,4096]{1,0:T(8,128)(2,1)S(1)} collective-permute-done((bf16[256,4096]{1,0:T(8,128)(2,1)}, bf16[256,4096]{1,0:T(8,128)(2,1)S(1)}, u32[]{:S(2)}, u32[]{:S(2)}) %collective-permute-start.5) | collective-permute-done | bytes 2097184 | tf_op jit(solution)/shard_map/ppermute | solution.py:104
  366.9 1.5 constant_dynamic-update-slice_fusion.5
  368.4 39.5 %collective-permute-done.6 = bf16[256,4096]{1,0:T(8,128)(2,1)S(1)} collective-permute-done((bf16[256,4096]{1,0:T(8,128)(2,1)}, bf16[256,4096]{1,0:T(8,128)(2,1)S(1)}, u32[]{:S(2)}, u32[]{:S(2)}) %collective-permute-start.6) | collective-permute-done | bytes 2097184 | tf_op jit(solution)/shard_map/ppermute | solution.py:104
  407.9 1.5 constant_dynamic-update-slice_fusion.4
  409.5 4.5 mini-gather-slice.5
  414.0 11.8 %fusion.145 = (bf16[4,4,512,512]{3,2,0,1:T(8,128)(2,1)}, bf16[4,4,512,512]{3,2,0,1:T(8,128)(2,1)}) fusion(bf16[4,4,512,1280]{3,2,0,1:T(8,128)(2,1)} %bitcast.241), kind=kLoop, calls=%fused_computation.274 | loop fusion | bytes 33554432 | tf_op jit(solution)/shard_map/jit(_take)/gather | solution.py:116
  425.8 4.2 broadcast.676.clone
  429.9 17.8 %while.3 = (s32[]{:T(128)}, bf16[4,4,512,512]{3,2,0,1:T(8,128)(2,1)}, s32[4,1]{0,1:T(1,128)S(1)}, bf16[4,4,512,512]{3,2,1,0:T(8,128)(2,1)}, s32[]{:T(128)}) while((s32[]{:T(128)}, bf16[4,4,512,512]{3,2,0,1:T(8,128)(2,1)}, s32[4,1]{0,1:T(1,128)S(1)}, bf16[4,4,512,512]{3,2,1,0:T(8,128)(2,1)}, s32[]{:T(128)}) %tuple.59), condition=%wide.while_cond.1, body=%wide.while_body.1.sunk | while | flops 2 | bytes 4194901 | solution.py:116
  430.6 3.8 bitcast_dynamic-update-slice_fusion.5
  435.0 3.8 bitcast_dynamic-update-slice_fusion.5
  439.5 3.7 bitcast_dynamic-update-slice_fusion.5
  443.9 3.9 bitcast_dynamic-update-slice_fusion.5
  447.8 4.1 broadcast.676.clone.1
  451.9 16.8 %while.2 = (s32[]{:T(128)}, bf16[4,4,512,512]{3,2,0,1:T(8,128)(2,1)}, s32[4,1]{0,1:T(1,128)S(1)}, bf16[4,4,512,512]{3,2,1,0:T(8,128)(2,1)}, s32[]{:T(128)}) while((s32[]{:T(128)}, bf16[4,4,512,512]{3,2,0,1:T(8,128)(2,1)}, s32[4,1]{0,1:T(1,128)S(1)}, bf16[4,4,512,512]{3,2,1,0:T(8,128)(2,1)}, s32[]{:T(128)}) %tuple.69), condition=%wide.while_cond, body=%wide.while_body.sunk | while | flops 2 | bytes 4194901 | solution.py:116
  452.5 3.6 bitcast_dynamic-update-slice_fusion.4
  456.7 3.6 bitcast_dynamic-update-slice_fusion.4
  460.9 3.6 bitcast_dynamic-update-slice_fusion.4
  465.1 3.7 bitcast_dynamic-update-slice_fusion.4
  468.7 4.9 gather_fusion.1
  473.7 18.7 %maximum_select_fusion = bf16[4,4,512,1280]{3,2,1,0:T(8,128)(2,1)} fusion(bf16[4,4,512,256]{3,2,1,0:T(8,128)(2,1)} %gather_fusion.1, bf16[4,4,512,512]{3,2,1,0:T(8,128)(2,1)} %get-tuple-element.25, bf16[4,4,512,512]{3,2,1,0:T(8,128)(2,1)} %get-tuple-element.17, pred[4]{0:T(512)(128)(4,1)S(1)} %compare_and_fusion), kind=kLoop, calls=%fused_computation.43 | loop fusion | flops 73400320 | bytes 41943044 | tf_op jit(solution)/shard_map/jit(_take)/select_n | solution.py:116
  492.4 12.5 %fusion.144 = (bf16[2,4,512,1280]{3,2,1,0:T(8,128)(2,1)S(1)}, bf16[2,4,512,1280]{3,2,1,0:T(8,128)(2,1)}) fusion(bf16[4,4,512,1280]{3,2,1,0:T(8,128)(2,1)} %maximum_select_fusion), kind=kLoop, calls=%fused_computation.273 | loop fusion | bytes 41943040 | tf_op jit(solution)/shard_map/slice | solution.py:125
  504.8 18.2 %fusion.44 = f32[1024,1280]{1,0:T(8,128)} fusion(bf16[4096,1280]{1,0:T(8,128)(2,1)} %bitcast.244, bf16[1024,4096]{1,0:T(8,128)(2,1)} %constant_dynamic-update-slice_fusion.4, bf16[1024,4096]{1,0:T(8,128)(2,1)} %copy-done.3, pred[]{:T(512)S(6)} %eq.13), kind=kOutput, calls=%fused_computation.77 | convolution fusion | flops 10741612544 | bytes 32505856 | tf_op jit(solution)/shard_map/dot_general | solution.py:125
  523.0 16.1 %fusion.54 = f32[1024,1280]{1,0:T(8,128)} fusion(f32[1024,1280]{1,0:T(8,128)} %fusion.44, bf16[4096,1280]{1,0:T(8,128)(2,1)S(1)} %bitcast.243, bf16[1024,4096]{1,0:T(8,128)(2,1)} %copy-done.3, bf16[1024,4096]{1,0:T(8,128)(2,1)} %constant_dynamic-update-slice_fusion.4, pred[]{:T(512)S(6)} %eq.13), kind=kOutput, calls=%fused_computation.89 | convolution fusion | flops 10742923264 | bytes 37748736 | tf_op jit(solution)/shard_map/dot_general | solution.py:125
  540.2 4.2 multiply_cosine_fusion
  549.6 2.5 slice_bitcast_fusion
  553.1 1.8 subtract_convert_fusion
  556.1 2.1 gather_fusion
  558.2 1.9 copy_select_fusion
  560.1 9.5 %all-gather.7.cloned.1.call-done = bf16[4096,2,128]{2,0,1:T(8,128)(2,1)} async-done(((bf16[1024,2,128]{2,0,1:T(8,128)(2,1)}), bf16[4096,2,128]{2,0,1:T(8,128)(2,1)}) %all-gather.7.cloned.1.call-update) | async-done | bytes 2097168 | tf_op jit(solution)/shard_map/all_gather | solution.py:143
  569.6 1.7 copy.59
  572.7 8.1 %fusion.73 = f32[2048,256,8]{1,0,2:T(8,128)} fusion(bf16[4,256,8,128]{3,1,2,0:T(8,128)(2,1)S(1)} %copy_select_fusion, bf16[4096,2,128]{2,0,1:T(8,128)(2,1)S(1)} %bitcast.249), kind=kOutput, calls=%fused_computation.127 | convolution fusion | flops 1073741824 | bytes 17825792 | tf_op jit(solution)/shard_map/qhe,ke->hqk/dot_general | solution.py:159
  580.8 17.1 %fusion.146 = (f32[8,256]{1,0:T(8,128)S(1)}, bf16[8,256,4096]{1,2,0:T(8,128)(2,1)}) fusion(pred[256,4096]{0,1:T(8,128)(4,1)S(1)} %iota_compare_fusion, bf16[4096,2,128]{2,0,1:T(8,128)(2,1)} %bitcast.250, bf16[4,256,8,128]{3,1,2,0:T(8,128)(2,1)S(1)} %copy_select_fusion), kind=kOutput, calls=%fused_computation.275 | convolution fusion | flops 4353691648 | bytes 22028288 | tf_op jit(solution)/shard_map/sub | solution.py:169
  597.9 14.1 %fusion.147 = (f32[8,256]{1,0:T(8,128)S(1)}, bf16[8,256,3072]{1,2,0:T(8,128)(2,1)}) fusion(pred[256,3072]{0,1:T(8,128)(4,1)} %iota_compare_fusion.1, bf16[4096,2,128]{2,0,1:T(8,128)(2,1)} %bitcast.251, bf16[4,256,8,128]{3,1,2,0:T(8,128)(2,1)S(1)} %copy_select_fusion), kind=kOutput, calls=%fused_computation.276 | convolution fusion | flops 3265268736 | bytes 16785408 | tf_op jit(solution)/shard_map/sub | solution.py:169
  612.1 16.9 %fusion.148 = (f32[8,256]{1,0:T(8,128)S(1)}, bf16[8,256,2048]{1,2,0:T(8,128)(2,1)}) fusion(f32[2048,256,8]{1,0,2:T(8,128)} %fusion.73, pred[256,2048]{0,1:T(8,128)(4,1)S(1)} %copy-done.4), kind=kOutput, calls=%fused_computation.277 | output fusion | flops 29362176 | bytes 25698304 | tf_op jit(solution)/shard_map/sub | solution.py:169
  629.0 6.5 fusion.149
  635.5 16.9 %divide_convert_fusion = bf16[256,8,128]{0,2,1:T(8,128)(2,1)S(1)} fusion(bf16[4096,2,128]{2,0,1:T(8,128)(2,1)} %bitcast.253, bf16[8,256,4096]{1,2,0:T(8,128)(2,1)} %get-tuple-element.89, s32[4096]{0:T(1024)S(1)} %iota_multiply_fusion, s32[8,256]{1,0:T(8,128)S(1)} %copy-done.11, f32[256,8]{0,1:T(8,128)S(1)} %multiply_bitcast_fusion), kind=kOutput, calls=%fused_computation.112 | convolution fusion | flops 2248671232 | bytes 18382848 | tf_op jit(solution)/shard_map/hqk,ke->hqe/dot_general | solution.py:175
  652.5 13.3 %divide_convert_fusion.1 = bf16[256,8,128]{0,2,1:T(8,128)(2,1)S(1)} fusion(bf16[8,256,3072]{1,2,0:T(8,128)(2,1)} %get-tuple-element.91, s32[3072]{0:T(1024)S(1)} %copy-done.6, s32[8,256]{1,0:T(8,128)S(1)} %copy-done.10, bf16[4096,2,128]{2,0,1:T(8,128)(2,1)S(1)} %bitcast.254, f32[256,8]{0,1:T(8,128)S(1)} %multiply_bitcast_fusion.1), kind=kOutput, calls=%fused_computation.113 | convolution fusion | flops 1686634496 | bytes 13922304 | tf_op jit(solution)/shard_map/hqk,ke->hqe/dot_general | solution.py:175
  665.8 6.7 divide_convert_fusion.2
  672.6 3.5 divide_convert_fusion.3
  676.3 53.0 %all_to_all.15 = bf16[4,256,1024]{1,2,0:T(8,128)(2,1)S(1)} all-to-all(bf16[4,256,1024]{1,2,0:T(8,128)(2,1)S(1)} %pad_maximum_fusion.3), channel_id=1, replica_groups=mesh['cg'=4,'ct'=4,'fsdp'=2] {'cg'}, dimensions={0} | all-to-all | bytes 4194304 | tf_op jit(solution)/shard_map/all_to_all | solution.py:181
  729.3 2.8 copy.82
  (88 shorter events, 25.2 us)
Async XLA Ops:
  6.5 402.9 %all-gather.5.cloned.1.call-start = ((), (), s32[]{:S(2)}) async-start(), calls=%async_computation.1 | async-start | bytes 26214400 | tf_op jit(solution)/shard_map/all_gather | solution.py:115
  6.5 48.9 %collective-permute-start.3 = (bf16[256,4096]{1,0:T(8,128)(2,1)}, bf16[256,4096]{1,0:T(8,128)(2,1)}, u32[]{:S(2)}, u32[]{:S(2)}) collective-permute-start(bf16[256,4096]{1,0:T(8,128)(2,1)} %param.9), channel_id=1, source_target_pairs={{0,1},{1,0},{2,3},{3,2},{4,5},{5,4},{6,7},{7,6},{8,9},{9,8},{10,11... | collective-permute-start | bytes 6291464 | tf_op jit(solution)/shard_map/ppermute | solution.py:81
  59.9 33.5 %collective-permute-start.9 = (bf16[512,1280]{1,0:T(8,128)(2,1)}, bf16[512,1280]{1,0:T(8,128)(2,1)}, u32[]{:S(2)}, u32[]{:S(2)}) collective-permute-start(bf16[512,1280]{1,0:T(8,128)(2,1)} %bitcast.260), channel_id=1, source_target_pairs={{0,24},{8,0},{16,8},{24,16},{1,25},{9,1},{17,9},{25,17},{2,26},{10... | collective-permute-start | bytes 3932168 | tf_op jit(solution)/shard_map/ppermute | solution.py:87
  66.1 109.2 %collective-permute-start.8 = (bf16[512,1280]{1,0:T(8,128)(2,1)}, bf16[512,1280]{1,0:T(8,128)(2,1)}, u32[]{:S(2)}, u32[]{:S(2)}) collective-permute-start(bf16[512,1280]{1,0:T(8,128)(2,1)} %bitcast.261), channel_id=1, source_target_pairs={{0,16},{8,24},{16,0},{24,8},{1,17},{9,25},{17,1},{25,9},{2,18},{10... | collective-permute-start | bytes 3932168 | tf_op jit(solution)/shard_map/ppermute | solution.py:87
  67.6 107.8 %collective-permute-start.7 = (bf16[512,1280]{1,0:T(8,128)(2,1)}, bf16[512,1280]{1,0:T(8,128)(2,1)}, u32[]{:S(2)}, u32[]{:S(2)}) collective-permute-start(bf16[512,1280]{1,0:T(8,128)(2,1)} %bitcast.262), channel_id=1, source_target_pairs={{0,8},{8,16},{16,24},{24,0},{1,9},{9,17},{17,25},{25,1},{2,10},{10... | collective-permute-start | bytes 3932168 | tf_op jit(solution)/shard_map/ppermute | solution.py:87
  69.2 111.4 %copy-start.2 = (bf16[256,4096]{1,0:T(8,128)(2,1)S(1)}, bf16[256,4096]{1,0:T(8,128)(2,1)}, u32[]{:S(2)}) copy-start(bf16[256,4096]{1,0:T(8,128)(2,1)} %param.9) | copy-start | bytes 6291460
  180.6 389.0 %all-gather.7.cloned.1.call-start = ((), (), s32[]{:S(2)}) async-start(), calls=%async_computation.2 | async-start | bytes 2621440 | tf_op jit(solution)/shard_map/all_gather | solution.py:143
  180.7 50.6 %collective-permute-start = (bf16[256,4096]{1,0:T(8,128)(2,1)S(1)}, bf16[256,4096]{1,0:T(8,128)(2,1)}, u32[]{:S(2)}, u32[]{:S(2)}) collective-permute-start(bf16[256,4096]{1,0:T(8,128)(2,1)S(1)} %copy-done.2), channel_id=1, source_target_pairs={{0,8},{8,16},{16,24},{24,0},{1,9},{9,17},{17,25},{25,1},{2,10},{10... | collective-permute-start | bytes 6291464 | tf_op jit(solution)/shard_map/ppermute | solution.py:96
  182.3 140.4 %collective-permute-start.2 = (bf16[256,4096]{1,0:T(8,128)(2,1)S(1)}, bf16[256,4096]{1,0:T(8,128)(2,1)}, u32[]{:S(2)}, u32[]{:S(2)}) collective-permute-start(bf16[256,4096]{1,0:T(8,128)(2,1)S(1)} %copy-done.2), channel_id=1, source_target_pairs={{0,24},{8,0},{16,8},{24,16},{1,25},{9,1},{17,9},{25,17},{2,26},{10... | collective-permute-start | bytes 6291464 | tf_op jit(solution)/shard_map/ppermute | solution.py:97
  231.2 86.9 %collective-permute-start.1 = (bf16[256,4096]{1,0:T(8,128)(2,1)}, bf16[256,4096]{1,0:T(8,128)(2,1)}, u32[]{:S(2)}, u32[]{:S(2)}) collective-permute-start(bf16[256,4096]{1,0:T(8,128)(2,1)} %collective-permute-done), channel_id=1, source_target_pairs={{0,8},{8,16},{16,24},{24,0},{1,9},{9,17},{17,25},{25,1},{2,10},{10... | collective-permute-start | bytes 6291464 | tf_op jit(solution)/shard_map/ppermute | solution.py:98
  281.7 46.8 %collective-permute-start.4 = (bf16[256,4096]{1,0:T(8,128)(2,1)}, bf16[256,4096]{1,0:T(8,128)(2,1)S(1)}, u32[]{:S(2)}, u32[]{:S(2)}) collective-permute-start(bf16[256,4096]{1,0:T(8,128)(2,1)} %collective-permute-done), channel_id=1, source_target_pairs={{0,1},{1,0},{2,3},{3,2},{4,5},{5,4},{6,7},{7,6},{8,9},{9,8},{10,11... | collective-permute-start | bytes 6291464 | tf_op jit(solution)/shard_map/ppermute | solution.py:104
  318.1 48.8 %collective-permute-start.5 = (bf16[256,4096]{1,0:T(8,128)(2,1)}, bf16[256,4096]{1,0:T(8,128)(2,1)S(1)}, u32[]{:S(2)}, u32[]{:S(2)}) collective-permute-start(bf16[256,4096]{1,0:T(8,128)(2,1)} %collective-permute-done.1), channel_id=1, source_target_pairs={{0,1},{1,0},{2,3},{3,2},{4,5},{5,4},{6,7},{7,6},{8,9},{9,8},{10,11... | collective-permute-start | bytes 6291464 | tf_op jit(solution)/shard_map/ppermute | solution.py:104
  322.8 85.2 %collective-permute-start.6 = (bf16[256,4096]{1,0:T(8,128)(2,1)}, bf16[256,4096]{1,0:T(8,128)(2,1)S(1)}, u32[]{:S(2)}, u32[]{:S(2)}) collective-permute-start(bf16[256,4096]{1,0:T(8,128)(2,1)} %collective-permute-done.2), channel_id=1, source_target_pairs={{0,1},{1,0},{2,3},{3,2},{4,5},{5,4},{6,7},{7,6},{8,9},{9,8},{10,11... | collective-permute-start | bytes 6291464 | tf_op jit(solution)/shard_map/ppermute | solution.py:104
  328.5 79.5 %copy-start.3 = (bf16[1024,4096]{1,0:T(8,128)(2,1)}, bf16[1024,4096]{1,0:T(8,128)(2,1)S(1)}, u32[]{:S(2)}) copy-start(bf16[1024,4096]{1,0:T(8,128)(2,1)S(1)} %constant_dynamic-update-slice_fusion) | copy-start | bytes 25165828
  571.4 1.3 copy-start
  597.9 14.1 %copy-start.4 = (pred[256,2048]{0,1:T(8,128)(4,1)S(1)}, pred[256,2048]{0,1:T(8,128)(4,1)}, u32[]{:S(2)}) copy-start(pred[256,2048]{0,1:T(8,128)(4,1)} %iota_compare_fusion.2) | copy-start | bytes 1572868
  612.1 16.9 %copy-start.5 = (pred[256,1024]{0,1:T(8,128)(4,1)S(1)}, pred[256,1024]{0,1:T(8,128)(4,1)}, u32[]{:S(2)}) copy-start(pred[256,1024]{0,1:T(8,128)(4,1)} %iota_compare_fusion.3) | copy-start | bytes 786436
  629.0 6.5 copy-start.11
  635.5 16.9 %copy-start.1 = (bf16[4,4,256,2,128]{4,2,1,0,3:T(8,128)(2,1)S(1)}, bf16[4,4,256,2,128]{4,2,1,0,3:T(8,128)(2,1)}, u32[]{:S(2)}) copy-start(bf16[4,4,256,2,128]{4,2,1,0,3:T(8,128)(2,1)} %copy-done) | copy-start | bytes 6291460
  635.5 16.9 %copy-start.6 = (s32[3072]{0:T(1024)S(1)}, s32[3072]{0:T(1024)}, u32[]{:S(2)}) copy-start(s32[3072]{0:T(1024)} %iota_multiply_fusion.1) | copy-start | bytes 36868
  635.5 16.9 %copy-start.10 = (s32[8,256]{1,0:T(8,128)S(1)}, s32[8,256]{1,0:T(8,128)}, u32[]{:S(2)}) copy-start(s32[8,256]{1,0:T(8,128)} %get-tuple-element.84) | copy-start | bytes 24580
  652.4 13.3 %copy-start.7 = (s32[2048]{0:T(1024)S(1)}, s32[2048]{0:T(1024)}, u32[]{:S(2)}) copy-start(s32[2048]{0:T(1024)} %iota_multiply_fusion.2) | copy-start | bytes 24580
  652.4 13.3 %copy-start.9 = (s32[8,256]{1,0:T(8,128)S(1)}, s32[8,256]{1,0:T(8,128)}, u32[]{:S(2)}) copy-start(s32[8,256]{1,0:T(8,128)} %get-tuple-element.83) | copy-start | bytes 24580
  652.5 13.3 %copy-start.13 = (bf16[8,256,2048]{1,2,0:T(8,128)(2,1)S(1)}, bf16[8,256,2048]{1,2,0:T(8,128)(2,1)}, u32[]{:S(2)}) copy-start(bf16[8,256,2048]{1,2,0:T(8,128)(2,1)} %get-tuple-element.93) | copy-start | bytes 25165828
  665.8 6.8 copy-start.8
  665.8 6.8 copy-start.12
  665.8 6.8 copy-start.14
Sparse Core Ops, SparseCore 0:
  180.7 132.7 all-gather.4
  547.0 22.6 all-gather.6

commit v16 on v13

--- a/solution.py
+++ b/solution.py
@@ -178,8 +178,13 @@
         result = (attended / (summed * (1.0 - drop_rate))[:, :, None]).astype(jnp.bfloat16)
         pieces.append(result.transpose(1, 0, 2).reshape(tok, qcols))
     out_rows = jnp.stack(pieces, axis=0)
-    returned = lax.all_to_all(out_rows, "cg", split_axis=0, concat_axis=2, tiled=True)
-    return returned.reshape(tok, n_g * qcols)
+    arrived = [lax.dynamic_index_in_dim(out_rows, g, 0, keepdims=False)]
+    for shift in range(1, n_g):
+        outgoing = lax.dynamic_index_in_dim(out_rows, (g + shift) % n_g, 0, keepdims=False)
+        perm = [(i, (i + shift) % n_g) for i in range(n_g)]
+        arrived.append(lax.ppermute(outgoing, "cg", perm))
+    returned = jnp.take(jnp.stack(arrived, axis=0), back, axis=0)
+    return returned.transpose(1, 0, 2).reshape(tok, n_g * qcols)
 
 
 def solution(mesh):

time: 652 us -> 652 us (level)
  blocking collectives: 53 us -> 0 us
  waiting for transfers between devices: 229 us -> 273 us
    all_to_all x1 -> x0, blocking collectives: 53 us -> none  [shards(): lax.all_to_all(out_rows, 'cg', split_axis=0, concat_axis=2, tiled=True)]
    ppermute x0 -> x3, waiting for transfers between devices: none -> 44.3 us  [shards(): arrived.append(lax.ppermute(outgoing, 'cg', perm))]
    gather x16 -> x17, local copies, waits for them, and re-layouts: 35.3 us -> 37.5 us
    select_n x3 -> x1, other arithmetic: 18.7 us -> 18.7 us  [shards(): every = jnp.take(every, back, axis=1).transpose(1, 0, 2, 3)]
    unnamed x33 -> x39, local copies, waits for them, and re-layouts: 22 us -> 22 us
  transfers between devices with their start and end apart: 12 -> 15, of which waited for: 6 -> 8; matrix products, arithmetic and copies ran while one was open for 22% -> 22% of each run, Pallas kernels for 0% -> 0%
where the time goes in v16:
time: 652 us; the launch traced here: 646 us
  waiting for transfers between devices  273 us (42%)
  matrix products  129 us (20%)
  local copies, waits for them, and re-layouts  98.6 us (15%)
  other arithmetic  65 us (10%)
  starting transfers between devices  64.5 us (10%)
  between operations  16.2 us (2%)
    ppermute x3, waiting for transfers between devices, shards(): received.append(lax.ppermute(outgoing, 'cg', perm))  106 us
    ppermute x1, waiting for transfers between devices, shards(): from_left = lax.ppermute(activations, 'cg', right)  44.9 us
    ppermute x1, starting transfers between devices, shards(): halves += [from_left, lax.ppermute(from_left, 'cg', right), from_right]  44.7 us
    ppermute x3, waiting for transfers between devices, shards(): arrived.append(lax.ppermute(outgoing, 'cg', perm))  44.3 us
    dot_general x4, matrix products, shards(): jnp.einsum('hqk,ke->hqe', dropped, all_values[:span], preferred_element_t...  40.4 us
    sub x3, matrix products, shards(): weights = jnp.where(visible, jnp.exp(scores - highest), 0.0)  37.1 us
    ppermute x1, waiting for transfers between devices, shards(): halves += [from_left, lax.ppermute(from_left, 'cg', right), from_right]  36.1 us
    gather x16, local copies, waits for them, and re-layouts  35.3 us
  transfers between devices with their start and end apart: 15, of which 8 were waited for; matrix products, arithmetic and copies ran while one was open for 22% of the time, Pallas kernels for 0%

profile of v16, /device:TPU:0, one launch (start us, length us, event | category | flops | bytes accessed | tf_op | source)
XLA Modules:
  0.0 646.5 jit_solution(2907644710924375699)
XLA Ops:
  6.5 3.0 collective-permute-start.3
  9.5 1.3 copy.48
  10.8 1.3 copy.47
  12.0 6.5 %copy.46 = bf16[512,4096]{0,1:T(8,128)(2,1)} copy(bf16[512,4096]{1,0:T(8,128)(2,1)} %param.10) | data formatting | bytes 8388608 | tf_op args[1]
  18.5 5.2 pad_maximum_fusion
  23.7 31.7 %collective-permute-done.3 = bf16[256,4096]{1,0:T(8,128)(2,1)} collective-permute-done((bf16[256,4096]{1,0:T(8,128)(2,1)}, bf16[256,4096]{1,0:T(8,128)(2,1)}, u32[]{:S(2)}, u32[]{:S(2)}) %collective-permute-start.3) | collective-permute-done | bytes 2097184 | tf_op jit(solution)/shard_map/ppermute | solution.py:81
  55.4 2.0 constant_dynamic-slice_fusion.6
  57.4 2.4 copy.52
  59.9 3.8 collective-permute-start.6
  63.7 2.4 copy.51
  66.1 1.5 copy.50
  69.2 24.1 %collective-permute-done.6 = bf16[512,1280]{1,0:T(8,128)(2,1)} collective-permute-done((bf16[512,1280]{1,0:T(8,128)(2,1)}, bf16[512,1280]{1,0:T(8,128)(2,1)}, u32[]{:S(2)}, u32[]{:S(2)}) %collective-permute-start.6) | collective-permute-done | bytes 1310752 | tf_op jit(solution)/shard_map/ppermute | solution.py:87
  93.3 82.0 %collective-permute-done.5 = bf16[512,1280]{1,0:T(8,128)(2,1)} collective-permute-done((bf16[512,1280]{1,0:T(8,128)(2,1)}, bf16[512,1280]{1,0:T(8,128)(2,1)}, u32[]{:S(2)}, u32[]{:S(2)}) %collective-permute-start.5) | collective-permute-done | bytes 1310752 | tf_op jit(solution)/shard_map/ppermute | solution.py:87
  175.3 5.2 pad_maximum_fusion.1
  180.6 1.7 collective-permute-start
  182.3 2.2 collective-permute-start.2
  186.5 44.9 %collective-permute-done = bf16[256,4096]{1,0:T(8,128)(2,1)} collective-permute-done((bf16[256,4096]{1,0:T(8,128)(2,1)}, bf16[256,4096]{1,0:T(8,128)(2,1)}, u32[]{:S(2)}, u32[]{:S(2)}) %collective-permute-start) | collective-permute-done | bytes 2097184 | tf_op jit(solution)/shard_map/ppermute | solution.py:96
  231.4 44.7 %collective-permute-start.1 = (bf16[256,4096]{1,0:T(8,128)(2,1)}, bf16[256,4096]{1,0:T(8,128)(2,1)}, u32[]{:S(2)}, u32[]{:S(2)}) collective-permute-start(bf16[256,4096]{1,0:T(8,128)(2,1)} %collective-permute-done), channel_id=1, source_target_pairs={{0,8},{8,16},{16,24},{24,0},{1,9},{9,17},{17,25},{25,1},{2,10},{10... | collective-permute-start | bytes 6291464 | tf_op jit(solution)/shard_map/ppermute | solution.py:98
  280.2 1.5 collective-permute-start.7
  282.2 36.1 %collective-permute-done.1 = bf16[256,4096]{1,0:T(8,128)(2,1)} collective-permute-done((bf16[256,4096]{1,0:T(8,128)(2,1)}, bf16[256,4096]{1,0:T(8,128)(2,1)}, u32[]{:S(2)}, u32[]{:S(2)}) %collective-permute-start.1) | collective-permute-done | bytes 2097184 | tf_op jit(solution)/shard_map/ppermute | solution.py:98
  318.3 1.5 collective-permute-start.8
  319.8 4.6 mini-gather-slice.5
  324.4 11.5 %fusion.164 = (bf16[4,4,512,512]{3,2,1,0:T(8,128)(2,1)}, bf16[4,4,512,512]{3,2,1,0:T(8,128)(2,1)}) fusion(bf16[4,4,512,1280]{3,2,1,0:T(8,128)(2,1)} %bitcast.258), kind=kLoop, calls=%fused_computation.290 | loop fusion | bytes 33554432 | tf_op jit(solution)/shard_map/jit(_take)/gather | solution.py:116
  335.8 4.0 broadcast.694.clone
  339.8 17.7 %while.3 = (s32[]{:T(128)}, bf16[4,4,512,512]{3,2,1,0:T(8,128)(2,1)}, s32[4,1]{0,1:T(1,128)S(1)}, bf16[4,4,512,512]{3,2,1,0:T(8,128)(2,1)}, s32[]{:T(128)}) while((s32[]{:T(128)}, bf16[4,4,512,512]{3,2,1,0:T(8,128)(2,1)}, s32[4,1]{0,1:T(1,128)S(1)}, bf16[4,4,512,512]{3,2,1,0:T(8,128)(2,1)}, s32[]{:T(128)}) %tuple.55), condition=%wide.while_cond.1, body=%wide.while_body.1.sunk | while | flops 2 | bytes 4194901 | solution.py:116
  340.5 3.7 bitcast_dynamic-update-slice_fusion.5
  344.9 3.8 bitcast_dynamic-update-slice_fusion.5
  349.3 3.8 bitcast_dynamic-update-slice_fusion.5
  353.8 3.7 bitcast_dynamic-update-slice_fusion.5
  357.5 4.2 broadcast.694.clone.1
  361.7 17.7 %while.2 = (s32[]{:T(128)}, bf16[4,4,512,512]{3,2,1,0:T(8,128)(2,1)}, s32[4,1]{0,1:T(1,128)S(1)}, bf16[4,4,512,512]{3,2,1,0:T(8,128)(2,1)}, s32[]{:T(128)}) while((s32[]{:T(128)}, bf16[4,4,512,512]{3,2,1,0:T(8,128)(2,1)}, s32[4,1]{0,1:T(1,128)S(1)}, bf16[4,4,512,512]{3,2,1,0:T(8,128)(2,1)}, s32[]{:T(128)}) %tuple.65), condition=%wide.while_cond, body=%wide.while_body.sunk | while | flops 2 | bytes 4194901 | solution.py:116
  362.4 3.7 bitcast_dynamic-update-slice_fusion.4
  366.8 3.7 bitcast_dynamic-update-slice_fusion.4
  371.2 3.7 bitcast_dynamic-update-slice_fusion.4
  375.6 3.8 bitcast_dynamic-update-slice_fusion.4
  379.4 5.0 gather_fusion.2
  384.4 18.7 %maximum_select_fusion = bf16[4,4,512,1280]{3,2,0,1:T(8,128)(2,1)} fusion(bf16[4,4,512,256]{3,2,0,1:T(8,128)(2,1)} %bitcast.262, bf16[4,4,512,512]{3,2,0,1:T(8,128)(2,1)} %bitcast.256, bf16[4,4,512,512]{3,2,0,1:T(8,128)(2,1)} %bitcast.255, pred[4]{0:T(512)(128)(4,1)S(1)} %compare_and_fusion), kind=kLoop, calls=%fused_computation.44 | loop fusion | flops 73400320 | bytes 41943044 | tf_op jit(solution)/shard_map/jit(_take)/select_n | solution.py:116
  403.0 21.3 %fusion.38 = f32[1024,1280]{1,0:T(8,128)} fusion(bf16[2,4096,1280]{2,1,0:T(8,128)(2,1)} %bitcast.259, s32[]{:T(128)S(6)} %select_n.193, bf16[256,4096]{1,0:T(8,128)(2,1)} %collective-permute-done.2, bf16[256,4096]{1,0:T(8,128)(2,1)} %collective-permute-done.1, bf16[256,4096]{1,0:T(8,128)(2,1)} %collective-permute-done, bf16[256,4096]{1,0:T(8,128)(2,1)} %param.9), kind=kOutput, calls=%fused_computation.69 | convolution fusion | flops 10770972672 | bytes 24117252 | tf_op jit(solution)/shard_map/dot_general | solution.py:125
  424.4 22.5 %fusion.72 = f32[1024,1280]{1,0:T(8,128)} fusion(f32[1024,1280]{1,0:T(8,128)} %fusion.38, bf16[2,4096,1280]{2,1,0:T(8,128)(2,1)} %bitcast.260, s32[]{:T(128)S(6)} %select_n.194, bf16[256,4096]{1,0:T(8,128)(2,1)} %collective-permute-done.9, bf16[256,4096]{1,0:T(8,128)(2,1)} %collective-permute-done.8, bf16[256,4096]{1,0:T(8,128)(2,1)} %collective-permute-done.7, ...), kind=kOutput, calls=%fused_computation.112 | convolution fusion | flops 10772283392 | bytes 29360132 | tf_op jit(solution)/shard_map/dot_general | solution.py:125
  447.9 3.8 multiply_cosine_fusion
  454.7 1.4 iota_compare_fusion.1
  456.8 2.5 slice_bitcast_fusion
  460.3 2.0 subtract_convert_fusion
  462.3 1.2 pad_maximum_fusion.2
  463.5 2.1 gather_fusion
  465.6 1.9 copy_select_fusion
  467.5 9.7 %all-gather.7.cloned.1.call-done = bf16[4096,2,128]{2,0,1:T(8,128)(2,1)} async-done(((bf16[1024,2,128]{2,0,1:T(8,128)(2,1)}), bf16[4096,2,128]{2,0,1:T(8,128)(2,1)}) %all-gather.7.cloned.1.call-update) | async-done | bytes 2097168 | tf_op jit(solution)/shard_map/all_gather | solution.py:143
  477.2 1.7 copy.53
  478.9 1.3 copy-done
  480.3 8.1 %fusion.89 = f32[2048,256,8]{1,0,2:T(8,128)} fusion(bf16[4,256,8,128]{3,1,2,0:T(8,128)(2,1)S(1)} %copy_select_fusion, bf16[4096,2,128]{2,0,1:T(8,128)(2,1)S(1)} %bitcast.267), kind=kOutput, calls=%fused_computation.144 | convolution fusion | flops 1073741824 | bytes 17825792 | tf_op jit(solution)/shard_map/qhe,ke->hqk/dot_general | solution.py:159
  488.3 16.9 %fusion.165 = (f32[8,256]{1,0:T(8,128)S(1)}, bf16[8,256,4096]{1,2,0:T(8,128)(2,1)}) fusion(pred[256,4096]{0,1:T(8,128)(4,1)S(1)} %iota_compare_fusion, bf16[4096,2,128]{2,0,1:T(8,128)(2,1)} %bitcast.268, bf16[4,256,8,128]{3,1,2,0:T(8,128)(2,1)S(1)} %copy_select_fusion), kind=kOutput, calls=%fused_computation.291 | convolution fusion | flops 4353691648 | bytes 22028288 | tf_op jit(solution)/shard_map/sub | solution.py:169
  505.2 13.9 %fusion.166 = (f32[8,256]{1,0:T(8,128)S(1)}, bf16[8,256,3072]{1,2,0:T(8,128)(2,1)}) fusion(pred[256,3072]{0,1:T(8,128)(4,1)} %iota_compare_fusion.1, bf16[4096,2,128]{2,0,1:T(8,128)(2,1)} %bitcast.269, bf16[4,256,8,128]{3,1,2,0:T(8,128)(2,1)S(1)} %copy_select_fusion), kind=kOutput, calls=%fused_computation.292 | convolution fusion | flops 3265268736 | bytes 16785408 | tf_op jit(solution)/shard_map/sub | solution.py:169
  519.1 16.8 %fusion.167 = (f32[8,256]{1,0:T(8,128)S(1)}, bf16[8,256,2048]{1,2,0:T(8,128)(2,1)}) fusion(f32[2048,256,8]{1,0,2:T(8,128)} %fusion.89, pred[256,2048]{0,1:T(8,128)(4,1)S(1)} %copy-done.2), kind=kOutput, calls=%fused_computation.293 | output fusion | flops 29362176 | bytes 25698304 | tf_op jit(solution)/shard_map/sub | solution.py:169
  535.9 6.4 fusion.168
  542.3 16.9 %divide_convert_fusion = bf16[256,8,128]{0,2,1:T(8,128)(2,1)S(1)} fusion(bf16[4096,2,128]{2,0,1:T(8,128)(2,1)} %bitcast.271, bf16[8,256,4096]{1,2,0:T(8,128)(2,1)} %get-tuple-element.67, s32[4096]{0:T(1024)S(1)} %iota_multiply_fusion, s32[8,256]{1,0:T(8,128)S(1)} %copy-done.9, f32[256,8]{0,1:T(8,128)S(1)} %multiply_bitcast_fusion), kind=kOutput, calls=%fused_computation.129 | convolution fusion | flops 2248671232 | bytes 18382848 | tf_op jit(solution)/shard_map/hqk,ke->hqe/dot_general | solution.py:175
  559.3 13.3 %divide_convert_fusion.1 = bf16[256,8,128]{0,2,1:T(8,128)(2,1)S(1)} fusion(bf16[8,256,3072]{1,2,0:T(8,128)(2,1)} %get-tuple-element.69, s32[3072]{0:T(1024)S(1)} %copy-done.4, s32[8,256]{1,0:T(8,128)S(1)} %copy-done.8, bf16[4096,2,128]{2,0,1:T(8,128)(2,1)S(1)} %bitcast.272, f32[256,8]{0,1:T(8,128)S(1)} %multiply_bitcast_fusion.1), kind=kOutput, calls=%fused_computation.130 | convolution fusion | flops 1686634496 | bytes 13922304 | tf_op jit(solution)/shard_map/hqk,ke->hqe/dot_general | solution.py:175
  572.6 6.7 %divide_convert_fusion.2 = bf16[256,8,128]{0,2,1:T(8,128)(2,1)S(1)} fusion(bf16[8,256,2048]{1,2,0:T(8,128)(2,1)S(1)} %copy-done.14, s32[2048]{0:T(1024)S(1)} %copy-done.5, s32[8,256]{1,0:T(8,128)S(1)} %copy-done.7, bf16[4096,2,128]{2,0,1:T(8,128)(2,1)S(1)} %bitcast.273, f32[256,8]{0,1:T(8,128)S(1)} %multiply_bitcast_fusion.2), kind=kOutput, calls=%fused_computation.131 | convolution fusion | flops 1124597760 | bytes 9461760 | tf_op jit(solution)/shard_map/hqk,ke->hqe/dot_general | solution.py:175
  579.4 3.5 divide_convert_fusion.3
  583.3 3.4 collective-permute-start.12
  587.8 11.3 %collective-permute-done.12 = bf16[256,1024]{0,1:T(8,128)(2,1)S(1)} collective-permute-done((bf16[256,1024]{0,1:T(8,128)(2,1)S(1)}, bf16[256,1024]{0,1:T(8,128)(2,1)S(1)}, u32[]{:S(2)}, u32[]{:S(2)}) %collective-permute-start.12) | collective-permute-done | bytes 524320 | tf_op jit(solution)/shard_map/ppermute | solution.py:185
  599.1 33.0 %collective-permute-done.11 = bf16[256,1024]{0,1:T(8,128)(2,1)S(1)} collective-permute-done((bf16[256,1024]{0,1:T(8,128)(2,1)S(1)}, bf16[256,1024]{0,1:T(8,128)(2,1)S(1)}, u32[]{:S(2)}, u32[]{:S(2)}) %collective-permute-start.11) | collective-permute-done | bytes 524320 | tf_op jit(solution)/shard_map/ppermute | solution.py:185
  632.4 2.1 gather_fusion.1
  634.5 1.9 broadcast_select_fusion
  636.3 2.9 copy.76
  (90 shorter events, 19.1 us)
Async XLA Ops:
  6.5 313.3 %all-gather.5.cloned.1.call-start = ((), (), s32[]{:S(2)}) async-start(), calls=%async_computation | async-start | bytes 26214400 | tf_op jit(solution)/shard_map/all_gather | solution.py:115
  6.5 48.9 %collective-permute-start.3 = (bf16[256,4096]{1,0:T(8,128)(2,1)}, bf16[256,4096]{1,0:T(8,128)(2,1)}, u32[]{:S(2)}, u32[]{:S(2)}) collective-permute-start(bf16[256,4096]{1,0:T(8,128)(2,1)} %param.9), channel_id=1, source_target_pairs={{0,1},{1,0},{2,3},{3,2},{4,5},{5,4},{6,7},{7,6},{8,9},{9,8},{10,11... | collective-permute-start | bytes 6291464 | tf_op jit(solution)/shard_map/ppermute | solution.py:81
  59.9 33.5 %collective-permute-start.6 = (bf16[512,1280]{1,0:T(8,128)(2,1)}, bf16[512,1280]{1,0:T(8,128)(2,1)}, u32[]{:S(2)}, u32[]{:S(2)}) collective-permute-start(bf16[512,1280]{1,0:T(8,128)(2,1)} %bitcast.278), channel_id=1, source_target_pairs={{0,24},{8,0},{16,8},{24,16},{1,25},{9,1},{17,9},{25,17},{2,26},{10... | collective-permute-start | bytes 3932168 | tf_op jit(solution)/shard_map/ppermute | solution.py:87
  66.1 109.2 %collective-permute-start.5 = (bf16[512,1280]{1,0:T(8,128)(2,1)}, bf16[512,1280]{1,0:T(8,128)(2,1)}, u32[]{:S(2)}, u32[]{:S(2)}) collective-permute-start(bf16[512,1280]{1,0:T(8,128)(2,1)} %bitcast.279), channel_id=1, source_target_pairs={{0,16},{8,24},{16,0},{24,8},{1,17},{9,25},{17,1},{25,9},{2,18},{10... | collective-permute-start | bytes 3932168 | tf_op jit(solution)/shard_map/ppermute | solution.py:87
  67.6 107.8 %collective-permute-start.4 = (bf16[512,1280]{1,0:T(8,128)(2,1)}, bf16[512,1280]{1,0:T(8,128)(2,1)}, u32[]{:S(2)}, u32[]{:S(2)}) collective-permute-start(bf16[512,1280]{1,0:T(8,128)(2,1)} %bitcast.280), channel_id=1, source_target_pairs={{0,8},{8,16},{16,24},{24,0},{1,9},{9,17},{17,25},{25,1},{2,10},{10... | collective-permute-start | bytes 3932168 | tf_op jit(solution)/shard_map/ppermute | solution.py:87
  180.6 296.6 %all-gather.7.cloned.1.call-start = ((), (), s32[]{:S(2)}) async-start(), calls=%async_computation.1 | async-start | bytes 2621440 | tf_op jit(solution)/shard_map/all_gather | solution.py:143
  180.6 50.8 %collective-permute-start = (bf16[256,4096]{1,0:T(8,128)(2,1)}, bf16[256,4096]{1,0:T(8,128)(2,1)}, u32[]{:S(2)}, u32[]{:S(2)}) collective-permute-start(bf16[256,4096]{1,0:T(8,128)(2,1)} %param.9), channel_id=1, source_target_pairs={{0,8},{8,16},{16,24},{24,0},{1,9},{9,17},{17,25},{25,1},{2,10},{10... | collective-permute-start | bytes 6291464 | tf_op jit(solution)/shard_map/ppermute | solution.py:96
  182.3 99.4 %collective-permute-start.2 = (bf16[256,4096]{1,0:T(8,128)(2,1)}, bf16[256,4096]{1,0:T(8,128)(2,1)}, u32[]{:S(2)}, u32[]{:S(2)}) collective-permute-start(bf16[256,4096]{1,0:T(8,128)(2,1)} %param.9), channel_id=1, source_target_pairs={{0,24},{8,0},{16,8},{24,16},{1,25},{9,1},{17,9},{25,17},{2,26},{10... | collective-permute-start | bytes 6291464 | tf_op jit(solution)/shard_map/ppermute | solution.py:97
  231.4 86.9 %collective-permute-start.1 = (bf16[256,4096]{1,0:T(8,128)(2,1)}, bf16[256,4096]{1,0:T(8,128)(2,1)}, u32[]{:S(2)}, u32[]{:S(2)}) collective-permute-start(bf16[256,4096]{1,0:T(8,128)(2,1)} %collective-permute-done), channel_id=1, source_target_pairs={{0,8},{8,16},{16,24},{24,0},{1,9},{9,17},{17,25},{25,1},{2,10},{10... | collective-permute-start | bytes 6291464 | tf_op jit(solution)/shard_map/ppermute | solution.py:98
  276.1 189.5 %copy-start.10 = (pred[4]{0:T(512)(128)(4,1)}, pred[4]{0:T(512)(128)(4,1)S(1)}, u32[]{:S(2)}) copy-start(pred[4]{0:T(512)(128)(4,1)S(1)} %compare_and_fusion) | copy-start | bytes 16
  276.3 187.2 %copy-start.12 = (s32[1024]{0:T(1024)}, s32[1024]{0:T(1024)S(1)}, u32[]{:S(2)}) copy-start(s32[1024]{0:T(1024)S(1)} %pad_clamp_fusion.1) | copy-start | bytes 12292
  280.2 144.2 %collective-permute-start.7 = (bf16[256,4096]{1,0:T(8,128)(2,1)}, bf16[256,4096]{1,0:T(8,128)(2,1)}, u32[]{:S(2)}, u32[]{:S(2)}) collective-permute-start(bf16[256,4096]{1,0:T(8,128)(2,1)} %collective-permute-done), channel_id=1, source_target_pairs={{0,1},{1,0},{2,3},{3,2},{4,5},{5,4},{6,7},{7,6},{8,9},{9,8},{10,11... | collective-permute-start | bytes 6291464 | tf_op jit(solution)/shard_map/ppermute | solution.py:104
  281.7 142.6 %collective-permute-start.9 = (bf16[256,4096]{1,0:T(8,128)(2,1)}, bf16[256,4096]{1,0:T(8,128)(2,1)}, u32[]{:S(2)}, u32[]{:S(2)}) collective-permute-start(bf16[256,4096]{1,0:T(8,128)(2,1)} %collective-permute-done.2), channel_id=1, source_target_pairs={{0,1},{1,0},{2,3},{3,2},{4,5},{5,4},{6,7},{7,6},{8,9},{9,8},{10,11... | collective-permute-start | bytes 6291464 | tf_op jit(solution)/shard_map/ppermute | solution.py:104
  318.3 106.1 %collective-permute-start.8 = (bf16[256,4096]{1,0:T(8,128)(2,1)}, bf16[256,4096]{1,0:T(8,128)(2,1)}, u32[]{:S(2)}, u32[]{:S(2)}) collective-permute-start(bf16[256,4096]{1,0:T(8,128)(2,1)} %collective-permute-done.1), channel_id=1, source_target_pairs={{0,1},{1,0},{2,3},{3,2},{4,5},{5,4},{6,7},{7,6},{8,9},{9,8},{10,11... | collective-permute-start | bytes 6291464 | tf_op jit(solution)/shard_map/ppermute | solution.py:104
  478.9 1.3 copy-start
  505.2 13.9 %copy-start.2 = (pred[256,2048]{0,1:T(8,128)(4,1)S(1)}, pred[256,2048]{0,1:T(8,128)(4,1)}, u32[]{:S(2)}) copy-start(pred[256,2048]{0,1:T(8,128)(4,1)} %iota_compare_fusion.2) | copy-start | bytes 1572868
  519.1 16.8 %copy-start.3 = (pred[256,1024]{0,1:T(8,128)(4,1)S(1)}, pred[256,1024]{0,1:T(8,128)(4,1)}, u32[]{:S(2)}) copy-start(pred[256,1024]{0,1:T(8,128)(4,1)} %iota_compare_fusion.3) | copy-start | bytes 786436
  535.9 6.4 copy-start.9
  542.3 16.9 %copy-start.1 = (bf16[4,4,256,2,128]{4,2,1,0,3:T(8,128)(2,1)S(1)}, bf16[4,4,256,2,128]{4,2,1,0,3:T(8,128)(2,1)}, u32[]{:S(2)}) copy-start(bf16[4,4,256,2,128]{4,2,1,0,3:T(8,128)(2,1)} %copy-done) | copy-start | bytes 6291460
  542.3 16.9 %copy-start.4 = (s32[3072]{0:T(1024)S(1)}, s32[3072]{0:T(1024)}, u32[]{:S(2)}) copy-start(s32[3072]{0:T(1024)} %iota_multiply_fusion.1) | copy-start | bytes 36868
  542.3 16.9 %copy-start.8 = (s32[8,256]{1,0:T(8,128)S(1)}, s32[8,256]{1,0:T(8,128)}, u32[]{:S(2)}) copy-start(s32[8,256]{1,0:T(8,128)} %get-tuple-element.62) | copy-start | bytes 24580
  559.3 13.3 %copy-start.5 = (s32[2048]{0:T(1024)S(1)}, s32[2048]{0:T(1024)}, u32[]{:S(2)}) copy-start(s32[2048]{0:T(1024)} %iota_multiply_fusion.2) | copy-start | bytes 24580
  559.3 13.3 %copy-start.7 = (s32[8,256]{1,0:T(8,128)S(1)}, s32[8,256]{1,0:T(8,128)}, u32[]{:S(2)}) copy-start(s32[8,256]{1,0:T(8,128)} %get-tuple-element.61) | copy-start | bytes 24580
  559.3 13.3 %copy-start.14 = (bf16[8,256,2048]{1,2,0:T(8,128)(2,1)S(1)}, bf16[8,256,2048]{1,2,0:T(8,128)(2,1)}, u32[]{:S(2)}) copy-start(bf16[8,256,2048]{1,2,0:T(8,128)(2,1)} %get-tuple-element.71) | copy-start | bytes 25165828
  572.6 6.8 %copy-start.6 = (s32[8,256]{1,0:T(8,128)S(1)}, s32[8,256]{1,0:T(8,128)}, u32[]{:S(2)}) copy-start(s32[8,256]{1,0:T(8,128)} %get-tuple-element.60) | copy-start | bytes 24580
  572.6 6.8 %copy-start.13 = (s32[1024]{0:T(1024)S(1)}, s32[1024]{0:T(1024)}, u32[]{:S(2)}) copy-start(s32[1024]{0:T(1024)} %iota_multiply_fusion.3) | copy-start | bytes 12292
  572.6 6.8 %copy-start.15 = (bf16[8,256,1024]{1,2,0:T(8,128)(2,1)S(1)}, bf16[8,256,1024]{1,2,0:T(8,128)(2,1)}, u32[]{:S(2)}) copy-start(bf16[8,256,1024]{1,2,0:T(8,128)(2,1)} %get-tuple-element.73) | copy-start | bytes 12582916
  582.9 51.6 %copy-start.11 = (pred[4]{0:T(512)(128)(4,1)S(1)}, pred[4]{0:T(512)(128)(4,1)}, u32[]{:S(2)}) copy-start(pred[4]{0:T(512)(128)(4,1)} %copy-done.10) | copy-start | bytes 16
  583.3 15.8 %collective-permute-start.12 = (bf16[256,1024]{0,1:T(8,128)(2,1)S(1)}, bf16[256,1024]{0,1:T(8,128)(2,1)S(1)}, u32[]{:S(2)}, u32[]{:S(2)}) collective-permute-start(bf16[256,1024]{0,1:T(8,128)(2,1)S(1)} %get-tuple-element.53), channel_id=1, source_target_pairs={{0,24},{8,0},{16,8},{24,16},{1,25},{9,1},{17,9},{25,17},{2,26},{10... | collective-permute-start | bytes 1572872 | tf_op jit(solution)/shard_map/ppermute | solution.py:185
  586.7 45.4 %collective-permute-start.11 = (bf16[256,1024]{0,1:T(8,128)(2,1)S(1)}, bf16[256,1024]{0,1:T(8,128)(2,1)S(1)}, u32[]{:S(2)}, u32[]{:S(2)}) collective-permute-start(bf16[256,1024]{0,1:T(8,128)(2,1)S(1)} %get-tuple-element.54), channel_id=1, source_target_pairs={{0,16},{8,24},{16,0},{24,8},{1,17},{9,25},{17,1},{25,9},{2,18},{10... | collective-permute-start | bytes 1572872 | tf_op jit(solution)/shard_map/ppermute | solution.py:185
  586.7 45.4 %collective-permute-start.10 = (bf16[256,1024]{0,1:T(8,128)(2,1)S(1)}, bf16[256,1024]{0,1:T(8,128)(2,1)S(1)}, u32[]{:S(2)}, u32[]{:S(2)}) collective-permute-start(bf16[256,1024]{0,1:T(8,128)(2,1)S(1)} %get-tuple-element.55), channel_id=1, source_target_pairs={{0,8},{8,16},{16,24},{24,0},{1,9},{9,17},{17,25},{25,1},{2,10},{10... | collective-permute-start | bytes 1572872 | tf_op jit(solution)/shard_map/ppermute | solution.py:185
Sparse Core Ops, SparseCore 0:
  180.7 132.7 all-gather.4
  454.2 22.9 all-gather.6

commit v17 on v13

--- a/solution.py
+++ b/solution.py
@@ -113,7 +113,13 @@
         split_rows = None
 
     every = lax.all_gather(by_shift, "ct", axis=0, tiled=False)
-    every = jnp.take(every, back, axis=1).transpose(1, 0, 2, 3)
+    slots = []
+    for slot in range(n_g):
+        chosen = every[:, 0]
+        for shift in range(1, n_g):
+            chosen = jnp.where(back[slot] == shift, every[:, shift], chosen)
+        slots.append(chosen)
+    every = jnp.stack(slots, axis=0)
     every = every.reshape(n_g * n_t * d_rows, qcols + 2 * HD)
 
     if split_rows is None:

time: 652 us -> 640 us (0.982)
  local copies, waits for them, and re-layouts: 96.2 us -> 36.6 us
  starting transfers between devices: 60 us -> 86 us
  other arithmetic: 62.9 us -> 72.3 us
  waiting for transfers between devices: 229 us -> 237 us
  between operations: 16.2 us -> 24 us
    ppermute x1, starting transfers between devices: 1.66 us -> 70.9 us  [shards(): from_left = lax.ppermute(activations, 'cg', right)]
    gather x19 -> x0, local copies, waits for them, and re-layouts: 56.3 us -> none
    ppermute x1, starting transfers between devices: 44.7 us -> 3.09 us  [shards(): halves += [from_left, lax.ppermute(from_left, 'cg', right), from_right]]
    ppermute x1, waiting for transfers between devices: 0.01 us -> 36.6 us  [shards(): from_right = lax.ppermute(activations, 'cg', left)]
    ppermute x3, waiting for transfers between devices: 106 us -> 80.8 us  [shards(): received.append(lax.ppermute(outgoing, 'cg', perm))]
    another operation x1 -> x2, other arithmetic: 1.97 us -> 15.1 us  [the longest x1 13.1 us: shards(): every = jnp.stack(slots, axis=0)]
    ppermute x1, waiting for transfers between devices: 44.9 us -> 35.8 us  [shards(): from_left = lax.ppermute(activations, 'cg', right)]
    select_n x3 -> x4, other arithmetic: 18.7 us -> 14.6 us  [the longest x3 14.6 us: shards(): chosen = jnp.where(back[slot] == shift, every[:, shift], chosen)]
  transfers between devices with their start and end apart: 12 -> 12, of which waited for: 6 -> 7; matrix products, arithmetic and copies ran while one was open for 22% -> 13% of each run, Pallas kernels for 0% -> 0%
where the time goes in v17:
time: 640 us; the launch traced here: 635 us
  waiting for transfers between devices  237 us (37%)
  matrix products  125 us (20%)
  starting transfers between devices  86 us (13%)
  other arithmetic  72.3 us (11%)
  blocking collectives  53 us (8%)
  local copies, waits for them, and re-layouts  36.6 us (6%)
  between operations  24 us (4%)
    ppermute x3, waiting for transfers between devices, shards(): received.append(lax.ppermute(outgoing, 'cg', perm))  80.8 us
    ppermute x1, starting transfers between devices, shards(): from_left = lax.ppermute(activations, 'cg', right)  70.9 us
    all_to_all x1, blocking collectives, shards(): lax.all_to_all(out_rows, 'cg', split_axis=0, concat_axis=2, tiled=True)  53 us
    ppermute x1, waiting for transfers between devices, shards(): halves += [from_left, lax.ppermute(from_left, 'cg', right), from_right]  41.6 us
    sub x3, matrix products, shards(): weights = jnp.where(visible, jnp.exp(scores - highest), 0.0)  37.4 us
    ppermute x1, waiting for transfers between devices, shards(): from_right = lax.ppermute(activations, 'cg', left)  36.6 us
    dot_general x4, matrix products, shards(): jnp.einsum('hqk,ke->hqe', dropped, all_values[:span], preferred_element_t...  36.4 us
    ppermute x1, waiting for transfers between devices, shards(): from_left = lax.ppermute(activations, 'cg', right)  35.8 us
  transfers between devices with their start and end apart: 12, of which 7 were waited for; matrix products, arithmetic and copies ran while one was open for 13% of the time, Pallas kernels for 0%

profile of v17, /device:TPU:0, one launch (start us, length us, event | category | flops | bytes accessed | tf_op | source)
XLA Modules:
  0.0 634.6 jit_solution(10325797480295757955)
XLA Ops:
  6.5 3.0 collective-permute-start.3
  9.5 6.5 %copy.68 = bf16[512,4096]{0,1:T(8,128)(2,1)} copy(bf16[512,4096]{1,0:T(8,128)(2,1)} %param.10) | data formatting | bytes 8388608 | tf_op args[1]
  16.4 5.2 pad_maximum_fusion.1
  21.7 33.8 %collective-permute-done.3 = bf16[256,4096]{1,0:T(8,128)(2,1)} collective-permute-done((bf16[256,4096]{1,0:T(8,128)(2,1)}, bf16[256,4096]{1,0:T(8,128)(2,1)}, u32[]{:S(2)}, u32[]{:S(2)}) %collective-permute-start.3) | collective-permute-done | bytes 2097184 | tf_op jit(solution)/shard_map/ppermute | solution.py:81
  55.5 2.0 constant_dynamic-slice_fusion.3
  57.5 2.5 copy.73
  59.9 2.8 collective-permute-start.5
  62.7 2.5 copy.74
  65.2 1.3 collective-permute-start.6
  66.5 1.4 copy.72
  68.0 0.7 collective-permute-start.4
  68.7 0.6 copy.71
  69.3 79.2 %collective-permute-done.5 = bf16[512,1280]{1,0:T(8,128)(2,1)} collective-permute-done((bf16[512,1280]{1,0:T(8,128)(2,1)}, bf16[512,1280]{1,0:T(8,128)(2,1)}, u32[]{:S(2)}, u32[]{:S(2)}) %collective-permute-start.5) | collective-permute-done | bytes 1310752 | tf_op jit(solution)/shard_map/ppermute | solution.py:87
  148.4 1.6 collective-permute-done.6
  150.0 5.2 pad_maximum_fusion.2
  155.3 1.5 copy-done.13
  156.9 70.9 %collective-permute-start = (bf16[256,4096]{1,0:T(8,128)(2,1)S(1)}, bf16[256,4096]{1,0:T(8,128)(2,1)}, u32[]{:S(2)}, u32[]{:S(2)}) collective-permute-start(bf16[256,4096]{1,0:T(8,128)(2,1)S(1)} %copy-done.13), channel_id=1, source_target_pairs={{0,8},{8,16},{16,24},{24,0},{1,9},{9,17},{17,25},{25,1},{2,10},{10... | collective-permute-start | bytes 6291464 | tf_op jit(solution)/shard_map/ppermute | solution.py:96
  227.8 0.7 fusion.173
  238.0 35.8 %collective-permute-done = bf16[256,4096]{1,0:T(8,128)(2,1)} collective-permute-done((bf16[256,4096]{1,0:T(8,128)(2,1)S(1)}, bf16[256,4096]{1,0:T(8,128)(2,1)}, u32[]{:S(2)}, u32[]{:S(2)}) %collective-permute-start) | collective-permute-done | bytes 2097184 | tf_op jit(solution)/shard_map/ppermute | solution.py:96
  273.8 3.1 collective-permute-start.1
  277.6 0.6 iota_multiply_fusion.2
  278.2 0.6 iota_multiply_fusion.1
  278.8 0.7 shift-right-logical_xor_fusion.21
  279.7 1.1 iota_compare_fusion.2
  280.8 1.4 collective-permute-start.7
  282.3 36.6 %collective-permute-done.2 = bf16[256,4096]{1,0:T(8,128)(2,1)} collective-permute-done((bf16[256,4096]{1,0:T(8,128)(2,1)S(1)}, bf16[256,4096]{1,0:T(8,128)(2,1)}, u32[]{:S(2)}, u32[]{:S(2)}) %collective-permute-start.2) | collective-permute-done | bytes 2097184 | tf_op jit(solution)/shard_map/ppermute | solution.py:97
  318.8 1.4 collective-permute-start.9
  320.2 41.6 %collective-permute-done.1 = bf16[256,4096]{1,0:T(8,128)(2,1)} collective-permute-done((bf16[256,4096]{1,0:T(8,128)(2,1)}, bf16[256,4096]{1,0:T(8,128)(2,1)}, u32[]{:S(2)}, u32[]{:S(2)}) %collective-permute-start.1) | collective-permute-done | bytes 2097184 | tf_op jit(solution)/shard_map/ppermute | solution.py:98
  361.9 1.3 collective-permute-start.8
  363.2 10.2 %fusion.73 = bf16[1,4,512,1280]{3,2,1,0:T(8,128)(2,1)} fusion(pred[]{:T(512)} %bitcast.21, pred[]{:T(512)} %bitcast.20, pred[]{:T(512)} %bitcast.19, bf16[4,4,512,1280]{3,2,1,0:T(8,128)(2,1)} %bitcast.290), kind=kLoop, calls=%fused_computation.106 | loop fusion | flops 7864320 | bytes 26214404 | tf_op jit(solution)/shard_map/jit(_where)/select_n | solution.py:120
  373.4 4.7 copy-done
  378.1 3.1 select_bitcast_fusion
  381.2 1.3 fusion.70
  382.5 13.1 %pad_maximum_fusion = bf16[4,4,512,1280]{3,2,1,0:T(8,128)(2,1)} fusion(bf16[1,4,512,1280]{3,2,1,0:T(8,128)(2,1)} %select_bitcast_fusion, bf16[1,4,512,1280]{3,2,1,0:T(8,128)(2,1)S(1)} %get-tuple-element.11, bf16[1,4,512,1280]{3,2,1,0:T(8,128)(2,1)} %fusion.73, bf16[1,4,512,1280]{3,2,1,0:T(8,128)(2,1)S(1)} %get-tuple-element.10), kind=kLoop, calls=%fused_computation.38 | loop fusion | flops 31457280 | bytes 41943040 | tf_op jit(solution)/shard_map/stack | solution.py:122
  395.6 21.2 %fusion.38 = f32[1024,1280]{1,0:T(8,128)} fusion(bf16[2,4096,1280]{2,1,0:T(8,128)(2,1)} %bitcast.294, s32[]{:T(128)S(6)} %select_n.363, bf16[256,4096]{1,0:T(8,128)(2,1)} %collective-permute-done.2, bf16[256,4096]{1,0:T(8,128)(2,1)} %collective-permute-done.1, bf16[256,4096]{1,0:T(8,128)(2,1)} %collective-permute-done, bf16[256,4096]{1,0:T(8,128)(2,1)} %param.9), kind=kOutput, calls=%fused_computation.63 | convolution fusion | flops 10770972672 | bytes 24117252 | tf_op jit(solution)/shard_map/dot_general | solution.py:131
  416.9 22.2 %fusion.81 = f32[1024,1280]{1,0:T(8,128)} fusion(f32[1024,1280]{1,0:T(8,128)} %fusion.38, bf16[2,4096,1280]{2,1,0:T(8,128)(2,1)} %bitcast.295, s32[]{:T(128)S(6)} %select_n.364, bf16[256,4096]{1,0:T(8,128)(2,1)} %collective-permute-done.9, bf16[256,4096]{1,0:T(8,128)(2,1)} %collective-permute-done.8, bf16[256,4096]{1,0:T(8,128)(2,1)} %collective-permute-done.7, ...), kind=kOutput, calls=%fused_computation.119 | convolution fusion | flops 10772283392 | bytes 29360132 | tf_op jit(solution)/shard_map/dot_general | solution.py:131
  439.1 1.1 slice.278
  440.1 3.8 multiply_cosine_fusion
  444.1 0.6 gather_fusion.1
  444.7 0.6 gather_fusion.2
  445.4 0.9 pad_maximum_fusion.5
  446.4 0.6 iota_multiply_fusion
  447.0 1.4 iota_compare_fusion.1
  448.4 0.7 iota_compare_fusion
  449.1 2.5 slice_bitcast_fusion
  451.6 1.0 copy.111
  452.6 2.0 subtract_convert_fusion
  454.6 1.2 pad_maximum_fusion.3
  455.8 2.1 gather_fusion
  457.9 1.9 copy_select_fusion
  459.8 8.8 %all-gather.7.cloned.1.call-done = bf16[4096,2,128]{2,0,1:T(8,128)(2,1)} async-done(((bf16[1024,2,128]{2,0,1:T(8,128)(2,1)}), bf16[4096,2,128]{2,0,1:T(8,128)(2,1)}) %all-gather.7.cloned.1.call-update) | async-done | bytes 2097168 | tf_op jit(solution)/shard_map/all_gather | solution.py:149
  468.6 1.7 copy.84
  470.4 1.3 copy-done.1
  471.7 8.1 %fusion.98 = f32[2048,256,8]{1,0,2:T(8,128)} fusion(bf16[4,256,8,128]{3,1,2,0:T(8,128)(2,1)S(1)} %copy_select_fusion, bf16[4096,2,128]{2,0,1:T(8,128)(2,1)S(1)} %bitcast.301), kind=kOutput, calls=%fused_computation.149 | convolution fusion | flops 1073741824 | bytes 17825792 | tf_op jit(solution)/shard_map/qhe,ke->hqk/dot_general | solution.py:165
  479.8 6.4 %fusion.177 = (f32[8,256]{1,0:T(8,128)S(1)}, bf16[8,256,1024]{1,2,0:T(8,128)(2,1)}) fusion(pred[256,1024]{0,1:T(8,128)(4,1)S(1)} %iota_compare_fusion.3, bf16[4,256,8,128]{3,1,2,0:T(8,128)(2,1)S(1)} %copy_select_fusion, bf16[4096,2,128]{2,0,1:T(8,128)(2,1)} %bitcast.302), kind=kOutput, calls=%fused_computation.295 | convolution fusion | flops 1088422912 | bytes 6299648 | tf_op jit(solution)/shard_map/sub | solution.py:175
  486.2 17.2 %fusion.176 = (f32[8,256]{1,0:T(8,128)S(1)}, bf16[8,256,2048]{1,2,0:T(8,128)(2,1)}) fusion(f32[2048,256,8]{1,0,2:T(8,128)} %fusion.98, pred[256,2048]{0,1:T(8,128)(4,1)} %iota_compare_fusion.2), kind=kOutput, calls=%fused_computation.294 | output fusion | flops 29362176 | bytes 25698304 | tf_op jit(solution)/shard_map/sub | solution.py:175
  503.4 13.9 %fusion.175 = (f32[8,256]{1,0:T(8,128)S(1)}, bf16[8,256,3072]{1,2,0:T(8,128)(2,1)}) fusion(pred[256,3072]{0,1:T(8,128)(4,1)} %iota_compare_fusion.1, bf16[4096,2,128]{2,0,1:T(8,128)(2,1)} %bitcast.303, bf16[4,256,8,128]{3,1,2,0:T(8,128)(2,1)S(1)} %copy_select_fusion), kind=kOutput, calls=%fused_computation.293 | convolution fusion | flops 3265268736 | bytes 16785408 | tf_op jit(solution)/shard_map/sub | solution.py:175
  517.4 17.1 %fusion.174 = (f32[8,256]{1,0:T(8,128)S(1)}, bf16[8,256,4096]{1,2,0:T(8,128)(2,1)}) fusion(pred[256,4096]{0,1:T(8,128)(4,1)S(1)} %iota_compare_fusion, bf16[4096,2,128]{2,0,1:T(8,128)(2,1)} %bitcast.304, bf16[4,256,8,128]{3,1,2,0:T(8,128)(2,1)S(1)} %copy_select_fusion), kind=kOutput, calls=%fused_computation.292 | convolution fusion | flops 4353691648 | bytes 22028288 | tf_op jit(solution)/shard_map/sub | solution.py:175
  534.5 5.8 divide_convert_fusion.3
  540.5 6.7 %divide_convert_fusion.2 = bf16[256,8,128]{0,2,1:T(8,128)(2,1)S(1)} fusion(bf16[8,256,2048]{1,2,0:T(8,128)(2,1)S(1)} %copy-done.14, s32[2048]{0:T(1024)S(1)} %copy-done.7, s32[8,256]{1,0:T(8,128)S(1)} %copy-done.10, bf16[4096,2,128]{2,0,1:T(8,128)(2,1)S(1)} %bitcast.306, f32[256,8]{0,1:T(8,128)S(1)} %multiply_bitcast_fusion.2), kind=kOutput, calls=%fused_computation.136 | convolution fusion | flops 1124597760 | bytes 9461760 | tf_op jit(solution)/shard_map/hqk,ke->hqe/dot_general | solution.py:181
  547.3 10.2 %divide_convert_fusion.1 = bf16[256,8,128]{0,2,1:T(8,128)(2,1)S(1)} fusion(bf16[8,256,3072]{1,2,0:T(8,128)(2,1)S(1)} %bitcast.327, s32[3072]{0:T(1024)S(1)} %copy-done.6, s32[8,256]{1,0:T(8,128)S(1)} %copy-done.9, bf16[4096,2,128]{2,0,1:T(8,128)(2,1)S(1)} %bitcast.307, f32[256,8]{0,1:T(8,128)S(1)} %multiply_bitcast_fusion.1), kind=kOutput, calls=%fused_computation.135 | convolution fusion | flops 1686634496 | bytes 13922304 | tf_op jit(solution)/shard_map/hqk,ke->hqe/dot_general | solution.py:181
  557.6 13.6 %divide_convert_fusion = bf16[256,8,128]{0,2,1:T(8,128)(2,1)S(1)} fusion(bf16[4096,2,128]{2,0,1:T(8,128)(2,1)S(1)} %bitcast.308, bf16[8,256,4096]{1,2,0:T(8,128)(2,1)S(1)} %bitcast.325, s32[4096]{0:T(1024)S(1)} %copy-done.5, s32[8,256]{1,0:T(8,128)S(1)} %copy-done.8, f32[256,8]{0,1:T(8,128)S(1)} %multiply_bitcast_fusion), kind=kOutput, calls=%fused_computation.134 | convolution fusion | flops 2248671232 | bytes 18382848 | tf_op jit(solution)/shard_map/hqk,ke->hqe/dot_general | solution.py:181
  571.5 53.0 %all_to_all.15 = bf16[4,256,1024]{1,2,0:T(8,128)(2,1)S(1)} all-to-all(bf16[4,256,1024]{1,2,0:T(8,128)(2,1)S(1)} %pad_maximum_fusion.4), channel_id=1, replica_groups=mesh['cg'=4,'ct'=4,'fsdp'=2] {'cg'}, dimensions={0} | all-to-all | bytes 4194304 | tf_op jit(solution)/shard_map/all_to_all | solution.py:187
  624.4 2.8 copy.107
  (76 shorter events, 2.0 us)
Async XLA Ops:
  6.5 9.4 %copy-start.3 = (bf16[512,512]{1,0:T(8,128)(2,1)S(1)}, bf16[512,512]{1,0:T(8,128)(2,1)}, u32[]{:S(2)}) copy-start(bf16[512,512]{1,0:T(8,128)(2,1)} %param.11) | copy-start | bytes 1572868
  6.5 9.7 %copy-start.4 = (bf16[512,512]{1,0:T(8,128)(2,1)S(1)}, bf16[512,512]{1,0:T(8,128)(2,1)}, u32[]{:S(2)}) copy-start(bf16[512,512]{1,0:T(8,128)(2,1)} %param.12) | copy-start | bytes 1572868
  6.5 356.7 %all-gather.5.cloned.1.call-start = ((), (), s32[]{:S(2)}) async-start(), calls=%async_computation.1 | async-start | bytes 26214400 | tf_op jit(solution)/shard_map/all_gather | solution.py:115
  6.5 48.9 %collective-permute-start.3 = (bf16[256,4096]{1,0:T(8,128)(2,1)}, bf16[256,4096]{1,0:T(8,128)(2,1)}, u32[]{:S(2)}, u32[]{:S(2)}) collective-permute-start(bf16[256,4096]{1,0:T(8,128)(2,1)} %param.9), channel_id=1, source_target_pairs={{0,1},{1,0},{2,3},{3,2},{4,5},{5,4},{6,7},{7,6},{8,9},{9,8},{10,11... | collective-permute-start | bytes 6291464 | tf_op jit(solution)/shard_map/ppermute | solution.py:81
  59.9 88.5 %collective-permute-start.5 = (bf16[512,1280]{1,0:T(8,128)(2,1)}, bf16[512,1280]{1,0:T(8,128)(2,1)}, u32[]{:S(2)}, u32[]{:S(2)}) collective-permute-start(bf16[512,1280]{1,0:T(8,128)(2,1)} %bitcast.312), channel_id=1, source_target_pairs={{0,16},{8,24},{16,0},{24,8},{1,17},{9,25},{17,1},{25,9},{2,18},{10... | collective-permute-start | bytes 3932168 | tf_op jit(solution)/shard_map/ppermute | solution.py:87
  65.2 84.8 %collective-permute-start.6 = (bf16[512,1280]{1,0:T(8,128)(2,1)}, bf16[512,1280]{1,0:T(8,128)(2,1)}, u32[]{:S(2)}, u32[]{:S(2)}) collective-permute-start(bf16[512,1280]{1,0:T(8,128)(2,1)} %bitcast.313), channel_id=1, source_target_pairs={{0,24},{8,0},{16,8},{24,16},{1,25},{9,1},{17,9},{25,17},{2,26},{10... | collective-permute-start | bytes 3932168 | tf_op jit(solution)/shard_map/ppermute | solution.py:87
  68.0 82.1 %collective-permute-start.4 = (bf16[512,1280]{1,0:T(8,128)(2,1)}, bf16[512,1280]{1,0:T(8,128)(2,1)}, u32[]{:S(2)}, u32[]{:S(2)}) collective-permute-start(bf16[512,1280]{1,0:T(8,128)(2,1)} %bitcast.314), channel_id=1, source_target_pairs={{0,8},{8,16},{16,24},{24,0},{1,9},{9,17},{17,25},{25,1},{2,10},{10... | collective-permute-start | bytes 3932168 | tf_op jit(solution)/shard_map/ppermute | solution.py:87
  155.3 1.6 copy-start.13
  155.3 313.3 %all-gather.7.cloned.1.call-start = ((), (), s32[]{:S(2)}) async-start(), calls=%async_computation.2 | async-start | bytes 2621440 | tf_op jit(solution)/shard_map/all_gather | solution.py:149
  156.9 117.0 %collective-permute-start = (bf16[256,4096]{1,0:T(8,128)(2,1)S(1)}, bf16[256,4096]{1,0:T(8,128)(2,1)}, u32[]{:S(2)}, u32[]{:S(2)}) collective-permute-start(bf16[256,4096]{1,0:T(8,128)(2,1)S(1)} %copy-done.13), channel_id=1, source_target_pairs={{0,8},{8,16},{16,24},{24,0},{1,9},{9,17},{17,25},{25,1},{2,10},{10... | collective-permute-start | bytes 6291464 | tf_op jit(solution)/shard_map/ppermute | solution.py:96
  227.7 91.1 %collective-permute-start.2 = (bf16[256,4096]{1,0:T(8,128)(2,1)S(1)}, bf16[256,4096]{1,0:T(8,128)(2,1)}, u32[]{:S(2)}, u32[]{:S(2)}) collective-permute-start(bf16[256,4096]{1,0:T(8,128)(2,1)S(1)} %copy-done.13), channel_id=1, source_target_pairs={{0,24},{8,0},{16,8},{24,16},{1,25},{9,1},{17,9},{25,17},{2,26},{10... | collective-permute-start | bytes 6291464 | tf_op jit(solution)/shard_map/ppermute | solution.py:97
  273.8 88.0 %collective-permute-start.1 = (bf16[256,4096]{1,0:T(8,128)(2,1)}, bf16[256,4096]{1,0:T(8,128)(2,1)}, u32[]{:S(2)}, u32[]{:S(2)}) collective-permute-start(bf16[256,4096]{1,0:T(8,128)(2,1)} %collective-permute-done), channel_id=1, source_target_pairs={{0,8},{8,16},{16,24},{24,0},{1,9},{9,17},{17,25},{25,1},{2,10},{10... | collective-permute-start | bytes 6291464 | tf_op jit(solution)/shard_map/ppermute | solution.py:98
  280.8 136.0 %collective-permute-start.7 = (bf16[256,4096]{1,0:T(8,128)(2,1)}, bf16[256,4096]{1,0:T(8,128)(2,1)}, u32[]{:S(2)}, u32[]{:S(2)}) collective-permute-start(bf16[256,4096]{1,0:T(8,128)(2,1)} %collective-permute-done), channel_id=1, source_target_pairs={{0,1},{1,0},{2,3},{3,2},{4,5},{5,4},{6,7},{7,6},{8,9},{9,8},{10,11... | collective-permute-start | bytes 6291464 | tf_op jit(solution)/shard_map/ppermute | solution.py:104
  318.8 98.0 %collective-permute-start.9 = (bf16[256,4096]{1,0:T(8,128)(2,1)}, bf16[256,4096]{1,0:T(8,128)(2,1)}, u32[]{:S(2)}, u32[]{:S(2)}) collective-permute-start(bf16[256,4096]{1,0:T(8,128)(2,1)} %collective-permute-done.2), channel_id=1, source_target_pairs={{0,1},{1,0},{2,3},{3,2},{4,5},{5,4},{6,7},{7,6},{8,9},{9,8},{10,11... | collective-permute-start | bytes 6291464 | tf_op jit(solution)/shard_map/ppermute | solution.py:104
  361.9 55.0 %collective-permute-start.8 = (bf16[256,4096]{1,0:T(8,128)(2,1)}, bf16[256,4096]{1,0:T(8,128)(2,1)}, u32[]{:S(2)}, u32[]{:S(2)}) collective-permute-start(bf16[256,4096]{1,0:T(8,128)(2,1)} %collective-permute-done.1), channel_id=1, source_target_pairs={{0,1},{1,0},{2,3},{3,2},{4,5},{5,4},{6,7},{7,6},{8,9},{9,8},{10,11... | collective-permute-start | bytes 6291464 | tf_op jit(solution)/shard_map/ppermute | solution.py:104
  363.2 14.9 %copy-start = (bf16[16,512,1280]{2,1,0:T(8,128)(2,1)S(1)}, bf16[16,512,1280]{2,1,0:T(8,128)(2,1)}, u32[]{:S(2)}) copy-start(bf16[16,512,1280]{2,1,0:T(8,128)(2,1)} %all-gather.5.cloned.1.call-done) | copy-start | bytes 62914564
  470.4 1.3 copy-start.1
  517.3 17.1 %copy-start.11 = (s32[8,256]{1,0:T(8,128)S(1)}, s32[8,256]{1,0:T(8,128)}, u32[]{:S(2)}) copy-start(s32[8,256]{1,0:T(8,128)} %get-tuple-element.24) | copy-start | bytes 24580
  517.3 17.1 %copy-start.12 = (s32[1024]{0:T(1024)S(1)}, s32[1024]{0:T(1024)}, u32[]{:S(2)}) copy-start(s32[1024]{0:T(1024)} %iota_multiply_fusion.3) | copy-start | bytes 12292
  534.5 5.9 copy-start.2
  534.5 5.9 copy-start.7
  534.5 5.9 copy-start.10
  534.5 5.9 copy-start.14
  534.5 12.7 %slice-start.4 = ((s8[12582912]{0:T(1024)(128)(4,1)}), s8[4194304]{0:T(1024)(128)(4,1)S(1)}, s32[]{:S(2)}) async-start(s8[12582912]{0:T(1024)(128)(4,1)} %bitcast.326), calls=%async_computation.7 | async-start | bytes 8388608
  540.4 6.8 %copy-start.6 = (s32[3072]{0:T(1024)S(1)}, s32[3072]{0:T(1024)}, u32[]{:S(2)}) copy-start(s32[3072]{0:T(1024)} %iota_multiply_fusion.1) | copy-start | bytes 36868
  540.4 6.8 %copy-start.9 = (s32[8,256]{1,0:T(8,128)S(1)}, s32[8,256]{1,0:T(8,128)}, u32[]{:S(2)}) copy-start(s32[8,256]{1,0:T(8,128)} %get-tuple-element.26) | copy-start | bytes 24580
  540.4 6.8 %slice-start.5 = ((s8[12582912]{0:T(1024)(128)(4,1)}), s8[4194304]{0:T(1024)(128)(4,1)S(1)}, s32[]{:S(2)}) async-start(s8[12582912]{0:T(1024)(128)(4,1)} %bitcast.326), calls=%async_computation.8 | async-start | bytes 8388608
  540.4 6.8 %slice-start.6 = ((s8[12582912]{0:T(1024)(128)(4,1)}), s8[4194304]{0:T(1024)(128)(4,1)S(1)}, s32[]{:S(2)}) async-start(s8[12582912]{0:T(1024)(128)(4,1)} %bitcast.326), calls=%async_computation.9 | async-start | bytes 8388608
  540.4 17.1 %slice-start = ((s8[16777216]{0:T(1024)(128)(4,1)}), s8[4194304]{0:T(1024)(128)(4,1)S(1)}, s32[]{:S(2)}) async-start(s8[16777216]{0:T(1024)(128)(4,1)} %bitcast.324), calls=%async_computation.3 | async-start | bytes 8388608
  540.4 17.1 %slice-start.1 = ((s8[16777216]{0:T(1024)(128)(4,1)}), s8[4194304]{0:T(1024)(128)(4,1)S(1)}, s32[]{:S(2)}) async-start(s8[16777216]{0:T(1024)(128)(4,1)} %bitcast.324), calls=%async_computation.4 | async-start | bytes 8388608
  547.3 10.3 %copy-start.5 = (s32[4096]{0:T(1024)S(1)}, s32[4096]{0:T(1024)}, u32[]{:S(2)}) copy-start(s32[4096]{0:T(1024)} %iota_multiply_fusion) | copy-start | bytes 49156
  547.3 10.3 %copy-start.8 = (s32[8,256]{1,0:T(8,128)S(1)}, s32[8,256]{1,0:T(8,128)}, u32[]{:S(2)}) copy-start(s32[8,256]{1,0:T(8,128)} %get-tuple-element.27) | copy-start | bytes 24580
  547.3 10.3 %slice-start.2 = ((s8[16777216]{0:T(1024)(128)(4,1)}), s8[4194304]{0:T(1024)(128)(4,1)S(1)}, s32[]{:S(2)}) async-start(s8[16777216]{0:T(1024)(128)(4,1)} %bitcast.324), calls=%async_computation.5 | async-start | bytes 8388608
  547.3 10.3 %slice-start.3 = ((s8[16777216]{0:T(1024)(128)(4,1)}), s8[4194304]{0:T(1024)(128)(4,1)S(1)}, s32[]{:S(2)}) async-start(s8[16777216]{0:T(1024)(128)(4,1)} %bitcast.324), calls=%async_computation.6 | async-start | bytes 8388608
Sparse Core Ops, SparseCore 0:
  155.4 200.0 all-gather.4
  446.5 22.1 all-gather.6
